TPU v7x, 512 devices: a whole 4x4x16 slice. The times are simulated.
512 devices in a mesh: lon: 32 (over x_hi, z), lat: 16 (over x_lo, y, core).
Axes of the slice: x: 4 (x_hi: 2, x_lo: 2; x = x_hi * 2 + x_lo), y: 4, z: 16, core: 2. Of those that a mesh axis runs over, the one named last changes fastest.
Arguments:
- surface: float32 [1792, 4096], P('lat', 'lon'), may hold values from -0.25 to 0.25
- momentum_x: float32 [1792, 4096], P('lat', 'lon'), may hold values from -1.2 to 1.2
- momentum_y: float32 [1792, 4096], P('lat', 'lon'), may hold values from -1.2 to 1.2
- water_depth: float32 [1792, 4096], P('lat', 'lon'), may hold values from 0.7 to 1.4
- wet_mask: int32 [1792, 4096], P('lat', 'lon'), may hold values 0 or 1
- slide_cells: int32 [16, 2048], P('lat', 'lon'), may hold values from 0 to 14335
- slide_rate: float32 [16, 2048], P('lat', 'lon'), may hold values from 1 to 4
Outputs:
- surface_next: float32 [1792, 4096], P('lat', 'lon')
- momentum_x_next: float32 [1792, 4096], P('lat', 'lon')
- momentum_y_next: float32 [1792, 4096], P('lat', 'lon')
- velocity_u: float32 [1792, 4096], P('lat', 'lon')
- velocity_v: float32 [1792, 4096], P('lat', 'lon')
Inputs may be any that keep to these rules, and one draw needn't show every extreme that they name: `slide_cells`: entry (r, c) lists a cell of the block of rows r * 112 onward and columns (c // 64) * 128 onward, as row * 128 + column inside that block; cells may repeat.
All inputs are finite; a program needn't handle non-finite values. No bound on the sum of `wet_mask` on one device may be relied on, other than what follows from the above.
Results may differ from a plain program's by a relative error of at most 0.0001.
Values sent between devices are 32-bit elements; how exact they have to be, the bound alone decides.
No kernel may reach another device: no remote copies, remote signals or barrier semaphores. Data moves between devices by JAX's collectives and lax.ppermute only.
A program may use at most 64 MiB of HBM per device.

v0:
```python
import jax
import jax.numpy as jnp
from jax import lax
from jax.sharding import PartitionSpec as P

GRAVITY = 1.0
LON_SPACING = 0.5
LAT_SPACING = 0.6
TIME_STEP = 0.1


def shifted(block, axis, distance):
    devices = range(lax.axis_size(axis))
    route = [((i - distance) % len(devices), i) for i in devices]
    return lax.ppermute(block, axis, route)


def passed_along(x, axis, by):
    peers = lax.axis_size(axis)
    pairs = [(i, i + by) for i in range(peers) if 0 <= i + by < peers]
    return lax.ppermute(x, axis, pairs)


def extended(cells, sides, width, closed):
    for axis, dim in sides:
        count = lax.axis_size(axis)
        ends = count if closed else count - 1
        head = lax.slice_in_dim(cells, 0, width, axis=dim)
        tail = lax.slice_in_dim(cells, cells.shape[dim] - width, cells.shape[dim], axis=dim)
        cells = jnp.concatenate(
            [
                lax.ppermute(tail, axis, [(i, (i + 1) % count) for i in range(ends)]),
                cells,
                lax.ppermute(head, axis, [((i + 1) % count, i) for i in range(ends)]),
            ],
            axis=dim,
        )
    return cells


def slab_of(values, start, stop, along_axis):
    return lax.slice_in_dim(values, start, stop, axis=along_axis)


def limited(former, latter):
    return jnp.maximum(jnp.minimum(former, latter), 0.0) + jnp.minimum(
        jnp.maximum(former, latter), 0.0
    )


def face_states(values, along_axis):
    length = values.shape[along_axis]
    jumps = slab_of(values, 1, length, along_axis) - slab_of(values, 0, length - 1, along_axis)
    slopes = limited(
        slab_of(jumps, 0, length - 2, along_axis), slab_of(jumps, 1, length - 1, along_axis)
    )
    left_state = slab_of(values, 1, length - 2, along_axis) + 0.5 * slab_of(
        slopes, 0, length - 3, along_axis
    )
    right_state = slab_of(values, 2, length - 1, along_axis) - 0.5 * slab_of(
        slopes, 1, length - 2, along_axis
    )
    return (left_state, right_state)


def wave_flux(
    surface_left,
    surface_right,
    normal_left,
    normal_right,
    tangent_left,
    tangent_right,
    face_depth,
    opened,
):
    height_left = surface_left + face_depth
    height_right = surface_right + face_depth
    celerity_left = jnp.sqrt(GRAVITY * height_left)
    celerity_right = jnp.sqrt(GRAVITY * height_right)
    slowest = jnp.minimum(
        jnp.minimum(normal_left - celerity_left, normal_right - celerity_right), 0.0
    )
    fastest = jnp.maximum(
        jnp.maximum(normal_left + celerity_left, normal_right + celerity_right), 0.0
    )
    spread = fastest - slowest
    product = slowest * fastest
    mass_left = height_left * normal_left
    mass_right = height_right * normal_right
    push_left = mass_left * normal_left + GRAVITY * (
        0.5 * surface_left * surface_left + face_depth * surface_left
    )
    push_right = mass_right * normal_right + GRAVITY * (
        0.5 * surface_right * surface_right + face_depth * surface_right
    )
    carry_left = mass_left * tangent_left
    carry_right = mass_right * tangent_right
    mass_flux = (
        opened
        * (fastest * mass_left - slowest * mass_right + product * (surface_right - surface_left))
        / spread
    )
    push_flux = (
        opened
        * (fastest * push_left - slowest * push_right + product * (mass_right - mass_left))
        / spread
    )
    carry_flux = (
        opened
        * (
            fastest * carry_left
            - slowest * carry_right
            + product * (height_right * tangent_right - height_left * tangent_left)
        )
        / spread
    )
    return (mass_flux, push_flux, carry_flux)


def tendencies(across, along):
    width = across[0].shape[1] - 4
    row_count = along[0].shape[0] - 4
    surface_pair = face_states(across[0], 1)
    east_pair = face_states(across[1], 1)
    north_pair = face_states(across[2], 1)
    depth_lon = 0.5 * (across[3][:, 1 : width + 2] + across[3][:, 2 : width + 3])
    open_lon = across[4][:, 1 : width + 2] * across[4][:, 2 : width + 3]
    mass_lon, push_lon, carry_lon = wave_flux(
        surface_pair[0],
        surface_pair[1],
        east_pair[0],
        east_pair[1],
        north_pair[0],
        north_pair[1],
        depth_lon,
        open_lon,
    )
    surface_pair = face_states(along[0], 0)
    east_pair = face_states(along[1], 0)
    north_pair = face_states(along[2], 0)
    depth_lat = 0.5 * (along[3][1 : row_count + 2] + along[3][2 : row_count + 3])
    open_lat = along[4][1 : row_count + 2] * along[4][2 : row_count + 3]
    mass_lat, push_lat, carry_lat = wave_flux(
        surface_pair[0],
        surface_pair[1],
        north_pair[0],
        north_pair[1],
        east_pair[0],
        east_pair[1],
        depth_lat,
        open_lat,
    )
    surface_mid = across[0][:, 2 : width + 2]
    wet_mid = across[4][:, 2 : width + 2]
    rate_surface = (
        -(mass_lon[:, 1:] - mass_lon[:, :-1]) / LON_SPACING
        - (mass_lat[1:] - mass_lat[:-1]) / LAT_SPACING
    )
    source_east = GRAVITY * surface_mid * (depth_lon[:, 1:] - depth_lon[:, :-1]) / LON_SPACING
    source_north = GRAVITY * surface_mid * (depth_lat[1:] - depth_lat[:-1]) / LAT_SPACING
    rate_east = wet_mid * (
        source_east
        - (push_lon[:, 1:] - push_lon[:, :-1]) / LON_SPACING
        - (carry_lat[1:] - carry_lat[:-1]) / LAT_SPACING
    )
    rate_north = wet_mid * (
        source_north
        - (carry_lon[:, 1:] - carry_lon[:, :-1]) / LON_SPACING
        - (push_lat[1:] - push_lat[:-1]) / LAT_SPACING
    )
    return (rate_surface, rate_east, rate_north)


def from_below(values, stride, along_axis, filler):
    length = values.shape[along_axis]
    padding = jnp.full_like(slab_of(values, 0, stride, along_axis), filler)
    return jnp.concatenate([padding, slab_of(values, 0, length - stride, along_axis)], along_axis)


def from_above(values, stride, along_axis, filler):
    length = values.shape[along_axis]
    padding = jnp.full_like(slab_of(values, 0, stride, along_axis), filler)
    return jnp.concatenate([slab_of(values, stride, length, along_axis), padding], along_axis)


def reduce_rows(lower_band, main_band, upper_band, rights, below, above):
    weight_below = lower_band / below[1]
    weight_above = upper_band / above[1]
    new_lower = -weight_below * below[0]
    new_main = main_band - weight_below * below[2] - weight_above * above[0]
    new_upper = -weight_above * above[2]
    new_rights = [
        member - weight_below * lower_member - weight_above * upper_member
        for member, lower_member, upper_member in zip(rights, below[3], above[3])
    ]
    return (new_lower, new_main, new_upper, new_rights)


def open_reduction(lower_band, main_band, upper_band, rights, along_axis):
    length = main_band.shape[along_axis]
    stride = 1
    while stride < length:
        below = (
            from_below(lower_band, stride, along_axis, 0.0),
            from_below(main_band, stride, along_axis, 1.0),
            from_below(upper_band, stride, along_axis, 0.0),
            [from_below(member, stride, along_axis, 0.0) for member in rights],
        )
        above = (
            from_above(lower_band, stride, along_axis, 0.0),
            from_above(main_band, stride, along_axis, 1.0),
            from_above(upper_band, stride, along_axis, 0.0),
            [from_above(member, stride, along_axis, 0.0) for member in rights],
        )
        lower_band, main_band, upper_band, rights = reduce_rows(
            lower_band, main_band, upper_band, rights, below, above
        )
        stride = stride * 2
    return [member / main_band for member in rights]


def local_spikes(rights, coef, along_axis):
    cell_count = coef.shape[along_axis]
    position = lax.broadcasted_iota(jnp.int32, coef.shape, along_axis)
    inner = position < cell_count - 1
    main_band = jnp.where(inner, 1.0 + 2.0 * coef, 1.0)
    lower_band = jnp.where(inner & (position > 0), -coef, 0.0)
    upper_band = jnp.where(position < cell_count - 2, -coef, 0.0)
    base_part = jnp.where(inner, rights, 0.0)
    from_left = jnp.where(position == 0, coef, 0.0)
    from_right = jnp.where(position == cell_count - 2, coef, 0.0)
    base_part, from_left, from_right = open_reduction(
        lower_band, main_band, upper_band, [base_part, from_left, from_right], along_axis
    )

    def pick_cell(values, spot):
        return lax.index_in_dim(values, spot, along_axis, keepdims=False)

    sep_coef = pick_cell(coef, cell_count - 1)
    sep_right = pick_cell(rights, cell_count - 1)
    packed = jnp.stack(
        [
            1.0 + 2.0 * sep_coef - sep_coef * pick_cell(from_right, cell_count - 2),
            sep_right + sep_coef * pick_cell(base_part, cell_count - 2),
            sep_coef,
            pick_cell(from_left, 0),
            pick_cell(base_part, 0),
        ]
    )
    return ((base_part, from_left, from_right), packed)


def rebuild(spikes, left_value, here_value, along_axis):
    base_part, from_left, from_right = spikes
    cell_count = base_part.shape[along_axis]
    left_value = jnp.expand_dims(left_value, along_axis)
    here_value = jnp.expand_dims(here_value, along_axis)
    position = lax.broadcasted_iota(jnp.int32, base_part.shape, along_axis)
    return (
        base_part
        + from_left * left_value
        + from_right * here_value
        + jnp.where(position == cell_count - 1, here_value, 0.0)
    )


def solve_east(rights, coef):
    spikes, packed = local_spikes(rights, coef, 1)
    neighbour = shifted(packed[3:5], "lon", -1)
    here_value = (packed[1] + packed[2] * neighbour[1]) / (packed[0] - packed[2] * neighbour[0])
    left_value = shifted(here_value, "lon", 1)
    return rebuild(spikes, left_value, here_value, 1)


def solve_north(rights, coef):
    spikes, packed = local_spikes(rights, coef, 0)
    neighbour = passed_along(packed[3:5], "lat", -1)
    here_value = (packed[1] + packed[2] * neighbour[1]) / (packed[0] - packed[2] * neighbour[0])
    left_value = passed_along(here_value, "lat", 1)
    return rebuild(spikes, left_value, here_value, 0)


def mirrored(along, signs, place, count):
    head_rows = jnp.where(place == 0, signs * along[:, 3:1:-1], along[:, :2])
    tail_rows = jnp.where(place == count - 1, signs * along[:, -3:-5:-1], along[:, -2:])
    return jnp.concatenate([head_rows, along[:, 2:-2], tail_rows], axis=1)


def section_tendency(
    surface, momentum_x, momentum_y, water_depth, wet_float, lift, coef_lon, coef_lat, place, count
):
    height = water_depth + surface
    velocity_u = wet_float * solve_east(momentum_x / height, coef_lon)
    velocity_v = wet_float * solve_north(momentum_y / height, coef_lat)
    fields = jnp.stack([surface, velocity_u, velocity_v, water_depth, wet_float])
    across = extended(fields, (("lon", 2),), 2, True)
    along = extended(fields, (("lat", 1),), 2, False)
    signs = jnp.array([1.0, 1.0, -1.0, 1.0, 1.0], jnp.float32)[:, None, None]
    along = mirrored(along, signs, place, count)
    rate_surface, rate_east, rate_north = tendencies(across, along)
    return ((rate_surface + lift, rate_east, rate_north), velocity_u, velocity_v)


def local(surface, momentum_x, momentum_y, water_depth, wet_mask, slide_cells, slide_rate):
    wet_float = wet_mask.astype(jnp.float32)
    place = lax.axis_index("lat")
    count = lax.axis_size("lat")
    tile_rows, tile_cols = surface.shape
    lift = (
        jnp.zeros((tile_rows * tile_cols,), jnp.float32)
        .at[slide_cells.reshape(-1)]
        .add(slide_rate.reshape(-1))
        .reshape(tile_rows, tile_cols)
    )
    coef_lon = water_depth * water_depth / (3.0 * LON_SPACING * LON_SPACING)
    coef_lat = water_depth * water_depth / (3.0 * LAT_SPACING * LAT_SPACING)
    initial = (surface, momentum_x, momentum_y)
    current = initial
    velocity_u = surface
    velocity_v = surface
    for first, second in ((0.0, 1.0), (0.75, 0.25), (1.0 / 3.0, 2.0 / 3.0)):
        rates, velocity_u, velocity_v = section_tendency(
            current[0],
            current[1],
            current[2],
            water_depth,
            wet_float,
            lift,
            coef_lon,
            coef_lat,
            place,
            count,
        )
        current = tuple(
            (
                first * start_value + second * (now + TIME_STEP * rate)
                for start_value, now, rate in zip(initial, current, rates)
            )
        )
    return (current[0], current[1], current[2], velocity_u, velocity_v)


def solution(mesh):
    in_specs = (
        P("lat", "lon"),
        P("lat", "lon"),
        P("lat", "lon"),
        P("lat", "lon"),
        P("lat", "lon"),
        P("lat", "lon"),
        P("lat", "lon"),
    )
    out_specs = (
        P("lat", "lon"),
        P("lat", "lon"),
        P("lat", "lon"),
        P("lat", "lon"),
        P("lat", "lon"),
    )
    return jax.shard_map(local, mesh=mesh, in_specs=in_specs, out_specs=out_specs, check_vma=False)
```

profile of v0, /device:TPU:25, one launch (start us, length us, event | category | flops | bytes accessed | tf_op | source)
XLA Modules:
  0.0 149.2 jit_solution(8384805036954950968)
XLA Ops:
  5.0 2.6 %collective-permute-start.2 = (f32[2,128]{1,0:T(2,128)S(1)}, f32[2,128]{1,0:T(2,128)S(1)}, u32[]{:S(2)}, u32[]{:S(2)}) collective-permute-start(f32[2,128]{1,0:T(2,128)S(1)} %pad_maximum_fusion.17), channel_id=1, source_target_pairs={{1,0},{2,1},{3,2},{4,3},{5,4},{6,5},{7,6},{8,7},{9,8},{10,9},{11,1... | collective-permute-start | bytes 3080 | tf_op jit(solution)/shard_map/ppermute | solution.py:21
  12.8 13.6 %collective-permute-start = (f32[2,112]{1,0:T(2,128)S(1)}, f32[2,112]{1,0:T(2,128)S(1)}, u32[]{:S(2)}, u32[]{:S(2)}) collective-permute-start(f32[2,112]{1,0:T(2,128)S(1)} %pad_maximum_fusion.14), channel_id=1, source_target_pairs={{16,0},{32,16},{48,32},{64,48},{80,64},{96,80},{112,96},{128,112},... | collective-permute-start | bytes 2696 | tf_op jit(solution)/shard_map/ppermute | solution.py:15
  28.7 1.9 %collective-permute-start.1 = (f32[112]{0:T(128)S(1)}, f32[112]{0:T(128)S(1)}, u32[]{:S(2)}, u32[]{:S(2)}) collective-permute-start(f32[112]{0:T(128)S(1)} %fusion.266), channel_id=1, source_target_pairs={{496,0},{0,16},{16,32},{32,48},{48,64},{64,80},{80,96},{96,112},{1... | collective-permute-start | bytes 1352 | tf_op jit(solution)/shard_map/ppermute | solution.py:15
  30.6 4.8 %collective-permute-start.3 = (f32[128]{0:T(128)S(1)}, f32[128]{0:T(128)S(1)}, u32[]{:S(2)}, u32[]{:S(2)}) collective-permute-start(f32[128]{0:T(128)S(1)} %fusion.268), channel_id=1, source_target_pairs={{0,1},{1,2},{2,3},{3,4},{4,5},{5,6},{6,7},{7,8},{8,9},{9,10},{10,1... | collective-permute-start | bytes 1544 | tf_op jit(solution)/shard_map/ppermute | solution.py:21
  37.0 1.9 %collective-permute-start.4 = (f32[5,112,2]{2,1,0:T(8,128)S(1)}, f32[5,112,2]{2,1,0:T(8,128)}, u32[]{:S(2)}, u32[]{:S(2)}) collective-permute-start(f32[5,112,2]{2,1,0:T(8,128)S(1)} %get-tuple-element.187), channel_id=1, source_target_pairs={{0,16},{16,32},{32,48},{48,64},{64,80},{80,96},{96,112},{112,128},... | collective-permute-start | bytes 13448 | tf_op jit(solution)/shard_map/ppermute | solution.py:32
  38.9 7.3 %collective-permute-start.5 = (f32[5,112,2]{2,1,0:T(8,128)S(1)}, f32[5,112,2]{2,1,0:T(8,128)}, u32[]{:S(2)}, u32[]{:S(2)}) collective-permute-start(f32[5,112,2]{2,1,0:T(8,128)S(1)} %get-tuple-element.188), channel_id=1, source_target_pairs={{16,0},{32,16},{48,32},{64,48},{80,64},{96,80},{112,96},{128,112},... | collective-permute-start | bytes 13448 | tf_op jit(solution)/shard_map/ppermute | solution.py:34
  46.2 6.2 %collective-permute-start.6 = (f32[5,2,128]{2,1,0:T(2,128)S(1)}, f32[5,2,128]{2,1,0:T(2,128)S(1)}, u32[]{:S(2)}, u32[]{:S(2)}) collective-permute-start(f32[5,2,128]{2,1,0:T(2,128)S(1)} %get-tuple-element.189), channel_id=1, source_target_pairs={{0,1},{1,2},{2,3},{3,4},{4,5},{5,6},{6,7},{7,8},{8,9},{9,10},{10,1... | collective-permute-start | bytes 15368 | tf_op jit(solution)/shard_map/ppermute | solution.py:32
  57.5 2.0 %collective-permute-done.7 = f32[5,2,128]{2,1,0:T(2,128)S(1)} collective-permute-done((f32[5,2,128]{2,1,0:T(2,128)S(1)}, f32[5,2,128]{2,1,0:T(2,128)S(1)}, u32[]{:S(2)}, u32[]{:S(2)}) %collective-permute-start.7) | collective-permute-done | bytes 5152 | tf_op jit(solution)/shard_map/ppermute | solution.py:34
  63.5 4.0 %collective-permute-start.8 = (f32[2,112]{1,0:T(2,128)S(1)}, f32[2,112]{1,0:T(2,128)S(1)}, u32[]{:S(2)}, u32[]{:S(2)}) collective-permute-start(f32[2,112]{1,0:T(2,128)S(1)} %pad_maximum_fusion.13), channel_id=1, source_target_pairs={{16,0},{32,16},{48,32},{64,48},{80,64},{96,80},{112,96},{128,112},... | collective-permute-start | bytes 2696 | tf_op jit(solution)/shard_map/ppermute | solution.py:15
  67.6 3.2 %collective-permute-start.10 = (f32[2,128]{1,0:T(2,128)S(1)}, f32[2,128]{1,0:T(2,128)S(1)}, u32[]{:S(2)}, u32[]{:S(2)}) collective-permute-start(f32[2,128]{1,0:T(2,128)S(1)} %pad_maximum_fusion.16), channel_id=1, source_target_pairs={{1,0},{2,1},{3,2},{4,3},{5,4},{6,5},{7,6},{8,7},{9,8},{10,9},{11,1... | collective-permute-start | bytes 3080 | tf_op jit(solution)/shard_map/ppermute | solution.py:21
  71.3 1.9 %collective-permute-start.9 = (f32[112]{0:T(128)S(1)}, f32[112]{0:T(128)S(1)}, u32[]{:S(2)}, u32[]{:S(2)}) collective-permute-start(f32[112]{0:T(128)S(1)} %fusion.263), channel_id=1, source_target_pairs={{496,0},{0,16},{16,32},{32,48},{48,64},{64,80},{80,96},{96,112},{1... | collective-permute-start | bytes 1352 | tf_op jit(solution)/shard_map/ppermute | solution.py:15
  75.3 3.3 %collective-permute-start.11 = (f32[128]{0:T(128)S(1)}, f32[128]{0:T(128)S(1)}, u32[]{:S(2)}, u32[]{:S(2)}) collective-permute-start(f32[128]{0:T(128)S(1)} %fusion.269), channel_id=1, source_target_pairs={{0,1},{1,2},{2,3},{3,4},{4,5},{5,6},{6,7},{7,8},{8,9},{9,10},{10,1... | collective-permute-start | bytes 1544 | tf_op jit(solution)/shard_map/ppermute | solution.py:21
  80.1 1.9 %collective-permute-start.12 = (f32[5,112,2]{2,1,0:T(8,128)S(1)}, f32[5,112,2]{2,1,0:T(8,128)}, u32[]{:S(2)}, u32[]{:S(2)}) collective-permute-start(f32[5,112,2]{2,1,0:T(8,128)S(1)} %get-tuple-element.183), channel_id=1, source_target_pairs={{0,16},{16,32},{32,48},{48,64},{64,80},{80,96},{96,112},{112,128},... | collective-permute-start | bytes 13448 | tf_op jit(solution)/shard_map/ppermute | solution.py:32
  82.0 7.3 %collective-permute-start.13 = (f32[5,112,2]{2,1,0:T(8,128)S(1)}, f32[5,112,2]{2,1,0:T(8,128)}, u32[]{:S(2)}, u32[]{:S(2)}) collective-permute-start(f32[5,112,2]{2,1,0:T(8,128)S(1)} %get-tuple-element.184), channel_id=1, source_target_pairs={{16,0},{32,16},{48,32},{64,48},{80,64},{96,80},{112,96},{128,112},... | collective-permute-start | bytes 13448 | tf_op jit(solution)/shard_map/ppermute | solution.py:34
  89.3 5.9 %collective-permute-start.14 = (f32[5,2,128]{2,1,0:T(2,128)S(1)}, f32[5,2,128]{2,1,0:T(2,128)S(1)}, u32[]{:S(2)}, u32[]{:S(2)}) collective-permute-start(f32[5,2,128]{2,1,0:T(2,128)S(1)} %get-tuple-element.185), channel_id=1, source_target_pairs={{0,1},{1,2},{2,3},{3,4},{4,5},{5,6},{6,7},{7,8},{8,9},{9,10},{10,1... | collective-permute-start | bytes 15368 | tf_op jit(solution)/shard_map/ppermute | solution.py:32
  95.3 2.1 %collective-permute-start.15 = (f32[5,2,128]{2,1,0:T(2,128)S(1)}, f32[5,2,128]{2,1,0:T(2,128)S(1)}, u32[]{:S(2)}, u32[]{:S(2)}) collective-permute-start(f32[5,2,128]{2,1,0:T(2,128)S(1)} %get-tuple-element.186), channel_id=1, source_target_pairs={{1,0},{2,1},{3,2},{4,3},{5,4},{6,5},{7,6},{8,7},{9,8},{10,9},{11,1... | collective-permute-start | bytes 15368 | tf_op jit(solution)/shard_map/ppermute | solution.py:34
  106.2 4.2 %collective-permute-start.16 = (f32[2,112]{1,0:T(2,128)S(1)}, f32[2,112]{1,0:T(2,128)S(1)}, u32[]{:S(2)}, u32[]{:S(2)}) collective-permute-start(f32[2,112]{1,0:T(2,128)S(1)} %pad_maximum_fusion.12), channel_id=1, source_target_pairs={{16,0},{32,16},{48,32},{64,48},{80,64},{96,80},{112,96},{128,112},... | collective-permute-start | bytes 2696 | tf_op jit(solution)/shard_map/ppermute | solution.py:15
  110.5 2.9 %collective-permute-start.18 = (f32[2,128]{1,0:T(2,128)S(1)}, f32[2,128]{1,0:T(2,128)S(1)}, u32[]{:S(2)}, u32[]{:S(2)}) collective-permute-start(f32[2,128]{1,0:T(2,128)S(1)} %pad_maximum_fusion.15), channel_id=1, source_target_pairs={{1,0},{2,1},{3,2},{4,3},{5,4},{6,5},{7,6},{8,7},{9,8},{10,9},{11,1... | collective-permute-start | bytes 3080 | tf_op jit(solution)/shard_map/ppermute | solution.py:21
  113.9 1.9 %collective-permute-start.17 = (f32[112]{0:T(128)S(1)}, f32[112]{0:T(128)S(1)}, u32[]{:S(2)}, u32[]{:S(2)}) collective-permute-start(f32[112]{0:T(128)S(1)} %fusion.260), channel_id=1, source_target_pairs={{496,0},{0,16},{16,32},{32,48},{48,64},{64,80},{80,96},{96,112},{1... | collective-permute-start | bytes 1352 | tf_op jit(solution)/shard_map/ppermute | solution.py:15
  118.2 3.3 %collective-permute-start.19 = (f32[128]{0:T(128)S(1)}, f32[128]{0:T(128)S(1)}, u32[]{:S(2)}, u32[]{:S(2)}) collective-permute-start(f32[128]{0:T(128)S(1)} %fusion.270), channel_id=1, source_target_pairs={{0,1},{1,2},{2,3},{3,4},{4,5},{5,6},{6,7},{7,8},{8,9},{9,10},{10,1... | collective-permute-start | bytes 1544 | tf_op jit(solution)/shard_map/ppermute | solution.py:21
  124.0 1.9 %collective-permute-start.20 = (f32[5,112,2]{2,1,0:T(8,128)S(1)}, f32[5,112,2]{2,1,0:T(8,128)S(1)}, u32[]{:S(2)}, u32[]{:S(2)}) collective-permute-start(f32[5,112,2]{2,1,0:T(8,128)S(1)} %get-tuple-element.179), channel_id=1, source_target_pairs={{0,16},{16,32},{32,48},{48,64},{64,80},{80,96},{96,112},{112,128},... | collective-permute-start | bytes 13448 | tf_op jit(solution)/shard_map/ppermute | solution.py:32
  125.9 7.5 %collective-permute-start.21 = (f32[5,112,2]{2,1,0:T(8,128)S(1)}, f32[5,112,2]{2,1,0:T(8,128)S(1)}, u32[]{:S(2)}, u32[]{:S(2)}) collective-permute-start(f32[5,112,2]{2,1,0:T(8,128)S(1)} %get-tuple-element.180), channel_id=1, source_target_pairs={{16,0},{32,16},{48,32},{64,48},{80,64},{96,80},{112,96},{128,112},... | collective-permute-start | bytes 13448 | tf_op jit(solution)/shard_map/ppermute | solution.py:34
  133.5 5.9 %collective-permute-start.22 = (f32[5,2,128]{2,1,0:T(2,128)S(1)}, f32[5,2,128]{2,1,0:T(2,128)S(1)}, u32[]{:S(2)}, u32[]{:S(2)}) collective-permute-start(f32[5,2,128]{2,1,0:T(2,128)S(1)} %get-tuple-element.181), channel_id=1, source_target_pairs={{0,1},{1,2},{2,3},{3,4},{4,5},{5,6},{6,7},{7,8},{8,9},{9,10},{10,1... | collective-permute-start | bytes 15368 | tf_op jit(solution)/shard_map/ppermute | solution.py:32
  143.5 3.0 %collective-permute-done.23 = f32[5,2,128]{2,1,0:T(2,128)S(1)} collective-permute-done((f32[5,2,128]{2,1,0:T(2,128)S(1)}, f32[5,2,128]{2,1,0:T(2,128)S(1)}, u32[]{:S(2)}, u32[]{:S(2)}) %collective-permute-start.23) | collective-permute-done | bytes 5152 | tf_op jit(solution)/shard_map/ppermute | solution.py:34
  (368 shorter events, 46.0 us)
Async XLA Ops:
  5.0 25.6 %collective-permute-start.2 = (f32[2,128]{1,0:T(2,128)S(1)}, f32[2,128]{1,0:T(2,128)S(1)}, u32[]{:S(2)}, u32[]{:S(2)}) collective-permute-start(f32[2,128]{1,0:T(2,128)S(1)} %pad_maximum_fusion.17), channel_id=1, source_target_pairs={{1,0},{2,1},{3,2},{4,3},{5,4},{6,5},{7,6},{8,7},{9,8},{10,9},{11,1... | collective-permute-start | bytes 3080 | tf_op jit(solution)/shard_map/ppermute | solution.py:21
  12.8 15.4 %collective-permute-start = (f32[2,112]{1,0:T(2,128)S(1)}, f32[2,112]{1,0:T(2,128)S(1)}, u32[]{:S(2)}, u32[]{:S(2)}) collective-permute-start(f32[2,112]{1,0:T(2,128)S(1)} %pad_maximum_fusion.14), channel_id=1, source_target_pairs={{16,0},{32,16},{48,32},{64,48},{80,64},{96,80},{112,96},{128,112},... | collective-permute-start | bytes 2696 | tf_op jit(solution)/shard_map/ppermute | solution.py:15
  28.7 7.9 %collective-permute-start.1 = (f32[112]{0:T(128)S(1)}, f32[112]{0:T(128)S(1)}, u32[]{:S(2)}, u32[]{:S(2)}) collective-permute-start(f32[112]{0:T(128)S(1)} %fusion.266), channel_id=1, source_target_pairs={{496,0},{0,16},{16,32},{32,48},{48,64},{64,80},{80,96},{96,112},{1... | collective-permute-start | bytes 1352 | tf_op jit(solution)/shard_map/ppermute | solution.py:15
  30.6 6.0 %collective-permute-start.3 = (f32[128]{0:T(128)S(1)}, f32[128]{0:T(128)S(1)}, u32[]{:S(2)}, u32[]{:S(2)}) collective-permute-start(f32[128]{0:T(128)S(1)} %fusion.268), channel_id=1, source_target_pairs={{0,1},{1,2},{2,3},{3,4},{4,5},{5,6},{6,7},{7,8},{8,9},{9,10},{10,1... | collective-permute-start | bytes 1544 | tf_op jit(solution)/shard_map/ppermute | solution.py:21
  37.0 17.4 %collective-permute-start.4 = (f32[5,112,2]{2,1,0:T(8,128)S(1)}, f32[5,112,2]{2,1,0:T(8,128)}, u32[]{:S(2)}, u32[]{:S(2)}) collective-permute-start(f32[5,112,2]{2,1,0:T(8,128)S(1)} %get-tuple-element.187), channel_id=1, source_target_pairs={{0,16},{16,32},{32,48},{48,64},{64,80},{80,96},{96,112},{112,128},... | collective-permute-start | bytes 13448 | tf_op jit(solution)/shard_map/ppermute | solution.py:32
  38.9 15.5 %collective-permute-start.5 = (f32[5,112,2]{2,1,0:T(8,128)S(1)}, f32[5,112,2]{2,1,0:T(8,128)}, u32[]{:S(2)}, u32[]{:S(2)}) collective-permute-start(f32[5,112,2]{2,1,0:T(8,128)S(1)} %get-tuple-element.188), channel_id=1, source_target_pairs={{16,0},{32,16},{48,32},{64,48},{80,64},{96,80},{112,96},{128,112},... | collective-permute-start | bytes 13448 | tf_op jit(solution)/shard_map/ppermute | solution.py:34
  46.2 11.3 %collective-permute-start.6 = (f32[5,2,128]{2,1,0:T(2,128)S(1)}, f32[5,2,128]{2,1,0:T(2,128)S(1)}, u32[]{:S(2)}, u32[]{:S(2)}) collective-permute-start(f32[5,2,128]{2,1,0:T(2,128)S(1)} %get-tuple-element.189), channel_id=1, source_target_pairs={{0,1},{1,2},{2,3},{3,4},{4,5},{5,6},{6,7},{7,8},{8,9},{9,10},{10,1... | collective-permute-start | bytes 15368 | tf_op jit(solution)/shard_map/ppermute | solution.py:32
  52.4 7.0 %collective-permute-start.7 = (f32[5,2,128]{2,1,0:T(2,128)S(1)}, f32[5,2,128]{2,1,0:T(2,128)S(1)}, u32[]{:S(2)}, u32[]{:S(2)}) collective-permute-start(f32[5,2,128]{2,1,0:T(2,128)S(1)} %get-tuple-element.190), channel_id=1, source_target_pairs={{1,0},{2,1},{3,2},{4,3},{5,4},{6,5},{7,6},{8,7},{9,8},{10,9},{11,1... | collective-permute-start | bytes 15368 | tf_op jit(solution)/shard_map/ppermute | solution.py:34
  63.5 7.3 %collective-permute-start.8 = (f32[2,112]{1,0:T(2,128)S(1)}, f32[2,112]{1,0:T(2,128)S(1)}, u32[]{:S(2)}, u32[]{:S(2)}) collective-permute-start(f32[2,112]{1,0:T(2,128)S(1)} %pad_maximum_fusion.13), channel_id=1, source_target_pairs={{16,0},{32,16},{48,32},{64,48},{80,64},{96,80},{112,96},{128,112},... | collective-permute-start | bytes 2696 | tf_op jit(solution)/shard_map/ppermute | solution.py:15
  67.6 7.0 %collective-permute-start.10 = (f32[2,128]{1,0:T(2,128)S(1)}, f32[2,128]{1,0:T(2,128)S(1)}, u32[]{:S(2)}, u32[]{:S(2)}) collective-permute-start(f32[2,128]{1,0:T(2,128)S(1)} %pad_maximum_fusion.16), channel_id=1, source_target_pairs={{1,0},{2,1},{3,2},{4,3},{5,4},{6,5},{7,6},{8,7},{9,8},{10,9},{11,1... | collective-permute-start | bytes 3080 | tf_op jit(solution)/shard_map/ppermute | solution.py:21
  71.3 7.9 %collective-permute-start.9 = (f32[112]{0:T(128)S(1)}, f32[112]{0:T(128)S(1)}, u32[]{:S(2)}, u32[]{:S(2)}) collective-permute-start(f32[112]{0:T(128)S(1)} %fusion.263), channel_id=1, source_target_pairs={{496,0},{0,16},{16,32},{32,48},{48,64},{64,80},{80,96},{96,112},{1... | collective-permute-start | bytes 1352 | tf_op jit(solution)/shard_map/ppermute | solution.py:15
  75.3 4.1 %collective-permute-start.11 = (f32[128]{0:T(128)S(1)}, f32[128]{0:T(128)S(1)}, u32[]{:S(2)}, u32[]{:S(2)}) collective-permute-start(f32[128]{0:T(128)S(1)} %fusion.269), channel_id=1, source_target_pairs={{0,1},{1,2},{2,3},{3,4},{4,5},{5,6},{6,7},{7,8},{8,9},{9,10},{10,1... | collective-permute-start | bytes 1544 | tf_op jit(solution)/shard_map/ppermute | solution.py:21
  80.1 17.4 %collective-permute-start.12 = (f32[5,112,2]{2,1,0:T(8,128)S(1)}, f32[5,112,2]{2,1,0:T(8,128)}, u32[]{:S(2)}, u32[]{:S(2)}) collective-permute-start(f32[5,112,2]{2,1,0:T(8,128)S(1)} %get-tuple-element.183), channel_id=1, source_target_pairs={{0,16},{16,32},{32,48},{48,64},{64,80},{80,96},{96,112},{112,128},... | collective-permute-start | bytes 13448 | tf_op jit(solution)/shard_map/ppermute | solution.py:32
  82.0 15.4 %collective-permute-start.13 = (f32[5,112,2]{2,1,0:T(8,128)S(1)}, f32[5,112,2]{2,1,0:T(8,128)}, u32[]{:S(2)}, u32[]{:S(2)}) collective-permute-start(f32[5,112,2]{2,1,0:T(8,128)S(1)} %get-tuple-element.184), channel_id=1, source_target_pairs={{16,0},{32,16},{48,32},{64,48},{80,64},{96,80},{112,96},{128,112},... | collective-permute-start | bytes 13448 | tf_op jit(solution)/shard_map/ppermute | solution.py:34
  89.3 11.2 %collective-permute-start.14 = (f32[5,2,128]{2,1,0:T(2,128)S(1)}, f32[5,2,128]{2,1,0:T(2,128)S(1)}, u32[]{:S(2)}, u32[]{:S(2)}) collective-permute-start(f32[5,2,128]{2,1,0:T(2,128)S(1)} %get-tuple-element.185), channel_id=1, source_target_pairs={{0,1},{1,2},{2,3},{3,4},{4,5},{5,6},{6,7},{7,8},{8,9},{9,10},{10,1... | collective-permute-start | bytes 15368 | tf_op jit(solution)/shard_map/ppermute | solution.py:32
  95.3 7.0 %collective-permute-start.15 = (f32[5,2,128]{2,1,0:T(2,128)S(1)}, f32[5,2,128]{2,1,0:T(2,128)S(1)}, u32[]{:S(2)}, u32[]{:S(2)}) collective-permute-start(f32[5,2,128]{2,1,0:T(2,128)S(1)} %get-tuple-element.186), channel_id=1, source_target_pairs={{1,0},{2,1},{3,2},{4,3},{5,4},{6,5},{7,6},{8,7},{9,8},{10,9},{11,1... | collective-permute-start | bytes 15368 | tf_op jit(solution)/shard_map/ppermute | solution.py:34
  106.2 7.2 %collective-permute-start.16 = (f32[2,112]{1,0:T(2,128)S(1)}, f32[2,112]{1,0:T(2,128)S(1)}, u32[]{:S(2)}, u32[]{:S(2)}) collective-permute-start(f32[2,112]{1,0:T(2,128)S(1)} %pad_maximum_fusion.12), channel_id=1, source_target_pairs={{16,0},{32,16},{48,32},{64,48},{80,64},{96,80},{112,96},{128,112},... | collective-permute-start | bytes 2696 | tf_op jit(solution)/shard_map/ppermute | solution.py:15
  110.5 7.0 %collective-permute-start.18 = (f32[2,128]{1,0:T(2,128)S(1)}, f32[2,128]{1,0:T(2,128)S(1)}, u32[]{:S(2)}, u32[]{:S(2)}) collective-permute-start(f32[2,128]{1,0:T(2,128)S(1)} %pad_maximum_fusion.15), channel_id=1, source_target_pairs={{1,0},{2,1},{3,2},{4,3},{5,4},{6,5},{7,6},{8,7},{9,8},{10,9},{11,1... | collective-permute-start | bytes 3080 | tf_op jit(solution)/shard_map/ppermute | solution.py:21
  113.9 7.9 %collective-permute-start.17 = (f32[112]{0:T(128)S(1)}, f32[112]{0:T(128)S(1)}, u32[]{:S(2)}, u32[]{:S(2)}) collective-permute-start(f32[112]{0:T(128)S(1)} %fusion.260), channel_id=1, source_target_pairs={{496,0},{0,16},{16,32},{32,48},{48,64},{64,80},{80,96},{96,112},{1... | collective-permute-start | bytes 1352 | tf_op jit(solution)/shard_map/ppermute | solution.py:15
  118.2 4.4 %collective-permute-start.19 = (f32[128]{0:T(128)S(1)}, f32[128]{0:T(128)S(1)}, u32[]{:S(2)}, u32[]{:S(2)}) collective-permute-start(f32[128]{0:T(128)S(1)} %fusion.270), channel_id=1, source_target_pairs={{0,1},{1,2},{2,3},{3,4},{4,5},{5,6},{6,7},{7,8},{8,9},{9,10},{10,1... | collective-permute-start | bytes 1544 | tf_op jit(solution)/shard_map/ppermute | solution.py:21
  124.0 17.4 %collective-permute-start.20 = (f32[5,112,2]{2,1,0:T(8,128)S(1)}, f32[5,112,2]{2,1,0:T(8,128)S(1)}, u32[]{:S(2)}, u32[]{:S(2)}) collective-permute-start(f32[5,112,2]{2,1,0:T(8,128)S(1)} %get-tuple-element.179), channel_id=1, source_target_pairs={{0,16},{16,32},{32,48},{48,64},{64,80},{80,96},{96,112},{112,128},... | collective-permute-start | bytes 13448 | tf_op jit(solution)/shard_map/ppermute | solution.py:32
  125.9 15.5 %collective-permute-start.21 = (f32[5,112,2]{2,1,0:T(8,128)S(1)}, f32[5,112,2]{2,1,0:T(8,128)S(1)}, u32[]{:S(2)}, u32[]{:S(2)}) collective-permute-start(f32[5,112,2]{2,1,0:T(8,128)S(1)} %get-tuple-element.180), channel_id=1, source_target_pairs={{16,0},{32,16},{48,32},{64,48},{80,64},{96,80},{112,96},{128,112},... | collective-permute-start | bytes 13448 | tf_op jit(solution)/shard_map/ppermute | solution.py:34
  133.5 10.0 %collective-permute-start.22 = (f32[5,2,128]{2,1,0:T(2,128)S(1)}, f32[5,2,128]{2,1,0:T(2,128)S(1)}, u32[]{:S(2)}, u32[]{:S(2)}) collective-permute-start(f32[5,2,128]{2,1,0:T(2,128)S(1)} %get-tuple-element.181), channel_id=1, source_target_pairs={{0,1},{1,2},{2,3},{3,4},{4,5},{5,6},{6,7},{7,8},{8,9},{9,10},{10,1... | collective-permute-start | bytes 15368 | tf_op jit(solution)/shard_map/ppermute | solution.py:32
  139.4 7.0 %collective-permute-start.23 = (f32[5,2,128]{2,1,0:T(2,128)S(1)}, f32[5,2,128]{2,1,0:T(2,128)S(1)}, u32[]{:S(2)}, u32[]{:S(2)}) collective-permute-start(f32[5,2,128]{2,1,0:T(2,128)S(1)} %get-tuple-element.182), channel_id=1, source_target_pairs={{1,0},{2,1},{3,2},{4,3},{5,4},{6,5},{7,6},{8,7},{9,8},{10,9},{11,1... | collective-permute-start | bytes 15368 | tf_op jit(solution)/shard_map/ppermute | solution.py:34
  (22 other events, 154.3 us)
where the time goes:
time: 150 us; the launch traced here: 149 us
  starting transfers between devices  99.4 us (66%)
  other arithmetic  22.4 us (15%)
  local copies, waits for them, and re-layouts  12.7 us (8%)
  waiting for transfers between devices  12 us (8%)
  between operations  2.61 us (2%)
    ppermute x6, starting transfers between devices, extended(): lax.ppermute(head, axis, [((i + 1) % count, i) for i in range(ends)])  28 us
    ppermute x6, starting transfers between devices, shifted(): return lax.ppermute(block, axis, route)  27.6 us
    ppermute x6, starting transfers between devices, extended(): lax.ppermute(tail, axis, [(i, (i + 1) % count) for i in range(ends)])  23.8 us
    ppermute x6, starting transfers between devices, passed_along(): return lax.ppermute(x, axis, pairs)  20 us
    ppermute x6, waiting for transfers between devices, extended(): lax.ppermute(head, axis, [((i + 1) % count, i) for i in range(ends)])  6.8 us
    unnamed x50, local copies, waits for them, and re-layouts  6.1 us
    slice x109, local copies, waits for them, and re-layouts, slab_of(): return lax.slice_in_dim(values, start, stop, axis=along_axis)  4.83 us
  transfers between devices with their start and end apart: 24, of which 8 were waited for; matrix products, arithmetic and copies ran while one was open for 12% of the time, Pallas kernels for 0%

commit v1 on v0

--- a/solution.py
+++ b/solution.py
@@ -7,6 +7,8 @@
 LON_SPACING = 0.5
 LAT_SPACING = 0.6
 TIME_STEP = 0.1
+WINDOW_LON = 40
+WINDOW_LAT = 32
 
 
 def shifted(block, axis, distance):
@@ -183,122 +185,53 @@
     return jnp.concatenate([slab_of(values, stride, length, along_axis), padding], along_axis)
 
 
-def reduce_rows(lower_band, main_band, upper_band, rights, below, above):
-    weight_below = lower_band / below[1]
-    weight_above = upper_band / above[1]
-    new_lower = -weight_below * below[0]
-    new_main = main_band - weight_below * below[2] - weight_above * above[0]
-    new_upper = -weight_above * above[2]
-    new_rights = [
-        member - weight_below * lower_member - weight_above * upper_member
-        for member, lower_member, upper_member in zip(rights, below[3], above[3])
-    ]
-    return (new_lower, new_main, new_upper, new_rights)
-
-
-def open_reduction(lower_band, main_band, upper_band, rights, along_axis):
+def reduction_plan(lower_band, main_band, upper_band, along_axis):
     length = main_band.shape[along_axis]
     stride = 1
+    weights = []
     while stride < length:
-        below = (
-            from_below(lower_band, stride, along_axis, 0.0),
-            from_below(main_band, stride, along_axis, 1.0),
-            from_below(upper_band, stride, along_axis, 0.0),
-            [from_below(member, stride, along_axis, 0.0) for member in rights],
-        )
-        above = (
-            from_above(lower_band, stride, along_axis, 0.0),
-            from_above(main_band, stride, along_axis, 1.0),
-            from_above(upper_band, stride, along_axis, 0.0),
-            [from_above(member, stride, along_axis, 0.0) for member in rights],
-        )
-        lower_band, main_band, upper_band, rights = reduce_rows(
-            lower_band, main_band, upper_band, rights, below, above
-        )
+        below = [from_below(band, stride, along_axis, fill) for band, fill in
+                 ((lower_band, 0.0), (main_band, 1.0), (upper_band, 0.0))]
+        above = [from_above(band, stride, along_axis, fill) for band, fill in
+                 ((lower_band, 0.0), (main_band, 1.0), (upper_band, 0.0))]
+        weight_below = lower_band / below[1]
+        weight_above = upper_band / above[1]
+        new_lower = -weight_below * below[0]
+        new_main = main_band - weight_below * below[2] - weight_above * above[0]
+        new_upper = -weight_above * above[2]
+        weights.append((weight_below, weight_above))
+        lower_band, main_band, upper_band = new_lower, new_main, new_upper
         stride = stride * 2
-    return [member / main_band for member in rights]
-
-
-def local_spikes(rights, coef, along_axis):
-    cell_count = coef.shape[along_axis]
-    position = lax.broadcasted_iota(jnp.int32, coef.shape, along_axis)
-    inner = position < cell_count - 1
-    main_band = jnp.where(inner, 1.0 + 2.0 * coef, 1.0)
-    lower_band = jnp.where(inner & (position > 0), -coef, 0.0)
-    upper_band = jnp.where(position < cell_count - 2, -coef, 0.0)
-    base_part = jnp.where(inner, rights, 0.0)
-    from_left = jnp.where(position == 0, coef, 0.0)
-    from_right = jnp.where(position == cell_count - 2, coef, 0.0)
-    base_part, from_left, from_right = open_reduction(
-        lower_band, main_band, upper_band, [base_part, from_left, from_right], along_axis
-    )
-
-    def pick_cell(values, spot):
-        return lax.index_in_dim(values, spot, along_axis, keepdims=False)
-
-    sep_coef = pick_cell(coef, cell_count - 1)
-    sep_right = pick_cell(rights, cell_count - 1)
-    packed = jnp.stack(
-        [
-            1.0 + 2.0 * sep_coef - sep_coef * pick_cell(from_right, cell_count - 2),
-            sep_right + sep_coef * pick_cell(base_part, cell_count - 2),
-            sep_coef,
-            pick_cell(from_left, 0),
-            pick_cell(base_part, 0),
-        ]
-    )
-    return ((base_part, from_left, from_right), packed)
-
-
-def rebuild(spikes, left_value, here_value, along_axis):
-    base_part, from_left, from_right = spikes
-    cell_count = base_part.shape[along_axis]
-    left_value = jnp.expand_dims(left_value, along_axis)
-    here_value = jnp.expand_dims(here_value, along_axis)
-    position = lax.broadcasted_iota(jnp.int32, base_part.shape, along_axis)
-    return (
-        base_part
-        + from_left * left_value
-        + from_right * here_value
-        + jnp.where(position == cell_count - 1, here_value, 0.0)
-    )
-
-
-def solve_east(rights, coef):
-    spikes, packed = local_spikes(rights, coef, 1)
-    neighbour = shifted(packed[3:5], "lon", -1)
-    here_value = (packed[1] + packed[2] * neighbour[1]) / (packed[0] - packed[2] * neighbour[0])
-    left_value = shifted(here_value, "lon", 1)
-    return rebuild(spikes, left_value, here_value, 1)
-
-
-def solve_north(rights, coef):
-    spikes, packed = local_spikes(rights, coef, 0)
-    neighbour = passed_along(packed[3:5], "lat", -1)
-    here_value = (packed[1] + packed[2] * neighbour[1]) / (packed[0] - packed[2] * neighbour[0])
-    left_value = passed_along(here_value, "lat", 1)
-    return rebuild(spikes, left_value, here_value, 0)
-
-
-def mirrored(along, signs, place, count):
-    head_rows = jnp.where(place == 0, signs * along[:, 3:1:-1], along[:, :2])
-    tail_rows = jnp.where(place == count - 1, signs * along[:, -3:-5:-1], along[:, -2:])
-    return jnp.concatenate([head_rows, along[:, 2:-2], tail_rows], axis=1)
-
-
-def section_tendency(
-    surface, momentum_x, momentum_y, water_depth, wet_float, lift, coef_lon, coef_lat, place, count
-):
-    height = water_depth + surface
-    velocity_u = wet_float * solve_east(momentum_x / height, coef_lon)
-    velocity_v = wet_float * solve_north(momentum_y / height, coef_lat)
-    fields = jnp.stack([surface, velocity_u, velocity_v, water_depth, wet_float])
-    across = extended(fields, (("lon", 2),), 2, True)
-    along = extended(fields, (("lat", 1),), 2, False)
-    signs = jnp.array([1.0, 1.0, -1.0, 1.0, 1.0], jnp.float32)[:, None, None]
-    along = mirrored(along, signs, place, count)
-    rate_surface, rate_east, rate_north = tendencies(across, along)
-    return ((rate_surface + lift, rate_east, rate_north), velocity_u, velocity_v)
+    return weights, main_band
+
+
+def apply_plan(plan, rights, along_axis):
+    weights, main_band = plan
+    stride = 1
+    for weight_below, weight_above in weights:
+        rights = (
+            rights
+            - weight_below * from_below(rights, stride, along_axis, 0.0)
+            - weight_above * from_above(rights, stride, along_axis, 0.0)
+        )
+        stride = stride * 2
+    return rights / main_band
+
+
+def halo_box(fields, wide_x, wide_y, place, count):
+    lon_count = lax.axis_size("lon")
+    west = lax.ppermute(
+        fields[:, :, -wide_x:], "lon", [(i, (i + 1) % lon_count) for i in range(lon_count)]
+    )
+    east = lax.ppermute(
+        fields[:, :, :wide_x], "lon", [((i + 1) % lon_count, i) for i in range(lon_count)]
+    )
+    wide = jnp.concatenate([west, fields, east], axis=2)
+    above = passed_along(wide[:, -wide_y:], "lat", 1)
+    below = passed_along(wide[:, :wide_y], "lat", -1)
+    above = jnp.where(place == 0, wide[:, wide_y - 1 :: -1], above)
+    below = jnp.where(place == count - 1, wide[:, : -wide_y - 1 : -1], below)
+    return jnp.concatenate([above, wide, below], axis=1)
 
 
 def local(surface, momentum_x, momentum_y, water_depth, wet_mask, slide_cells, slide_rate):
@@ -306,31 +239,69 @@
     place = lax.axis_index("lat")
     count = lax.axis_size("lat")
     tile_rows, tile_cols = surface.shape
+    wide_x = WINDOW_LON + 2
+    wide_y = WINDOW_LAT + 2
     lift = (
         jnp.zeros((tile_rows * tile_cols,), jnp.float32)
         .at[slide_cells.reshape(-1)]
         .add(slide_rate.reshape(-1))
         .reshape(tile_rows, tile_cols)
     )
-    coef_lon = water_depth * water_depth / (3.0 * LON_SPACING * LON_SPACING)
-    coef_lat = water_depth * water_depth / (3.0 * LAT_SPACING * LAT_SPACING)
+    box_rows = tile_rows + 2 * wide_y
+    box_cols = tile_cols + 2 * wide_x
+    core_rows = slice(wide_y - 2, wide_y + tile_rows + 2)
+    core_cols = slice(wide_x - 2, wide_x + tile_cols + 2)
+    global_row = place * tile_rows - wide_y + lax.broadcasted_iota(
+        jnp.int32, (box_rows, tile_cols + 4), 0
+    )
+    inside = (global_row >= 0) & (global_row < count * tile_rows)
+
     initial = (surface, momentum_x, momentum_y)
     current = initial
     velocity_u = surface
     velocity_v = surface
+    plans = None
     for first, second in ((0.0, 1.0), (0.75, 0.25), (1.0 / 3.0, 2.0 / 3.0)):
-        rates, velocity_u, velocity_v = section_tendency(
-            current[0],
-            current[1],
-            current[2],
-            water_depth,
-            wet_float,
-            lift,
-            coef_lon,
-            coef_lat,
-            place,
-            count,
-        )
+        if plans is None:
+            box = halo_box(
+                jnp.stack([current[0], current[1], current[2], water_depth, wet_float]),
+                wide_x, wide_y, place, count,
+            )
+            depth_box, wet_box = box[3], box[4]
+            coef_lon = depth_box[core_rows] * depth_box[core_rows] / (3.0 * LON_SPACING * LON_SPACING)
+            coef_lat = depth_box[:, core_cols] * depth_box[:, core_cols] / (3.0 * LAT_SPACING * LAT_SPACING)
+            plans = (
+                reduction_plan(-coef_lon, 1.0 + 2.0 * coef_lon, -coef_lon, 1),
+                reduction_plan(
+                    jnp.where(inside, -coef_lat, 0.0),
+                    jnp.where(inside, 1.0 + 2.0 * coef_lat, 1.0),
+                    jnp.where(inside, -coef_lat, 0.0),
+                    0,
+                ),
+            )
+        else:
+            box = halo_box(jnp.stack(list(current)), wide_x, wide_y, place, count)
+        surface_box, east_box, north_box = box[0], box[1], box[2]
+        height_box = depth_box + surface_box
+        east_raw = apply_plan(plans[0], east_box[core_rows] / height_box[core_rows], 1)[:, core_cols]
+        north_rights = jnp.where(inside, north_box[:, core_cols] / height_box[:, core_cols], 0.0)
+        north_raw = apply_plan(plans[1], north_rights, 0)[core_rows]
+        wet_core = wet_box[core_rows, core_cols]
+        u_core = wet_core * east_raw
+        v_core = wet_core * north_raw
+        v_core = jnp.where(place == 0, jnp.concatenate([-v_core[3:1:-1], v_core[2:]], axis=0), v_core)
+        v_core = jnp.where(
+            place == count - 1, jnp.concatenate([v_core[:-2], -v_core[-3:-5:-1]], axis=0), v_core
+        )
+        fields = jnp.stack(
+            [surface_box[core_rows, core_cols], u_core, v_core, depth_box[core_rows, core_cols], wet_core]
+        )
+        across = fields[:, 2:-2, :]
+        along = fields[:, :, 2:-2]
+        rate_surface, rate_east, rate_north = tendencies(across, along)
+        rates = (rate_surface + lift, rate_east, rate_north)
+        velocity_u = u_core[2:-2, 2:-2]
+        velocity_v = v_core[2:-2, 2:-2]
         current = tuple(
             (
                 first * start_value + second * (now + TIME_STEP * rate)
@@ -341,20 +312,6 @@
 
 
 def solution(mesh):
-    in_specs = (
-        P("lat", "lon"),
-        P("lat", "lon"),
-        P("lat", "lon"),
-        P("lat", "lon"),
-        P("lat", "lon"),
-        P("lat", "lon"),
-        P("lat", "lon"),
-    )
-    out_specs = (
-        P("lat", "lon"),
-        P("lat", "lon"),
-        P("lat", "lon"),
-        P("lat", "lon"),
-        P("lat", "lon"),
-    )
+    in_specs = (P("lat", "lon"),) * 7
+    out_specs = (P("lat", "lon"),) * 5
     return jax.shard_map(local, mesh=mesh, in_specs=in_specs, out_specs=out_specs, check_vma=False)

time: 150 us -> 171 us (1.14)
  the two profiles are of different devices: /device:TPU:25 before, /device:TPU:2 now
where the time goes in v1:
time: 171 us; the launch traced here: 169 us
  local copies, waits for them, and re-layouts  56.6 us (33%)
  starting transfers between devices  49.4 us (29%)
  waiting for transfers between devices  29.6 us (17%)
  other arithmetic  29.5 us (17%)
  between operations  3.42 us (2%)
    unnamed x262, local copies, waits for them, and re-layouts  42.4 us
    ppermute x3, starting transfers between devices, halo_box(): lax.ppermute(fields[:, :, :wide_x], 'lon', [((i + 1) % lon_count, i) for...  26.5 us
    ppermute x6, waiting for transfers between devices, passed_along(): return lax.ppermute(x, axis, pairs)  17.7 us
    ppermute x6, starting transfers between devices, passed_along(): return lax.ppermute(x, axis, pairs)  15.3 us
    ppermute x3, waiting for transfers between devices, halo_box(): lax.ppermute(fields[:, :, -wide_x:], 'lon', [(i, (i + 1) % lon_count) for...  7.77 us
    ppermute x3, starting transfers between devices, halo_box(): lax.ppermute(fields[:, :, -wide_x:], 'lon', [(i, (i + 1) % lon_count) for...  7.67 us
    slice x92, local copies, waits for them, and re-layouts, slab_of(): return lax.slice_in_dim(values, start, stop, axis=along_axis)  4.72 us
    sub x40, other arithmetic, apply_plan(): rights - weight_below * from_below(rights, stride, along_axis, 0.0)  4.37 us
  transfers between devices with their start and end apart: 12, of which 9 were waited for; matrix products, arithmetic and copies ran while one was open for 5% of the time, Pallas kernels for 0%

profile of v1, /device:TPU:2, one launch (start us, length us, event | category | flops | bytes accessed | tf_op | source)
XLA Modules:
  0.0 168.6 jit_solution(14007813834160343261)
XLA Ops:
  4.1 3.8 %collective-permute-start = (f32[5,112,42]{2,1,0:T(8,128)S(1)}, f32[5,112,42]{2,1,0:T(8,128)S(1)}, u32[]{:S(2)}, u32[]{:S(2)}) collective-permute-start(f32[5,112,42]{2,1,0:T(8,128)S(1)} %get-tuple-element.107), channel_id=1, source_target_pairs={{0,16},{16,32},{32,48},{48,64},{64,80},{80,96},{96,112},{112,128},... | collective-permute-start | bytes 282248 | tf_op jit(solution)/shard_map/ppermute | solution.py:223
  7.9 11.1 %collective-permute-start.1 = (f32[5,112,42]{2,1,0:T(8,128)S(1)}, f32[5,112,42]{2,1,0:T(8,128)S(1)}, u32[]{:S(2)}, u32[]{:S(2)}) collective-permute-start(f32[5,112,42]{2,1,0:T(8,128)S(1)} %get-tuple-element.108), channel_id=1, source_target_pairs={{16,0},{32,16},{48,32},{64,48},{80,64},{96,80},{112,96},{128,112},... | collective-permute-start | bytes 282248 | tf_op jit(solution)/shard_map/ppermute | solution.py:226
  19.0 4.9 %collective-permute-done = f32[5,112,42]{2,1,0:T(8,128)S(1)} collective-permute-done((f32[5,112,42]{2,1,0:T(8,128)S(1)}, f32[5,112,42]{2,1,0:T(8,128)S(1)}, u32[]{:S(2)}, u32[]{:S(2)}) %collective-permute-start) | collective-permute-done | bytes 94112 | tf_op jit(solution)/shard_map/ppermute | solution.py:223
  25.3 4.4 %collective-permute-start.3 = (f32[5,34,212]{2,1,0:T(8,128)S(1)}, f32[5,34,212]{2,1,0:T(8,128)S(1)}, u32[]{:S(2)}, u32[]{:S(2)}) collective-permute-start(f32[5,34,212]{2,1,0:T(8,128)S(1)} %get-tuple-element.91), channel_id=1, source_target_pairs={{1,0},{2,1},{3,2},{4,3},{5,4},{6,5},{7,6},{8,7},{9,8},{10,9},{11,1... | collective-permute-start | bytes 432488 | tf_op jit(solution)/shard_map/ppermute | solution.py:23
  29.7 1.6 scatter_custom_fusion
  31.6 1.9 %collective-permute-start.2 = (f32[5,34,212]{2,1,0:T(8,128)S(1)}, f32[5,34,212]{2,1,0:T(8,128)S(1)}, u32[]{:S(2)}, u32[]{:S(2)}) collective-permute-start(f32[5,34,212]{2,1,0:T(8,128)S(1)} %get-tuple-element.92), channel_id=1, source_target_pairs={{0,1},{1,2},{2,3},{3,4},{4,5},{5,6},{6,7},{7,8},{8,9},{9,10},{10,1... | collective-permute-start | bytes 432488 | tf_op jit(solution)/shard_map/ppermute | solution.py:23
  33.6 7.2 %collective-permute-done.2 = f32[5,34,212]{2,1,0:T(8,128)S(1)} collective-permute-done((f32[5,34,212]{2,1,0:T(8,128)S(1)}, f32[5,34,212]{2,1,0:T(8,128)S(1)}, u32[]{:S(2)}, u32[]{:S(2)}) %collective-permute-start.2) | collective-permute-done | bytes 144192 | tf_op jit(solution)/shard_map/ppermute | solution.py:23
  64.3 1.9 %collective-permute-start.4 = (f32[3,112,42]{2,1,0:T(8,128)S(1)}, f32[3,112,42]{2,1,0:T(8,128)S(1)}, u32[]{:S(2)}, u32[]{:S(2)}) collective-permute-start(f32[3,112,42]{2,1,0:T(8,128)S(1)} %get-tuple-element.216), channel_id=1, source_target_pairs={{0,16},{16,32},{32,48},{48,64},{64,80},{80,96},{96,112},{112,128},... | collective-permute-start | bytes 169352 | tf_op jit(solution)/shard_map/ppermute | solution.py:223
  66.3 7.5 %collective-permute-start.5 = (f32[3,112,42]{2,1,0:T(8,128)S(1)}, f32[3,112,42]{2,1,0:T(8,128)S(1)}, u32[]{:S(2)}, u32[]{:S(2)}) collective-permute-start(f32[3,112,42]{2,1,0:T(8,128)S(1)} %get-tuple-element.217), channel_id=1, source_target_pairs={{16,0},{32,16},{48,32},{64,48},{80,64},{96,80},{112,96},{128,112},... | collective-permute-start | bytes 169352 | tf_op jit(solution)/shard_map/ppermute | solution.py:226
  73.8 1.4 collective-permute-done.4
  75.3 1.5 collective-permute-done.5
  77.5 2.0 %collective-permute-start.7 = (f32[3,34,212]{2,1,0:T(8,128)}, f32[3,34,212]{2,1,0:T(8,128)}, u32[]{:S(2)}, u32[]{:S(2)}) collective-permute-start(f32[3,34,212]{2,1,0:T(8,128)} %get-tuple-element.99), channel_id=1, source_target_pairs={{1,0},{2,1},{3,2},{4,3},{5,4},{6,5},{7,6},{8,7},{9,8},{10,9},{11,1... | collective-permute-start | bytes 259496 | tf_op jit(solution)/shard_map/ppermute | solution.py:23
  79.5 1.5 rev.40
  81.8 2.6 %collective-permute-start.6 = (f32[3,34,212]{2,1,0:T(8,128)S(1)}, f32[3,34,212]{2,1,0:T(8,128)S(1)}, u32[]{:S(2)}, u32[]{:S(2)}) collective-permute-start(f32[3,34,212]{2,1,0:T(8,128)S(1)} %get-tuple-element.100), channel_id=1, source_target_pairs={{0,1},{1,2},{2,3},{3,4},{4,5},{5,6},{6,7},{7,8},{8,9},{9,10},{10,1... | collective-permute-start | bytes 259496 | tf_op jit(solution)/shard_map/ppermute | solution.py:23
  85.3 4.9 %collective-permute-done.6 = f32[3,34,212]{2,1,0:T(8,128)S(1)} collective-permute-done((f32[3,34,212]{2,1,0:T(8,128)S(1)}, f32[3,34,212]{2,1,0:T(8,128)S(1)}, u32[]{:S(2)}, u32[]{:S(2)}) %collective-permute-start.6) | collective-permute-done | bytes 86528 | tf_op jit(solution)/shard_map/ppermute | solution.py:23
  117.7 1.9 %collective-permute-start.8 = (f32[3,112,42]{2,1,0:T(8,128)S(1)}, f32[3,112,42]{2,1,0:T(8,128)S(1)}, u32[]{:S(2)}, u32[]{:S(2)}) collective-permute-start(f32[3,112,42]{2,1,0:T(8,128)S(1)} %get-tuple-element.214), channel_id=1, source_target_pairs={{0,16},{16,32},{32,48},{48,64},{64,80},{80,96},{96,112},{112,128},... | collective-permute-start | bytes 169352 | tf_op jit(solution)/shard_map/ppermute | solution.py:223
  119.6 7.9 %collective-permute-start.9 = (f32[3,112,42]{2,1,0:T(8,128)S(1)}, f32[3,112,42]{2,1,0:T(8,128)S(1)}, u32[]{:S(2)}, u32[]{:S(2)}) collective-permute-start(f32[3,112,42]{2,1,0:T(8,128)S(1)} %get-tuple-element.215), channel_id=1, source_target_pairs={{16,0},{32,16},{48,32},{64,48},{80,64},{96,80},{112,96},{128,112},... | collective-permute-start | bytes 169352 | tf_op jit(solution)/shard_map/ppermute | solution.py:226
  127.5 1.4 collective-permute-done.8
  129.0 1.5 collective-permute-done.9
  131.3 2.4 %collective-permute-start.11 = (f32[3,34,212]{2,1,0:T(8,128)}, f32[3,34,212]{2,1,0:T(8,128)}, u32[]{:S(2)}, u32[]{:S(2)}) collective-permute-start(f32[3,34,212]{2,1,0:T(8,128)} %get-tuple-element.97), channel_id=1, source_target_pairs={{1,0},{2,1},{3,2},{4,3},{5,4},{6,5},{7,6},{8,7},{9,8},{10,9},{11,1... | collective-permute-start | bytes 259496 | tf_op jit(solution)/shard_map/ppermute | solution.py:23
  133.7 1.5 rev.44
  135.2 1.5 rev.45
  136.7 2.0 %collective-permute-start.10 = (f32[3,34,212]{2,1,0:T(8,128)}, f32[3,34,212]{2,1,0:T(8,128)S(1)}, u32[]{:S(2)}, u32[]{:S(2)}) collective-permute-start(f32[3,34,212]{2,1,0:T(8,128)} %get-tuple-element.98), channel_id=1, source_target_pairs={{0,1},{1,2},{2,3},{3,4},{4,5},{5,6},{6,7},{7,8},{8,9},{9,10},{10,1... | collective-permute-start | bytes 259496 | tf_op jit(solution)/shard_map/ppermute | solution.py:23
  139.8 5.6 %collective-permute-done.10 = f32[3,34,212]{2,1,0:T(8,128)S(1)} collective-permute-done((f32[3,34,212]{2,1,0:T(8,128)}, f32[3,34,212]{2,1,0:T(8,128)S(1)}, u32[]{:S(2)}, u32[]{:S(2)}) %collective-permute-start.10) | collective-permute-done | bytes 86528 | tf_op jit(solution)/shard_map/ppermute | solution.py:23
  (559 shorter events, 81.1 us)
Async XLA Ops:
  4.1 19.8 %collective-permute-start = (f32[5,112,42]{2,1,0:T(8,128)S(1)}, f32[5,112,42]{2,1,0:T(8,128)S(1)}, u32[]{:S(2)}, u32[]{:S(2)}) collective-permute-start(f32[5,112,42]{2,1,0:T(8,128)S(1)} %get-tuple-element.107), channel_id=1, source_target_pairs={{0,16},{16,32},{32,48},{48,64},{64,80},{80,96},{96,112},{112,128},... | collective-permute-start | bytes 282248 | tf_op jit(solution)/shard_map/ppermute | solution.py:223
  7.9 17.1 %collective-permute-start.1 = (f32[5,112,42]{2,1,0:T(8,128)S(1)}, f32[5,112,42]{2,1,0:T(8,128)S(1)}, u32[]{:S(2)}, u32[]{:S(2)}) collective-permute-start(f32[5,112,42]{2,1,0:T(8,128)S(1)} %get-tuple-element.108), channel_id=1, source_target_pairs={{16,0},{32,16},{48,32},{64,48},{80,64},{96,80},{112,96},{128,112},... | collective-permute-start | bytes 282248 | tf_op jit(solution)/shard_map/ppermute | solution.py:226
  25.3 8.2 %collective-permute-start.3 = (f32[5,34,212]{2,1,0:T(8,128)S(1)}, f32[5,34,212]{2,1,0:T(8,128)S(1)}, u32[]{:S(2)}, u32[]{:S(2)}) collective-permute-start(f32[5,34,212]{2,1,0:T(8,128)S(1)} %get-tuple-element.91), channel_id=1, source_target_pairs={{1,0},{2,1},{3,2},{4,3},{5,4},{6,5},{7,6},{8,7},{9,8},{10,9},{11,1... | collective-permute-start | bytes 432488 | tf_op jit(solution)/shard_map/ppermute | solution.py:23
  31.6 9.2 %collective-permute-start.2 = (f32[5,34,212]{2,1,0:T(8,128)S(1)}, f32[5,34,212]{2,1,0:T(8,128)S(1)}, u32[]{:S(2)}, u32[]{:S(2)}) collective-permute-start(f32[5,34,212]{2,1,0:T(8,128)S(1)} %get-tuple-element.92), channel_id=1, source_target_pairs={{0,1},{1,2},{2,3},{3,4},{4,5},{5,6},{6,7},{7,8},{8,9},{9,10},{10,1... | collective-permute-start | bytes 432488 | tf_op jit(solution)/shard_map/ppermute | solution.py:23
  41.2 14.1 %copy-start.95 = (f32[180,212]{1,0:T(8,128)}, f32[180,212]{1,0:T(8,128)S(1)}, u32[]{:S(2)}) copy-start(f32[180,212]{1,0:T(8,128)S(1)} %get-tuple-element.90) | copy-start | bytes 457924
  63.3 29.1 %copy-start.55 = (f32[112,128]{1,0:T(8,128)}, f32[112,128]{1,0:T(8,128)S(1)}, u32[]{:S(2)}) copy-start(f32[112,128]{1,0:T(8,128)S(1)} %fusion.208) | copy-start | bytes 172036
  64.2 26.1 %copy-start.59 = (f32[112,128]{1,0:T(8,128)}, f32[112,128]{1,0:T(8,128)S(1)}, u32[]{:S(2)}) copy-start(f32[112,128]{1,0:T(8,128)S(1)} %get-tuple-element.110) | copy-start | bytes 172036
  64.2 28.2 %copy-start.57 = (f32[112,128]{1,0:T(8,128)}, f32[112,128]{1,0:T(8,128)S(1)}, u32[]{:S(2)}) copy-start(f32[112,128]{1,0:T(8,128)S(1)} %get-tuple-element.109) | copy-start | bytes 172036
  64.3 10.9 %collective-permute-start.4 = (f32[3,112,42]{2,1,0:T(8,128)S(1)}, f32[3,112,42]{2,1,0:T(8,128)S(1)}, u32[]{:S(2)}, u32[]{:S(2)}) collective-permute-start(f32[3,112,42]{2,1,0:T(8,128)S(1)} %get-tuple-element.216), channel_id=1, source_target_pairs={{0,16},{16,32},{32,48},{48,64},{64,80},{80,96},{96,112},{112,128},... | collective-permute-start | bytes 169352 | tf_op jit(solution)/shard_map/ppermute | solution.py:223
  66.3 10.4 %collective-permute-start.5 = (f32[3,112,42]{2,1,0:T(8,128)S(1)}, f32[3,112,42]{2,1,0:T(8,128)S(1)}, u32[]{:S(2)}, u32[]{:S(2)}) collective-permute-start(f32[3,112,42]{2,1,0:T(8,128)S(1)} %get-tuple-element.217), channel_id=1, source_target_pairs={{16,0},{32,16},{48,32},{64,48},{80,64},{96,80},{112,96},{128,112},... | collective-permute-start | bytes 169352 | tf_op jit(solution)/shard_map/ppermute | solution.py:226
  77.5 6.9 %collective-permute-start.7 = (f32[3,34,212]{2,1,0:T(8,128)}, f32[3,34,212]{2,1,0:T(8,128)}, u32[]{:S(2)}, u32[]{:S(2)}) collective-permute-start(f32[3,34,212]{2,1,0:T(8,128)} %get-tuple-element.99), channel_id=1, source_target_pairs={{1,0},{2,1},{3,2},{4,3},{5,4},{6,5},{7,6},{8,7},{9,8},{10,9},{11,1... | collective-permute-start | bytes 259496 | tf_op jit(solution)/shard_map/ppermute | solution.py:23
  81.8 8.4 %copy-start.124 = (f32[3,34,212]{2,1,0:T(8,128)S(1)}, f32[3,34,212]{2,1,0:T(8,128)}, u32[]{:S(2)}) copy-start(f32[3,34,212]{2,1,0:T(8,128)} %rev.40) | copy-start | bytes 259492
  81.8 8.4 %collective-permute-start.6 = (f32[3,34,212]{2,1,0:T(8,128)S(1)}, f32[3,34,212]{2,1,0:T(8,128)S(1)}, u32[]{:S(2)}, u32[]{:S(2)}) collective-permute-start(f32[3,34,212]{2,1,0:T(8,128)S(1)} %get-tuple-element.100), channel_id=1, source_target_pairs={{0,1},{1,2},{2,3},{3,4},{4,5},{5,6},{6,7},{7,8},{8,9},{9,10},{10,1... | collective-permute-start | bytes 259496 | tf_op jit(solution)/shard_map/ppermute | solution.py:23
  85.3 4.9 %copy-start.65 = (f32[3,112,42]{2,1,0:T(8,128)S(1)}, f32[3,112,42]{2,1,0:T(8,128)}, u32[]{:S(2)}) copy-start(f32[3,112,42]{2,1,0:T(8,128)} %copy-done.64) | copy-start | bytes 169348
  85.3 4.9 %copy-start.69 = (f32[3,112,42]{2,1,0:T(8,128)S(1)}, f32[3,112,42]{2,1,0:T(8,128)}, u32[]{:S(2)}) copy-start(f32[3,112,42]{2,1,0:T(8,128)} %copy-done.68) | copy-start | bytes 169348
  115.8 30.9 %copy-start.51 = (f32[112,128]{1,0:T(8,128)}, f32[112,128]{1,0:T(8,128)S(1)}, u32[]{:S(2)}) copy-start(f32[112,128]{1,0:T(8,128)S(1)} %fusion.165) | copy-start | bytes 172036
  116.7 30.0 %copy-start.53 = (f32[112,128]{1,0:T(8,128)}, f32[112,128]{1,0:T(8,128)S(1)}, u32[]{:S(2)}) copy-start(f32[112,128]{1,0:T(8,128)S(1)} %fusion.183) | copy-start | bytes 172036
  117.7 11.3 %collective-permute-start.8 = (f32[3,112,42]{2,1,0:T(8,128)S(1)}, f32[3,112,42]{2,1,0:T(8,128)S(1)}, u32[]{:S(2)}, u32[]{:S(2)}) collective-permute-start(f32[3,112,42]{2,1,0:T(8,128)S(1)} %get-tuple-element.214), channel_id=1, source_target_pairs={{0,16},{16,32},{32,48},{48,64},{64,80},{80,96},{96,112},{112,128},... | collective-permute-start | bytes 169352 | tf_op jit(solution)/shard_map/ppermute | solution.py:223
  119.6 10.8 %collective-permute-start.9 = (f32[3,112,42]{2,1,0:T(8,128)S(1)}, f32[3,112,42]{2,1,0:T(8,128)S(1)}, u32[]{:S(2)}, u32[]{:S(2)}) collective-permute-start(f32[3,112,42]{2,1,0:T(8,128)S(1)} %get-tuple-element.215), channel_id=1, source_target_pairs={{16,0},{32,16},{48,32},{64,48},{80,64},{96,80},{112,96},{128,112},... | collective-permute-start | bytes 169352 | tf_op jit(solution)/shard_map/ppermute | solution.py:226
  131.3 7.5 %collective-permute-start.11 = (f32[3,34,212]{2,1,0:T(8,128)}, f32[3,34,212]{2,1,0:T(8,128)}, u32[]{:S(2)}, u32[]{:S(2)}) collective-permute-start(f32[3,34,212]{2,1,0:T(8,128)} %get-tuple-element.97), channel_id=1, source_target_pairs={{1,0},{2,1},{3,2},{4,3},{5,4},{6,5},{7,6},{8,7},{9,8},{10,9},{11,1... | collective-permute-start | bytes 259496 | tf_op jit(solution)/shard_map/ppermute | solution.py:23
  136.7 8.6 %copy-start.125 = (f32[3,34,212]{2,1,0:T(8,128)S(1)}, f32[3,34,212]{2,1,0:T(8,128)}, u32[]{:S(2)}) copy-start(f32[3,34,212]{2,1,0:T(8,128)} %rev.44) | copy-start | bytes 259492
  136.7 8.6 %collective-permute-start.10 = (f32[3,34,212]{2,1,0:T(8,128)}, f32[3,34,212]{2,1,0:T(8,128)S(1)}, u32[]{:S(2)}, u32[]{:S(2)}) collective-permute-start(f32[3,34,212]{2,1,0:T(8,128)} %get-tuple-element.98), channel_id=1, source_target_pairs={{0,1},{1,2},{2,3},{3,4},{4,5},{5,6},{6,7},{7,8},{8,9},{9,10},{10,1... | collective-permute-start | bytes 259496 | tf_op jit(solution)/shard_map/ppermute | solution.py:23
  139.7 5.7 %copy-start.63 = (f32[3,112,42]{2,1,0:T(8,128)S(1)}, f32[3,112,42]{2,1,0:T(8,128)}, u32[]{:S(2)}) copy-start(f32[3,112,42]{2,1,0:T(8,128)} %copy-done.62) | copy-start | bytes 169348
  139.7 5.7 %copy-start.67 = (f32[3,112,42]{2,1,0:T(8,128)S(1)}, f32[3,112,42]{2,1,0:T(8,128)}, u32[]{:S(2)}) copy-start(f32[3,112,42]{2,1,0:T(8,128)} %copy-done.66) | copy-start | bytes 169348
  (117 other events, 108.7 us)

commit v2 on v1

--- a/solution.py
+++ b/solution.py
@@ -2,6 +2,8 @@
 import jax.numpy as jnp
 from jax import lax
 from jax.sharding import PartitionSpec as P
+from jax.experimental import pallas as pl
+from jax.experimental.pallas import tpu as pltpu
 
 GRAVITY = 1.0
 LON_SPACING = 0.5
@@ -9,6 +11,7 @@
 TIME_STEP = 0.1
 WINDOW_LON = 40
 WINDOW_LAT = 32
+PCR_STEPS = 6
 
 
 def shifted(block, axis, distance):
@@ -185,37 +188,64 @@
     return jnp.concatenate([slab_of(values, stride, length, along_axis), padding], along_axis)
 
 
-def reduction_plan(lower_band, main_band, upper_band, along_axis):
-    length = main_band.shape[along_axis]
+def reduction_kernel(lower_ref, main_ref, upper_ref, rights_ref, out_ref, *, along_axis):
+    lower_band, main_band, upper_band = lower_ref[...], main_ref[...], upper_ref[...]
+    rights = rights_ref[...]
+    length = rights.shape[along_axis]
+    position = lax.broadcasted_iota(jnp.int32, rights.shape, along_axis)
     stride = 1
-    weights = []
-    while stride < length:
-        below = [from_below(band, stride, along_axis, fill) for band, fill in
-                 ((lower_band, 0.0), (main_band, 1.0), (upper_band, 0.0))]
-        above = [from_above(band, stride, along_axis, fill) for band, fill in
-                 ((lower_band, 0.0), (main_band, 1.0), (upper_band, 0.0))]
+    for _ in range(PCR_STEPS):
+        def from_lower(values, fill):
+            return jnp.where(position >= stride, pltpu.roll(values, stride, along_axis), fill)
+
+        def from_upper(values, fill):
+            return jnp.where(
+                position < length - stride, pltpu.roll(values, length - stride, along_axis), fill
+            )
+
+        below = [from_lower(band, fill) for band, fill in
+                 ((lower_band, 0.0), (main_band, 1.0), (upper_band, 0.0), (rights, 0.0))]
+        above = [from_upper(band, fill) for band, fill in
+                 ((lower_band, 0.0), (main_band, 1.0), (upper_band, 0.0), (rights, 0.0))]
         weight_below = lower_band / below[1]
         weight_above = upper_band / above[1]
         new_lower = -weight_below * below[0]
         new_main = main_band - weight_below * below[2] - weight_above * above[0]
         new_upper = -weight_above * above[2]
-        weights.append((weight_below, weight_above))
+        rights = rights - weight_below * below[3] - weight_above * above[3]
         lower_band, main_band, upper_band = new_lower, new_main, new_upper
         stride = stride * 2
-    return weights, main_band
-
-
-def apply_plan(plan, rights, along_axis):
-    weights, main_band = plan
-    stride = 1
-    for weight_below, weight_above in weights:
-        rights = (
-            rights
-            - weight_below * from_below(rights, stride, along_axis, 0.0)
-            - weight_above * from_above(rights, stride, along_axis, 0.0)
-        )
-        stride = stride * 2
-    return rights / main_band
+    out_ref[...] = rights / main_band
+
+
+def padded(values, shape, fill):
+    return jnp.pad(
+        values, [(0, want - have) for want, have in zip(shape, values.shape)], constant_values=fill
+    )
+
+
+def line_solve(bands, rights, along_axis):
+    lower_band, main_band, upper_band = bands
+    shape = main_band.shape
+    count = rights.shape
+    spec = pl.BlockSpec(memory_space=pltpu.VMEM)
+    solved = pl.pallas_call(
+        lambda *refs: reduction_kernel(*refs, along_axis=along_axis),
+        out_shape=jax.ShapeDtypeStruct(shape, jnp.float32),
+        in_specs=[spec] * 4,
+        out_specs=spec,
+        name="line_solve",
+    )(lower_band, main_band, upper_band, padded(rights, shape, 0.0))
+    return solved[: count[0], : count[1]]
+
+
+def band_set(coef, keep):
+    shape = tuple(-(-size // unit) * unit for size, unit in zip(coef.shape, (8, 128)))
+    return (
+        padded(jnp.where(keep, -coef, 0.0), shape, 0.0),
+        padded(jnp.where(keep, 1.0 + 2.0 * coef, 1.0), shape, 1.0),
+        padded(jnp.where(keep, -coef, 0.0), shape, 0.0),
+    )
 
 
 def halo_box(fields, wide_x, wide_y, place, count):
@@ -260,9 +290,9 @@
     current = initial
     velocity_u = surface
     velocity_v = surface
-    plans = None
+    bands = None
     for first, second in ((0.0, 1.0), (0.75, 0.25), (1.0 / 3.0, 2.0 / 3.0)):
-        if plans is None:
+        if bands is None:
             box = halo_box(
                 jnp.stack([current[0], current[1], current[2], water_depth, wet_float]),
                 wide_x, wide_y, place, count,
@@ -270,22 +300,14 @@
             depth_box, wet_box = box[3], box[4]
             coef_lon = depth_box[core_rows] * depth_box[core_rows] / (3.0 * LON_SPACING * LON_SPACING)
             coef_lat = depth_box[:, core_cols] * depth_box[:, core_cols] / (3.0 * LAT_SPACING * LAT_SPACING)
-            plans = (
-                reduction_plan(-coef_lon, 1.0 + 2.0 * coef_lon, -coef_lon, 1),
-                reduction_plan(
-                    jnp.where(inside, -coef_lat, 0.0),
-                    jnp.where(inside, 1.0 + 2.0 * coef_lat, 1.0),
-                    jnp.where(inside, -coef_lat, 0.0),
-                    0,
-                ),
-            )
+            bands = (band_set(coef_lon, True), band_set(coef_lat, inside))
         else:
             box = halo_box(jnp.stack(list(current)), wide_x, wide_y, place, count)
         surface_box, east_box, north_box = box[0], box[1], box[2]
         height_box = depth_box + surface_box
-        east_raw = apply_plan(plans[0], east_box[core_rows] / height_box[core_rows], 1)[:, core_cols]
+        east_raw = line_solve(bands[0], east_box[core_rows] / height_box[core_rows], 1)[:, core_cols]
         north_rights = jnp.where(inside, north_box[:, core_cols] / height_box[:, core_cols], 0.0)
-        north_raw = apply_plan(plans[1], north_rights, 0)[core_rows]
+        north_raw = line_solve(bands[1], north_rights, 0)[core_rows]
         wet_core = wet_box[core_rows, core_cols]
         u_core = wet_core * east_raw
         v_core = wet_core * north_raw

time: 171 us -> 137 us (0.80); the launches traced: 169 us -> 137 us
  local copies, waits for them, and re-layouts: 56.6 us -> 14.1 us
  Pallas kernels: 0 us -> 18.3 us
  waiting for transfers between devices: 29.6 us -> 44.6 us
  other arithmetic: 29.5 us -> 16.4 us
  starting transfers between devices: 49.4 us -> 41.4 us
    unnamed x262 -> x22, local copies, waits for them, and re-layouts: 42.4 us -> 3.91 us
    pallas_call x0 -> x6, Pallas kernels: none -> 18.3 us  [line_solve(): pl.pallas_call(lambda *refs: reduction_kernel(*refs, along_axis=along_axi...]
    ppermute x3, waiting for transfers between devices: 7.77 us -> 18.8 us  [halo_box(): lax.ppermute(fields[:, :, -wide_x:], 'lon', [(i, (i + 1) % lon_count) for...]
    ppermute x3, starting transfers between devices: 26.5 us -> 16.8 us  [halo_box(): lax.ppermute(fields[:, :, :wide_x], 'lon', [((i + 1) % lon_count, i) for...]
    pad x0 -> x10, local copies, waits for them, and re-layouts: none -> 6.72 us  [padded(): jnp.pad(values, [(0, want - have) for want, have in zip(shape, values.sha...]
    sub x54 -> x0, other arithmetic: 5.66 us -> none  [the longest x40 4.37 us: apply_plan(): rights - weight_below * from_below(rights, stride, along_axis, 0.0)]
    slice x92 -> x0, local copies, waits for them, and re-layouts: 4.72 us -> none  [slab_of(): return lax.slice_in_dim(values, start, stop, axis=along_axis)]
    ppermute x3, waiting for transfers between devices: 4.1 us -> 7.02 us  [halo_box(): lax.ppermute(fields[:, :, :wide_x], 'lon', [((i + 1) % lon_count, i) for...]
  transfers between devices with their start and end apart: 12 -> 12, of which waited for: 9 -> 9; matrix products, arithmetic and copies ran while one was open for 5% -> 1% of each run, Pallas kernels for 0% -> 0%
where the time goes in v2:
time: 137 us
  waiting for transfers between devices  44.6 us (33%)
  starting transfers between devices  41.4 us (30%)
  Pallas kernels  18.3 us (13%)
  other arithmetic  16.4 us (12%)
  local copies, waits for them, and re-layouts  14.1 us (10%)
  between operations  1.76 us (1%)
    ppermute x3, waiting for transfers between devices, halo_box(): lax.ppermute(fields[:, :, -wide_x:], 'lon', [(i, (i + 1) % lon_count) for...  18.8 us
    ppermute x6, waiting for transfers between devices, passed_along(): return lax.ppermute(x, axis, pairs)  18.8 us
    pallas_call x6, Pallas kernels, line_solve(): pl.pallas_call(lambda *refs: reduction_kernel(*refs, along_axis=along_axi...  18.3 us
    ppermute x3, starting transfers between devices, halo_box(): lax.ppermute(fields[:, :, :wide_x], 'lon', [((i + 1) % lon_count, i) for...  16.8 us
    ppermute x6, starting transfers between devices, passed_along(): return lax.ppermute(x, axis, pairs)  14.8 us
    ppermute x3, starting transfers between devices, halo_box(): lax.ppermute(fields[:, :, -wide_x:], 'lon', [(i, (i + 1) % lon_count) for...  9.76 us
    ppermute x3, waiting for transfers between devices, halo_box(): lax.ppermute(fields[:, :, :wide_x], 'lon', [((i + 1) % lon_count, i) for...  7.02 us
    pad x10, local copies, waits for them, and re-layouts, padded(): jnp.pad(values, [(0, want - have) for want, have in zip(shape, values.sha...  6.72 us
  transfers between devices with their start and end apart: 12, of which 9 were waited for; matrix products, arithmetic and copies ran while one was open for 1% of the time, Pallas kernels for 0%

profile of v2, /device:TPU:2, one launch (start us, length us, event | category | flops | bytes accessed | tf_op | source)
XLA Modules:
  0.0 136.5 jit_solution(8812330822093309823)
XLA Ops:
  4.1 13.0 %collective-permute-start.1 = (f32[5,112,42]{2,1,0:T(8,128)S(1)}, f32[5,112,42]{2,1,0:T(8,128)S(1)}, u32[]{:S(2)}, u32[]{:S(2)}) collective-permute-start(f32[5,112,42]{2,1,0:T(8,128)S(1)} %get-tuple-element.37), channel_id=1, source_target_pairs={{16,0},{32,16},{48,32},{64,48},{80,64},{96,80},{112,96},{128,112},... | collective-permute-start | bytes 282248 | tf_op jit(solution)/shard_map/ppermute | solution.py:256
  17.1 1.9 %collective-permute-start = (f32[5,112,42]{2,1,0:T(8,128)S(1)}, f32[5,112,42]{2,1,0:T(8,128)S(1)}, u32[]{:S(2)}, u32[]{:S(2)}) collective-permute-start(f32[5,112,42]{2,1,0:T(8,128)S(1)} %get-tuple-element.36), channel_id=1, source_target_pairs={{0,16},{16,32},{32,48},{48,64},{64,80},{80,96},{96,112},{112,128},... | collective-permute-start | bytes 282248 | tf_op jit(solution)/shard_map/ppermute | solution.py:253
  19.0 4.1 %collective-permute-done.1 = f32[5,112,42]{2,1,0:T(8,128)S(1)} collective-permute-done((f32[5,112,42]{2,1,0:T(8,128)S(1)}, f32[5,112,42]{2,1,0:T(8,128)S(1)}, u32[]{:S(2)}, u32[]{:S(2)}) %collective-permute-start.1) | collective-permute-done | bytes 94112 | tf_op jit(solution)/shard_map/ppermute | solution.py:256
  23.1 7.7 %collective-permute-done = f32[5,112,42]{2,1,0:T(8,128)S(1)} collective-permute-done((f32[5,112,42]{2,1,0:T(8,128)S(1)}, f32[5,112,42]{2,1,0:T(8,128)S(1)}, u32[]{:S(2)}, u32[]{:S(2)}) %collective-permute-start) | collective-permute-done | bytes 94112 | tf_op jit(solution)/shard_map/ppermute | solution.py:253
  31.1 4.0 %collective-permute-start.3 = (f32[5,34,212]{2,1,0:T(8,128)S(1)}, f32[5,34,212]{2,1,0:T(8,128)S(1)}, u32[]{:S(2)}, u32[]{:S(2)}) collective-permute-start(f32[5,34,212]{2,1,0:T(8,128)S(1)} %get-tuple-element.20), channel_id=1, source_target_pairs={{1,0},{2,1},{3,2},{4,3},{5,4},{6,5},{7,6},{8,7},{9,8},{10,9},{11,1... | collective-permute-start | bytes 432488 | tf_op jit(solution)/shard_map/ppermute | solution.py:26
  36.5 1.9 %collective-permute-start.2 = (f32[5,34,212]{2,1,0:T(8,128)S(1)}, f32[5,34,212]{2,1,0:T(8,128)S(1)}, u32[]{:S(2)}, u32[]{:S(2)}) collective-permute-start(f32[5,34,212]{2,1,0:T(8,128)S(1)} %get-tuple-element.21), channel_id=1, source_target_pairs={{0,1},{1,2},{2,3},{3,4},{4,5},{5,6},{6,7},{7,8},{8,9},{9,10},{10,1... | collective-permute-start | bytes 432488 | tf_op jit(solution)/shard_map/ppermute | solution.py:26
  38.5 7.2 %collective-permute-done.2 = f32[5,34,212]{2,1,0:T(8,128)S(1)} collective-permute-done((f32[5,34,212]{2,1,0:T(8,128)S(1)}, f32[5,34,212]{2,1,0:T(8,128)S(1)}, u32[]{:S(2)}, u32[]{:S(2)}) %collective-permute-start.2) | collective-permute-done | bytes 144192 | tf_op jit(solution)/shard_map/ppermute | solution.py:26
  50.9 3.3 %line_solve.6 = f32[120,256]{1,0:T(8,128)} custom-call(f32[120,256]{1,0:T(8,128)} %pad.34.refs_0_.refs_2_, f32[120,256]{1,0:T(8,128)} %pad.35.refs_1_, f32[120,256]{1,0:T(8,128)} %pad.34.refs_0_.refs_2_, f32[120,256]{1,0:T(8,128)} %pad.36.refs_3_), custom_call_target="tpu_custom_call" | custom-call | tf_op jit(solution)/shard_map/line_solve/pallas_call | solution.py:232
  54.2 2.8 %line_solve.7 = f32[184,256]{1,0:T(8,128)} custom-call(f32[184,256]{1,0:T(8,128)} %pad.37.refs_0_.refs_2_, f32[184,256]{1,0:T(8,128)} %pad.38.refs_1_, f32[184,256]{1,0:T(8,128)} %pad.37.refs_0_.refs_2_, f32[184,256]{1,0:T(8,128)} %pad.39.refs_3_), custom_call_target="tpu_custom_call" | custom-call | tf_op jit(solution)/shard_map/line_solve/pallas_call | solution.py:232
  62.1 1.9 %collective-permute-start.5 = (f32[3,112,42]{2,1,0:T(8,128)S(1)}, f32[3,112,42]{2,1,0:T(8,128)S(1)}, u32[]{:S(2)}, u32[]{:S(2)}) collective-permute-start(f32[3,112,42]{2,1,0:T(8,128)S(1)} %get-tuple-element.52), channel_id=1, source_target_pairs={{16,0},{32,16},{48,32},{64,48},{80,64},{96,80},{112,96},{128,112},... | collective-permute-start | bytes 169352 | tf_op jit(solution)/shard_map/ppermute | solution.py:256
  64.0 3.9 %collective-permute-start.4 = (f32[3,112,42]{2,1,0:T(8,128)S(1)}, f32[3,112,42]{2,1,0:T(8,128)S(1)}, u32[]{:S(2)}, u32[]{:S(2)}) collective-permute-start(f32[3,112,42]{2,1,0:T(8,128)S(1)} %get-tuple-element.51), channel_id=1, source_target_pairs={{0,16},{16,32},{32,48},{48,64},{64,80},{80,96},{96,112},{112,128},... | collective-permute-start | bytes 169352 | tf_op jit(solution)/shard_map/ppermute | solution.py:253
  69.4 5.5 %collective-permute-done.4 = f32[3,112,42]{2,1,0:T(8,128)S(1)} collective-permute-done((f32[3,112,42]{2,1,0:T(8,128)S(1)}, f32[3,112,42]{2,1,0:T(8,128)S(1)}, u32[]{:S(2)}, u32[]{:S(2)}) %collective-permute-start.4) | collective-permute-done | bytes 56480 | tf_op jit(solution)/shard_map/ppermute | solution.py:253
  75.1 1.9 %collective-permute-start.7 = (f32[3,34,212]{2,1,0:T(8,128)S(1)}, f32[3,34,212]{2,1,0:T(8,128)S(1)}, u32[]{:S(2)}, u32[]{:S(2)}) collective-permute-start(f32[3,34,212]{2,1,0:T(8,128)S(1)} %get-tuple-element.28), channel_id=1, source_target_pairs={{1,0},{2,1},{3,2},{4,3},{5,4},{6,5},{7,6},{8,7},{9,8},{10,9},{11,1... | collective-permute-start | bytes 259496 | tf_op jit(solution)/shard_map/ppermute | solution.py:26
  77.3 2.6 %collective-permute-start.6 = (f32[3,34,212]{2,1,0:T(8,128)S(1)}, f32[3,34,212]{2,1,0:T(8,128)S(1)}, u32[]{:S(2)}, u32[]{:S(2)}) collective-permute-start(f32[3,34,212]{2,1,0:T(8,128)S(1)} %get-tuple-element.29), channel_id=1, source_target_pairs={{0,1},{1,2},{2,3},{3,4},{4,5},{5,6},{6,7},{7,8},{8,9},{9,10},{10,1... | collective-permute-start | bytes 259496 | tf_op jit(solution)/shard_map/ppermute | solution.py:26
  79.9 5.7 %collective-permute-done.6 = f32[3,34,212]{2,1,0:T(8,128)S(1)} collective-permute-done((f32[3,34,212]{2,1,0:T(8,128)S(1)}, f32[3,34,212]{2,1,0:T(8,128)S(1)}, u32[]{:S(2)}, u32[]{:S(2)}) %collective-permute-start.6) | collective-permute-done | bytes 86528 | tf_op jit(solution)/shard_map/ppermute | solution.py:26
  86.5 3.3 %line_solve.8 = f32[120,256]{1,0:T(8,128)} custom-call(f32[120,256]{1,0:T(8,128)} %pad.34.refs_0_.refs_2_, f32[120,256]{1,0:T(8,128)} %pad.35.refs_1_, f32[120,256]{1,0:T(8,128)} %pad.34.refs_0_.refs_2_, f32[120,256]{1,0:T(8,128)} %pad.40.refs_3_), custom_call_target="tpu_custom_call" | custom-call | tf_op jit(solution)/shard_map/line_solve/pallas_call | solution.py:232
  90.8 2.8 %line_solve.9 = f32[184,256]{1,0:T(8,128)} custom-call(f32[184,256]{1,0:T(8,128)} %pad.37.refs_0_.refs_2_, f32[184,256]{1,0:T(8,128)} %pad.38.refs_1_, f32[184,256]{1,0:T(8,128)} %pad.37.refs_0_.refs_2_, f32[184,256]{1,0:T(8,128)} %pad.41.refs_3_), custom_call_target="tpu_custom_call" | custom-call | tf_op jit(solution)/shard_map/line_solve/pallas_call | solution.py:232
  99.7 3.9 %collective-permute-start.8 = (f32[3,112,42]{2,1,0:T(8,128)S(1)}, f32[3,112,42]{2,1,0:T(8,128)S(1)}, u32[]{:S(2)}, u32[]{:S(2)}) collective-permute-start(f32[3,112,42]{2,1,0:T(8,128)S(1)} %get-tuple-element.49), channel_id=1, source_target_pairs={{0,16},{16,32},{32,48},{48,64},{64,80},{80,96},{96,112},{112,128},... | collective-permute-start | bytes 169352 | tf_op jit(solution)/shard_map/ppermute | solution.py:253
  105.1 5.5 %collective-permute-done.8 = f32[3,112,42]{2,1,0:T(8,128)S(1)} collective-permute-done((f32[3,112,42]{2,1,0:T(8,128)S(1)}, f32[3,112,42]{2,1,0:T(8,128)S(1)}, u32[]{:S(2)}, u32[]{:S(2)}) %collective-permute-start.8) | collective-permute-done | bytes 56480 | tf_op jit(solution)/shard_map/ppermute | solution.py:253
  110.8 1.9 %collective-permute-start.11 = (f32[3,34,212]{2,1,0:T(8,128)S(1)}, f32[3,34,212]{2,1,0:T(8,128)S(1)}, u32[]{:S(2)}, u32[]{:S(2)}) collective-permute-start(f32[3,34,212]{2,1,0:T(8,128)S(1)} %get-tuple-element.26), channel_id=1, source_target_pairs={{1,0},{2,1},{3,2},{4,3},{5,4},{6,5},{7,6},{8,7},{9,8},{10,9},{11,1... | collective-permute-start | bytes 259496 | tf_op jit(solution)/shard_map/ppermute | solution.py:26
  112.9 2.4 %collective-permute-start.10 = (f32[3,34,212]{2,1,0:T(8,128)S(1)}, f32[3,34,212]{2,1,0:T(8,128)S(1)}, u32[]{:S(2)}, u32[]{:S(2)}) collective-permute-start(f32[3,34,212]{2,1,0:T(8,128)S(1)} %get-tuple-element.27), channel_id=1, source_target_pairs={{0,1},{1,2},{2,3},{3,4},{4,5},{5,6},{6,7},{7,8},{8,9},{9,10},{10,1... | collective-permute-start | bytes 259496 | tf_op jit(solution)/shard_map/ppermute | solution.py:26
  115.4 5.9 %collective-permute-done.10 = f32[3,34,212]{2,1,0:T(8,128)S(1)} collective-permute-done((f32[3,34,212]{2,1,0:T(8,128)S(1)}, f32[3,34,212]{2,1,0:T(8,128)S(1)}, u32[]{:S(2)}, u32[]{:S(2)}) %collective-permute-start.10) | collective-permute-done | bytes 86528 | tf_op jit(solution)/shard_map/ppermute | solution.py:26
  122.2 3.3 %line_solve.10 = f32[120,256]{1,0:T(8,128)} custom-call(f32[120,256]{1,0:T(8,128)} %pad.34.refs_0_.refs_2_, f32[120,256]{1,0:T(8,128)} %pad.35.refs_1_, f32[120,256]{1,0:T(8,128)} %pad.34.refs_0_.refs_2_, f32[120,256]{1,0:T(8,128)} %pad.42.refs_3_), custom_call_target="tpu_custom_call" | custom-call | tf_op jit(solution)/shard_map/line_solve/pallas_call | solution.py:232
  126.5 2.8 %line_solve.11 = f32[184,256]{1,0:T(8,128)} custom-call(f32[184,256]{1,0:T(8,128)} %pad.37.refs_0_.refs_2_, f32[184,256]{1,0:T(8,128)} %pad.38.refs_1_, f32[184,256]{1,0:T(8,128)} %pad.37.refs_0_.refs_2_, f32[184,256]{1,0:T(8,128)} %pad.43.refs_3_), custom_call_target="tpu_custom_call" | custom-call | tf_op jit(solution)/shard_map/line_solve/pallas_call | solution.py:232
  (179 shorter events, 35.3 us)
Async XLA Ops:
  0.6 0.9 copy-start
  1.5 0.8 copy-start.1
  2.3 0.8 copy-start.6
  3.1 0.8 copy-start.7
  4.1 19.0 %collective-permute-start.1 = (f32[5,112,42]{2,1,0:T(8,128)S(1)}, f32[5,112,42]{2,1,0:T(8,128)S(1)}, u32[]{:S(2)}, u32[]{:S(2)}) collective-permute-start(f32[5,112,42]{2,1,0:T(8,128)S(1)} %get-tuple-element.37), channel_id=1, source_target_pairs={{16,0},{32,16},{48,32},{64,48},{80,64},{96,80},{112,96},{128,112},... | collective-permute-start | bytes 282248 | tf_op jit(solution)/shard_map/ppermute | solution.py:256
  17.1 13.8 %collective-permute-start = (f32[5,112,42]{2,1,0:T(8,128)S(1)}, f32[5,112,42]{2,1,0:T(8,128)S(1)}, u32[]{:S(2)}, u32[]{:S(2)}) collective-permute-start(f32[5,112,42]{2,1,0:T(8,128)S(1)} %get-tuple-element.36), channel_id=1, source_target_pairs={{0,16},{16,32},{32,48},{48,64},{64,80},{80,96},{96,112},{112,128},... | collective-permute-start | bytes 282248 | tf_op jit(solution)/shard_map/ppermute | solution.py:253
  31.1 4.1 %copy-start.8 = (s32[1,64]{1,0:T(1,128)S(1)}, s32[1,64]{1,0:T(1,128)}, u32[]{:S(2)}) copy-start(s32[1,64]{1,0:T(1,128)} %param.12) | copy-start | bytes 772
  31.1 7.4 %collective-permute-start.3 = (f32[5,34,212]{2,1,0:T(8,128)S(1)}, f32[5,34,212]{2,1,0:T(8,128)S(1)}, u32[]{:S(2)}, u32[]{:S(2)}) collective-permute-start(f32[5,34,212]{2,1,0:T(8,128)S(1)} %get-tuple-element.20), channel_id=1, source_target_pairs={{1,0},{2,1},{3,2},{4,3},{5,4},{6,5},{7,6},{8,7},{9,8},{10,9},{11,1... | collective-permute-start | bytes 432488 | tf_op jit(solution)/shard_map/ppermute | solution.py:26
  36.5 9.2 %collective-permute-start.2 = (f32[5,34,212]{2,1,0:T(8,128)S(1)}, f32[5,34,212]{2,1,0:T(8,128)S(1)}, u32[]{:S(2)}, u32[]{:S(2)}) collective-permute-start(f32[5,34,212]{2,1,0:T(8,128)S(1)} %get-tuple-element.21), channel_id=1, source_target_pairs={{0,1},{1,2},{2,3},{3,4},{4,5},{5,6},{6,7},{7,8},{8,9},{9,10},{10,1... | collective-permute-start | bytes 432488 | tf_op jit(solution)/shard_map/ppermute | solution.py:26
  54.2 2.8 %copy-start.5 = (f32[120,256]{1,0:T(8,128)S(1)}, f32[120,256]{1,0:T(8,128)}, u32[]{:S(2)}) copy-start(f32[120,256]{1,0:T(8,128)} %line_solve.6) | copy-start | bytes 368644
  60.9 0.8 copy-start.2
  62.1 7.3 %collective-permute-start.5 = (f32[3,112,42]{2,1,0:T(8,128)S(1)}, f32[3,112,42]{2,1,0:T(8,128)S(1)}, u32[]{:S(2)}, u32[]{:S(2)}) collective-permute-start(f32[3,112,42]{2,1,0:T(8,128)S(1)} %get-tuple-element.52), channel_id=1, source_target_pairs={{16,0},{32,16},{48,32},{64,48},{80,64},{96,80},{112,96},{128,112},... | collective-permute-start | bytes 169352 | tf_op jit(solution)/shard_map/ppermute | solution.py:256
  64.0 10.9 %collective-permute-start.4 = (f32[3,112,42]{2,1,0:T(8,128)S(1)}, f32[3,112,42]{2,1,0:T(8,128)S(1)}, u32[]{:S(2)}, u32[]{:S(2)}) collective-permute-start(f32[3,112,42]{2,1,0:T(8,128)S(1)} %get-tuple-element.51), channel_id=1, source_target_pairs={{0,16},{16,32},{32,48},{48,64},{64,80},{80,96},{96,112},{112,128},... | collective-permute-start | bytes 169352 | tf_op jit(solution)/shard_map/ppermute | solution.py:253
  75.1 4.8 %collective-permute-start.7 = (f32[3,34,212]{2,1,0:T(8,128)S(1)}, f32[3,34,212]{2,1,0:T(8,128)S(1)}, u32[]{:S(2)}, u32[]{:S(2)}) collective-permute-start(f32[3,34,212]{2,1,0:T(8,128)S(1)} %get-tuple-element.28), channel_id=1, source_target_pairs={{1,0},{2,1},{3,2},{4,3},{5,4},{6,5},{7,6},{8,7},{9,8},{10,9},{11,1... | collective-permute-start | bytes 259496 | tf_op jit(solution)/shard_map/ppermute | solution.py:26
  77.3 8.3 %collective-permute-start.6 = (f32[3,34,212]{2,1,0:T(8,128)S(1)}, f32[3,34,212]{2,1,0:T(8,128)S(1)}, u32[]{:S(2)}, u32[]{:S(2)}) collective-permute-start(f32[3,34,212]{2,1,0:T(8,128)S(1)} %get-tuple-element.29), channel_id=1, source_target_pairs={{0,1},{1,2},{2,3},{3,4},{4,5},{5,6},{6,7},{7,8},{8,9},{9,10},{10,1... | collective-permute-start | bytes 259496 | tf_op jit(solution)/shard_map/ppermute | solution.py:26
  90.8 2.8 %copy-start.4 = (f32[120,256]{1,0:T(8,128)S(1)}, f32[120,256]{1,0:T(8,128)}, u32[]{:S(2)}) copy-start(f32[120,256]{1,0:T(8,128)} %line_solve.8) | copy-start | bytes 368644
  97.8 7.3 %collective-permute-start.9 = (f32[3,112,42]{2,1,0:T(8,128)S(1)}, f32[3,112,42]{2,1,0:T(8,128)S(1)}, u32[]{:S(2)}, u32[]{:S(2)}) collective-permute-start(f32[3,112,42]{2,1,0:T(8,128)S(1)} %get-tuple-element.50), channel_id=1, source_target_pairs={{16,0},{32,16},{48,32},{64,48},{80,64},{96,80},{112,96},{128,112},... | collective-permute-start | bytes 169352 | tf_op jit(solution)/shard_map/ppermute | solution.py:256
  99.7 10.9 %collective-permute-start.8 = (f32[3,112,42]{2,1,0:T(8,128)S(1)}, f32[3,112,42]{2,1,0:T(8,128)S(1)}, u32[]{:S(2)}, u32[]{:S(2)}) collective-permute-start(f32[3,112,42]{2,1,0:T(8,128)S(1)} %get-tuple-element.49), channel_id=1, source_target_pairs={{0,16},{16,32},{32,48},{48,64},{64,80},{80,96},{96,112},{112,128},... | collective-permute-start | bytes 169352 | tf_op jit(solution)/shard_map/ppermute | solution.py:253
  110.8 4.6 %collective-permute-start.11 = (f32[3,34,212]{2,1,0:T(8,128)S(1)}, f32[3,34,212]{2,1,0:T(8,128)S(1)}, u32[]{:S(2)}, u32[]{:S(2)}) collective-permute-start(f32[3,34,212]{2,1,0:T(8,128)S(1)} %get-tuple-element.26), channel_id=1, source_target_pairs={{1,0},{2,1},{3,2},{4,3},{5,4},{6,5},{7,6},{8,7},{9,8},{10,9},{11,1... | collective-permute-start | bytes 259496 | tf_op jit(solution)/shard_map/ppermute | solution.py:26
  112.9 8.3 %collective-permute-start.10 = (f32[3,34,212]{2,1,0:T(8,128)S(1)}, f32[3,34,212]{2,1,0:T(8,128)S(1)}, u32[]{:S(2)}, u32[]{:S(2)}) collective-permute-start(f32[3,34,212]{2,1,0:T(8,128)S(1)} %get-tuple-element.27), channel_id=1, source_target_pairs={{0,1},{1,2},{2,3},{3,4},{4,5},{5,6},{6,7},{7,8},{8,9},{9,10},{10,1... | collective-permute-start | bytes 259496 | tf_op jit(solution)/shard_map/ppermute | solution.py:26
  126.5 2.8 %copy-start.3 = (f32[120,256]{1,0:T(8,128)S(1)}, f32[120,256]{1,0:T(8,128)}, u32[]{:S(2)}) copy-start(f32[120,256]{1,0:T(8,128)} %line_solve.10) | copy-start | bytes 368644

commit v3 on v2

--- a/solution.py
+++ b/solution.py
@@ -248,20 +248,33 @@
     )
 
 
+def moved(block, lat_step, lon_step):
+    lat_count = lax.axis_size("lat")
+    lon_count = lax.axis_size("lon")
+    pairs = [
+        (lon * lat_count + lat, ((lon + lon_step) % lon_count) * lat_count + lat + lat_step)
+        for lon in range(lon_count)
+        for lat in range(lat_count)
+        if 0 <= lat + lat_step < lat_count
+    ]
+    return lax.ppermute(block, ("lon", "lat"), pairs)
+
+
 def halo_box(fields, wide_x, wide_y, place, count):
-    lon_count = lax.axis_size("lon")
-    west = lax.ppermute(
-        fields[:, :, -wide_x:], "lon", [(i, (i + 1) % lon_count) for i in range(lon_count)]
-    )
-    east = lax.ppermute(
-        fields[:, :, :wide_x], "lon", [((i + 1) % lon_count, i) for i in range(lon_count)]
-    )
+    west = moved(fields[:, :, -wide_x:], 0, 1)
+    east = moved(fields[:, :, :wide_x], 0, -1)
+    above = moved(fields[:, -wide_y:], 1, 0)
+    below = moved(fields[:, :wide_y], -1, 0)
+    above_west = moved(fields[:, -wide_y:, -wide_x:], 1, 1)
+    above_east = moved(fields[:, -wide_y:, :wide_x], 1, -1)
+    below_west = moved(fields[:, :wide_y, -wide_x:], -1, 1)
+    below_east = moved(fields[:, :wide_y, :wide_x], -1, -1)
     wide = jnp.concatenate([west, fields, east], axis=2)
-    above = passed_along(wide[:, -wide_y:], "lat", 1)
-    below = passed_along(wide[:, :wide_y], "lat", -1)
-    above = jnp.where(place == 0, wide[:, wide_y - 1 :: -1], above)
-    below = jnp.where(place == count - 1, wide[:, : -wide_y - 1 : -1], below)
-    return jnp.concatenate([above, wide, below], axis=1)
+    top = jnp.concatenate([above_west, above, above_east], axis=2)
+    bottom = jnp.concatenate([below_west, below, below_east], axis=2)
+    top = jnp.where(place == 0, wide[:, wide_y - 1 :: -1], top)
+    bottom = jnp.where(place == count - 1, wide[:, : -wide_y - 1 : -1], bottom)
+    return jnp.concatenate([top, wide, bottom], axis=1)
 
 
 def local(surface, momentum_x, momentum_y, water_depth, wet_mask, slide_cells, slide_rate):

time: 137 us -> 178 us (1.30)
  the two profiles are of different devices: /device:TPU:2 before, /device:TPU:25 now
where the time goes in v3:
time: 178 us; the launch traced here: 176 us
  starting transfers between devices  103 us (58%)
  waiting for transfers between devices  21.1 us (12%)
  Pallas kernels  18.3 us (10%)
  other arithmetic  17 us (10%)
  local copies, waits for them, and re-layouts  15.1 us (8%)
  between operations  2.02 us (1%)
    ppermute x24, starting transfers between devices, moved(): return lax.ppermute(block, ('lon', 'lat'), pairs)  103 us
    ppermute x24, waiting for transfers between devices, moved(): return lax.ppermute(block, ('lon', 'lat'), pairs)  21.1 us
    pallas_call x6, Pallas kernels, line_solve(): pl.pallas_call(lambda *refs: reduction_kernel(*refs, along_axis=along_axi...  18.3 us
    pad x10, local copies, waits for them, and re-layouts, padded(): jnp.pad(values, [(0, want - have) for want, have in zip(shape, values.sha...  6.75 us
    unnamed x22, local copies, waits for them, and re-layouts  4.56 us
  transfers between devices with their start and end apart: 24, of which 3 were waited for; matrix products, arithmetic and copies ran while one was open for 2% of the time, Pallas kernels for 0%

profile of v3, /device:TPU:25, one launch (start us, length us, event | category | flops | bytes accessed | tf_op | source)
XLA Modules:
  0.0 176.3 jit_solution(12246472338790200109)
XLA Ops:
  4.1 13.6 %collective-permute-start.1 = (f32[5,112,42]{2,1,0:T(8,128)S(1)}, f32[5,112,42]{2,1,0:T(8,128)S(1)}, u32[]{:S(2)}, u32[]{:S(2)}) collective-permute-start(f32[5,112,42]{2,1,0:T(8,128)S(1)} %get-tuple-element.43), channel_id=1, source_target_pairs={{0,496},{1,497},{2,498},{3,499},{4,500},{5,501},{6,502},{7,503},{8... | collective-permute-start | bytes 282248 | tf_op jit(solution)/shard_map/ppermute | solution.py:260
  19.7 8.1 %collective-permute-start.7 = (f32[5,34,42]{2,1,0:T(8,128)S(1)}, f32[5,34,42]{2,1,0:T(8,128)S(1)}, u32[]{:S(2)}, u32[]{:S(2)}) collective-permute-start(f32[5,34,42]{2,1,0:T(8,128)S(1)} %get-tuple-element.37), channel_id=1, source_target_pairs={{1,496},{2,497},{3,498},{4,499},{5,500},{6,501},{7,502},{8,503},{9... | collective-permute-start | bytes 85688 | tf_op jit(solution)/shard_map/ppermute | solution.py:260
  33.5 9.1 %collective-permute-start.4 = (f32[5,34,42]{2,1,0:T(8,128)S(1)}, f32[5,34,42]{2,1,0:T(8,128)S(1)}, u32[]{:S(2)}, u32[]{:S(2)}) collective-permute-start(f32[5,34,42]{2,1,0:T(8,128)S(1)} %get-tuple-element.39), channel_id=1, source_target_pairs={{0,497},{1,498},{2,499},{3,500},{4,501},{5,502},{6,503},{7,504},{8... | collective-permute-start | bytes 85688 | tf_op jit(solution)/shard_map/ppermute | solution.py:260
  42.6 3.9 %collective-permute-start.3 = (f32[5,34,128]{2,1,0:T(8,128)S(1)}, f32[5,34,128]{2,1,0:T(8,128)S(1)}, u32[]{:S(2)}, u32[]{:S(2)}) collective-permute-start(f32[5,34,128]{2,1,0:T(8,128)S(1)} %get-tuple-element.40), channel_id=1, source_target_pairs={{0,1},{1,2},{2,3},{3,4},{4,5},{5,6},{6,7},{7,8},{8,9},{9,10},{10,1... | collective-permute-start | bytes 261128 | tf_op jit(solution)/shard_map/ppermute | solution.py:260
  46.9 1.9 %collective-permute-start.2 = (f32[5,34,42]{2,1,0:T(8,128)S(1)}, f32[5,34,42]{2,1,0:T(8,128)S(1)}, u32[]{:S(2)}, u32[]{:S(2)}) collective-permute-start(f32[5,34,42]{2,1,0:T(8,128)S(1)} %get-tuple-element.36), channel_id=1, source_target_pairs={{0,17},{1,18},{2,19},{3,20},{4,21},{5,22},{6,23},{7,24},{8,25},{9,... | collective-permute-start | bytes 85688 | tf_op jit(solution)/shard_map/ppermute | solution.py:260
  49.2 7.3 %collective-permute-done.2 = f32[5,34,42]{2,1,0:T(8,128)S(1)} collective-permute-done((f32[5,34,42]{2,1,0:T(8,128)S(1)}, f32[5,34,42]{2,1,0:T(8,128)S(1)}, u32[]{:S(2)}, u32[]{:S(2)}) %collective-permute-start.2) | collective-permute-done | bytes 28592 | tf_op jit(solution)/shard_map/ppermute | solution.py:260
  61.9 3.3 %line_solve.6 = f32[120,256]{1,0:T(8,128)} custom-call(f32[120,256]{1,0:T(8,128)} %pad.34.refs_0_.refs_2_, f32[120,256]{1,0:T(8,128)} %pad.35.refs_1_, f32[120,256]{1,0:T(8,128)} %pad.34.refs_0_.refs_2_, f32[120,256]{1,0:T(8,128)} %pad.36.refs_3_), custom_call_target="tpu_custom_call" | custom-call | tf_op jit(solution)/shard_map/line_solve/pallas_call | solution.py:232
  65.1 2.8 %line_solve.7 = f32[184,256]{1,0:T(8,128)} custom-call(f32[184,256]{1,0:T(8,128)} %pad.37.refs_0_.refs_2_, f32[184,256]{1,0:T(8,128)} %pad.38.refs_1_, f32[184,256]{1,0:T(8,128)} %pad.37.refs_0_.refs_2_, f32[184,256]{1,0:T(8,128)} %pad.39.refs_3_), custom_call_target="tpu_custom_call" | custom-call | tf_op jit(solution)/shard_map/line_solve/pallas_call | solution.py:232
  75.1 3.4 %collective-permute-start.8 = (f32[3,112,42]{2,1,0:T(8,128)S(1)}, f32[3,112,42]{2,1,0:T(8,128)S(1)}, u32[]{:S(2)}, u32[]{:S(2)}) collective-permute-start(f32[3,112,42]{2,1,0:T(8,128)S(1)} %get-tuple-element.69), channel_id=1, source_target_pairs={{0,16},{1,17},{2,18},{3,19},{4,20},{5,21},{6,22},{7,23},{8,24},{9,... | collective-permute-start | bytes 169352 | tf_op jit(solution)/shard_map/ppermute | solution.py:260
  78.4 6.0 %collective-permute-start.15 = (f32[3,34,42]{2,1,0:T(8,128)S(1)}, f32[3,34,42]{2,1,0:T(8,128)S(1)}, u32[]{:S(2)}, u32[]{:S(2)}) collective-permute-start(f32[3,34,42]{2,1,0:T(8,128)S(1)} %get-tuple-element.66), channel_id=1, source_target_pairs={{1,496},{2,497},{3,498},{4,499},{5,500},{6,501},{7,502},{8,503},{9... | collective-permute-start | bytes 51416 | tf_op jit(solution)/shard_map/ppermute | solution.py:260
  86.4 1.9 %collective-permute-start.13 = (f32[3,34,42]{2,1,0:T(8,128)S(1)}, f32[3,34,42]{2,1,0:T(8,128)S(1)}, u32[]{:S(2)}, u32[]{:S(2)}) collective-permute-start(f32[3,34,42]{2,1,0:T(8,128)S(1)} %get-tuple-element.64), channel_id=1, source_target_pairs={{1,16},{2,17},{3,18},{4,19},{5,20},{6,21},{7,22},{8,23},{9,24},{10... | collective-permute-start | bytes 51416 | tf_op jit(solution)/shard_map/ppermute | solution.py:260
  88.3 9.1 %collective-permute-start.12 = (f32[3,34,42]{2,1,0:T(8,128)S(1)}, f32[3,34,42]{2,1,0:T(8,128)S(1)}, u32[]{:S(2)}, u32[]{:S(2)}) collective-permute-start(f32[3,34,42]{2,1,0:T(8,128)S(1)} %get-tuple-element.65), channel_id=1, source_target_pairs={{0,497},{1,498},{2,499},{3,500},{4,501},{5,502},{6,503},{7,504},{8... | collective-permute-start | bytes 51416 | tf_op jit(solution)/shard_map/ppermute | solution.py:260
  97.4 3.9 %collective-permute-start.11 = (f32[3,34,128]{2,1,0:T(8,128)S(1)}, f32[3,34,128]{2,1,0:T(8,128)S(1)}, u32[]{:S(2)}, u32[]{:S(2)}) collective-permute-start(f32[3,34,128]{2,1,0:T(8,128)S(1)} %get-tuple-element.67), channel_id=1, source_target_pairs={{0,1},{1,2},{2,3},{3,4},{4,5},{5,6},{6,7},{7,8},{8,9},{9,10},{10,1... | collective-permute-start | bytes 156680 | tf_op jit(solution)/shard_map/ppermute | solution.py:260
  101.6 2.1 %collective-permute-start.10 = (f32[3,34,42]{2,1,0:T(8,128)S(1)}, f32[3,34,42]{2,1,0:T(8,128)S(1)}, u32[]{:S(2)}, u32[]{:S(2)}) collective-permute-start(f32[3,34,42]{2,1,0:T(8,128)S(1)} %get-tuple-element.63), channel_id=1, source_target_pairs={{0,17},{1,18},{2,19},{3,20},{4,21},{5,22},{6,23},{7,24},{8,25},{9,... | collective-permute-start | bytes 51416 | tf_op jit(solution)/shard_map/ppermute | solution.py:260
  104.0 6.8 %collective-permute-done.10 = f32[3,34,42]{2,1,0:T(8,128)S(1)} collective-permute-done((f32[3,34,42]{2,1,0:T(8,128)S(1)}, f32[3,34,42]{2,1,0:T(8,128)S(1)}, u32[]{:S(2)}, u32[]{:S(2)}) %collective-permute-start.10) | collective-permute-done | bytes 17168 | tf_op jit(solution)/shard_map/ppermute | solution.py:260
  111.8 3.3 %line_solve.8 = f32[120,256]{1,0:T(8,128)} custom-call(f32[120,256]{1,0:T(8,128)} %pad.34.refs_0_.refs_2_, f32[120,256]{1,0:T(8,128)} %pad.35.refs_1_, f32[120,256]{1,0:T(8,128)} %pad.34.refs_0_.refs_2_, f32[120,256]{1,0:T(8,128)} %pad.40.refs_3_), custom_call_target="tpu_custom_call" | custom-call | tf_op jit(solution)/shard_map/line_solve/pallas_call | solution.py:232
  116.1 2.8 %line_solve.9 = f32[184,256]{1,0:T(8,128)} custom-call(f32[184,256]{1,0:T(8,128)} %pad.37.refs_0_.refs_2_, f32[184,256]{1,0:T(8,128)} %pad.38.refs_1_, f32[184,256]{1,0:T(8,128)} %pad.37.refs_0_.refs_2_, f32[184,256]{1,0:T(8,128)} %pad.41.refs_3_), custom_call_target="tpu_custom_call" | custom-call | tf_op jit(solution)/shard_map/line_solve/pallas_call | solution.py:232
  125.1 3.4 %collective-permute-start.16 = (f32[3,112,42]{2,1,0:T(8,128)S(1)}, f32[3,112,42]{2,1,0:T(8,128)S(1)}, u32[]{:S(2)}, u32[]{:S(2)}) collective-permute-start(f32[3,112,42]{2,1,0:T(8,128)S(1)} %get-tuple-element.61), channel_id=1, source_target_pairs={{0,16},{1,17},{2,18},{3,19},{4,20},{5,21},{6,22},{7,23},{8,24},{9,... | collective-permute-start | bytes 169352 | tf_op jit(solution)/shard_map/ppermute | solution.py:260
  128.5 6.0 %collective-permute-start.23 = (f32[3,34,42]{2,1,0:T(8,128)S(1)}, f32[3,34,42]{2,1,0:T(8,128)S(1)}, u32[]{:S(2)}, u32[]{:S(2)}) collective-permute-start(f32[3,34,42]{2,1,0:T(8,128)S(1)} %get-tuple-element.58), channel_id=1, source_target_pairs={{1,496},{2,497},{3,498},{4,499},{5,500},{6,501},{7,502},{8,503},{9... | collective-permute-start | bytes 51416 | tf_op jit(solution)/shard_map/ppermute | solution.py:260
  138.4 9.1 %collective-permute-start.20 = (f32[3,34,42]{2,1,0:T(8,128)S(1)}, f32[3,34,42]{2,1,0:T(8,128)S(1)}, u32[]{:S(2)}, u32[]{:S(2)}) collective-permute-start(f32[3,34,42]{2,1,0:T(8,128)S(1)} %get-tuple-element.57), channel_id=1, source_target_pairs={{0,497},{1,498},{2,499},{3,500},{4,501},{5,502},{6,503},{7,504},{8... | collective-permute-start | bytes 51416 | tf_op jit(solution)/shard_map/ppermute | solution.py:260
  147.5 3.9 %collective-permute-start.19 = (f32[3,34,128]{2,1,0:T(8,128)S(1)}, f32[3,34,128]{2,1,0:T(8,128)S(1)}, u32[]{:S(2)}, u32[]{:S(2)}) collective-permute-start(f32[3,34,128]{2,1,0:T(8,128)S(1)} %get-tuple-element.59), channel_id=1, source_target_pairs={{0,1},{1,2},{2,3},{3,4},{4,5},{5,6},{6,7},{7,8},{8,9},{9,10},{10,1... | collective-permute-start | bytes 156680 | tf_op jit(solution)/shard_map/ppermute | solution.py:260
  154.0 7.0 %collective-permute-done.18 = f32[3,34,42]{2,1,0:T(8,128)S(1)} collective-permute-done((f32[3,34,42]{2,1,0:T(8,128)S(1)}, f32[3,34,42]{2,1,0:T(8,128)S(1)}, u32[]{:S(2)}, u32[]{:S(2)}) %collective-permute-start.18) | collective-permute-done | bytes 17168 | tf_op jit(solution)/shard_map/ppermute | solution.py:260
  162.0 3.3 %line_solve.10 = f32[120,256]{1,0:T(8,128)} custom-call(f32[120,256]{1,0:T(8,128)} %pad.34.refs_0_.refs_2_, f32[120,256]{1,0:T(8,128)} %pad.35.refs_1_, f32[120,256]{1,0:T(8,128)} %pad.34.refs_0_.refs_2_, f32[120,256]{1,0:T(8,128)} %pad.42.refs_3_), custom_call_target="tpu_custom_call" | custom-call | tf_op jit(solution)/shard_map/line_solve/pallas_call | solution.py:232
  166.3 2.8 %line_solve.11 = f32[184,256]{1,0:T(8,128)} custom-call(f32[184,256]{1,0:T(8,128)} %pad.37.refs_0_.refs_2_, f32[184,256]{1,0:T(8,128)} %pad.38.refs_1_, f32[184,256]{1,0:T(8,128)} %pad.37.refs_0_.refs_2_, f32[184,256]{1,0:T(8,128)} %pad.43.refs_3_), custom_call_target="tpu_custom_call" | custom-call | tf_op jit(solution)/shard_map/line_solve/pallas_call | solution.py:232
  (209 shorter events, 49.5 us)
Async XLA Ops:
  4.1 29.4 %collective-permute-start.1 = (f32[5,112,42]{2,1,0:T(8,128)S(1)}, f32[5,112,42]{2,1,0:T(8,128)S(1)}, u32[]{:S(2)}, u32[]{:S(2)}) collective-permute-start(f32[5,112,42]{2,1,0:T(8,128)S(1)} %get-tuple-element.43), channel_id=1, source_target_pairs={{0,496},{1,497},{2,498},{3,499},{4,500},{5,501},{6,502},{7,503},{8... | collective-permute-start | bytes 282248 | tf_op jit(solution)/shard_map/ppermute | solution.py:260
  17.7 24.9 %collective-permute-start = (f32[5,112,42]{2,1,0:T(8,128)S(1)}, f32[5,112,42]{2,1,0:T(8,128)S(1)}, u32[]{:S(2)}, u32[]{:S(2)}) collective-permute-start(f32[5,112,42]{2,1,0:T(8,128)S(1)} %get-tuple-element.42), channel_id=1, source_target_pairs={{0,16},{1,17},{2,18},{3,19},{4,20},{5,21},{6,22},{7,23},{8,24},{9,... | collective-permute-start | bytes 282248 | tf_op jit(solution)/shard_map/ppermute | solution.py:260
  19.7 27.2 %collective-permute-start.7 = (f32[5,34,42]{2,1,0:T(8,128)S(1)}, f32[5,34,42]{2,1,0:T(8,128)S(1)}, u32[]{:S(2)}, u32[]{:S(2)}) collective-permute-start(f32[5,34,42]{2,1,0:T(8,128)S(1)} %get-tuple-element.37), channel_id=1, source_target_pairs={{1,496},{2,497},{3,498},{4,499},{5,500},{6,501},{7,502},{8,503},{9... | collective-permute-start | bytes 85688 | tf_op jit(solution)/shard_map/ppermute | solution.py:260
  27.9 21.0 %collective-permute-start.6 = (f32[5,34,128]{2,1,0:T(8,128)S(1)}, f32[5,34,128]{2,1,0:T(8,128)S(1)}, u32[]{:S(2)}, u32[]{:S(2)}) collective-permute-start(f32[5,34,128]{2,1,0:T(8,128)S(1)} %get-tuple-element.41), channel_id=1, source_target_pairs={{1,0},{2,1},{3,2},{4,3},{5,4},{6,5},{7,6},{8,7},{9,8},{10,9},{11,1... | collective-permute-start | bytes 261128 | tf_op jit(solution)/shard_map/ppermute | solution.py:260
  29.8 19.0 %collective-permute-start.5 = (f32[5,34,42]{2,1,0:T(8,128)S(1)}, f32[5,34,42]{2,1,0:T(8,128)S(1)}, u32[]{:S(2)}, u32[]{:S(2)}) collective-permute-start(f32[5,34,42]{2,1,0:T(8,128)S(1)} %get-tuple-element.38), channel_id=1, source_target_pairs={{1,16},{2,17},{3,18},{4,19},{5,20},{6,21},{7,22},{8,23},{9,24},{10... | collective-permute-start | bytes 85688 | tf_op jit(solution)/shard_map/ppermute | solution.py:260
  33.5 15.7 %collective-permute-start.4 = (f32[5,34,42]{2,1,0:T(8,128)S(1)}, f32[5,34,42]{2,1,0:T(8,128)S(1)}, u32[]{:S(2)}, u32[]{:S(2)}) collective-permute-start(f32[5,34,42]{2,1,0:T(8,128)S(1)} %get-tuple-element.39), channel_id=1, source_target_pairs={{0,497},{1,498},{2,499},{3,500},{4,501},{5,502},{6,503},{7,504},{8... | collective-permute-start | bytes 85688 | tf_op jit(solution)/shard_map/ppermute | solution.py:260
  42.6 13.9 %collective-permute-start.3 = (f32[5,34,128]{2,1,0:T(8,128)S(1)}, f32[5,34,128]{2,1,0:T(8,128)S(1)}, u32[]{:S(2)}, u32[]{:S(2)}) collective-permute-start(f32[5,34,128]{2,1,0:T(8,128)S(1)} %get-tuple-element.40), channel_id=1, source_target_pairs={{0,1},{1,2},{2,3},{3,4},{4,5},{5,6},{6,7},{7,8},{8,9},{9,10},{10,1... | collective-permute-start | bytes 261128 | tf_op jit(solution)/shard_map/ppermute | solution.py:260
  46.9 9.6 %collective-permute-start.2 = (f32[5,34,42]{2,1,0:T(8,128)S(1)}, f32[5,34,42]{2,1,0:T(8,128)S(1)}, u32[]{:S(2)}, u32[]{:S(2)}) collective-permute-start(f32[5,34,42]{2,1,0:T(8,128)S(1)} %get-tuple-element.36), channel_id=1, source_target_pairs={{0,17},{1,18},{2,19},{3,20},{4,21},{5,22},{6,23},{7,24},{8,25},{9,... | collective-permute-start | bytes 85688 | tf_op jit(solution)/shard_map/ppermute | solution.py:260
  73.1 15.2 %collective-permute-start.9 = (f32[3,112,42]{2,1,0:T(8,128)S(1)}, f32[3,112,42]{2,1,0:T(8,128)S(1)}, u32[]{:S(2)}, u32[]{:S(2)}) collective-permute-start(f32[3,112,42]{2,1,0:T(8,128)S(1)} %get-tuple-element.70), channel_id=1, source_target_pairs={{0,496},{1,497},{2,498},{3,499},{4,500},{5,501},{6,502},{7,503},{8... | collective-permute-start | bytes 169352 | tf_op jit(solution)/shard_map/ppermute | solution.py:260
  75.1 22.3 %collective-permute-start.8 = (f32[3,112,42]{2,1,0:T(8,128)S(1)}, f32[3,112,42]{2,1,0:T(8,128)S(1)}, u32[]{:S(2)}, u32[]{:S(2)}) collective-permute-start(f32[3,112,42]{2,1,0:T(8,128)S(1)} %get-tuple-element.69), channel_id=1, source_target_pairs={{0,16},{1,17},{2,18},{3,19},{4,20},{5,21},{6,22},{7,23},{8,24},{9,... | collective-permute-start | bytes 169352 | tf_op jit(solution)/shard_map/ppermute | solution.py:260
  78.4 23.2 %collective-permute-start.15 = (f32[3,34,42]{2,1,0:T(8,128)S(1)}, f32[3,34,42]{2,1,0:T(8,128)S(1)}, u32[]{:S(2)}, u32[]{:S(2)}) collective-permute-start(f32[3,34,42]{2,1,0:T(8,128)S(1)} %get-tuple-element.66), channel_id=1, source_target_pairs={{1,496},{2,497},{3,498},{4,499},{5,500},{6,501},{7,502},{8,503},{9... | collective-permute-start | bytes 51416 | tf_op jit(solution)/shard_map/ppermute | solution.py:260
  84.4 19.3 %collective-permute-start.14 = (f32[3,34,128]{2,1,0:T(8,128)S(1)}, f32[3,34,128]{2,1,0:T(8,128)S(1)}, u32[]{:S(2)}, u32[]{:S(2)}) collective-permute-start(f32[3,34,128]{2,1,0:T(8,128)S(1)} %get-tuple-element.68), channel_id=1, source_target_pairs={{1,0},{2,1},{3,2},{4,3},{5,4},{6,5},{7,6},{8,7},{9,8},{10,9},{11,1... | collective-permute-start | bytes 156680 | tf_op jit(solution)/shard_map/ppermute | solution.py:260
  86.4 17.4 %collective-permute-start.13 = (f32[3,34,42]{2,1,0:T(8,128)S(1)}, f32[3,34,42]{2,1,0:T(8,128)S(1)}, u32[]{:S(2)}, u32[]{:S(2)}) collective-permute-start(f32[3,34,42]{2,1,0:T(8,128)S(1)} %get-tuple-element.64), channel_id=1, source_target_pairs={{1,16},{2,17},{3,18},{4,19},{5,20},{6,21},{7,22},{8,23},{9,24},{10... | collective-permute-start | bytes 51416 | tf_op jit(solution)/shard_map/ppermute | solution.py:260
  88.3 15.7 %collective-permute-start.12 = (f32[3,34,42]{2,1,0:T(8,128)S(1)}, f32[3,34,42]{2,1,0:T(8,128)S(1)}, u32[]{:S(2)}, u32[]{:S(2)}) collective-permute-start(f32[3,34,42]{2,1,0:T(8,128)S(1)} %get-tuple-element.65), channel_id=1, source_target_pairs={{0,497},{1,498},{2,499},{3,500},{4,501},{5,502},{6,503},{7,504},{8... | collective-permute-start | bytes 51416 | tf_op jit(solution)/shard_map/ppermute | solution.py:260
  97.4 13.4 %collective-permute-start.11 = (f32[3,34,128]{2,1,0:T(8,128)S(1)}, f32[3,34,128]{2,1,0:T(8,128)S(1)}, u32[]{:S(2)}, u32[]{:S(2)}) collective-permute-start(f32[3,34,128]{2,1,0:T(8,128)S(1)} %get-tuple-element.67), channel_id=1, source_target_pairs={{0,1},{1,2},{2,3},{3,4},{4,5},{5,6},{6,7},{7,8},{8,9},{9,10},{10,1... | collective-permute-start | bytes 156680 | tf_op jit(solution)/shard_map/ppermute | solution.py:260
  101.6 9.2 %collective-permute-start.10 = (f32[3,34,42]{2,1,0:T(8,128)S(1)}, f32[3,34,42]{2,1,0:T(8,128)S(1)}, u32[]{:S(2)}, u32[]{:S(2)}) collective-permute-start(f32[3,34,42]{2,1,0:T(8,128)S(1)} %get-tuple-element.63), channel_id=1, source_target_pairs={{0,17},{1,18},{2,19},{3,20},{4,21},{5,22},{6,23},{7,24},{8,25},{9,... | collective-permute-start | bytes 51416 | tf_op jit(solution)/shard_map/ppermute | solution.py:260
  123.2 15.2 %collective-permute-start.17 = (f32[3,112,42]{2,1,0:T(8,128)S(1)}, f32[3,112,42]{2,1,0:T(8,128)S(1)}, u32[]{:S(2)}, u32[]{:S(2)}) collective-permute-start(f32[3,112,42]{2,1,0:T(8,128)S(1)} %get-tuple-element.62), channel_id=1, source_target_pairs={{0,496},{1,497},{2,498},{3,499},{4,500},{5,501},{6,502},{7,503},{8... | collective-permute-start | bytes 169352 | tf_op jit(solution)/shard_map/ppermute | solution.py:260
  125.1 22.4 %collective-permute-start.16 = (f32[3,112,42]{2,1,0:T(8,128)S(1)}, f32[3,112,42]{2,1,0:T(8,128)S(1)}, u32[]{:S(2)}, u32[]{:S(2)}) collective-permute-start(f32[3,112,42]{2,1,0:T(8,128)S(1)} %get-tuple-element.61), channel_id=1, source_target_pairs={{0,16},{1,17},{2,18},{3,19},{4,20},{5,21},{6,22},{7,23},{8,24},{9,... | collective-permute-start | bytes 169352 | tf_op jit(solution)/shard_map/ppermute | solution.py:260
  128.5 23.2 %collective-permute-start.23 = (f32[3,34,42]{2,1,0:T(8,128)S(1)}, f32[3,34,42]{2,1,0:T(8,128)S(1)}, u32[]{:S(2)}, u32[]{:S(2)}) collective-permute-start(f32[3,34,42]{2,1,0:T(8,128)S(1)} %get-tuple-element.58), channel_id=1, source_target_pairs={{1,496},{2,497},{3,498},{4,499},{5,500},{6,501},{7,502},{8,503},{9... | collective-permute-start | bytes 51416 | tf_op jit(solution)/shard_map/ppermute | solution.py:260
  134.6 19.1 %collective-permute-start.22 = (f32[3,34,128]{2,1,0:T(8,128)S(1)}, f32[3,34,128]{2,1,0:T(8,128)S(1)}, u32[]{:S(2)}, u32[]{:S(2)}) collective-permute-start(f32[3,34,128]{2,1,0:T(8,128)S(1)} %get-tuple-element.60), channel_id=1, source_target_pairs={{1,0},{2,1},{3,2},{4,3},{5,4},{6,5},{7,6},{8,7},{9,8},{10,9},{11,1... | collective-permute-start | bytes 156680 | tf_op jit(solution)/shard_map/ppermute | solution.py:260
  136.5 17.2 %collective-permute-start.21 = (f32[3,34,42]{2,1,0:T(8,128)S(1)}, f32[3,34,42]{2,1,0:T(8,128)S(1)}, u32[]{:S(2)}, u32[]{:S(2)}) collective-permute-start(f32[3,34,42]{2,1,0:T(8,128)S(1)} %get-tuple-element.56), channel_id=1, source_target_pairs={{1,16},{2,17},{3,18},{4,19},{5,20},{6,21},{7,22},{8,23},{9,24},{10... | collective-permute-start | bytes 51416 | tf_op jit(solution)/shard_map/ppermute | solution.py:260
  138.4 15.5 %collective-permute-start.20 = (f32[3,34,42]{2,1,0:T(8,128)S(1)}, f32[3,34,42]{2,1,0:T(8,128)S(1)}, u32[]{:S(2)}, u32[]{:S(2)}) collective-permute-start(f32[3,34,42]{2,1,0:T(8,128)S(1)} %get-tuple-element.57), channel_id=1, source_target_pairs={{0,497},{1,498},{2,499},{3,500},{4,501},{5,502},{6,503},{7,504},{8... | collective-permute-start | bytes 51416 | tf_op jit(solution)/shard_map/ppermute | solution.py:260
  147.5 13.4 %collective-permute-start.19 = (f32[3,34,128]{2,1,0:T(8,128)S(1)}, f32[3,34,128]{2,1,0:T(8,128)S(1)}, u32[]{:S(2)}, u32[]{:S(2)}) collective-permute-start(f32[3,34,128]{2,1,0:T(8,128)S(1)} %get-tuple-element.59), channel_id=1, source_target_pairs={{0,1},{1,2},{2,3},{3,4},{4,5},{5,6},{6,7},{7,8},{8,9},{9,10},{10,1... | collective-permute-start | bytes 156680 | tf_op jit(solution)/shard_map/ppermute | solution.py:260
  151.8 9.2 %collective-permute-start.18 = (f32[3,34,42]{2,1,0:T(8,128)S(1)}, f32[3,34,42]{2,1,0:T(8,128)S(1)}, u32[]{:S(2)}, u32[]{:S(2)}) collective-permute-start(f32[3,34,42]{2,1,0:T(8,128)S(1)} %get-tuple-element.55), channel_id=1, source_target_pairs={{0,17},{1,18},{2,19},{3,20},{4,21},{5,22},{6,23},{7,24},{8,25},{9,... | collective-permute-start | bytes 51416 | tf_op jit(solution)/shard_map/ppermute | solution.py:260
  (9 other events, 13.3 us)

commit v4 on v2

--- a/solution.py
+++ b/solution.py
@@ -188,9 +188,7 @@
     return jnp.concatenate([slab_of(values, stride, length, along_axis), padding], along_axis)
 
 
-def reduction_kernel(lower_ref, main_ref, upper_ref, rights_ref, out_ref, *, along_axis):
-    lower_band, main_band, upper_band = lower_ref[...], main_ref[...], upper_ref[...]
-    rights = rights_ref[...]
+def reduce_lines(lower_band, main_band, upper_band, rights, along_axis):
     length = rights.shape[along_axis]
     position = lax.broadcasted_iota(jnp.int32, rights.shape, along_axis)
     stride = 1
@@ -215,37 +213,48 @@
         rights = rights - weight_below * below[3] - weight_above * above[3]
         lower_band, main_band, upper_band = new_lower, new_main, new_upper
         stride = stride * 2
-    out_ref[...] = rights / main_band
-
-
-def padded(values, shape, fill):
-    return jnp.pad(
-        values, [(0, want - have) for want, have in zip(shape, values.shape)], constant_values=fill
-    )
-
-
-def line_solve(bands, rights, along_axis):
-    lower_band, main_band, upper_band = bands
-    shape = main_band.shape
-    count = rights.shape
+    return rights / main_band
+
+
+def solve_kernel(surface_ref, east_ref, north_ref, depth_ref, keep_ref, east_out, north_out, *,
+                 first_row, used_cols):
+    rows = east_out.shape[0]
+    depth = depth_ref[pl.ds(first_row, rows), :]
+    coef = depth * depth / (3.0 * LON_SPACING * LON_SPACING)
+    keep = lax.broadcasted_iota(jnp.int32, depth.shape, 1) < used_cols
+    rights = east_ref[pl.ds(first_row, rows), :] / (depth + surface_ref[pl.ds(first_row, rows), :])
+    east_out[...] = reduce_lines(
+        jnp.where(keep, -coef, 0.0),
+        jnp.where(keep, 1.0 + 2.0 * coef, 1.0),
+        jnp.where(keep, -coef, 0.0),
+        jnp.where(keep, rights, 0.0),
+        1,
+    )
+    depth = depth_ref[...]
+    coef = depth * depth / (3.0 * LAT_SPACING * LAT_SPACING)
+    keep = keep_ref[...] > 0.0
+    rights = north_ref[...] / (depth + surface_ref[...])
+    north_out[...] = reduce_lines(
+        jnp.where(keep, -coef, 0.0),
+        jnp.where(keep, 1.0 + 2.0 * coef, 1.0),
+        jnp.where(keep, -coef, 0.0),
+        jnp.where(keep, rights, 0.0),
+        0,
+    )
+
+
+def line_solves(box, depth_box, keep, first_row, rows, used_cols):
     spec = pl.BlockSpec(memory_space=pltpu.VMEM)
-    solved = pl.pallas_call(
-        lambda *refs: reduction_kernel(*refs, along_axis=along_axis),
-        out_shape=jax.ShapeDtypeStruct(shape, jnp.float32),
-        in_specs=[spec] * 4,
-        out_specs=spec,
-        name="line_solve",
-    )(lower_band, main_band, upper_band, padded(rights, shape, 0.0))
-    return solved[: count[0], : count[1]]
-
-
-def band_set(coef, keep):
-    shape = tuple(-(-size // unit) * unit for size, unit in zip(coef.shape, (8, 128)))
-    return (
-        padded(jnp.where(keep, -coef, 0.0), shape, 0.0),
-        padded(jnp.where(keep, 1.0 + 2.0 * coef, 1.0), shape, 1.0),
-        padded(jnp.where(keep, -coef, 0.0), shape, 0.0),
-    )
+    return pl.pallas_call(
+        lambda *refs: solve_kernel(*refs, first_row=first_row, used_cols=used_cols),
+        out_shape=(
+            jax.ShapeDtypeStruct((rows, depth_box.shape[1]), jnp.float32),
+            jax.ShapeDtypeStruct(depth_box.shape, jnp.float32),
+        ),
+        in_specs=[spec] * 5,
+        out_specs=(spec, spec),
+        name="line_solves",
+    )(box[0], box[1], box[2], depth_box, keep)
 
 
 def halo_box(fields, wide_x, wide_y, place, count):
@@ -261,7 +270,9 @@
     below = passed_along(wide[:, :wide_y], "lat", -1)
     above = jnp.where(place == 0, wide[:, wide_y - 1 :: -1], above)
     below = jnp.where(place == count - 1, wide[:, : -wide_y - 1 : -1], below)
-    return jnp.concatenate([above, wide, below], axis=1)
+    box = jnp.concatenate([above, wide, below], axis=1)
+    aligned = [-(-size // unit) * unit for size, unit in zip(box.shape[1:], (8, 128))]
+    return jnp.pad(box, ((0, 0), (0, aligned[0] - box.shape[1]), (0, aligned[1] - box.shape[2])))
 
 
 def local(surface, momentum_x, momentum_y, water_depth, wet_mask, slide_cells, slide_rate):
@@ -281,33 +292,34 @@
     box_cols = tile_cols + 2 * wide_x
     core_rows = slice(wide_y - 2, wide_y + tile_rows + 2)
     core_cols = slice(wide_x - 2, wide_x + tile_cols + 2)
+    aligned_rows = -(-box_rows // 8) * 8
+    aligned_cols = -(-box_cols // 128) * 128
     global_row = place * tile_rows - wide_y + lax.broadcasted_iota(
-        jnp.int32, (box_rows, tile_cols + 4), 0
-    )
-    inside = (global_row >= 0) & (global_row < count * tile_rows)
+        jnp.int32, (aligned_rows, aligned_cols), 0
+    )
+    inside = (global_row >= 0) & (global_row < count * tile_rows) & (global_row < place * tile_rows - wide_y + box_rows)
+    keep = inside.astype(jnp.float32)
+    first_row = (wide_y - 2) // 8 * 8
+    east_rows = -(-(wide_y + tile_rows + 2 - first_row) // 8) * 8
 
     initial = (surface, momentum_x, momentum_y)
     current = initial
     velocity_u = surface
     velocity_v = surface
-    bands = None
+    depth_box = None
     for first, second in ((0.0, 1.0), (0.75, 0.25), (1.0 / 3.0, 2.0 / 3.0)):
-        if bands is None:
+        if depth_box is None:
             box = halo_box(
                 jnp.stack([current[0], current[1], current[2], water_depth, wet_float]),
                 wide_x, wide_y, place, count,
             )
             depth_box, wet_box = box[3], box[4]
-            coef_lon = depth_box[core_rows] * depth_box[core_rows] / (3.0 * LON_SPACING * LON_SPACING)
-            coef_lat = depth_box[:, core_cols] * depth_box[:, core_cols] / (3.0 * LAT_SPACING * LAT_SPACING)
-            bands = (band_set(coef_lon, True), band_set(coef_lat, inside))
         else:
             box = halo_box(jnp.stack(list(current)), wide_x, wide_y, place, count)
         surface_box, east_box, north_box = box[0], box[1], box[2]
-        height_box = depth_box + surface_box
-        east_raw = line_solve(bands[0], east_box[core_rows] / height_box[core_rows], 1)[:, core_cols]
-        north_rights = jnp.where(inside, north_box[:, core_cols] / height_box[:, core_cols], 0.0)
-        north_raw = line_solve(bands[1], north_rights, 0)[core_rows]
+        east_solved, north_solved = line_solves(box, depth_box, keep, first_row, east_rows, box_cols)
+        east_raw = east_solved[core_rows.start - first_row : core_rows.stop - first_row, core_cols]
+        north_raw = north_solved[core_rows, core_cols]
         wet_core = wet_box[core_rows, core_cols]
         u_core = wet_core * east_raw
         v_core = wet_core * north_raw

time: 137 us -> 125 us (0.912)
  waiting for transfers between devices: 44.6 us -> 31.2 us
  starting transfers between devices: 41.4 us -> 49.3 us
  Pallas kernels: 18.3 us -> 14.3 us
  local copies, waits for them, and re-layouts: 14.1 us -> 12.1 us
    ppermute x3, waiting for transfers between devices: 18.8 us -> 7.77 us  [halo_box(): lax.ppermute(fields[:, :, -wide_x:], 'lon', [(i, (i + 1) % lon_count) for...]
    ppermute x3, starting transfers between devices: 16.8 us -> 26.5 us  [halo_box(): lax.ppermute(fields[:, :, :wide_x], 'lon', [((i + 1) % lon_count, i) for...]
    pad x10 -> x0, local copies, waits for them, and re-layouts: 6.72 us -> none  [padded(): jnp.pad(values, [(0, want - have) for want, have in zip(shape, values.sha...]
    pallas_call x6 -> x3, Pallas kernels: 18.3 us -> 14.3 us  [line_solves(): pl.pallas_call(lambda *refs: solve_kernel(*refs, first_row=first_row, use...]
    ppermute x3, waiting for transfers between devices: 7.02 us -> 4.1 us  [halo_box(): lax.ppermute(fields[:, :, :wide_x], 'lon', [((i + 1) % lon_count, i) for...]
    ppermute x3, starting transfers between devices: 9.76 us -> 7.67 us  [halo_box(): lax.ppermute(fields[:, :, -wide_x:], 'lon', [(i, (i + 1) % lon_count) for...]
    squeeze x0 -> x2, local copies, waits for them, and re-layouts: none -> 1.62 us  [line_solves(): box[2]]
    unnamed x22 -> x24, local copies, waits for them, and re-layouts: 3.91 us -> 5.44 us
  transfers between devices with their start and end apart: 12 -> 12, of which waited for: 9 -> 10; matrix products, arithmetic and copies ran while one was open for 1% -> 1% of each run, Pallas kernels for 0% -> 0%
where the time goes in v4:
time: 125 us; the launch traced here: 124 us
  starting transfers between devices  49.3 us (39%)
  waiting for transfers between devices  31.2 us (25%)
  other arithmetic  15.3 us (12%)
  Pallas kernels  14.3 us (11%)
  local copies, waits for them, and re-layouts  12.1 us (10%)
  between operations  1.63 us (1%)
    ppermute x3, starting transfers between devices, halo_box(): lax.ppermute(fields[:, :, :wide_x], 'lon', [((i + 1) % lon_count, i) for...  26.5 us
    ppermute x6, waiting for transfers between devices, passed_along(): return lax.ppermute(x, axis, pairs)  19.3 us
    ppermute x6, starting transfers between devices, passed_along(): return lax.ppermute(x, axis, pairs)  15.1 us
    pallas_call x3, Pallas kernels, line_solves(): pl.pallas_call(lambda *refs: solve_kernel(*refs, first_row=first_row, use...  14.3 us
    ppermute x3, waiting for transfers between devices, halo_box(): lax.ppermute(fields[:, :, -wide_x:], 'lon', [(i, (i + 1) % lon_count) for...  7.77 us
    ppermute x3, starting transfers between devices, halo_box(): lax.ppermute(fields[:, :, -wide_x:], 'lon', [(i, (i + 1) % lon_count) for...  7.67 us
    unnamed x24, local copies, waits for them, and re-layouts  5.44 us
    ppermute x3, waiting for transfers between devices, halo_box(): lax.ppermute(fields[:, :, :wide_x], 'lon', [((i + 1) % lon_count, i) for...  4.1 us
  transfers between devices with their start and end apart: 12, of which 10 were waited for; matrix products, arithmetic and copies ran while one was open for 1% of the time, Pallas kernels for 0%

profile of v4, /device:TPU:2, one launch (start us, length us, event | category | flops | bytes accessed | tf_op | source)
XLA Modules:
  0.0 123.7 jit_solution(13417149873151745248)
XLA Ops:
  4.1 3.8 %collective-permute-start = (f32[5,112,42]{2,1,0:T(8,128)S(1)}, f32[5,112,42]{2,1,0:T(8,128)S(1)}, u32[]{:S(2)}, u32[]{:S(2)}) collective-permute-start(f32[5,112,42]{2,1,0:T(8,128)S(1)} %get-tuple-element.50), channel_id=1, source_target_pairs={{0,16},{16,32},{32,48},{48,64},{64,80},{80,96},{96,112},{112,128},... | collective-permute-start | bytes 282248 | tf_op jit(solution)/shard_map/ppermute | solution.py:262
  7.9 11.1 %collective-permute-start.1 = (f32[5,112,42]{2,1,0:T(8,128)S(1)}, f32[5,112,42]{2,1,0:T(8,128)S(1)}, u32[]{:S(2)}, u32[]{:S(2)}) collective-permute-start(f32[5,112,42]{2,1,0:T(8,128)S(1)} %get-tuple-element.51), channel_id=1, source_target_pairs={{16,0},{32,16},{48,32},{64,48},{80,64},{96,80},{112,96},{128,112},... | collective-permute-start | bytes 282248 | tf_op jit(solution)/shard_map/ppermute | solution.py:265
  19.0 4.9 %collective-permute-done = f32[5,112,42]{2,1,0:T(8,128)S(1)} collective-permute-done((f32[5,112,42]{2,1,0:T(8,128)S(1)}, f32[5,112,42]{2,1,0:T(8,128)S(1)}, u32[]{:S(2)}, u32[]{:S(2)}) %collective-permute-start) | collective-permute-done | bytes 94112 | tf_op jit(solution)/shard_map/ppermute | solution.py:262
  23.9 1.2 collective-permute-done.1
  25.3 4.4 %collective-permute-start.3 = (f32[5,34,212]{2,1,0:T(8,128)S(1)}, f32[5,34,212]{2,1,0:T(8,128)S(1)}, u32[]{:S(2)}, u32[]{:S(2)}) collective-permute-start(f32[5,34,212]{2,1,0:T(8,128)S(1)} %get-tuple-element.28), channel_id=1, source_target_pairs={{1,0},{2,1},{3,2},{4,3},{5,4},{6,5},{7,6},{8,7},{9,8},{10,9},{11,1... | collective-permute-start | bytes 432488 | tf_op jit(solution)/shard_map/ppermute | solution.py:26
  31.1 1.9 %collective-permute-start.2 = (f32[5,34,212]{2,1,0:T(8,128)S(1)}, f32[5,34,212]{2,1,0:T(8,128)S(1)}, u32[]{:S(2)}, u32[]{:S(2)}) collective-permute-start(f32[5,34,212]{2,1,0:T(8,128)S(1)} %get-tuple-element.29), channel_id=1, source_target_pairs={{0,1},{1,2},{2,3},{3,4},{4,5},{5,6},{6,7},{7,8},{8,9},{9,10},{10,1... | collective-permute-start | bytes 432488 | tf_op jit(solution)/shard_map/ppermute | solution.py:26
  33.0 7.2 %collective-permute-done.2 = f32[5,34,212]{2,1,0:T(8,128)S(1)} collective-permute-done((f32[5,34,212]{2,1,0:T(8,128)S(1)}, f32[5,34,212]{2,1,0:T(8,128)S(1)}, u32[]{:S(2)}, u32[]{:S(2)}) %collective-permute-start.2) | collective-permute-done | bytes 144192 | tf_op jit(solution)/shard_map/ppermute | solution.py:26
  43.1 4.8 %line_solves.3 = (f32[120,256]{1,0:T(8,128)}, f32[184,256]{1,0:T(8,128)}) custom-call(f32[184,256]{1,0:T(8,128)} %copy-done.1, f32[184,256]{1,0:T(8,128)} %get-tuple-element.25.refs_1_, f32[184,256]{1,0:T(8,128)} %get-tuple-element.24.refs_2_, f32[184,256]{1,0:T(8,128)} %copy-done, f32[184,256]{1,0:T(8,128)} %iota.7.refs_4_), custom_call_target="tpu_custom_call" | custom-call | tf_op jit(solution)/shard_map/line_solves/pallas_call | solution.py:248
  52.7 1.9 %collective-permute-start.4 = (f32[3,112,42]{2,1,0:T(8,128)S(1)}, f32[3,112,42]{2,1,0:T(8,128)S(1)}, u32[]{:S(2)}, u32[]{:S(2)}) collective-permute-start(f32[3,112,42]{2,1,0:T(8,128)S(1)} %get-tuple-element.63), channel_id=1, source_target_pairs={{0,16},{16,32},{32,48},{48,64},{64,80},{80,96},{96,112},{112,128},... | collective-permute-start | bytes 169352 | tf_op jit(solution)/shard_map/ppermute | solution.py:262
  54.6 7.5 %collective-permute-start.5 = (f32[3,112,42]{2,1,0:T(8,128)S(1)}, f32[3,112,42]{2,1,0:T(8,128)S(1)}, u32[]{:S(2)}, u32[]{:S(2)}) collective-permute-start(f32[3,112,42]{2,1,0:T(8,128)S(1)} %get-tuple-element.64), channel_id=1, source_target_pairs={{16,0},{32,16},{48,32},{64,48},{80,64},{96,80},{112,96},{128,112},... | collective-permute-start | bytes 169352 | tf_op jit(solution)/shard_map/ppermute | solution.py:265
  62.2 1.4 %collective-permute-done.4 = f32[3,112,42]{2,1,0:T(8,128)S(1)} collective-permute-done((f32[3,112,42]{2,1,0:T(8,128)S(1)}, f32[3,112,42]{2,1,0:T(8,128)S(1)}, u32[]{:S(2)}, u32[]{:S(2)}) %collective-permute-start.4) | collective-permute-done | bytes 56480 | tf_op jit(solution)/shard_map/ppermute | solution.py:262
  63.6 1.5 %collective-permute-done.5 = f32[3,112,42]{2,1,0:T(8,128)S(1)} collective-permute-done((f32[3,112,42]{2,1,0:T(8,128)S(1)}, f32[3,112,42]{2,1,0:T(8,128)S(1)}, u32[]{:S(2)}, u32[]{:S(2)}) %collective-permute-start.5) | collective-permute-done | bytes 56480 | tf_op jit(solution)/shard_map/ppermute | solution.py:265
  65.2 2.0 %collective-permute-start.7 = (f32[3,34,212]{2,1,0:T(8,128)S(1)}, f32[3,34,212]{2,1,0:T(8,128)S(1)}, u32[]{:S(2)}, u32[]{:S(2)}) collective-permute-start(f32[3,34,212]{2,1,0:T(8,128)S(1)} %get-tuple-element.42), channel_id=1, source_target_pairs={{1,0},{2,1},{3,2},{4,3},{5,4},{6,5},{7,6},{8,7},{9,8},{10,9},{11,1... | collective-permute-start | bytes 259496 | tf_op jit(solution)/shard_map/ppermute | solution.py:26
  67.5 2.5 %collective-permute-start.6 = (f32[3,34,212]{2,1,0:T(8,128)S(1)}, f32[3,34,212]{2,1,0:T(8,128)S(1)}, u32[]{:S(2)}, u32[]{:S(2)}) collective-permute-start(f32[3,34,212]{2,1,0:T(8,128)S(1)} %get-tuple-element.43), channel_id=1, source_target_pairs={{0,1},{1,2},{2,3},{3,4},{4,5},{5,6},{6,7},{7,8},{8,9},{9,10},{10,1... | collective-permute-start | bytes 259496 | tf_op jit(solution)/shard_map/ppermute | solution.py:26
  70.0 5.8 %collective-permute-done.6 = f32[3,34,212]{2,1,0:T(8,128)S(1)} collective-permute-done((f32[3,34,212]{2,1,0:T(8,128)S(1)}, f32[3,34,212]{2,1,0:T(8,128)S(1)}, u32[]{:S(2)}, u32[]{:S(2)}) %collective-permute-start.6) | collective-permute-done | bytes 86528 | tf_op jit(solution)/shard_map/ppermute | solution.py:26
  77.6 4.8 %line_solves.4 = (f32[120,256]{1,0:T(8,128)}, f32[184,256]{1,0:T(8,128)}) custom-call(f32[184,256]{1,0:T(8,128)} %copy-done.3, f32[184,256]{1,0:T(8,128)} %get-tuple-element.38.refs_1_, f32[184,256]{1,0:T(8,128)} %get-tuple-element.37.refs_2_, f32[184,256]{1,0:T(8,128)} %copy-done, f32[184,256]{1,0:T(8,128)} %iota.7.refs_4_), custom_call_target="tpu_custom_call" | custom-call | tf_op jit(solution)/shard_map/line_solves/pallas_call | solution.py:248
  86.3 1.9 %collective-permute-start.8 = (f32[3,112,42]{2,1,0:T(8,128)S(1)}, f32[3,112,42]{2,1,0:T(8,128)S(1)}, u32[]{:S(2)}, u32[]{:S(2)}) collective-permute-start(f32[3,112,42]{2,1,0:T(8,128)S(1)} %get-tuple-element.61), channel_id=1, source_target_pairs={{0,16},{16,32},{32,48},{48,64},{64,80},{80,96},{96,112},{112,128},... | collective-permute-start | bytes 169352 | tf_op jit(solution)/shard_map/ppermute | solution.py:262
  88.2 7.9 %collective-permute-start.9 = (f32[3,112,42]{2,1,0:T(8,128)S(1)}, f32[3,112,42]{2,1,0:T(8,128)S(1)}, u32[]{:S(2)}, u32[]{:S(2)}) collective-permute-start(f32[3,112,42]{2,1,0:T(8,128)S(1)} %get-tuple-element.62), channel_id=1, source_target_pairs={{16,0},{32,16},{48,32},{64,48},{80,64},{96,80},{112,96},{128,112},... | collective-permute-start | bytes 169352 | tf_op jit(solution)/shard_map/ppermute | solution.py:265
  96.1 1.4 %collective-permute-done.8 = f32[3,112,42]{2,1,0:T(8,128)S(1)} collective-permute-done((f32[3,112,42]{2,1,0:T(8,128)S(1)}, f32[3,112,42]{2,1,0:T(8,128)S(1)}, u32[]{:S(2)}, u32[]{:S(2)}) %collective-permute-start.8) | collective-permute-done | bytes 56480 | tf_op jit(solution)/shard_map/ppermute | solution.py:262
  97.6 1.5 %collective-permute-done.9 = f32[3,112,42]{2,1,0:T(8,128)S(1)} collective-permute-done((f32[3,112,42]{2,1,0:T(8,128)S(1)}, f32[3,112,42]{2,1,0:T(8,128)S(1)}, u32[]{:S(2)}, u32[]{:S(2)}) %collective-permute-start.9) | collective-permute-done | bytes 56480 | tf_op jit(solution)/shard_map/ppermute | solution.py:265
  99.2 2.4 %collective-permute-start.11 = (f32[3,34,212]{2,1,0:T(8,128)S(1)}, f32[3,34,212]{2,1,0:T(8,128)S(1)}, u32[]{:S(2)}, u32[]{:S(2)}) collective-permute-start(f32[3,34,212]{2,1,0:T(8,128)S(1)} %get-tuple-element.40), channel_id=1, source_target_pairs={{1,0},{2,1},{3,2},{4,3},{5,4},{6,5},{7,6},{8,7},{9,8},{10,9},{11,1... | collective-permute-start | bytes 259496 | tf_op jit(solution)/shard_map/ppermute | solution.py:26
  101.8 2.0 %collective-permute-start.10 = (f32[3,34,212]{2,1,0:T(8,128)S(1)}, f32[3,34,212]{2,1,0:T(8,128)S(1)}, u32[]{:S(2)}, u32[]{:S(2)}) collective-permute-start(f32[3,34,212]{2,1,0:T(8,128)S(1)} %get-tuple-element.41), channel_id=1, source_target_pairs={{0,1},{1,2},{2,3},{3,4},{4,5},{5,6},{6,7},{7,8},{8,9},{9,10},{10,1... | collective-permute-start | bytes 259496 | tf_op jit(solution)/shard_map/ppermute | solution.py:26
  104.0 6.1 %collective-permute-done.10 = f32[3,34,212]{2,1,0:T(8,128)S(1)} collective-permute-done((f32[3,34,212]{2,1,0:T(8,128)S(1)}, f32[3,34,212]{2,1,0:T(8,128)S(1)}, u32[]{:S(2)}, u32[]{:S(2)}) %collective-permute-start.10) | collective-permute-done | bytes 86528 | tf_op jit(solution)/shard_map/ppermute | solution.py:26
  111.9 4.8 %line_solves.5 = (f32[120,256]{1,0:T(8,128)}, f32[184,256]{1,0:T(8,128)}) custom-call(f32[184,256]{1,0:T(8,128)} %copy-done.2, f32[184,256]{1,0:T(8,128)} %get-tuple-element.35.refs_1_, f32[184,256]{1,0:T(8,128)} %get-tuple-element.34.refs_2_, f32[184,256]{1,0:T(8,128)} %copy-done, f32[184,256]{1,0:T(8,128)} %iota.7.refs_4_), custom_call_target="tpu_custom_call" | custom-call | tf_op jit(solution)/shard_map/line_solves/pallas_call | solution.py:248
  (159 shorter events, 27.6 us)
Async XLA Ops:
  0.6 0.9 copy-start.5
  1.5 0.8 copy-start.4
  2.3 0.8 copy-start.7
  3.1 0.8 copy-start.8
  4.1 19.8 %collective-permute-start = (f32[5,112,42]{2,1,0:T(8,128)S(1)}, f32[5,112,42]{2,1,0:T(8,128)S(1)}, u32[]{:S(2)}, u32[]{:S(2)}) collective-permute-start(f32[5,112,42]{2,1,0:T(8,128)S(1)} %get-tuple-element.50), channel_id=1, source_target_pairs={{0,16},{16,32},{32,48},{48,64},{64,80},{80,96},{96,112},{112,128},... | collective-permute-start | bytes 282248 | tf_op jit(solution)/shard_map/ppermute | solution.py:262
  7.9 17.1 %collective-permute-start.1 = (f32[5,112,42]{2,1,0:T(8,128)S(1)}, f32[5,112,42]{2,1,0:T(8,128)S(1)}, u32[]{:S(2)}, u32[]{:S(2)}) collective-permute-start(f32[5,112,42]{2,1,0:T(8,128)S(1)} %get-tuple-element.51), channel_id=1, source_target_pairs={{16,0},{32,16},{48,32},{64,48},{80,64},{96,80},{112,96},{128,112},... | collective-permute-start | bytes 282248 | tf_op jit(solution)/shard_map/ppermute | solution.py:265
  25.3 4.4 %copy-start.9 = (s32[1,64]{1,0:T(1,128)S(1)}, s32[1,64]{1,0:T(1,128)}, u32[]{:S(2)}) copy-start(s32[1,64]{1,0:T(1,128)} %param.12) | copy-start | bytes 772
  25.3 7.7 %collective-permute-start.3 = (f32[5,34,212]{2,1,0:T(8,128)S(1)}, f32[5,34,212]{2,1,0:T(8,128)S(1)}, u32[]{:S(2)}, u32[]{:S(2)}) collective-permute-start(f32[5,34,212]{2,1,0:T(8,128)S(1)} %get-tuple-element.28), channel_id=1, source_target_pairs={{1,0},{2,1},{3,2},{4,3},{5,4},{6,5},{7,6},{8,7},{9,8},{10,9},{11,1... | collective-permute-start | bytes 432488 | tf_op jit(solution)/shard_map/ppermute | solution.py:26
  31.1 9.2 %collective-permute-start.2 = (f32[5,34,212]{2,1,0:T(8,128)S(1)}, f32[5,34,212]{2,1,0:T(8,128)S(1)}, u32[]{:S(2)}, u32[]{:S(2)}) collective-permute-start(f32[5,34,212]{2,1,0:T(8,128)S(1)} %get-tuple-element.29), channel_id=1, source_target_pairs={{0,1},{1,2},{2,3},{3,4},{4,5},{5,6},{6,7},{7,8},{8,9},{9,10},{10,1... | collective-permute-start | bytes 432488 | tf_op jit(solution)/shard_map/ppermute | solution.py:26
  41.4 0.7 copy-start
  41.4 0.7 copy-start.1
  51.5 0.8 copy-start.6
  52.7 10.9 %collective-permute-start.4 = (f32[3,112,42]{2,1,0:T(8,128)S(1)}, f32[3,112,42]{2,1,0:T(8,128)S(1)}, u32[]{:S(2)}, u32[]{:S(2)}) collective-permute-start(f32[3,112,42]{2,1,0:T(8,128)S(1)} %get-tuple-element.63), channel_id=1, source_target_pairs={{0,16},{16,32},{32,48},{48,64},{64,80},{80,96},{96,112},{112,128},... | collective-permute-start | bytes 169352 | tf_op jit(solution)/shard_map/ppermute | solution.py:262
  54.6 10.4 %collective-permute-start.5 = (f32[3,112,42]{2,1,0:T(8,128)S(1)}, f32[3,112,42]{2,1,0:T(8,128)S(1)}, u32[]{:S(2)}, u32[]{:S(2)}) collective-permute-start(f32[3,112,42]{2,1,0:T(8,128)S(1)} %get-tuple-element.64), channel_id=1, source_target_pairs={{16,0},{32,16},{48,32},{64,48},{80,64},{96,80},{112,96},{128,112},... | collective-permute-start | bytes 169352 | tf_op jit(solution)/shard_map/ppermute | solution.py:265
  65.2 4.8 %collective-permute-start.7 = (f32[3,34,212]{2,1,0:T(8,128)S(1)}, f32[3,34,212]{2,1,0:T(8,128)S(1)}, u32[]{:S(2)}, u32[]{:S(2)}) collective-permute-start(f32[3,34,212]{2,1,0:T(8,128)S(1)} %get-tuple-element.42), channel_id=1, source_target_pairs={{1,0},{2,1},{3,2},{4,3},{5,4},{6,5},{7,6},{8,7},{9,8},{10,9},{11,1... | collective-permute-start | bytes 259496 | tf_op jit(solution)/shard_map/ppermute | solution.py:26
  67.5 8.3 %collective-permute-start.6 = (f32[3,34,212]{2,1,0:T(8,128)S(1)}, f32[3,34,212]{2,1,0:T(8,128)S(1)}, u32[]{:S(2)}, u32[]{:S(2)}) collective-permute-start(f32[3,34,212]{2,1,0:T(8,128)S(1)} %get-tuple-element.43), channel_id=1, source_target_pairs={{0,1},{1,2},{2,3},{3,4},{4,5},{5,6},{6,7},{7,8},{8,9},{9,10},{10,1... | collective-permute-start | bytes 259496 | tf_op jit(solution)/shard_map/ppermute | solution.py:26
  76.9 0.7 copy-start.3
  86.3 11.3 %collective-permute-start.8 = (f32[3,112,42]{2,1,0:T(8,128)S(1)}, f32[3,112,42]{2,1,0:T(8,128)S(1)}, u32[]{:S(2)}, u32[]{:S(2)}) collective-permute-start(f32[3,112,42]{2,1,0:T(8,128)S(1)} %get-tuple-element.61), channel_id=1, source_target_pairs={{0,16},{16,32},{32,48},{48,64},{64,80},{80,96},{96,112},{112,128},... | collective-permute-start | bytes 169352 | tf_op jit(solution)/shard_map/ppermute | solution.py:262
  88.2 10.8 %collective-permute-start.9 = (f32[3,112,42]{2,1,0:T(8,128)S(1)}, f32[3,112,42]{2,1,0:T(8,128)S(1)}, u32[]{:S(2)}, u32[]{:S(2)}) collective-permute-start(f32[3,112,42]{2,1,0:T(8,128)S(1)} %get-tuple-element.62), channel_id=1, source_target_pairs={{16,0},{32,16},{48,32},{64,48},{80,64},{96,80},{112,96},{128,112},... | collective-permute-start | bytes 169352 | tf_op jit(solution)/shard_map/ppermute | solution.py:265
  99.2 4.8 %collective-permute-start.11 = (f32[3,34,212]{2,1,0:T(8,128)S(1)}, f32[3,34,212]{2,1,0:T(8,128)S(1)}, u32[]{:S(2)}, u32[]{:S(2)}) collective-permute-start(f32[3,34,212]{2,1,0:T(8,128)S(1)} %get-tuple-element.40), channel_id=1, source_target_pairs={{1,0},{2,1},{3,2},{4,3},{5,4},{6,5},{7,6},{8,7},{9,8},{10,9},{11,1... | collective-permute-start | bytes 259496 | tf_op jit(solution)/shard_map/ppermute | solution.py:26
  101.8 8.3 %collective-permute-start.10 = (f32[3,34,212]{2,1,0:T(8,128)S(1)}, f32[3,34,212]{2,1,0:T(8,128)S(1)}, u32[]{:S(2)}, u32[]{:S(2)}) collective-permute-start(f32[3,34,212]{2,1,0:T(8,128)S(1)} %get-tuple-element.41), channel_id=1, source_target_pairs={{0,1},{1,2},{2,3},{3,4},{4,5},{5,6},{6,7},{7,8},{8,9},{9,10},{10,1... | collective-permute-start | bytes 259496 | tf_op jit(solution)/shard_map/ppermute | solution.py:26
  111.2 0.7 copy-start.2

commit v5 on v4

--- a/solution.py
+++ b/solution.py
@@ -216,45 +216,113 @@
     return rights / main_band
 
 
-def solve_kernel(surface_ref, east_ref, north_ref, depth_ref, keep_ref, east_out, north_out, *,
-                 first_row, used_cols):
-    rows = east_out.shape[0]
+def section_kernel(surface_ref, east_ref, north_ref, depth_ref, wet_ref, keep_ref, mirror_ref,
+                   rate_surface_out, rate_east_out, rate_north_out, east_out, north_out, *,
+                   first_row, used_cols, tile_offset):
+    rows, cols = rate_surface_out.shape
     depth = depth_ref[pl.ds(first_row, rows), :]
+    surface = surface_ref[pl.ds(first_row, rows), :]
     coef = depth * depth / (3.0 * LON_SPACING * LON_SPACING)
     keep = lax.broadcasted_iota(jnp.int32, depth.shape, 1) < used_cols
-    rights = east_ref[pl.ds(first_row, rows), :] / (depth + surface_ref[pl.ds(first_row, rows), :])
-    east_out[...] = reduce_lines(
+    rights = east_ref[pl.ds(first_row, rows), :] / (depth + surface)
+    east_raw = reduce_lines(
         jnp.where(keep, -coef, 0.0),
         jnp.where(keep, 1.0 + 2.0 * coef, 1.0),
         jnp.where(keep, -coef, 0.0),
         jnp.where(keep, rights, 0.0),
         1,
     )
-    depth = depth_ref[...]
-    coef = depth * depth / (3.0 * LAT_SPACING * LAT_SPACING)
+    full_depth = depth_ref[...]
+    coef = full_depth * full_depth / (3.0 * LAT_SPACING * LAT_SPACING)
     keep = keep_ref[...] > 0.0
-    rights = north_ref[...] / (depth + surface_ref[...])
-    north_out[...] = reduce_lines(
+    rights = north_ref[...] / (full_depth + surface_ref[...])
+    north_raw = reduce_lines(
         jnp.where(keep, -coef, 0.0),
         jnp.where(keep, 1.0 + 2.0 * coef, 1.0),
         jnp.where(keep, -coef, 0.0),
         jnp.where(keep, rights, 0.0),
         0,
-    )
-
-
-def line_solves(box, depth_box, keep, first_row, rows, used_cols):
+    )[first_row : first_row + rows]
+
+    def wrapped(values):
+        values = pltpu.roll(values, rows - (tile_offset[0] - first_row), 0)
+        return pltpu.roll(values, cols - tile_offset[1], 1)
+
+    wet = wrapped(wet_ref[pl.ds(first_row, rows), :])
+    surface = wrapped(surface)
+    depth = wrapped(depth)
+    velocity_u = wet * wrapped(east_raw)
+    velocity_v = wet * wrapped(north_raw)
+    mirror = mirror_ref[...]
+    for code, shift in ((1, rows - 1), (2, rows - 3), (3, 1), (4, 3)):
+        velocity_v = jnp.where(mirror == code, -pltpu.roll(velocity_v, shift, 0), velocity_v)
+
+    def east_of(values):
+        return pltpu.roll(values, cols - 1, 1)
+
+    def west_of(values):
+        return pltpu.roll(values, 1, 1)
+
+    def north_of(values):
+        return pltpu.roll(values, rows - 1, 0)
+
+    def south_of(values):
+        return pltpu.roll(values, 1, 0)
+
+    def face_pair(values, later, earlier):
+        jump = later(values) - values
+        slope = limited(earlier(jump), jump)
+        return values + 0.5 * slope, later(values - 0.5 * slope)
+
+    surface_pair = face_pair(surface, east_of, west_of)
+    east_pair = face_pair(velocity_u, east_of, west_of)
+    north_pair = face_pair(velocity_v, east_of, west_of)
+    depth_lon = 0.5 * (depth + east_of(depth))
+    open_lon = wet * east_of(wet)
+    mass_lon, push_lon, carry_lon = wave_flux(
+        surface_pair[0], surface_pair[1], east_pair[0], east_pair[1],
+        north_pair[0], north_pair[1], depth_lon, open_lon,
+    )
+    surface_pair = face_pair(surface, north_of, south_of)
+    east_pair = face_pair(velocity_u, north_of, south_of)
+    north_pair = face_pair(velocity_v, north_of, south_of)
+    depth_lat = 0.5 * (depth + north_of(depth))
+    open_lat = wet * north_of(wet)
+    mass_lat, push_lat, carry_lat = wave_flux(
+        surface_pair[0], surface_pair[1], north_pair[0], north_pair[1],
+        east_pair[0], east_pair[1], depth_lat, open_lat,
+    )
+    rate_surface_out[...] = (
+        -(mass_lon - west_of(mass_lon)) / LON_SPACING - (mass_lat - south_of(mass_lat)) / LAT_SPACING
+    )
+    source_east = GRAVITY * surface * (depth_lon - west_of(depth_lon)) / LON_SPACING
+    source_north = GRAVITY * surface * (depth_lat - south_of(depth_lat)) / LAT_SPACING
+    rate_east_out[...] = wet * (
+        source_east
+        - (push_lon - west_of(push_lon)) / LON_SPACING
+        - (carry_lat - south_of(carry_lat)) / LAT_SPACING
+    )
+    rate_north_out[...] = wet * (
+        source_north
+        - (carry_lon - west_of(carry_lon)) / LON_SPACING
+        - (push_lat - south_of(push_lat)) / LAT_SPACING
+    )
+    east_out[...] = velocity_u
+    north_out[...] = velocity_v
+
+
+def section_rates(box, keep, mirror, first_row, used_cols, tile_offset):
     spec = pl.BlockSpec(memory_space=pltpu.VMEM)
+    shape = jax.ShapeDtypeStruct(mirror.shape, jnp.float32)
     return pl.pallas_call(
-        lambda *refs: solve_kernel(*refs, first_row=first_row, used_cols=used_cols),
-        out_shape=(
-            jax.ShapeDtypeStruct((rows, depth_box.shape[1]), jnp.float32),
-            jax.ShapeDtypeStruct(depth_box.shape, jnp.float32),
+        lambda *refs: section_kernel(
+            *refs, first_row=first_row, used_cols=used_cols, tile_offset=tile_offset
         ),
-        in_specs=[spec] * 5,
-        out_specs=(spec, spec),
-        name="line_solves",
-    )(box[0], box[1], box[2], depth_box, keep)
+        out_shape=(shape,) * 5,
+        in_specs=[spec] * 7,
+        out_specs=(spec,) * 5,
+        name="section_rates",
+    )(box[0], box[1], box[2], box[3], box[4], keep, mirror)
 
 
 def halo_box(fields, wide_x, wide_y, place, count):
@@ -301,6 +369,15 @@
     keep = inside.astype(jnp.float32)
     first_row = (wide_y - 2) // 8 * 8
     east_rows = -(-(wide_y + tile_rows + 2 - first_row) // 8) * 8
+    wrapped_row = lax.broadcasted_iota(jnp.int32, (east_rows, aligned_cols), 0)
+    top = place == 0
+    bottom = place == count - 1
+    mirror = jnp.where(
+        top & (wrapped_row == east_rows - 1), 1,
+        jnp.where(top & (wrapped_row == east_rows - 2), 2,
+        jnp.where(bottom & (wrapped_row == tile_rows), 3,
+        jnp.where(bottom & (wrapped_row == tile_rows + 1), 4, 0))),
+    ).astype(jnp.int32)
 
     initial = (surface, momentum_x, momentum_y)
     current = initial
@@ -316,26 +393,17 @@
             depth_box, wet_box = box[3], box[4]
         else:
             box = halo_box(jnp.stack(list(current)), wide_x, wide_y, place, count)
-        surface_box, east_box, north_box = box[0], box[1], box[2]
-        east_solved, north_solved = line_solves(box, depth_box, keep, first_row, east_rows, box_cols)
-        east_raw = east_solved[core_rows.start - first_row : core_rows.stop - first_row, core_cols]
-        north_raw = north_solved[core_rows, core_cols]
-        wet_core = wet_box[core_rows, core_cols]
-        u_core = wet_core * east_raw
-        v_core = wet_core * north_raw
-        v_core = jnp.where(place == 0, jnp.concatenate([-v_core[3:1:-1], v_core[2:]], axis=0), v_core)
-        v_core = jnp.where(
-            place == count - 1, jnp.concatenate([v_core[:-2], -v_core[-3:-5:-1]], axis=0), v_core
+        rate_surface, rate_east, rate_north, east_wrapped, north_wrapped = section_rates(
+            (box[0], box[1], box[2], depth_box, wet_box), keep, mirror, first_row, box_cols,
+            (wide_y, wide_x),
         )
-        fields = jnp.stack(
-            [surface_box[core_rows, core_cols], u_core, v_core, depth_box[core_rows, core_cols], wet_core]
+        rates = (
+            rate_surface[:tile_rows, :tile_cols] + lift,
+            rate_east[:tile_rows, :tile_cols],
+            rate_north[:tile_rows, :tile_cols],
         )
-        across = fields[:, 2:-2, :]
-        along = fields[:, :, 2:-2]
-        rate_surface, rate_east, rate_north = tendencies(across, along)
-        rates = (rate_surface + lift, rate_east, rate_north)
-        velocity_u = u_core[2:-2, 2:-2]
-        velocity_v = v_core[2:-2, 2:-2]
+        velocity_u = east_wrapped[:tile_rows, :tile_cols]
+        velocity_v = north_wrapped[:tile_rows, :tile_cols]
         current = tuple(
             (
                 first * start_value + second * (now + TIME_STEP * rate)

time: 125 us -> 122 us (0.976)
  other arithmetic: 15.3 us -> 9.65 us
  Pallas kernels: 14.3 us -> 18.1 us
    pallas_call x3, Pallas kernels: 14.3 us -> 18.1 us  [section_rates(): pl.pallas_call(lambda *refs: section_kernel(*refs, first_row=first_row, u...]
    div x13 -> x0, other arithmetic: 3.6 us -> none  [the longest x6 1.68 us: wave_flux(): opened * (fastest * carry_left - slowest * carry_right + product * (heigh...]
    another operation x4 -> x0, other arithmetic: 2.27 us -> none  [local(): jnp.stack([surface_box[core_rows, core_cols], u_core, v_core, depth_box[c...]
    another operation x2 -> x8, other arithmetic: 0.03 us -> 1.87 us  [local(): box = halo_box(jnp.stack(list(current)), wide_x, wide_y, place, count)]
    sub x18 -> x0, other arithmetic: 1.72 us -> none  [face_states(): slab_of(values, 1, length, along_axis)]
    add x8 -> x3, other arithmetic: 2.82 us -> 4.46 us  [local(): first * start_value + second * (now + TIME_STEP * rate)]
    slice x11 -> x2, local copies, waits for them, and re-layouts: 1.47 us -> 2.89 us  [the longest x1 1.44 us: local(): velocity_u = east_wrapped[:tile_rows, :tile_cols]]
    unnamed x24 -> x26, local copies, waits for them, and re-layouts: 5.44 us -> 5.05 us
  transfers between devices with their start and end apart: 12 -> 12, of which waited for: 10 -> 9; matrix products, arithmetic and copies ran while one was open for 1% -> 2% of each run, Pallas kernels for 0% -> 0%
where the time goes in v5:
time: 122 us; the launch traced here: 121 us
  starting transfers between devices  49.3 us (40%)
  waiting for transfers between devices  30.4 us (25%)
  Pallas kernels  18.1 us (15%)
  local copies, waits for them, and re-layouts  12.4 us (10%)
  other arithmetic  9.65 us (8%)
    ppermute x3, starting transfers between devices, halo_box(): lax.ppermute(fields[:, :, :wide_x], 'lon', [((i + 1) % lon_count, i) for...  26.5 us
    ppermute x6, waiting for transfers between devices, passed_along(): return lax.ppermute(x, axis, pairs)  19.3 us
    pallas_call x3, Pallas kernels, section_rates(): pl.pallas_call(lambda *refs: section_kernel(*refs, first_row=first_row, u...  18.1 us
    ppermute x6, starting transfers between devices, passed_along(): return lax.ppermute(x, axis, pairs)  15.1 us
    ppermute x3, starting transfers between devices, halo_box(): lax.ppermute(fields[:, :, -wide_x:], 'lon', [(i, (i + 1) % lon_count) for...  7.67 us
    ppermute x3, waiting for transfers between devices, halo_box(): lax.ppermute(fields[:, :, -wide_x:], 'lon', [(i, (i + 1) % lon_count) for...  6.93 us
    unnamed x26, local copies, waits for them, and re-layouts  5.05 us
    add x3, other arithmetic, local(): first * start_value + second * (now + TIME_STEP * rate)  4.46 us
  transfers between devices with their start and end apart: 12, of which 9 were waited for; matrix products, arithmetic and copies ran while one was open for 2% of the time, Pallas kernels for 0%

profile of v5, /device:TPU:2, one launch (start us, length us, event | category | flops | bytes accessed | tf_op | source)
XLA Modules:
  0.0 120.8 jit_solution(1999577847384875900)
XLA Ops:
  4.1 3.8 %collective-permute-start = (f32[5,112,42]{2,1,0:T(8,128)S(1)}, f32[5,112,42]{2,1,0:T(8,128)S(1)}, u32[]{:S(2)}, u32[]{:S(2)}) collective-permute-start(f32[5,112,42]{2,1,0:T(8,128)S(1)} %get-tuple-element.44), channel_id=1, source_target_pairs={{0,16},{16,32},{32,48},{48,64},{64,80},{80,96},{96,112},{112,128},... | collective-permute-start | bytes 282248 | tf_op jit(solution)/shard_map/ppermute | solution.py:330
  7.9 11.1 %collective-permute-start.1 = (f32[5,112,42]{2,1,0:T(8,128)S(1)}, f32[5,112,42]{2,1,0:T(8,128)S(1)}, u32[]{:S(2)}, u32[]{:S(2)}) collective-permute-start(f32[5,112,42]{2,1,0:T(8,128)S(1)} %get-tuple-element.45), channel_id=1, source_target_pairs={{16,0},{32,16},{48,32},{64,48},{80,64},{96,80},{112,96},{128,112},... | collective-permute-start | bytes 282248 | tf_op jit(solution)/shard_map/ppermute | solution.py:333
  19.8 4.0 %collective-permute-done = f32[5,112,42]{2,1,0:T(8,128)S(1)} collective-permute-done((f32[5,112,42]{2,1,0:T(8,128)S(1)}, f32[5,112,42]{2,1,0:T(8,128)S(1)}, u32[]{:S(2)}, u32[]{:S(2)}) %collective-permute-start) | collective-permute-done | bytes 94112 | tf_op jit(solution)/shard_map/ppermute | solution.py:330
  25.3 4.4 %collective-permute-start.3 = (f32[5,34,212]{2,1,0:T(8,128)S(1)}, f32[5,34,212]{2,1,0:T(8,128)S(1)}, u32[]{:S(2)}, u32[]{:S(2)}) collective-permute-start(f32[5,34,212]{2,1,0:T(8,128)S(1)} %get-tuple-element.32), channel_id=1, source_target_pairs={{1,0},{2,1},{3,2},{4,3},{5,4},{6,5},{7,6},{8,7},{9,8},{10,9},{11,1... | collective-permute-start | bytes 432488 | tf_op jit(solution)/shard_map/ppermute | solution.py:26
  31.1 1.9 %collective-permute-start.2 = (f32[5,34,212]{2,1,0:T(8,128)S(1)}, f32[5,34,212]{2,1,0:T(8,128)S(1)}, u32[]{:S(2)}, u32[]{:S(2)}) collective-permute-start(f32[5,34,212]{2,1,0:T(8,128)S(1)} %get-tuple-element.33), channel_id=1, source_target_pairs={{0,1},{1,2},{2,3},{3,4},{4,5},{5,6},{6,7},{7,8},{8,9},{9,10},{10,1... | collective-permute-start | bytes 432488 | tf_op jit(solution)/shard_map/ppermute | solution.py:26
  33.0 7.2 %collective-permute-done.2 = f32[5,34,212]{2,1,0:T(8,128)S(1)} collective-permute-done((f32[5,34,212]{2,1,0:T(8,128)S(1)}, f32[5,34,212]{2,1,0:T(8,128)S(1)}, u32[]{:S(2)}, u32[]{:S(2)}) %collective-permute-start.2) | collective-permute-done | bytes 144192 | tf_op jit(solution)/shard_map/ppermute | solution.py:26
  42.3 6.0 %section_rates.3 = (f32[120,256]{1,0:T(8,128)}, f32[120,256]{1,0:T(8,128)}, f32[120,256]{1,0:T(8,128)}, f32[120,256]{1,0:T(8,128)}, f32[120,256]{1,0:T(8,128)}) custom-call(f32[184,256]{1,0:T(8,128)} %get-tuple-element.31.refs_0_, f32[184,256]{1,0:T(8,128)} %get-tuple-element.30.refs_1_, f32[184,256]{1,0:T(8,128)} %get-tuple-element.29.refs_2_, ...), custom_call_target="tpu_custom_call" | custom-call | tf_op jit(solution)/shard_map/section_rates/pallas_call | solution.py:317
  50.3 1.9 %collective-permute-start.4 = (f32[3,112,42]{2,1,0:T(8,128)S(1)}, f32[3,112,42]{2,1,0:T(8,128)S(1)}, u32[]{:S(2)}, u32[]{:S(2)}) collective-permute-start(f32[3,112,42]{2,1,0:T(8,128)S(1)} %get-tuple-element.48), channel_id=1, source_target_pairs={{0,16},{16,32},{32,48},{48,64},{64,80},{80,96},{96,112},{112,128},... | collective-permute-start | bytes 169352 | tf_op jit(solution)/shard_map/ppermute | solution.py:330
  52.2 7.5 %collective-permute-start.5 = (f32[3,112,42]{2,1,0:T(8,128)S(1)}, f32[3,112,42]{2,1,0:T(8,128)S(1)}, u32[]{:S(2)}, u32[]{:S(2)}) collective-permute-start(f32[3,112,42]{2,1,0:T(8,128)S(1)} %get-tuple-element.49), channel_id=1, source_target_pairs={{16,0},{32,16},{48,32},{64,48},{80,64},{96,80},{112,96},{128,112},... | collective-permute-start | bytes 169352 | tf_op jit(solution)/shard_map/ppermute | solution.py:333
  61.2 1.5 %collective-permute-done.5 = f32[3,112,42]{2,1,0:T(8,128)S(1)} collective-permute-done((f32[3,112,42]{2,1,0:T(8,128)S(1)}, f32[3,112,42]{2,1,0:T(8,128)S(1)}, u32[]{:S(2)}, u32[]{:S(2)}) %collective-permute-start.5) | collective-permute-done | bytes 56480 | tf_op jit(solution)/shard_map/ppermute | solution.py:333
  62.8 2.0 %collective-permute-start.7 = (f32[3,34,212]{2,1,0:T(8,128)S(1)}, f32[3,34,212]{2,1,0:T(8,128)S(1)}, u32[]{:S(2)}, u32[]{:S(2)}) collective-permute-start(f32[3,34,212]{2,1,0:T(8,128)S(1)} %get-tuple-element.42), channel_id=1, source_target_pairs={{1,0},{2,1},{3,2},{4,3},{5,4},{6,5},{7,6},{8,7},{9,8},{10,9},{11,1... | collective-permute-start | bytes 259496 | tf_op jit(solution)/shard_map/ppermute | solution.py:26
  65.1 2.3 %collective-permute-start.6 = (f32[3,34,212]{2,1,0:T(8,128)S(1)}, f32[3,34,212]{2,1,0:T(8,128)S(1)}, u32[]{:S(2)}, u32[]{:S(2)}) collective-permute-start(f32[3,34,212]{2,1,0:T(8,128)S(1)} %get-tuple-element.43), channel_id=1, source_target_pairs={{0,1},{1,2},{2,3},{3,4},{4,5},{5,6},{6,7},{7,8},{8,9},{9,10},{10,1... | collective-permute-start | bytes 259496 | tf_op jit(solution)/shard_map/ppermute | solution.py:26
  67.4 6.0 %collective-permute-done.6 = f32[3,34,212]{2,1,0:T(8,128)S(1)} collective-permute-done((f32[3,34,212]{2,1,0:T(8,128)S(1)}, f32[3,34,212]{2,1,0:T(8,128)S(1)}, u32[]{:S(2)}, u32[]{:S(2)}) %collective-permute-start.6) | collective-permute-done | bytes 86528 | tf_op jit(solution)/shard_map/ppermute | solution.py:26
  74.5 6.1 %section_rates.4 = (f32[120,256]{1,0:T(8,128)}, f32[120,256]{1,0:T(8,128)}, f32[120,256]{1,0:T(8,128)}, f32[120,256]{1,0:T(8,128)}, f32[120,256]{1,0:T(8,128)}) custom-call(f32[184,256]{1,0:T(8,128)} %get-tuple-element.39.refs_0_, f32[184,256]{1,0:T(8,128)} %get-tuple-element.38.refs_1_, f32[184,256]{1,0:T(8,128)} %get-tuple-element.37.refs_2_, ...), custom_call_target="tpu_custom_call" | custom-call | tf_op jit(solution)/shard_map/section_rates/pallas_call | solution.py:317
  82.5 1.9 %collective-permute-start.8 = (f32[3,112,42]{2,1,0:T(8,128)S(1)}, f32[3,112,42]{2,1,0:T(8,128)S(1)}, u32[]{:S(2)}, u32[]{:S(2)}) collective-permute-start(f32[3,112,42]{2,1,0:T(8,128)S(1)} %get-tuple-element.46), channel_id=1, source_target_pairs={{0,16},{16,32},{32,48},{48,64},{64,80},{80,96},{96,112},{112,128},... | collective-permute-start | bytes 169352 | tf_op jit(solution)/shard_map/ppermute | solution.py:330
  84.5 7.9 %collective-permute-start.9 = (f32[3,112,42]{2,1,0:T(8,128)S(1)}, f32[3,112,42]{2,1,0:T(8,128)S(1)}, u32[]{:S(2)}, u32[]{:S(2)}) collective-permute-start(f32[3,112,42]{2,1,0:T(8,128)S(1)} %get-tuple-element.47), channel_id=1, source_target_pairs={{16,0},{32,16},{48,32},{64,48},{80,64},{96,80},{112,96},{128,112},... | collective-permute-start | bytes 169352 | tf_op jit(solution)/shard_map/ppermute | solution.py:333
  93.8 1.5 %collective-permute-done.9 = f32[3,112,42]{2,1,0:T(8,128)S(1)} collective-permute-done((f32[3,112,42]{2,1,0:T(8,128)S(1)}, f32[3,112,42]{2,1,0:T(8,128)S(1)}, u32[]{:S(2)}, u32[]{:S(2)}) %collective-permute-start.9) | collective-permute-done | bytes 56480 | tf_op jit(solution)/shard_map/ppermute | solution.py:333
  95.4 2.4 %collective-permute-start.11 = (f32[3,34,212]{2,1,0:T(8,128)S(1)}, f32[3,34,212]{2,1,0:T(8,128)S(1)}, u32[]{:S(2)}, u32[]{:S(2)}) collective-permute-start(f32[3,34,212]{2,1,0:T(8,128)S(1)} %get-tuple-element.40), channel_id=1, source_target_pairs={{1,0},{2,1},{3,2},{4,3},{5,4},{6,5},{7,6},{8,7},{9,8},{10,9},{11,1... | collective-permute-start | bytes 259496 | tf_op jit(solution)/shard_map/ppermute | solution.py:26
  98.0 2.1 %collective-permute-start.10 = (f32[3,34,212]{2,1,0:T(8,128)S(1)}, f32[3,34,212]{2,1,0:T(8,128)S(1)}, u32[]{:S(2)}, u32[]{:S(2)}) collective-permute-start(f32[3,34,212]{2,1,0:T(8,128)S(1)} %get-tuple-element.41), channel_id=1, source_target_pairs={{0,1},{1,2},{2,3},{3,4},{4,5},{5,6},{6,7},{7,8},{8,9},{9,10},{10,1... | collective-permute-start | bytes 259496 | tf_op jit(solution)/shard_map/ppermute | solution.py:26
  100.2 6.1 %collective-permute-done.10 = f32[3,34,212]{2,1,0:T(8,128)S(1)} collective-permute-done((f32[3,34,212]{2,1,0:T(8,128)S(1)}, f32[3,34,212]{2,1,0:T(8,128)S(1)}, u32[]{:S(2)}, u32[]{:S(2)}) %collective-permute-start.10) | collective-permute-done | bytes 86528 | tf_op jit(solution)/shard_map/ppermute | solution.py:26
  107.4 6.0 %section_rates.5 = (f32[120,256]{1,0:T(8,128)}, f32[120,256]{1,0:T(8,128)}, f32[120,256]{1,0:T(8,128)}, f32[120,256]{1,0:T(8,128)}, f32[120,256]{1,0:T(8,128)}) custom-call(f32[184,256]{1,0:T(8,128)} %get-tuple-element.36.refs_0_, f32[184,256]{1,0:T(8,128)} %get-tuple-element.35.refs_1_, f32[184,256]{1,0:T(8,128)} %get-tuple-element.34.refs_2_, ...), custom_call_target="tpu_custom_call" | custom-call | tf_op jit(solution)/shard_map/section_rates/pallas_call | solution.py:317
  113.5 1.5 %multiply_add_fusion = f32[112,128]{1,0:T(8,128)} fusion(f32[120,256]{1,0:T(8,128)} %get-tuple-element.24, f32[112,128]{1,0:T(8,128)S(1)} %copy-done, f32[120,256]{1,0:T(8,128)S(1)} %copy-done.7, f32[120,256]{1,0:T(8,128)S(1)} %copy-done.5), kind=kLoop, calls=%fused_computation.91 | loop fusion | flops 200704 | bytes 286720 | tf_op jit(solution)/shard_map/add | solution.py:409
  114.9 1.5 %multiply_add_fusion.1 = f32[112,128]{1,0:T(8,128)} fusion(f32[120,256]{1,0:T(8,128)} %get-tuple-element.23, f32[112,128]{1,0:T(8,128)S(1)} %copy-done.1, f32[120,256]{1,0:T(8,128)S(1)} %copy-done.6, f32[120,256]{1,0:T(8,128)S(1)} %copy-done.4), kind=kLoop, calls=%fused_computation.92 | loop fusion | flops 200704 | bytes 286720 | tf_op jit(solution)/shard_map/add | solution.py:409
  116.4 1.5 %fusion.34 = f32[112,128]{1,0:T(8,128)} fusion(f32[14336]{0:T(1024)S(1)} %scatter_custom_fusion, f32[120,256]{1,0:T(8,128)} %get-tuple-element.22, f32[112,128]{1,0:T(8,128)S(1)} %copy-done.2, f32[120,256]{1,0:T(8,128)} %get-tuple-element.19, f32[120,256]{1,0:T(8,128)S(1)} %copy-done.3), kind=kLoop, calls=%fused_computation.85 | loop fusion | flops 243712 | bytes 344064 | tf_op jit(solution)/shard_map/add | solution.py:409
  (75 shorter events, 21.7 us)
Async XLA Ops:
  0.6 0.9 copy-start.1
  1.5 0.8 copy-start
  2.3 0.8 copy-start.8
  3.1 0.8 copy-start.9
  4.1 19.8 %collective-permute-start = (f32[5,112,42]{2,1,0:T(8,128)S(1)}, f32[5,112,42]{2,1,0:T(8,128)S(1)}, u32[]{:S(2)}, u32[]{:S(2)}) collective-permute-start(f32[5,112,42]{2,1,0:T(8,128)S(1)} %get-tuple-element.44), channel_id=1, source_target_pairs={{0,16},{16,32},{32,48},{48,64},{64,80},{80,96},{96,112},{112,128},... | collective-permute-start | bytes 282248 | tf_op jit(solution)/shard_map/ppermute | solution.py:330
  7.9 17.1 %collective-permute-start.1 = (f32[5,112,42]{2,1,0:T(8,128)S(1)}, f32[5,112,42]{2,1,0:T(8,128)S(1)}, u32[]{:S(2)}, u32[]{:S(2)}) collective-permute-start(f32[5,112,42]{2,1,0:T(8,128)S(1)} %get-tuple-element.45), channel_id=1, source_target_pairs={{16,0},{32,16},{48,32},{64,48},{80,64},{96,80},{112,96},{128,112},... | collective-permute-start | bytes 282248 | tf_op jit(solution)/shard_map/ppermute | solution.py:333
  25.3 4.4 %copy-start.10 = (s32[1,64]{1,0:T(1,128)S(1)}, s32[1,64]{1,0:T(1,128)}, u32[]{:S(2)}) copy-start(s32[1,64]{1,0:T(1,128)} %param.12) | copy-start | bytes 772
  25.3 7.7 %collective-permute-start.3 = (f32[5,34,212]{2,1,0:T(8,128)S(1)}, f32[5,34,212]{2,1,0:T(8,128)S(1)}, u32[]{:S(2)}, u32[]{:S(2)}) collective-permute-start(f32[5,34,212]{2,1,0:T(8,128)S(1)} %get-tuple-element.32), channel_id=1, source_target_pairs={{1,0},{2,1},{3,2},{4,3},{5,4},{6,5},{7,6},{8,7},{9,8},{10,9},{11,1... | collective-permute-start | bytes 432488 | tf_op jit(solution)/shard_map/ppermute | solution.py:26
  31.1 9.2 %collective-permute-start.2 = (f32[5,34,212]{2,1,0:T(8,128)S(1)}, f32[5,34,212]{2,1,0:T(8,128)S(1)}, u32[]{:S(2)}, u32[]{:S(2)}) collective-permute-start(f32[5,34,212]{2,1,0:T(8,128)S(1)} %get-tuple-element.33), channel_id=1, source_target_pairs={{0,1},{1,2},{2,3},{3,4},{4,5},{5,6},{6,7},{7,8},{8,9},{9,10},{10,1... | collective-permute-start | bytes 432488 | tf_op jit(solution)/shard_map/ppermute | solution.py:26
  48.4 0.9 copy-start.5
  48.4 1.0 copy-start.3
  49.3 0.8 copy-start.2
  50.3 10.9 %collective-permute-start.4 = (f32[3,112,42]{2,1,0:T(8,128)S(1)}, f32[3,112,42]{2,1,0:T(8,128)S(1)}, u32[]{:S(2)}, u32[]{:S(2)}) collective-permute-start(f32[3,112,42]{2,1,0:T(8,128)S(1)} %get-tuple-element.48), channel_id=1, source_target_pairs={{0,16},{16,32},{32,48},{48,64},{64,80},{80,96},{96,112},{112,128},... | collective-permute-start | bytes 169352 | tf_op jit(solution)/shard_map/ppermute | solution.py:330
  52.2 10.4 %collective-permute-start.5 = (f32[3,112,42]{2,1,0:T(8,128)S(1)}, f32[3,112,42]{2,1,0:T(8,128)S(1)}, u32[]{:S(2)}, u32[]{:S(2)}) collective-permute-start(f32[3,112,42]{2,1,0:T(8,128)S(1)} %get-tuple-element.49), channel_id=1, source_target_pairs={{16,0},{32,16},{48,32},{64,48},{80,64},{96,80},{112,96},{128,112},... | collective-permute-start | bytes 169352 | tf_op jit(solution)/shard_map/ppermute | solution.py:333
  62.8 4.6 %collective-permute-start.7 = (f32[3,34,212]{2,1,0:T(8,128)S(1)}, f32[3,34,212]{2,1,0:T(8,128)S(1)}, u32[]{:S(2)}, u32[]{:S(2)}) collective-permute-start(f32[3,34,212]{2,1,0:T(8,128)S(1)} %get-tuple-element.42), channel_id=1, source_target_pairs={{1,0},{2,1},{3,2},{4,3},{5,4},{6,5},{7,6},{8,7},{9,8},{10,9},{11,1... | collective-permute-start | bytes 259496 | tf_op jit(solution)/shard_map/ppermute | solution.py:26
  65.1 8.3 %collective-permute-start.6 = (f32[3,34,212]{2,1,0:T(8,128)S(1)}, f32[3,34,212]{2,1,0:T(8,128)S(1)}, u32[]{:S(2)}, u32[]{:S(2)}) collective-permute-start(f32[3,34,212]{2,1,0:T(8,128)S(1)} %get-tuple-element.43), channel_id=1, source_target_pairs={{0,1},{1,2},{2,3},{3,4},{4,5},{5,6},{6,7},{7,8},{8,9},{9,10},{10,1... | collective-permute-start | bytes 259496 | tf_op jit(solution)/shard_map/ppermute | solution.py:26
  80.5 0.9 copy-start.4
  80.5 1.0 copy-start.6
  81.4 0.9 copy-start.7
  82.5 11.3 %collective-permute-start.8 = (f32[3,112,42]{2,1,0:T(8,128)S(1)}, f32[3,112,42]{2,1,0:T(8,128)S(1)}, u32[]{:S(2)}, u32[]{:S(2)}) collective-permute-start(f32[3,112,42]{2,1,0:T(8,128)S(1)} %get-tuple-element.46), channel_id=1, source_target_pairs={{0,16},{16,32},{32,48},{48,64},{64,80},{80,96},{96,112},{112,128},... | collective-permute-start | bytes 169352 | tf_op jit(solution)/shard_map/ppermute | solution.py:330
  84.5 10.8 %collective-permute-start.9 = (f32[3,112,42]{2,1,0:T(8,128)S(1)}, f32[3,112,42]{2,1,0:T(8,128)S(1)}, u32[]{:S(2)}, u32[]{:S(2)}) collective-permute-start(f32[3,112,42]{2,1,0:T(8,128)S(1)} %get-tuple-element.47), channel_id=1, source_target_pairs={{16,0},{32,16},{48,32},{64,48},{80,64},{96,80},{112,96},{128,112},... | collective-permute-start | bytes 169352 | tf_op jit(solution)/shard_map/ppermute | solution.py:333
  95.4 4.8 %collective-permute-start.11 = (f32[3,34,212]{2,1,0:T(8,128)S(1)}, f32[3,34,212]{2,1,0:T(8,128)S(1)}, u32[]{:S(2)}, u32[]{:S(2)}) collective-permute-start(f32[3,34,212]{2,1,0:T(8,128)S(1)} %get-tuple-element.40), channel_id=1, source_target_pairs={{1,0},{2,1},{3,2},{4,3},{5,4},{6,5},{7,6},{8,7},{9,8},{10,9},{11,1... | collective-permute-start | bytes 259496 | tf_op jit(solution)/shard_map/ppermute | solution.py:26
  98.0 8.3 %collective-permute-start.10 = (f32[3,34,212]{2,1,0:T(8,128)S(1)}, f32[3,34,212]{2,1,0:T(8,128)S(1)}, u32[]{:S(2)}, u32[]{:S(2)}) collective-permute-start(f32[3,34,212]{2,1,0:T(8,128)S(1)} %get-tuple-element.41), channel_id=1, source_target_pairs={{0,1},{1,2},{2,3},{3,4},{4,5},{5,6},{6,7},{7,8},{8,9},{9,10},{10,1... | collective-permute-start | bytes 259496 | tf_op jit(solution)/shard_map/ppermute | solution.py:26

commit v6 on v5

--- a/solution.py
+++ b/solution.py
@@ -217,9 +217,11 @@
 
 
 def section_kernel(surface_ref, east_ref, north_ref, depth_ref, wet_ref, keep_ref, mirror_ref,
-                   rate_surface_out, rate_east_out, rate_north_out, east_out, north_out, *,
-                   first_row, used_cols, tile_offset):
-    rows, cols = rate_surface_out.shape
+                   lift_ref, start_surface, start_east, start_north, now_surface, now_east,
+                   now_north, next_surface, next_east, next_north, east_out, north_out, *,
+                   first_row, used_cols, tile_offset, weights):
+    rows, cols = mirror_ref.shape
+    tile_rows, tile_cols = lift_ref.shape
     depth = depth_ref[pl.ds(first_row, rows), :]
     surface = surface_ref[pl.ds(first_row, rows), :]
     coef = depth * depth / (3.0 * LON_SPACING * LON_SPACING)
@@ -292,37 +294,52 @@
         surface_pair[0], surface_pair[1], north_pair[0], north_pair[1],
         east_pair[0], east_pair[1], depth_lat, open_lat,
     )
-    rate_surface_out[...] = (
+    rate_surface = (
         -(mass_lon - west_of(mass_lon)) / LON_SPACING - (mass_lat - south_of(mass_lat)) / LAT_SPACING
     )
     source_east = GRAVITY * surface * (depth_lon - west_of(depth_lon)) / LON_SPACING
     source_north = GRAVITY * surface * (depth_lat - south_of(depth_lat)) / LAT_SPACING
-    rate_east_out[...] = wet * (
+    rate_east = wet * (
         source_east
         - (push_lon - west_of(push_lon)) / LON_SPACING
         - (carry_lat - south_of(carry_lat)) / LAT_SPACING
     )
-    rate_north_out[...] = wet * (
+    rate_north = wet * (
         source_north
         - (carry_lon - west_of(carry_lon)) / LON_SPACING
         - (push_lat - south_of(push_lat)) / LAT_SPACING
     )
-    east_out[...] = velocity_u
-    north_out[...] = velocity_v
-
-
-def section_rates(box, keep, mirror, first_row, used_cols, tile_offset):
+    first, second = weights
+    rates = (
+        rate_surface[:tile_rows, :tile_cols] + lift_ref[...],
+        rate_east[:tile_rows, :tile_cols],
+        rate_north[:tile_rows, :tile_cols],
+    )
+    for out, start, now, rate in zip(
+        (next_surface, next_east, next_north),
+        (start_surface, start_east, start_north),
+        (now_surface, now_east, now_north),
+        rates,
+    ):
+        out[...] = first * start[...] + second * (now[...] + TIME_STEP * rate)
+    east_out[...] = velocity_u[:tile_rows, :tile_cols]
+    north_out[...] = velocity_v[:tile_rows, :tile_cols]
+
+
+def section_step(fields, keep, mirror, lift, initial, current, first_row, used_cols, tile_offset,
+                 weights):
     spec = pl.BlockSpec(memory_space=pltpu.VMEM)
-    shape = jax.ShapeDtypeStruct(mirror.shape, jnp.float32)
+    shape = jax.ShapeDtypeStruct(lift.shape, jnp.float32)
     return pl.pallas_call(
         lambda *refs: section_kernel(
-            *refs, first_row=first_row, used_cols=used_cols, tile_offset=tile_offset
+            *refs, first_row=first_row, used_cols=used_cols, tile_offset=tile_offset,
+            weights=weights,
         ),
         out_shape=(shape,) * 5,
-        in_specs=[spec] * 7,
+        in_specs=[spec] * 14,
         out_specs=(spec,) * 5,
-        name="section_rates",
-    )(box[0], box[1], box[2], box[3], box[4], keep, mirror)
+        name="section_step",
+    )(*fields, keep, mirror, lift, *initial, *current)
 
 
 def halo_box(fields, wide_x, wide_y, place, count):
@@ -393,23 +410,11 @@
             depth_box, wet_box = box[3], box[4]
         else:
             box = halo_box(jnp.stack(list(current)), wide_x, wide_y, place, count)
-        rate_surface, rate_east, rate_north, east_wrapped, north_wrapped = section_rates(
-            (box[0], box[1], box[2], depth_box, wet_box), keep, mirror, first_row, box_cols,
-            (wide_y, wide_x),
+        next_surface, next_east, next_north, velocity_u, velocity_v = section_step(
+            (box[0], box[1], box[2], depth_box, wet_box), keep, mirror, lift, initial, current,
+            first_row, box_cols, (wide_y, wide_x), (first, second),
         )
-        rates = (
-            rate_surface[:tile_rows, :tile_cols] + lift,
-            rate_east[:tile_rows, :tile_cols],
-            rate_north[:tile_rows, :tile_cols],
-        )
-        velocity_u = east_wrapped[:tile_rows, :tile_cols]
-        velocity_v = north_wrapped[:tile_rows, :tile_cols]
-        current = tuple(
-            (
-                first * start_value + second * (now + TIME_STEP * rate)
-                for start_value, now, rate in zip(initial, current, rates)
-            )
-        )
+        current = (next_surface, next_east, next_north)
     return (current[0], current[1], current[2], velocity_u, velocity_v)
 
 

time: 122 us -> 113 us (0.926)
  the two profiles are of different devices: /device:TPU:2 before, /device:TPU:25 now
where the time goes in v6:
time: 113 us; the launch traced here: 112 us
  starting transfers between devices  55.1 us (49%)
  waiting for transfers between devices  24.9 us (22%)
  Pallas kernels  17.7 us (16%)
  local copies, waits for them, and re-layouts  7.77 us (7%)
  other arithmetic  5.67 us (5%)
    ppermute x3, starting transfers between devices, halo_box(): lax.ppermute(fields[:, :, :wide_x], 'lon', [((i + 1) % lon_count, i) for...  28 us
    ppermute x6, starting transfers between devices, passed_along(): return lax.ppermute(x, axis, pairs)  19.7 us
    pallas_call x3, Pallas kernels, section_step(): pl.pallas_call(lambda *refs: section_kernel(*refs, first_row=first_row, u...  17.7 us
    ppermute x6, waiting for transfers between devices, passed_along(): return lax.ppermute(x, axis, pairs)  14.4 us
    ppermute x3, starting transfers between devices, halo_box(): lax.ppermute(fields[:, :, -wide_x:], 'lon', [(i, (i + 1) % lon_count) for...  7.39 us
    ppermute x3, waiting for transfers between devices, halo_box(): lax.ppermute(fields[:, :, -wide_x:], 'lon', [(i, (i + 1) % lon_count) for...  7.34 us
    unnamed x26, local copies, waits for them, and re-layouts  3.33 us
    ppermute x3, waiting for transfers between devices, halo_box(): lax.ppermute(fields[:, :, :wide_x], 'lon', [((i + 1) % lon_count, i) for...  3.2 us
  transfers between devices with their start and end apart: 12, of which 9 were waited for; matrix products, arithmetic and copies ran while one was open for 3% of the time, Pallas kernels for 0%

profile of v6, /device:TPU:25, one launch (start us, length us, event | category | flops | bytes accessed | tf_op | source)
XLA Modules:
  0.0 112.2 jit_solution(1976216041864365130)
XLA Ops:
  4.1 3.5 %collective-permute-start = (f32[5,112,42]{2,1,0:T(8,128)S(1)}, f32[5,112,42]{2,1,0:T(8,128)S(1)}, u32[]{:S(2)}, u32[]{:S(2)}) collective-permute-start(f32[5,112,42]{2,1,0:T(8,128)S(1)} %get-tuple-element.34), channel_id=1, source_target_pairs={{0,16},{16,32},{32,48},{48,64},{64,80},{80,96},{96,112},{112,128},... | collective-permute-start | bytes 282248 | tf_op jit(solution)/shard_map/ppermute | solution.py:347
  7.6 12.0 %collective-permute-start.1 = (f32[5,112,42]{2,1,0:T(8,128)S(1)}, f32[5,112,42]{2,1,0:T(8,128)S(1)}, u32[]{:S(2)}, u32[]{:S(2)}) collective-permute-start(f32[5,112,42]{2,1,0:T(8,128)S(1)} %get-tuple-element.35), channel_id=1, source_target_pairs={{16,0},{32,16},{48,32},{64,48},{80,64},{96,80},{112,96},{128,112},... | collective-permute-start | bytes 282248 | tf_op jit(solution)/shard_map/ppermute | solution.py:350
  20.5 3.8 %collective-permute-done = f32[5,112,42]{2,1,0:T(8,128)S(1)} collective-permute-done((f32[5,112,42]{2,1,0:T(8,128)S(1)}, f32[5,112,42]{2,1,0:T(8,128)S(1)}, u32[]{:S(2)}, u32[]{:S(2)}) %collective-permute-start) | collective-permute-done | bytes 94112 | tf_op jit(solution)/shard_map/ppermute | solution.py:347
  25.3 3.5 %collective-permute-start.3 = (f32[5,34,212]{2,1,0:T(8,128)S(1)}, f32[5,34,212]{2,1,0:T(8,128)S(1)}, u32[]{:S(2)}, u32[]{:S(2)}) collective-permute-start(f32[5,34,212]{2,1,0:T(8,128)S(1)} %get-tuple-element.22), channel_id=1, source_target_pairs={{1,0},{2,1},{3,2},{4,3},{5,4},{6,5},{7,6},{8,7},{9,8},{10,9},{11,1... | collective-permute-start | bytes 432488 | tf_op jit(solution)/shard_map/ppermute | solution.py:26
  28.8 1.6 %scatter_custom_fusion = f32[14336]{0:T(1024)} fusion(s32[64]{0:T(128)S(1)} %fusion.46, f32[64]{0:T(128)} %bitcast.65, f32[]{:T(128)} %constant.19.clone.1), kind=kCustom, calls=%fused_computation.91 | custom fusion | flops 64 | bytes 57856 | tf_op jit(solution)/shard_map/scatter-add | solution.py:373
  30.6 4.2 %collective-permute-start.2 = (f32[5,34,212]{2,1,0:T(8,128)S(1)}, f32[5,34,212]{2,1,0:T(8,128)S(1)}, u32[]{:S(2)}, u32[]{:S(2)}) collective-permute-start(f32[5,34,212]{2,1,0:T(8,128)S(1)} %get-tuple-element.23), channel_id=1, source_target_pairs={{0,1},{1,2},{2,3},{3,4},{4,5},{5,6},{6,7},{7,8},{8,9},{9,10},{10,1... | collective-permute-start | bytes 432488 | tf_op jit(solution)/shard_map/ppermute | solution.py:26
  35.0 2.5 %collective-permute-done.2 = f32[5,34,212]{2,1,0:T(8,128)S(1)} collective-permute-done((f32[5,34,212]{2,1,0:T(8,128)S(1)}, f32[5,34,212]{2,1,0:T(8,128)S(1)}, u32[]{:S(2)}, u32[]{:S(2)}) %collective-permute-start.2) | collective-permute-done | bytes 144192 | tf_op jit(solution)/shard_map/ppermute | solution.py:26
  37.8 1.0 slice_bitcast_fusion.6
  39.6 5.9 %section_step.3 = (f32[112,128]{1,0:T(8,128)}, f32[112,128]{1,0:T(8,128)}, f32[112,128]{1,0:T(8,128)}, f32[112,128]{1,0:T(8,128)}, f32[112,128]{1,0:T(8,128)}) custom-call(f32[184,256]{1,0:T(8,128)} %get-tuple-element.21.refs_0_, f32[184,256]{1,0:T(8,128)} %get-tuple-element.20.refs_1_, f32[184,256]{1,0:T(8,128)} %get-tuple-element.19.refs_2_, ...), custom_call_target="tpu_custom_call" | custom-call | tf_op jit(solution)/shard_map/section_step/pallas_call | solution.py:333
  46.5 1.9 %collective-permute-start.4 = (f32[3,112,42]{2,1,0:T(8,128)S(1)}, f32[3,112,42]{2,1,0:T(8,128)S(1)}, u32[]{:S(2)}, u32[]{:S(2)}) collective-permute-start(f32[3,112,42]{2,1,0:T(8,128)S(1)} %get-tuple-element.38), channel_id=1, source_target_pairs={{0,16},{16,32},{32,48},{48,64},{64,80},{80,96},{96,112},{112,128},... | collective-permute-start | bytes 169352 | tf_op jit(solution)/shard_map/ppermute | solution.py:347
  48.4 7.7 %collective-permute-start.5 = (f32[3,112,42]{2,1,0:T(8,128)S(1)}, f32[3,112,42]{2,1,0:T(8,128)S(1)}, u32[]{:S(2)}, u32[]{:S(2)}) collective-permute-start(f32[3,112,42]{2,1,0:T(8,128)S(1)} %get-tuple-element.39), channel_id=1, source_target_pairs={{16,0},{32,16},{48,32},{64,48},{80,64},{96,80},{112,96},{128,112},... | collective-permute-start | bytes 169352 | tf_op jit(solution)/shard_map/ppermute | solution.py:350
  56.2 2.7 %collective-permute-done.4 = f32[3,112,42]{2,1,0:T(8,128)S(1)} collective-permute-done((f32[3,112,42]{2,1,0:T(8,128)S(1)}, f32[3,112,42]{2,1,0:T(8,128)S(1)}, u32[]{:S(2)}, u32[]{:S(2)}) %collective-permute-start.4) | collective-permute-done | bytes 56480 | tf_op jit(solution)/shard_map/ppermute | solution.py:347
  59.9 5.6 %collective-permute-start.6 = (f32[3,34,212]{2,1,0:T(8,128)S(1)}, f32[3,34,212]{2,1,0:T(8,128)S(1)}, u32[]{:S(2)}, u32[]{:S(2)}) collective-permute-start(f32[3,34,212]{2,1,0:T(8,128)S(1)} %get-tuple-element.33), channel_id=1, source_target_pairs={{0,1},{1,2},{2,3},{3,4},{4,5},{5,6},{6,7},{7,8},{8,9},{9,10},{10,1... | collective-permute-start | bytes 259496 | tf_op jit(solution)/shard_map/ppermute | solution.py:26
  65.7 1.9 %collective-permute-start.7 = (f32[3,34,212]{2,1,0:T(8,128)S(1)}, f32[3,34,212]{2,1,0:T(8,128)S(1)}, u32[]{:S(2)}, u32[]{:S(2)}) collective-permute-start(f32[3,34,212]{2,1,0:T(8,128)S(1)} %get-tuple-element.32), channel_id=1, source_target_pairs={{1,0},{2,1},{3,2},{4,3},{5,4},{6,5},{7,6},{8,7},{9,8},{10,9},{11,1... | collective-permute-start | bytes 259496 | tf_op jit(solution)/shard_map/ppermute | solution.py:26
  67.8 6.2 %collective-permute-done.7 = f32[3,34,212]{2,1,0:T(8,128)S(1)} collective-permute-done((f32[3,34,212]{2,1,0:T(8,128)S(1)}, f32[3,34,212]{2,1,0:T(8,128)S(1)}, u32[]{:S(2)}, u32[]{:S(2)}) %collective-permute-start.7) | collective-permute-done | bytes 86528 | tf_op jit(solution)/shard_map/ppermute | solution.py:26
  75.1 5.9 %section_step.4 = (f32[112,128]{1,0:T(8,128)}, f32[112,128]{1,0:T(8,128)}, f32[112,128]{1,0:T(8,128)}, f32[112,128]{1,0:T(8,128)}, f32[112,128]{1,0:T(8,128)}) custom-call(f32[184,256]{1,0:T(8,128)} %get-tuple-element.29.refs_0_, f32[184,256]{1,0:T(8,128)} %get-tuple-element.28.refs_1_, f32[184,256]{1,0:T(8,128)} %get-tuple-element.27.refs_2_, ...), custom_call_target="tpu_custom_call" | custom-call | tf_op jit(solution)/shard_map/section_step/pallas_call | solution.py:333
  81.0 0.9 pad_maximum_fusion.4
  82.0 1.9 %collective-permute-start.8 = (f32[3,112,42]{2,1,0:T(8,128)S(1)}, f32[3,112,42]{2,1,0:T(8,128)S(1)}, u32[]{:S(2)}, u32[]{:S(2)}) collective-permute-start(f32[3,112,42]{2,1,0:T(8,128)S(1)} %get-tuple-element.36), channel_id=1, source_target_pairs={{0,16},{16,32},{32,48},{48,64},{64,80},{80,96},{96,112},{112,128},... | collective-permute-start | bytes 169352 | tf_op jit(solution)/shard_map/ppermute | solution.py:347
  83.9 8.3 %collective-permute-start.9 = (f32[3,112,42]{2,1,0:T(8,128)S(1)}, f32[3,112,42]{2,1,0:T(8,128)S(1)}, u32[]{:S(2)}, u32[]{:S(2)}) collective-permute-start(f32[3,112,42]{2,1,0:T(8,128)S(1)} %get-tuple-element.37), channel_id=1, source_target_pairs={{16,0},{32,16},{48,32},{64,48},{80,64},{96,80},{112,96},{128,112},... | collective-permute-start | bytes 169352 | tf_op jit(solution)/shard_map/ppermute | solution.py:350
  93.1 1.5 %collective-permute-done.9 = f32[3,112,42]{2,1,0:T(8,128)S(1)} collective-permute-done((f32[3,112,42]{2,1,0:T(8,128)S(1)}, f32[3,112,42]{2,1,0:T(8,128)S(1)}, u32[]{:S(2)}, u32[]{:S(2)}) %collective-permute-start.9) | collective-permute-done | bytes 56480 | tf_op jit(solution)/shard_map/ppermute | solution.py:350
  94.8 2.0 %collective-permute-start.10 = (f32[3,34,212]{2,1,0:T(8,128)S(1)}, f32[3,34,212]{2,1,0:T(8,128)S(1)}, u32[]{:S(2)}, u32[]{:S(2)}) collective-permute-start(f32[3,34,212]{2,1,0:T(8,128)S(1)} %get-tuple-element.31), channel_id=1, source_target_pairs={{0,1},{1,2},{2,3},{3,4},{4,5},{5,6},{6,7},{7,8},{8,9},{9,10},{10,1... | collective-permute-start | bytes 259496 | tf_op jit(solution)/shard_map/ppermute | solution.py:26
  97.0 2.5 %collective-permute-start.11 = (f32[3,34,212]{2,1,0:T(8,128)S(1)}, f32[3,34,212]{2,1,0:T(8,128)S(1)}, u32[]{:S(2)}, u32[]{:S(2)}) collective-permute-start(f32[3,34,212]{2,1,0:T(8,128)S(1)} %get-tuple-element.30), channel_id=1, source_target_pairs={{1,0},{2,1},{3,2},{4,3},{5,4},{6,5},{7,6},{8,7},{9,8},{10,9},{11,1... | collective-permute-start | bytes 259496 | tf_op jit(solution)/shard_map/ppermute | solution.py:26
  99.6 5.7 %collective-permute-done.11 = f32[3,34,212]{2,1,0:T(8,128)S(1)} collective-permute-done((f32[3,34,212]{2,1,0:T(8,128)S(1)}, f32[3,34,212]{2,1,0:T(8,128)S(1)}, u32[]{:S(2)}, u32[]{:S(2)}) %collective-permute-start.11) | collective-permute-done | bytes 86528 | tf_op jit(solution)/shard_map/ppermute | solution.py:26
  106.3 5.9 %section_step.5 = (f32[112,128]{1,0:T(8,128)}, f32[112,128]{1,0:T(8,128)}, f32[112,128]{1,0:T(8,128)}, f32[112,128]{1,0:T(8,128)}, f32[112,128]{1,0:T(8,128)}) custom-call(f32[184,256]{1,0:T(8,128)} %get-tuple-element.26.refs_0_, f32[184,256]{1,0:T(8,128)} %get-tuple-element.25.refs_1_, f32[184,256]{1,0:T(8,128)} %get-tuple-element.24.refs_2_, ...), custom_call_target="tpu_custom_call" | custom-call | tf_op jit(solution)/shard_map/section_step/pallas_call | solution.py:333
  (64 shorter events, 12.6 us)
Async XLA Ops:
  0.6 0.9 copy-start
  1.5 0.8 copy-start.1
  2.3 0.8 copy-start.8
  3.1 0.8 copy-start.9
  4.1 20.1 %collective-permute-start = (f32[5,112,42]{2,1,0:T(8,128)S(1)}, f32[5,112,42]{2,1,0:T(8,128)S(1)}, u32[]{:S(2)}, u32[]{:S(2)}) collective-permute-start(f32[5,112,42]{2,1,0:T(8,128)S(1)} %get-tuple-element.34), channel_id=1, source_target_pairs={{0,16},{16,32},{32,48},{48,64},{64,80},{80,96},{96,112},{112,128},... | collective-permute-start | bytes 282248 | tf_op jit(solution)/shard_map/ppermute | solution.py:347
  7.6 17.4 %collective-permute-start.1 = (f32[5,112,42]{2,1,0:T(8,128)S(1)}, f32[5,112,42]{2,1,0:T(8,128)S(1)}, u32[]{:S(2)}, u32[]{:S(2)}) collective-permute-start(f32[5,112,42]{2,1,0:T(8,128)S(1)} %get-tuple-element.35), channel_id=1, source_target_pairs={{16,0},{32,16},{48,32},{64,48},{80,64},{96,80},{112,96},{128,112},... | collective-permute-start | bytes 282248 | tf_op jit(solution)/shard_map/ppermute | solution.py:350
  25.3 3.5 %copy-start.10 = (s32[1,64]{1,0:T(1,128)S(1)}, s32[1,64]{1,0:T(1,128)}, u32[]{:S(2)}) copy-start(s32[1,64]{1,0:T(1,128)} %param.12) | copy-start | bytes 772
  25.3 9.6 %collective-permute-start.3 = (f32[5,34,212]{2,1,0:T(8,128)S(1)}, f32[5,34,212]{2,1,0:T(8,128)S(1)}, u32[]{:S(2)}, u32[]{:S(2)}) collective-permute-start(f32[5,34,212]{2,1,0:T(8,128)S(1)} %get-tuple-element.22), channel_id=1, source_target_pairs={{1,0},{2,1},{3,2},{4,3},{5,4},{6,5},{7,6},{8,7},{9,8},{10,9},{11,1... | collective-permute-start | bytes 432488 | tf_op jit(solution)/shard_map/ppermute | solution.py:26
  30.6 6.9 %collective-permute-start.2 = (f32[5,34,212]{2,1,0:T(8,128)S(1)}, f32[5,34,212]{2,1,0:T(8,128)S(1)}, u32[]{:S(2)}, u32[]{:S(2)}) collective-permute-start(f32[5,34,212]{2,1,0:T(8,128)S(1)} %get-tuple-element.23), channel_id=1, source_target_pairs={{0,1},{1,2},{2,3},{3,4},{4,5},{5,6},{6,7},{7,8},{8,9},{9,10},{10,1... | collective-permute-start | bytes 432488 | tf_op jit(solution)/shard_map/ppermute | solution.py:26
  46.4 13.4 %copy-start.5 = (f32[112,128]{1,0:T(8,128)S(1)}, f32[112,128]{1,0:T(8,128)}, u32[]{:S(2)}) copy-start(f32[112,128]{1,0:T(8,128)} %get-tuple-element.11.refs_11_) | copy-start | bytes 172036
  46.4 13.4 %copy-start.6 = (f32[112,128]{1,0:T(8,128)S(1)}, f32[112,128]{1,0:T(8,128)}, u32[]{:S(2)}) copy-start(f32[112,128]{1,0:T(8,128)} %get-tuple-element.12.refs_12_) | copy-start | bytes 172036
  46.4 13.4 %copy-start.7 = (f32[112,128]{1,0:T(8,128)S(1)}, f32[112,128]{1,0:T(8,128)}, u32[]{:S(2)}) copy-start(f32[112,128]{1,0:T(8,128)} %get-tuple-element.13.refs_13_) | copy-start | bytes 172036
  46.5 12.4 %collective-permute-start.4 = (f32[3,112,42]{2,1,0:T(8,128)S(1)}, f32[3,112,42]{2,1,0:T(8,128)S(1)}, u32[]{:S(2)}, u32[]{:S(2)}) collective-permute-start(f32[3,112,42]{2,1,0:T(8,128)S(1)} %get-tuple-element.38), channel_id=1, source_target_pairs={{0,16},{16,32},{32,48},{48,64},{64,80},{80,96},{96,112},{112,128},... | collective-permute-start | bytes 169352 | tf_op jit(solution)/shard_map/ppermute | solution.py:347
  48.4 11.3 %collective-permute-start.5 = (f32[3,112,42]{2,1,0:T(8,128)S(1)}, f32[3,112,42]{2,1,0:T(8,128)S(1)}, u32[]{:S(2)}, u32[]{:S(2)}) collective-permute-start(f32[3,112,42]{2,1,0:T(8,128)S(1)} %get-tuple-element.39), channel_id=1, source_target_pairs={{16,0},{32,16},{48,32},{64,48},{80,64},{96,80},{112,96},{128,112},... | collective-permute-start | bytes 169352 | tf_op jit(solution)/shard_map/ppermute | solution.py:350
  59.9 7.8 %collective-permute-start.6 = (f32[3,34,212]{2,1,0:T(8,128)S(1)}, f32[3,34,212]{2,1,0:T(8,128)S(1)}, u32[]{:S(2)}, u32[]{:S(2)}) collective-permute-start(f32[3,34,212]{2,1,0:T(8,128)S(1)} %get-tuple-element.33), channel_id=1, source_target_pairs={{0,1},{1,2},{2,3},{3,4},{4,5},{5,6},{6,7},{7,8},{8,9},{9,10},{10,1... | collective-permute-start | bytes 259496 | tf_op jit(solution)/shard_map/ppermute | solution.py:26
  65.7 8.3 %collective-permute-start.7 = (f32[3,34,212]{2,1,0:T(8,128)S(1)}, f32[3,34,212]{2,1,0:T(8,128)S(1)}, u32[]{:S(2)}, u32[]{:S(2)}) collective-permute-start(f32[3,34,212]{2,1,0:T(8,128)S(1)} %get-tuple-element.32), channel_id=1, source_target_pairs={{1,0},{2,1},{3,2},{4,3},{5,4},{6,5},{7,6},{8,7},{9,8},{10,9},{11,1... | collective-permute-start | bytes 259496 | tf_op jit(solution)/shard_map/ppermute | solution.py:26
  81.9 12.7 %copy-start.2 = (f32[112,128]{1,0:T(8,128)S(1)}, f32[112,128]{1,0:T(8,128)}, u32[]{:S(2)}) copy-start(f32[112,128]{1,0:T(8,128)} %get-tuple-element.14.refs_11_) | copy-start | bytes 172036
  81.9 12.7 %copy-start.3 = (f32[112,128]{1,0:T(8,128)S(1)}, f32[112,128]{1,0:T(8,128)}, u32[]{:S(2)}) copy-start(f32[112,128]{1,0:T(8,128)} %get-tuple-element.15.refs_12_) | copy-start | bytes 172036
  81.9 12.7 %copy-start.4 = (f32[112,128]{1,0:T(8,128)S(1)}, f32[112,128]{1,0:T(8,128)}, u32[]{:S(2)}) copy-start(f32[112,128]{1,0:T(8,128)} %get-tuple-element.16.refs_13_) | copy-start | bytes 172036
  82.0 11.1 %collective-permute-start.8 = (f32[3,112,42]{2,1,0:T(8,128)S(1)}, f32[3,112,42]{2,1,0:T(8,128)S(1)}, u32[]{:S(2)}, u32[]{:S(2)}) collective-permute-start(f32[3,112,42]{2,1,0:T(8,128)S(1)} %get-tuple-element.36), channel_id=1, source_target_pairs={{0,16},{16,32},{32,48},{48,64},{64,80},{80,96},{96,112},{112,128},... | collective-permute-start | bytes 169352 | tf_op jit(solution)/shard_map/ppermute | solution.py:347
  83.9 10.7 %collective-permute-start.9 = (f32[3,112,42]{2,1,0:T(8,128)S(1)}, f32[3,112,42]{2,1,0:T(8,128)S(1)}, u32[]{:S(2)}, u32[]{:S(2)}) collective-permute-start(f32[3,112,42]{2,1,0:T(8,128)S(1)} %get-tuple-element.37), channel_id=1, source_target_pairs={{16,0},{32,16},{48,32},{64,48},{80,64},{96,80},{112,96},{128,112},... | collective-permute-start | bytes 169352 | tf_op jit(solution)/shard_map/ppermute | solution.py:350
  94.8 4.8 %collective-permute-start.10 = (f32[3,34,212]{2,1,0:T(8,128)S(1)}, f32[3,34,212]{2,1,0:T(8,128)S(1)}, u32[]{:S(2)}, u32[]{:S(2)}) collective-permute-start(f32[3,34,212]{2,1,0:T(8,128)S(1)} %get-tuple-element.31), channel_id=1, source_target_pairs={{0,1},{1,2},{2,3},{3,4},{4,5},{5,6},{6,7},{7,8},{8,9},{9,10},{10,1... | collective-permute-start | bytes 259496 | tf_op jit(solution)/shard_map/ppermute | solution.py:26
  97.0 8.3 %collective-permute-start.11 = (f32[3,34,212]{2,1,0:T(8,128)S(1)}, f32[3,34,212]{2,1,0:T(8,128)S(1)}, u32[]{:S(2)}, u32[]{:S(2)}) collective-permute-start(f32[3,34,212]{2,1,0:T(8,128)S(1)} %get-tuple-element.30), channel_id=1, source_target_pairs={{1,0},{2,1},{3,2},{4,3},{5,4},{6,5},{7,6},{8,7},{9,8},{10,9},{11,1... | collective-permute-start | bytes 259496 | tf_op jit(solution)/shard_map/ppermute | solution.py:26

commit v7 on v6

--- a/solution.py
+++ b/solution.py
@@ -342,7 +342,7 @@
     )(*fields, keep, mirror, lift, *initial, *current)
 
 
-def halo_box(fields, wide_x, wide_y, place, count):
+def halo_box(fields, wide_x, wide_y, place, count, padded_shape):
     lon_count = lax.axis_size("lon")
     west = lax.ppermute(
         fields[:, :, -wide_x:], "lon", [(i, (i + 1) % lon_count) for i in range(lon_count)]
@@ -356,8 +356,55 @@
     above = jnp.where(place == 0, wide[:, wide_y - 1 :: -1], above)
     below = jnp.where(place == count - 1, wide[:, : -wide_y - 1 : -1], below)
     box = jnp.concatenate([above, wide, below], axis=1)
-    aligned = [-(-size // unit) * unit for size, unit in zip(box.shape[1:], (8, 128))]
-    return jnp.pad(box, ((0, 0), (0, aligned[0] - box.shape[1]), (0, aligned[1] - box.shape[2])))
+    return pad_to(box, padded_shape)
+
+
+def pad_to(values, shape):
+    widths = [(0, 0)] * (values.ndim - 2) + [
+        (0, want - have) for want, have in zip(shape, values.shape[-2:])
+    ]
+    return jnp.pad(values, widths)
+
+
+def wall_mirrored(values, halo, place, count):
+    rows = values.shape[-2]
+    top = jnp.concatenate([values[..., 2 * halo - 1 : halo - 1 : -1, :], values[..., halo:, :]], axis=-2)
+    values = jnp.where(place == 0, top, values)
+    bottom = jnp.concatenate(
+        [values[..., : rows - halo, :], values[..., rows - halo - 1 : rows - 2 * halo - 1 : -1, :]],
+        axis=-2,
+    )
+    return jnp.where(place == count - 1, bottom, values)
+
+
+class Geometry:
+    def __init__(self, out_rows, out_cols, halo_y, halo_x):
+        self.box_rows = out_rows + 2 * halo_y
+        self.box_cols = out_cols + 2 * halo_x
+        self.first_row = (halo_y - 2) // 8 * 8
+        self.rows = -(-(halo_y + out_rows + 2 - self.first_row) // 8) * 8
+        self.padded = (
+            max(-(-self.box_rows // 8) * 8, self.first_row + self.rows),
+            -(-self.box_cols // 128) * 128,
+        )
+        self.offset = (halo_y, halo_x)
+
+    def masks(self, region_above, place, count, tile_rows):
+        box_row = lax.broadcasted_iota(jnp.int32, self.padded, 0)
+        global_row = place * tile_rows - region_above - self.offset[0] + box_row
+        inside = (global_row >= 0) & (global_row < count * tile_rows) & (box_row < self.box_rows)
+        wrapped_row = lax.broadcasted_iota(jnp.int32, (self.rows, self.padded[1]), 0)
+        tile_row = jnp.where(wrapped_row >= self.rows - 2, wrapped_row - self.rows, wrapped_row)
+        tile_row = tile_row - region_above
+        top = place == 0
+        bottom = place == count - 1
+        mirror = jnp.where(
+            top & (tile_row == -1), 1,
+            jnp.where(top & (tile_row == -2), 2,
+            jnp.where(bottom & (tile_row == tile_rows), 3,
+            jnp.where(bottom & (tile_row == tile_rows + 1), 4, 0))),
+        ).astype(jnp.int32)
+        return inside.astype(jnp.float32), mirror
 
 
 def local(surface, momentum_x, momentum_y, water_depth, wet_mask, slide_cells, slide_rate):
@@ -373,48 +420,37 @@
         .add(slide_rate.reshape(-1))
         .reshape(tile_rows, tile_cols)
     )
-    box_rows = tile_rows + 2 * wide_y
-    box_cols = tile_cols + 2 * wide_x
-    core_rows = slice(wide_y - 2, wide_y + tile_rows + 2)
-    core_cols = slice(wide_x - 2, wide_x + tile_cols + 2)
-    aligned_rows = -(-box_rows // 8) * 8
-    aligned_cols = -(-box_cols // 128) * 128
-    global_row = place * tile_rows - wide_y + lax.broadcasted_iota(
-        jnp.int32, (aligned_rows, aligned_cols), 0
-    )
-    inside = (global_row >= 0) & (global_row < count * tile_rows) & (global_row < place * tile_rows - wide_y + box_rows)
-    keep = inside.astype(jnp.float32)
-    first_row = (wide_y - 2) // 8 * 8
-    east_rows = -(-(wide_y + tile_rows + 2 - first_row) // 8) * 8
-    wrapped_row = lax.broadcasted_iota(jnp.int32, (east_rows, aligned_cols), 0)
-    top = place == 0
-    bottom = place == count - 1
-    mirror = jnp.where(
-        top & (wrapped_row == east_rows - 1), 1,
-        jnp.where(top & (wrapped_row == east_rows - 2), 2,
-        jnp.where(bottom & (wrapped_row == tile_rows), 3,
-        jnp.where(bottom & (wrapped_row == tile_rows + 1), 4, 0))),
-    ).astype(jnp.int32)
-
+    ring = Geometry(tile_rows + 2 * wide_y, tile_cols + 2 * wide_x, wide_y, wide_x)
+    plain = Geometry(tile_rows, tile_cols, wide_y, wide_x)
+    ring_keep, ring_mirror = ring.masks(wide_y, place, count, tile_rows)
+    plain_keep, plain_mirror = plain.masks(0, place, count, tile_rows)
     initial = (surface, momentum_x, momentum_y)
-    current = initial
-    velocity_u = surface
-    velocity_v = surface
-    depth_box = None
-    for first, second in ((0.0, 1.0), (0.75, 0.25), (1.0 / 3.0, 2.0 / 3.0)):
-        if depth_box is None:
-            box = halo_box(
-                jnp.stack([current[0], current[1], current[2], water_depth, wet_float]),
-                wide_x, wide_y, place, count,
-            )
-            depth_box, wet_box = box[3], box[4]
-        else:
-            box = halo_box(jnp.stack(list(current)), wide_x, wide_y, place, count)
+
+    big = halo_box(
+        jnp.stack([surface, momentum_x, momentum_y, water_depth, wet_float, lift]),
+        2 * wide_x, 2 * wide_y, place, count, ring.padded,
+    )
+    region = (slice(wide_y, wide_y + plain.box_rows), slice(wide_x, wide_x + plain.box_cols))
+    start_ring = tuple(big[k][region] for k in range(3))
+    first_state = section_step(
+        tuple(big[k] for k in range(5)), ring_keep, ring_mirror, big[5][region], start_ring,
+        start_ring, ring.first_row, ring.box_cols, ring.offset, (0.0, 1.0),
+    )[:3]
+    first_state = wall_mirrored(jnp.stack(first_state), wide_y, place, count)
+    depth_box = pad_to(big[3][region], plain.padded)
+    wet_box = pad_to(big[4][region], plain.padded)
+    tile = (slice(wide_y, wide_y + tile_rows), slice(wide_x, wide_x + tile_cols))
+    current = tuple(first_state[k][tile] for k in range(3))
+    box = pad_to(first_state, plain.padded)
+    for first, second in ((0.75, 0.25), (1.0 / 3.0, 2.0 / 3.0)):
+        if box is None:
+            box = halo_box(jnp.stack(list(current)), wide_x, wide_y, place, count, plain.padded)
         next_surface, next_east, next_north, velocity_u, velocity_v = section_step(
-            (box[0], box[1], box[2], depth_box, wet_box), keep, mirror, lift, initial, current,
-            first_row, box_cols, (wide_y, wide_x), (first, second),
+            (box[0], box[1], box[2], depth_box, wet_box), plain_keep, plain_mirror, lift, initial,
+            current, plain.first_row, plain.box_cols, plain.offset, (first, second),
         )
         current = (next_surface, next_east, next_north)
+        box = None
     return (current[0], current[1], current[2], velocity_u, velocity_v)
 
 

time: 113 us -> 116 us (1.027)
  starting transfers between devices: 55.1 us -> 35.7 us
  local copies, waits for them, and re-layouts: 7.77 us -> 19.6 us
  Pallas kernels: 17.7 us -> 23.2 us
  other arithmetic: 5.67 us -> 11.1 us
    ppermute x6 -> x4, starting transfers between devices: 19.7 us -> 9.91 us  [passed_along(): return lax.ppermute(x, axis, pairs)]
    slice x0 -> x14, local copies, waits for them, and re-layouts: none -> 7.73 us  [the longest x3 2.49 us: local(): start_ring = tuple((big[k][region] for k in range(3)))]
    ppermute x3 -> x2, starting transfers between devices: 28 us -> 20.3 us  [halo_box(): lax.ppermute(fields[:, :, :wide_x], 'lon', [((i + 1) % lon_count, i) for...]
    pallas_call x3, Pallas kernels: 17.7 us -> 23.2 us  [section_step(): pl.pallas_call(lambda *refs: section_kernel(*refs, first_row=first_row, u...]
    ppermute x3 -> x2, starting transfers between devices: 7.39 us -> 5.46 us  [halo_box(): lax.ppermute(fields[:, :, -wide_x:], 'lon', [(i, (i + 1) % lon_count) for...]
    pad x0 -> x2, local copies, waits for them, and re-layouts: none -> 1.37 us  [pad_to(): return jnp.pad(values, widths)]
    ppermute x3 -> x2, waiting for transfers between devices: 3.2 us -> 2.33 us  [halo_box(): lax.ppermute(fields[:, :, :wide_x], 'lon', [((i + 1) % lon_count, i) for...]
    ppermute x6 -> x4, waiting for transfers between devices: 14.4 us -> 15.2 us  [passed_along(): return lax.ppermute(x, axis, pairs)]
  transfers between devices with their start and end apart: 12 -> 8, of which waited for: 9 -> 7; matrix products, arithmetic and copies ran while one was open for 3% -> 4% of each run, Pallas kernels for 0% -> 0%
where the time goes in v7:
time: 116 us; the launch traced here: 115 us
  starting transfers between devices  35.7 us (31%)
  waiting for transfers between devices  24.1 us (21%)
  Pallas kernels  23.2 us (20%)
  local copies, waits for them, and re-layouts  19.6 us (17%)
  other arithmetic  11.1 us (10%)
    pallas_call x3, Pallas kernels, section_step(): pl.pallas_call(lambda *refs: section_kernel(*refs, first_row=first_row, u...  23.2 us
    ppermute x2, starting transfers between devices, halo_box(): lax.ppermute(fields[:, :, :wide_x], 'lon', [((i + 1) % lon_count, i) for...  20.3 us
    ppermute x4, waiting for transfers between devices, passed_along(): return lax.ppermute(x, axis, pairs)  15.2 us
    ppermute x4, starting transfers between devices, passed_along(): return lax.ppermute(x, axis, pairs)  9.91 us
    ppermute x2, waiting for transfers between devices, halo_box(): lax.ppermute(fields[:, :, -wide_x:], 'lon', [(i, (i + 1) % lon_count) for...  6.63 us
    ppermute x2, starting transfers between devices, halo_box(): lax.ppermute(fields[:, :, -wide_x:], 'lon', [(i, (i + 1) % lon_count) for...  5.46 us
    unnamed x28, local copies, waits for them, and re-layouts  4.06 us
    slice x3, local copies, waits for them, and re-layouts, local(): start_ring = tuple((big[k][region] for k in range(3)))  2.49 us
  transfers between devices with their start and end apart: 8, of which 7 were waited for; matrix products, arithmetic and copies ran while one was open for 4% of the time, Pallas kernels for 0%

profile of v7, /device:TPU:25, one launch (start us, length us, event | category | flops | bytes accessed | tf_op | source)
XLA Modules:
  0.0 114.7 jit_solution(6677237795883816505)
XLA Ops:
  5.4 1.1 scatter_custom_fusion
  6.7 3.5 %collective-permute-start = (f32[6,112,84]{2,1,0:T(8,128)S(1)}, f32[6,112,84]{2,1,0:T(8,128)S(1)}, u32[]{:S(2)}, u32[]{:S(2)}) collective-permute-start(f32[6,112,84]{2,1,0:T(8,128)S(1)} %get-tuple-element.36), channel_id=1, source_target_pairs={{0,16},{16,32},{32,48},{48,64},{64,80},{80,96},{96,112},{112,128},... | collective-permute-start | bytes 677384 | tf_op jit(solution)/shard_map/ppermute | solution.py:347
  10.2 12.0 %collective-permute-start.1 = (f32[6,112,84]{2,1,0:T(8,128)S(1)}, f32[6,112,84]{2,1,0:T(8,128)S(1)}, u32[]{:S(2)}, u32[]{:S(2)}) collective-permute-start(f32[6,112,84]{2,1,0:T(8,128)S(1)} %get-tuple-element.37), channel_id=1, source_target_pairs={{16,0},{32,16},{48,32},{64,48},{80,64},{96,80},{112,96},{128,112},... | collective-permute-start | bytes 677384 | tf_op jit(solution)/shard_map/ppermute | solution.py:350
  22.2 5.8 %collective-permute-done = f32[6,112,84]{2,1,0:T(8,128)S(1)} collective-permute-done((f32[6,112,84]{2,1,0:T(8,128)S(1)}, f32[6,112,84]{2,1,0:T(8,128)S(1)}, u32[]{:S(2)}, u32[]{:S(2)}) %collective-permute-start) | collective-permute-done | bytes 225824 | tf_op jit(solution)/shard_map/ppermute | solution.py:347
  30.1 3.3 %collective-permute-start.2 = (f32[6,68,296]{2,1,0:T(8,128)S(1)}, f32[6,68,296]{2,1,0:T(8,128)}, u32[]{:S(2)}, u32[]{:S(2)}) collective-permute-start(f32[6,68,296]{2,1,0:T(8,128)S(1)} %get-tuple-element.24), channel_id=1, source_target_pairs={{0,1},{1,2},{2,3},{3,4},{4,5},{5,6},{6,7},{7,8},{8,9},{9,10},{10,1... | collective-permute-start | bytes 1449224 | tf_op jit(solution)/shard_map/ppermute | solution.py:26
  34.4 2.1 %collective-permute-start.3 = (f32[6,68,296]{2,1,0:T(8,128)S(1)}, f32[6,68,296]{2,1,0:T(8,128)}, u32[]{:S(2)}, u32[]{:S(2)}) collective-permute-start(f32[6,68,296]{2,1,0:T(8,128)S(1)} %get-tuple-element.23), channel_id=1, source_target_pairs={{1,0},{2,1},{3,2},{4,3},{5,4},{6,5},{7,6},{8,7},{9,8},{10,9},{11,1... | collective-permute-start | bytes 1449224 | tf_op jit(solution)/shard_map/ppermute | solution.py:26
  38.4 2.6 %collective-permute-done.2 = f32[6,68,296]{2,1,0:T(8,128)} collective-permute-done((f32[6,68,296]{2,1,0:T(8,128)S(1)}, f32[6,68,296]{2,1,0:T(8,128)}, u32[]{:S(2)}, u32[]{:S(2)}) %collective-permute-start.2) | collective-permute-done | bytes 483104 | tf_op jit(solution)/shard_map/ppermute | solution.py:26
  41.1 1.2 %broadcast_select_fusion.1 = f32[6,68,296]{2,1,0:T(8,128)S(1)} fusion(f32[6,68,296]{2,1,0:T(8,128)S(1)} %rev.18, f32[6,68,296]{2,1,0:T(8,128)} %collective-permute-done.2, pred[]{:T(512)S(6)} %eq.62), kind=kLoop, calls=%fused_computation.42 | loop fusion | flops 120768 | bytes 1449217 | tf_op jit(solution)/shard_map/jit(_where)/select_n | solution.py:356
  42.2 6.3 %collective-permute-done.3 = f32[6,68,296]{2,1,0:T(8,128)} collective-permute-done((f32[6,68,296]{2,1,0:T(8,128)S(1)}, f32[6,68,296]{2,1,0:T(8,128)}, u32[]{:S(2)}, u32[]{:S(2)}) %collective-permute-start.3) | collective-permute-done | bytes 483104 | tf_op jit(solution)/shard_map/ppermute | solution.py:26
  48.6 1.2 %broadcast_select_fusion = f32[6,68,296]{2,1,0:T(8,128)S(1)} fusion(f32[6,68,296]{2,1,0:T(8,128)S(1)} %rev.19, f32[6,68,296]{2,1,0:T(8,128)} %collective-permute-done.3, pred[]{:T(512)S(6)} %eq.63), kind=kLoop, calls=%fused_computation.41 | loop fusion | flops 120768 | bytes 1449217 | tf_op jit(solution)/shard_map/jit(_where)/select_n | solution.py:357
  50.3 1.0 slice_bitcast_fusion
  55.4 11.4 %section_step.3 = (f32[180,212]{1,0:T(8,128)}, f32[180,212]{1,0:T(8,128)}, f32[180,212]{1,0:T(8,128)}, f32[180,212]{1,0:T(8,128)}, f32[180,212]{1,0:T(8,128)}) custom-call(f32[248,384]{1,0:T(8,128)} %copy-done.2, f32[248,384]{1,0:T(8,128)} %copy-done.1, f32[248,384]{1,0:T(8,128)} %copy-done, f32[248,384]{1,0:T(8,128)} %get-tuple-element.19.refs_3_, ...), custom_call_target="tpu_custom_call" | custom-call | tf_op jit(solution)/shard_map/section_step/pallas_call | solution.py:333
  66.8 1.2 %pad_maximum_fusion.1 = f32[3,180,212]{2,1,0:T(8,128)S(1)} fusion(f32[1,180,212]{2,1,0:T(8,128)} %bitcast.69, f32[1,180,212]{2,1,0:T(8,128)} %bitcast.67, f32[1,180,212]{2,1,0:T(8,128)} %bitcast.65), kind=kLoop, calls=%fused_computation.29 | loop fusion | flops 228960 | bytes 915840 | tf_op jit(solution)/shard_map/stack | solution.py:439
  69.7 1.1 slice.171
  70.8 1.1 slice.172
  76.2 5.9 %section_step.4 = (f32[112,128]{1,0:T(8,128)}, f32[112,128]{1,0:T(8,128)}, f32[112,128]{1,0:T(8,128)}, f32[112,128]{1,0:T(8,128)}, f32[112,128]{1,0:T(8,128)}) custom-call(f32[184,256]{1,0:T(8,128)} %get-tuple-element.33.refs_0_, f32[184,256]{1,0:T(8,128)} %get-tuple-element.32.refs_1_, f32[184,256]{1,0:T(8,128)} %get-tuple-element.31.refs_2_, ...), custom_call_target="tpu_custom_call" | custom-call | tf_op jit(solution)/shard_map/section_step/pallas_call | solution.py:333
  83.1 1.9 %collective-permute-start.4 = (f32[3,112,42]{2,1,0:T(8,128)S(1)}, f32[3,112,42]{2,1,0:T(8,128)S(1)}, u32[]{:S(2)}, u32[]{:S(2)}) collective-permute-start(f32[3,112,42]{2,1,0:T(8,128)S(1)} %get-tuple-element.38), channel_id=1, source_target_pairs={{0,16},{16,32},{32,48},{48,64},{64,80},{80,96},{96,112},{112,128},... | collective-permute-start | bytes 169352 | tf_op jit(solution)/shard_map/ppermute | solution.py:347
  85.0 8.3 %collective-permute-start.5 = (f32[3,112,42]{2,1,0:T(8,128)S(1)}, f32[3,112,42]{2,1,0:T(8,128)S(1)}, u32[]{:S(2)}, u32[]{:S(2)}) collective-permute-start(f32[3,112,42]{2,1,0:T(8,128)S(1)} %get-tuple-element.39), channel_id=1, source_target_pairs={{16,0},{32,16},{48,32},{64,48},{80,64},{96,80},{112,96},{128,112},... | collective-permute-start | bytes 169352 | tf_op jit(solution)/shard_map/ppermute | solution.py:350
  94.2 1.5 %collective-permute-done.5 = f32[3,112,42]{2,1,0:T(8,128)S(1)} collective-permute-done((f32[3,112,42]{2,1,0:T(8,128)S(1)}, f32[3,112,42]{2,1,0:T(8,128)S(1)}, u32[]{:S(2)}, u32[]{:S(2)}) %collective-permute-start.5) | collective-permute-done | bytes 56480 | tf_op jit(solution)/shard_map/ppermute | solution.py:350
  95.7 1.0 pad_maximum_fusion.7
  96.7 2.6 %collective-permute-start.6 = (f32[3,34,212]{2,1,0:T(8,128)S(1)}, f32[3,34,212]{2,1,0:T(8,128)S(1)}, u32[]{:S(2)}, u32[]{:S(2)}) collective-permute-start(f32[3,34,212]{2,1,0:T(8,128)S(1)} %get-tuple-element.35), channel_id=1, source_target_pairs={{0,1},{1,2},{2,3},{3,4},{4,5},{5,6},{6,7},{7,8},{8,9},{9,10},{10,1... | collective-permute-start | bytes 259496 | tf_op jit(solution)/shard_map/ppermute | solution.py:26
  99.4 1.9 %collective-permute-start.7 = (f32[3,34,212]{2,1,0:T(8,128)S(1)}, f32[3,34,212]{2,1,0:T(8,128)S(1)}, u32[]{:S(2)}, u32[]{:S(2)}) collective-permute-start(f32[3,34,212]{2,1,0:T(8,128)S(1)} %get-tuple-element.34), channel_id=1, source_target_pairs={{1,0},{2,1},{3,2},{4,3},{5,4},{6,5},{7,6},{8,7},{9,8},{10,9},{11,1... | collective-permute-start | bytes 259496 | tf_op jit(solution)/shard_map/ppermute | solution.py:26
  101.5 6.2 %collective-permute-done.7 = f32[3,34,212]{2,1,0:T(8,128)S(1)} collective-permute-done((f32[3,34,212]{2,1,0:T(8,128)S(1)}, f32[3,34,212]{2,1,0:T(8,128)S(1)}, u32[]{:S(2)}, u32[]{:S(2)}) %collective-permute-start.7) | collective-permute-done | bytes 86528 | tf_op jit(solution)/shard_map/ppermute | solution.py:26
  108.8 5.9 %section_step.5 = (f32[112,128]{1,0:T(8,128)}, f32[112,128]{1,0:T(8,128)}, f32[112,128]{1,0:T(8,128)}, f32[112,128]{1,0:T(8,128)}, f32[112,128]{1,0:T(8,128)}) custom-call(f32[184,256]{1,0:T(8,128)} %get-tuple-element.27.refs_0_, f32[184,256]{1,0:T(8,128)} %get-tuple-element.26.refs_1_, f32[184,256]{1,0:T(8,128)} %get-tuple-element.25.refs_2_, ...), custom_call_target="tpu_custom_call" | custom-call | tf_op jit(solution)/shard_map/section_step/pallas_call | solution.py:333
  (77 shorter events, 23.7 us)
Async XLA Ops:
  6.5 23.6 %copy-start.5 = (f32[14336]{0:T(1024)}, f32[14336]{0:T(1024)S(1)}, u32[]{:S(2)}) copy-start(f32[14336]{0:T(1024)S(1)} %scatter_custom_fusion) | copy-start | bytes 172036
  6.7 21.4 %collective-permute-start = (f32[6,112,84]{2,1,0:T(8,128)S(1)}, f32[6,112,84]{2,1,0:T(8,128)S(1)}, u32[]{:S(2)}, u32[]{:S(2)}) collective-permute-start(f32[6,112,84]{2,1,0:T(8,128)S(1)} %get-tuple-element.36), channel_id=1, source_target_pairs={{0,16},{16,32},{32,48},{48,64},{64,80},{80,96},{96,112},{112,128},... | collective-permute-start | bytes 677384 | tf_op jit(solution)/shard_map/ppermute | solution.py:347
  10.2 18.7 %collective-permute-start.1 = (f32[6,112,84]{2,1,0:T(8,128)S(1)}, f32[6,112,84]{2,1,0:T(8,128)S(1)}, u32[]{:S(2)}, u32[]{:S(2)}) collective-permute-start(f32[6,112,84]{2,1,0:T(8,128)S(1)} %get-tuple-element.37), channel_id=1, source_target_pairs={{16,0},{32,16},{48,32},{64,48},{80,64},{96,80},{112,96},{128,112},... | collective-permute-start | bytes 677384 | tf_op jit(solution)/shard_map/ppermute | solution.py:350
  28.9 0.7 copy-start.3
  30.1 10.9 %collective-permute-start.2 = (f32[6,68,296]{2,1,0:T(8,128)S(1)}, f32[6,68,296]{2,1,0:T(8,128)}, u32[]{:S(2)}, u32[]{:S(2)}) collective-permute-start(f32[6,68,296]{2,1,0:T(8,128)S(1)} %get-tuple-element.24), channel_id=1, source_target_pairs={{0,1},{1,2},{2,3},{3,4},{4,5},{5,6},{6,7},{7,8},{8,9},{9,10},{10,1... | collective-permute-start | bytes 1449224 | tf_op jit(solution)/shard_map/ppermute | solution.py:26
  34.4 14.2 %collective-permute-start.3 = (f32[6,68,296]{2,1,0:T(8,128)S(1)}, f32[6,68,296]{2,1,0:T(8,128)}, u32[]{:S(2)}, u32[]{:S(2)}) collective-permute-start(f32[6,68,296]{2,1,0:T(8,128)S(1)} %get-tuple-element.23), channel_id=1, source_target_pairs={{1,0},{2,1},{3,2},{4,3},{5,4},{6,5},{7,6},{8,7},{9,8},{10,9},{11,1... | collective-permute-start | bytes 1449224 | tf_op jit(solution)/shard_map/ppermute | solution.py:26
  38.4 11.3 %copy-start.4 = (f32[6,112,84]{2,1,0:T(8,128)S(1)}, f32[6,112,84]{2,1,0:T(8,128)}, u32[]{:S(2)}) copy-start(f32[6,112,84]{2,1,0:T(8,128)} %copy-done.3) | copy-start | bytes 677380
  51.3 4.1 %copy-start = (f32[248,384]{1,0:T(8,128)}, f32[248,384]{1,0:T(8,128)S(1)}, u32[]{:S(2)}) copy-start(f32[248,384]{1,0:T(8,128)S(1)} %get-tuple-element.20.refs_2_) | copy-start | bytes 1142788
  51.3 4.1 %copy-start.1 = (f32[248,384]{1,0:T(8,128)}, f32[248,384]{1,0:T(8,128)S(1)}, u32[]{:S(2)}) copy-start(f32[248,384]{1,0:T(8,128)S(1)} %get-tuple-element.21.refs_1_) | copy-start | bytes 1142788
  51.3 4.1 %copy-start.2 = (f32[248,384]{1,0:T(8,128)}, f32[248,384]{1,0:T(8,128)S(1)}, u32[]{:S(2)}) copy-start(f32[248,384]{1,0:T(8,128)S(1)} %get-tuple-element.22.refs_0_) | copy-start | bytes 1142788
  66.8 1.4 %copy-start.9 = (f32[180,212]{1,0:T(8,128)S(1)}, f32[180,212]{1,0:T(8,128)}, u32[]{:S(2)}) copy-start(f32[180,212]{1,0:T(8,128)} %get-tuple-element.11) | copy-start | bytes 457924
  66.8 1.4 %copy-start.10 = (f32[180,212]{1,0:T(8,128)S(1)}, f32[180,212]{1,0:T(8,128)}, u32[]{:S(2)}) copy-start(f32[180,212]{1,0:T(8,128)} %get-tuple-element.12) | copy-start | bytes 457924
  66.8 1.4 %copy-start.11 = (f32[180,212]{1,0:T(8,128)S(1)}, f32[180,212]{1,0:T(8,128)}, u32[]{:S(2)}) copy-start(f32[180,212]{1,0:T(8,128)} %get-tuple-element.13) | copy-start | bytes 457924
  82.0 25.7 %copy-start.6 = (f32[112,128]{1,0:T(8,128)S(1)}, f32[112,128]{1,0:T(8,128)}, u32[]{:S(2)}) copy-start(f32[112,128]{1,0:T(8,128)} %get-tuple-element.14.refs_11_) | copy-start | bytes 172036
  82.1 25.7 %copy-start.7 = (f32[112,128]{1,0:T(8,128)S(1)}, f32[112,128]{1,0:T(8,128)}, u32[]{:S(2)}) copy-start(f32[112,128]{1,0:T(8,128)} %get-tuple-element.15.refs_12_) | copy-start | bytes 172036
  82.1 25.7 %copy-start.8 = (f32[112,128]{1,0:T(8,128)S(1)}, f32[112,128]{1,0:T(8,128)}, u32[]{:S(2)}) copy-start(f32[112,128]{1,0:T(8,128)} %get-tuple-element.16.refs_13_) | copy-start | bytes 172036
  83.1 11.1 %collective-permute-start.4 = (f32[3,112,42]{2,1,0:T(8,128)S(1)}, f32[3,112,42]{2,1,0:T(8,128)S(1)}, u32[]{:S(2)}, u32[]{:S(2)}) collective-permute-start(f32[3,112,42]{2,1,0:T(8,128)S(1)} %get-tuple-element.38), channel_id=1, source_target_pairs={{0,16},{16,32},{32,48},{48,64},{64,80},{80,96},{96,112},{112,128},... | collective-permute-start | bytes 169352 | tf_op jit(solution)/shard_map/ppermute | solution.py:347
  85.0 10.7 %collective-permute-start.5 = (f32[3,112,42]{2,1,0:T(8,128)S(1)}, f32[3,112,42]{2,1,0:T(8,128)S(1)}, u32[]{:S(2)}, u32[]{:S(2)}) collective-permute-start(f32[3,112,42]{2,1,0:T(8,128)S(1)} %get-tuple-element.39), channel_id=1, source_target_pairs={{16,0},{32,16},{48,32},{64,48},{80,64},{96,80},{112,96},{128,112},... | collective-permute-start | bytes 169352 | tf_op jit(solution)/shard_map/ppermute | solution.py:350
  96.7 4.8 %collective-permute-start.6 = (f32[3,34,212]{2,1,0:T(8,128)S(1)}, f32[3,34,212]{2,1,0:T(8,128)S(1)}, u32[]{:S(2)}, u32[]{:S(2)}) collective-permute-start(f32[3,34,212]{2,1,0:T(8,128)S(1)} %get-tuple-element.35), channel_id=1, source_target_pairs={{0,1},{1,2},{2,3},{3,4},{4,5},{5,6},{6,7},{7,8},{8,9},{9,10},{10,1... | collective-permute-start | bytes 259496 | tf_op jit(solution)/shard_map/ppermute | solution.py:26
  99.4 8.3 %collective-permute-start.7 = (f32[3,34,212]{2,1,0:T(8,128)S(1)}, f32[3,34,212]{2,1,0:T(8,128)S(1)}, u32[]{:S(2)}, u32[]{:S(2)}) collective-permute-start(f32[3,34,212]{2,1,0:T(8,128)S(1)} %get-tuple-element.34), channel_id=1, source_target_pairs={{1,0},{2,1},{3,2},{4,3},{5,4},{6,5},{7,6},{8,7},{9,8},{10,9},{11,1... | collective-permute-start | bytes 259496 | tf_op jit(solution)/shard_map/ppermute | solution.py:26

commit v8 on v7

--- a/solution.py
+++ b/solution.py
@@ -216,12 +216,9 @@
     return rights / main_band
 
 
-def section_kernel(surface_ref, east_ref, north_ref, depth_ref, wet_ref, keep_ref, mirror_ref,
-                   lift_ref, start_surface, start_east, start_north, now_surface, now_east,
-                   now_north, next_surface, next_east, next_north, east_out, north_out, *,
-                   first_row, used_cols, tile_offset, weights):
+def tendency_body(surface_ref, east_ref, north_ref, depth_ref, wet_ref, keep_ref, mirror_ref,
+                  first_row, used_cols, tile_offset):
     rows, cols = mirror_ref.shape
-    tile_rows, tile_cols = lift_ref.shape
     depth = depth_ref[pl.ds(first_row, rows), :]
     surface = surface_ref[pl.ds(first_row, rows), :]
     coef = depth * depth / (3.0 * LON_SPACING * LON_SPACING)
@@ -309,24 +306,78 @@
         - (carry_lon - west_of(carry_lon)) / LON_SPACING
         - (push_lat - south_of(push_lat)) / LAT_SPACING
     )
+    return (rate_surface, rate_east, rate_north), (surface, velocity_u, velocity_v), wrapped
+
+
+def section_kernel(surface_ref, east_ref, north_ref, depth_ref, wet_ref, keep_ref, mirror_ref,
+                   lift_ref, start_surface, start_east, start_north,
+                   next_surface, next_east, next_north, east_out, north_out, *,
+                   first_row, used_cols, tile_offset, weights):
+    tile_rows, tile_cols = lift_ref.shape
+    rates, (surface, velocity_u, velocity_v), wrapped = tendency_body(
+        surface_ref, east_ref, north_ref, depth_ref, wet_ref, keep_ref, mirror_ref,
+        first_row, used_cols, tile_offset,
+    )
+    rows = mirror_ref.shape[0]
+    nows = (
+        surface,
+        wrapped(east_ref[pl.ds(first_row, rows), :]),
+        wrapped(north_ref[pl.ds(first_row, rows), :]),
+    )
     first, second = weights
     rates = (
-        rate_surface[:tile_rows, :tile_cols] + lift_ref[...],
-        rate_east[:tile_rows, :tile_cols],
-        rate_north[:tile_rows, :tile_cols],
+        rates[0][:tile_rows, :tile_cols] + lift_ref[...],
+        rates[1][:tile_rows, :tile_cols],
+        rates[2][:tile_rows, :tile_cols],
     )
     for out, start, now, rate in zip(
         (next_surface, next_east, next_north),
         (start_surface, start_east, start_north),
-        (now_surface, now_east, now_north),
+        nows,
         rates,
     ):
-        out[...] = first * start[...] + second * (now[...] + TIME_STEP * rate)
+        out[...] = first * start[...] + second * (now[:tile_rows, :tile_cols] + TIME_STEP * rate)
     east_out[...] = velocity_u[:tile_rows, :tile_cols]
     north_out[...] = velocity_v[:tile_rows, :tile_cols]
 
 
-def section_step(fields, keep, mirror, lift, initial, current, first_row, used_cols, tile_offset,
+def ring_kernel(surface_ref, east_ref, north_ref, depth_ref, wet_ref, keep_ref, mirror_ref,
+                lift_ref, next_surface, next_east, next_north, depth_out, wet_out, *,
+                first_row, used_cols, tile_offset):
+    rows = mirror_ref.shape[0]
+    out_rows, out_cols = next_surface.shape
+    rates, (surface, _, _), wrapped = tendency_body(
+        surface_ref, east_ref, north_ref, depth_ref, wet_ref, keep_ref, mirror_ref,
+        first_row, used_cols, tile_offset,
+    )
+    lift = wrapped(lift_ref[pl.ds(first_row, rows), :])
+    nows = (
+        surface,
+        wrapped(east_ref[pl.ds(first_row, rows), :]),
+        wrapped(north_ref[pl.ds(first_row, rows), :]),
+    )
+    rates = (rates[0] + lift, rates[1], rates[2])
+    for out, now, rate in zip((next_surface, next_east, next_north), nows, rates):
+        out[...] = (0.0 * now + 1.0 * (now + TIME_STEP * rate))[:out_rows, :out_cols]
+    depth_out[...] = wrapped(depth_ref[pl.ds(first_row, rows), :])[:out_rows, :out_cols]
+    wet_out[...] = wrapped(wet_ref[pl.ds(first_row, rows), :])[:out_rows, :out_cols]
+
+
+def ring_step(fields, keep, mirror, out_shape, first_row, used_cols, tile_offset):
+    spec = pl.BlockSpec(memory_space=pltpu.VMEM)
+    shape = jax.ShapeDtypeStruct(out_shape, jnp.float32)
+    return pl.pallas_call(
+        lambda *refs: ring_kernel(
+            *refs, first_row=first_row, used_cols=used_cols, tile_offset=tile_offset
+        ),
+        out_shape=(shape,) * 5,
+        in_specs=[spec] * 8,
+        out_specs=(spec,) * 5,
+        name="ring_step",
+    )(*fields[:5], keep, mirror, fields[5])
+
+
+def section_step(fields, keep, mirror, lift, initial, first_row, used_cols, tile_offset,
                  weights):
     spec = pl.BlockSpec(memory_space=pltpu.VMEM)
     shape = jax.ShapeDtypeStruct(lift.shape, jnp.float32)
@@ -336,10 +387,10 @@
             weights=weights,
         ),
         out_shape=(shape,) * 5,
-        in_specs=[spec] * 14,
+        in_specs=[spec] * 11,
         out_specs=(spec,) * 5,
         name="section_step",
-    )(*fields, keep, mirror, lift, *initial, *current)
+    )(*fields, keep, mirror, lift, *initial)
 
 
 def halo_box(fields, wide_x, wide_y, place, count, padded_shape):
@@ -366,12 +417,15 @@
     return jnp.pad(values, widths)
 
 
-def wall_mirrored(values, halo, place, count):
-    rows = values.shape[-2]
+def wall_mirrored(values, halo, place, count, rows):
     top = jnp.concatenate([values[..., 2 * halo - 1 : halo - 1 : -1, :], values[..., halo:, :]], axis=-2)
     values = jnp.where(place == 0, top, values)
     bottom = jnp.concatenate(
-        [values[..., : rows - halo, :], values[..., rows - halo - 1 : rows - 2 * halo - 1 : -1, :]],
+        [
+            values[..., : rows - halo, :],
+            values[..., rows - halo - 1 : rows - 2 * halo - 1 : -1, :],
+            values[..., rows:, :],
+        ],
         axis=-2,
     )
     return jnp.where(place == count - 1, bottom, values)
@@ -430,24 +484,18 @@
         jnp.stack([surface, momentum_x, momentum_y, water_depth, wet_float, lift]),
         2 * wide_x, 2 * wide_y, place, count, ring.padded,
     )
-    region = (slice(wide_y, wide_y + plain.box_rows), slice(wide_x, wide_x + plain.box_cols))
-    start_ring = tuple(big[k][region] for k in range(3))
-    first_state = section_step(
-        tuple(big[k] for k in range(5)), ring_keep, ring_mirror, big[5][region], start_ring,
-        start_ring, ring.first_row, ring.box_cols, ring.offset, (0.0, 1.0),
-    )[:3]
-    first_state = wall_mirrored(jnp.stack(first_state), wide_y, place, count)
-    depth_box = pad_to(big[3][region], plain.padded)
-    wet_box = pad_to(big[4][region], plain.padded)
-    tile = (slice(wide_y, wide_y + tile_rows), slice(wide_x, wide_x + tile_cols))
-    current = tuple(first_state[k][tile] for k in range(3))
-    box = pad_to(first_state, plain.padded)
+    ring_state = ring_step(
+        tuple(big[k] for k in range(6)), ring_keep, ring_mirror, plain.padded,
+        ring.first_row, ring.box_cols, ring.offset,
+    )
+    box = wall_mirrored(jnp.stack(ring_state[:3]), wide_y, place, count, plain.box_rows)
+    depth_box, wet_box = ring_state[3], ring_state[4]
     for first, second in ((0.75, 0.25), (1.0 / 3.0, 2.0 / 3.0)):
         if box is None:
             box = halo_box(jnp.stack(list(current)), wide_x, wide_y, place, count, plain.padded)
         next_surface, next_east, next_north, velocity_u, velocity_v = section_step(
             (box[0], box[1], box[2], depth_box, wet_box), plain_keep, plain_mirror, lift, initial,
-            current, plain.first_row, plain.box_cols, plain.offset, (first, second),
+            plain.first_row, plain.box_cols, plain.offset, (first, second),
         )
         current = (next_surface, next_east, next_north)
         box = None

time: 116 us -> 107 us (0.922)
  local copies, waits for them, and re-layouts: 19.6 us -> 11.1 us
    pallas_call x3 -> x2, Pallas kernels: 23.2 us -> 11.9 us  [section_step(): pl.pallas_call(lambda *refs: section_kernel(*refs, first_row=first_row, u...]
    pallas_call x0 -> x1, Pallas kernels: none -> 11.3 us  [ring_step(): pl.pallas_call(lambda *refs: ring_kernel(*refs, first_row=first_row, used...]
    slice x9 -> x1, local copies, waits for them, and re-layouts: 7.56 us -> 0.01 us  [wall_mirrored(): values[..., rows:, :]]
    pad x2 -> x0, local copies, waits for them, and re-layouts: 1.37 us -> none  [pad_to(): return jnp.pad(values, widths)]
    unnamed x28 -> x22, local copies, waits for them, and re-layouts: 4.06 us -> 4.07 us
where the time goes in v8:
time: 107 us; the launch traced here: 106 us
  starting transfers between devices  35.7 us (33%)
  waiting for transfers between devices  24.1 us (23%)
  Pallas kernels  23.2 us (22%)
  other arithmetic  11.1 us (10%)
  local copies, waits for them, and re-layouts  11.1 us (10%)
    ppermute x2, starting transfers between devices, halo_box(): lax.ppermute(fields[:, :, :wide_x], 'lon', [((i + 1) % lon_count, i) for...  20.3 us
    ppermute x4, waiting for transfers between devices, passed_along(): return lax.ppermute(x, axis, pairs)  15.2 us
    pallas_call x2, Pallas kernels, section_step(): pl.pallas_call(lambda *refs: section_kernel(*refs, first_row=first_row, u...  11.9 us
    pallas_call x1, Pallas kernels, ring_step(): pl.pallas_call(lambda *refs: ring_kernel(*refs, first_row=first_row, used...  11.3 us
    ppermute x4, starting transfers between devices, passed_along(): return lax.ppermute(x, axis, pairs)  9.9 us
    ppermute x2, waiting for transfers between devices, halo_box(): lax.ppermute(fields[:, :, -wide_x:], 'lon', [(i, (i + 1) % lon_count) for...  6.62 us
    ppermute x2, starting transfers between devices, halo_box(): lax.ppermute(fields[:, :, -wide_x:], 'lon', [(i, (i + 1) % lon_count) for...  5.46 us
    unnamed x22, local copies, waits for them, and re-layouts  4.07 us
  transfers between devices with their start and end apart: 8, of which 7 were waited for; matrix products, arithmetic and copies ran while one was open for 4% of the time, Pallas kernels for 0%

profile of v8, /device:TPU:25, one launch (start us, length us, event | category | flops | bytes accessed | tf_op | source)
XLA Modules:
  0.0 106.1 jit_solution(16829484403961782668)
XLA Ops:
  5.4 1.1 scatter_custom_fusion
  6.7 3.5 %collective-permute-start = (f32[6,112,84]{2,1,0:T(8,128)S(1)}, f32[6,112,84]{2,1,0:T(8,128)S(1)}, u32[]{:S(2)}, u32[]{:S(2)}) collective-permute-start(f32[6,112,84]{2,1,0:T(8,128)S(1)} %get-tuple-element.37), channel_id=1, source_target_pairs={{0,16},{16,32},{32,48},{48,64},{64,80},{80,96},{96,112},{112,128},... | collective-permute-start | bytes 677384 | tf_op jit(solution)/shard_map/ppermute | solution.py:398
  10.2 12.0 %collective-permute-start.1 = (f32[6,112,84]{2,1,0:T(8,128)S(1)}, f32[6,112,84]{2,1,0:T(8,128)S(1)}, u32[]{:S(2)}, u32[]{:S(2)}) collective-permute-start(f32[6,112,84]{2,1,0:T(8,128)S(1)} %get-tuple-element.38), channel_id=1, source_target_pairs={{16,0},{32,16},{48,32},{64,48},{80,64},{96,80},{112,96},{128,112},... | collective-permute-start | bytes 677384 | tf_op jit(solution)/shard_map/ppermute | solution.py:401
  22.2 5.8 %collective-permute-done = f32[6,112,84]{2,1,0:T(8,128)S(1)} collective-permute-done((f32[6,112,84]{2,1,0:T(8,128)S(1)}, f32[6,112,84]{2,1,0:T(8,128)S(1)}, u32[]{:S(2)}, u32[]{:S(2)}) %collective-permute-start) | collective-permute-done | bytes 225824 | tf_op jit(solution)/shard_map/ppermute | solution.py:398
  30.2 3.3 %collective-permute-start.2 = (f32[6,68,296]{2,1,0:T(8,128)S(1)}, f32[6,68,296]{2,1,0:T(8,128)}, u32[]{:S(2)}, u32[]{:S(2)}) collective-permute-start(f32[6,68,296]{2,1,0:T(8,128)S(1)} %get-tuple-element.28), channel_id=1, source_target_pairs={{0,1},{1,2},{2,3},{3,4},{4,5},{5,6},{6,7},{7,8},{8,9},{9,10},{10,1... | collective-permute-start | bytes 1449224 | tf_op jit(solution)/shard_map/ppermute | solution.py:26
  33.5 0.9 select_select_fusion.refs_6_
  34.4 2.1 %collective-permute-start.3 = (f32[6,68,296]{2,1,0:T(8,128)S(1)}, f32[6,68,296]{2,1,0:T(8,128)}, u32[]{:S(2)}, u32[]{:S(2)}) collective-permute-start(f32[6,68,296]{2,1,0:T(8,128)S(1)} %get-tuple-element.27), channel_id=1, source_target_pairs={{1,0},{2,1},{3,2},{4,3},{5,4},{6,5},{7,6},{8,7},{9,8},{10,9},{11,1... | collective-permute-start | bytes 1449224 | tf_op jit(solution)/shard_map/ppermute | solution.py:26
  38.5 2.6 %collective-permute-done.2 = f32[6,68,296]{2,1,0:T(8,128)} collective-permute-done((f32[6,68,296]{2,1,0:T(8,128)S(1)}, f32[6,68,296]{2,1,0:T(8,128)}, u32[]{:S(2)}, u32[]{:S(2)}) %collective-permute-start.2) | collective-permute-done | bytes 483104 | tf_op jit(solution)/shard_map/ppermute | solution.py:26
  41.1 1.2 %broadcast_select_fusion.1 = f32[6,68,296]{2,1,0:T(8,128)S(1)} fusion(f32[6,68,296]{2,1,0:T(8,128)S(1)} %rev.18, f32[6,68,296]{2,1,0:T(8,128)} %collective-permute-done.2, pred[]{:T(512)S(6)} %eq.62), kind=kLoop, calls=%fused_computation.39 | loop fusion | flops 120768 | bytes 1449217 | tf_op jit(solution)/shard_map/jit(_where)/select_n | solution.py:407
  42.3 6.3 %collective-permute-done.3 = f32[6,68,296]{2,1,0:T(8,128)} collective-permute-done((f32[6,68,296]{2,1,0:T(8,128)S(1)}, f32[6,68,296]{2,1,0:T(8,128)}, u32[]{:S(2)}, u32[]{:S(2)}) %collective-permute-start.3) | collective-permute-done | bytes 483104 | tf_op jit(solution)/shard_map/ppermute | solution.py:26
  48.6 1.2 %broadcast_select_fusion = f32[6,68,296]{2,1,0:T(8,128)S(1)} fusion(f32[6,68,296]{2,1,0:T(8,128)S(1)} %rev.19, f32[6,68,296]{2,1,0:T(8,128)} %collective-permute-done.3, pred[]{:T(512)S(6)} %eq.63), kind=kLoop, calls=%fused_computation.38 | loop fusion | flops 120768 | bytes 1449217 | tf_op jit(solution)/shard_map/jit(_where)/select_n | solution.py:408
  50.3 1.4 %slice_bitcast_fusion = (f32[248,384]{1,0:T(8,128)}, f32[248,384]{1,0:T(8,128)}, f32[248,384]{1,0:T(8,128)}, f32[248,384]{1,0:T(8,128)}, f32[248,384]{1,0:T(8,128)}, /*index=5*/f32[248,384]{1,0:T(8,128)}) fusion(f32[6,248,384]{2,1,0:T(8,128)S(1)} %select_maximum_fusion), kind=kLoop, calls=%fused_computation.32 | loop fusion | bytes 4571136 | tf_op jit(solution)/shard_map/squeeze | solution.py:488
  52.6 11.3 %ring_step.1 = (f32[184,256]{1,0:T(8,128)}, f32[184,256]{1,0:T(8,128)}, f32[184,256]{1,0:T(8,128)}, f32[184,256]{1,0:T(8,128)}, f32[184,256]{1,0:T(8,128)}) custom-call(f32[248,384]{1,0:T(8,128)} %get-tuple-element.26.refs_0_, f32[248,384]{1,0:T(8,128)} %get-tuple-element.25.refs_1_, f32[248,384]{1,0:T(8,128)} %get-tuple-element.24.refs_2_, ...), custom_call_target="tpu_custom_call" | custom-call | tf_op jit(solution)/shard_map/ring_step/pallas_call | solution.py:369
  63.9 1.2 %pad_maximum_fusion.1 = f32[3,184,256]{2,1,0:T(8,128)S(1)} fusion(f32[1,184,256]{2,1,0:T(8,128)} %bitcast.54, f32[1,184,256]{2,1,0:T(8,128)} %bitcast.52, f32[1,184,256]{2,1,0:T(8,128)} %bitcast.50), kind=kLoop, calls=%fused_computation.29 | loop fusion | flops 282624 | bytes 1130496 | tf_op jit(solution)/shard_map/stack | solution.py:491
  67.4 5.9 %section_step.2 = (f32[112,128]{1,0:T(8,128)}, f32[112,128]{1,0:T(8,128)}, f32[112,128]{1,0:T(8,128)}, f32[112,128]{1,0:T(8,128)}, f32[112,128]{1,0:T(8,128)}) custom-call(f32[184,256]{1,0:T(8,128)} %get-tuple-element.34.refs_0_, f32[184,256]{1,0:T(8,128)} %get-tuple-element.33.refs_1_, f32[184,256]{1,0:T(8,128)} %get-tuple-element.32.refs_2_, ...), custom_call_target="tpu_custom_call" | custom-call | tf_op jit(solution)/shard_map/section_step/pallas_call | solution.py:384
  73.4 0.9 pad_maximum_fusion.2
  74.4 1.9 %collective-permute-start.4 = (f32[3,112,42]{2,1,0:T(8,128)S(1)}, f32[3,112,42]{2,1,0:T(8,128)S(1)}, u32[]{:S(2)}, u32[]{:S(2)}) collective-permute-start(f32[3,112,42]{2,1,0:T(8,128)S(1)} %get-tuple-element.39), channel_id=1, source_target_pairs={{0,16},{16,32},{32,48},{48,64},{64,80},{80,96},{96,112},{112,128},... | collective-permute-start | bytes 169352 | tf_op jit(solution)/shard_map/ppermute | solution.py:398
  76.4 8.3 %collective-permute-start.5 = (f32[3,112,42]{2,1,0:T(8,128)S(1)}, f32[3,112,42]{2,1,0:T(8,128)S(1)}, u32[]{:S(2)}, u32[]{:S(2)}) collective-permute-start(f32[3,112,42]{2,1,0:T(8,128)S(1)} %get-tuple-element.40), channel_id=1, source_target_pairs={{16,0},{32,16},{48,32},{64,48},{80,64},{96,80},{112,96},{128,112},... | collective-permute-start | bytes 169352 | tf_op jit(solution)/shard_map/ppermute | solution.py:401
  85.5 1.5 %collective-permute-done.5 = f32[3,112,42]{2,1,0:T(8,128)S(1)} collective-permute-done((f32[3,112,42]{2,1,0:T(8,128)S(1)}, f32[3,112,42]{2,1,0:T(8,128)S(1)}, u32[]{:S(2)}, u32[]{:S(2)}) %collective-permute-start.5) | collective-permute-done | bytes 56480 | tf_op jit(solution)/shard_map/ppermute | solution.py:401
  87.0 1.0 pad_maximum_fusion.7
  88.0 2.6 %collective-permute-start.6 = (f32[3,34,212]{2,1,0:T(8,128)S(1)}, f32[3,34,212]{2,1,0:T(8,128)S(1)}, u32[]{:S(2)}, u32[]{:S(2)}) collective-permute-start(f32[3,34,212]{2,1,0:T(8,128)S(1)} %get-tuple-element.36), channel_id=1, source_target_pairs={{0,1},{1,2},{2,3},{3,4},{4,5},{5,6},{6,7},{7,8},{8,9},{9,10},{10,1... | collective-permute-start | bytes 259496 | tf_op jit(solution)/shard_map/ppermute | solution.py:26
  90.7 1.9 %collective-permute-start.7 = (f32[3,34,212]{2,1,0:T(8,128)S(1)}, f32[3,34,212]{2,1,0:T(8,128)S(1)}, u32[]{:S(2)}, u32[]{:S(2)}) collective-permute-start(f32[3,34,212]{2,1,0:T(8,128)S(1)} %get-tuple-element.35), channel_id=1, source_target_pairs={{1,0},{2,1},{3,2},{4,3},{5,4},{6,5},{7,6},{8,7},{9,8},{10,9},{11,1... | collective-permute-start | bytes 259496 | tf_op jit(solution)/shard_map/ppermute | solution.py:26
  92.8 6.2 %collective-permute-done.7 = f32[3,34,212]{2,1,0:T(8,128)S(1)} collective-permute-done((f32[3,34,212]{2,1,0:T(8,128)S(1)}, f32[3,34,212]{2,1,0:T(8,128)S(1)}, u32[]{:S(2)}, u32[]{:S(2)}) %collective-permute-start.7) | collective-permute-done | bytes 86528 | tf_op jit(solution)/shard_map/ppermute | solution.py:26
  100.2 5.9 %section_step.3 = (f32[112,128]{1,0:T(8,128)}, f32[112,128]{1,0:T(8,128)}, f32[112,128]{1,0:T(8,128)}, f32[112,128]{1,0:T(8,128)}, f32[112,128]{1,0:T(8,128)}) custom-call(f32[184,256]{1,0:T(8,128)} %get-tuple-element.31.refs_0_, f32[184,256]{1,0:T(8,128)} %get-tuple-element.30.refs_1_, f32[184,256]{1,0:T(8,128)} %get-tuple-element.29.refs_2_, ...), custom_call_target="tpu_custom_call" | custom-call | tf_op jit(solution)/shard_map/section_step/pallas_call | solution.py:384
  (60 shorter events, 15.0 us)
Async XLA Ops:
  6.5 23.7 %copy-start.2 = (f32[14336]{0:T(1024)}, f32[14336]{0:T(1024)S(1)}, u32[]{:S(2)}) copy-start(f32[14336]{0:T(1024)S(1)} %scatter_custom_fusion) | copy-start | bytes 172036
  6.7 21.4 %collective-permute-start = (f32[6,112,84]{2,1,0:T(8,128)S(1)}, f32[6,112,84]{2,1,0:T(8,128)S(1)}, u32[]{:S(2)}, u32[]{:S(2)}) collective-permute-start(f32[6,112,84]{2,1,0:T(8,128)S(1)} %get-tuple-element.37), channel_id=1, source_target_pairs={{0,16},{16,32},{32,48},{48,64},{64,80},{80,96},{96,112},{112,128},... | collective-permute-start | bytes 677384 | tf_op jit(solution)/shard_map/ppermute | solution.py:398
  10.2 18.7 %collective-permute-start.1 = (f32[6,112,84]{2,1,0:T(8,128)S(1)}, f32[6,112,84]{2,1,0:T(8,128)S(1)}, u32[]{:S(2)}, u32[]{:S(2)}) collective-permute-start(f32[6,112,84]{2,1,0:T(8,128)S(1)} %get-tuple-element.38), channel_id=1, source_target_pairs={{16,0},{32,16},{48,32},{64,48},{80,64},{96,80},{112,96},{128,112},... | collective-permute-start | bytes 677384 | tf_op jit(solution)/shard_map/ppermute | solution.py:401
  28.9 0.7 copy-start
  30.2 10.9 %collective-permute-start.2 = (f32[6,68,296]{2,1,0:T(8,128)S(1)}, f32[6,68,296]{2,1,0:T(8,128)}, u32[]{:S(2)}, u32[]{:S(2)}) collective-permute-start(f32[6,68,296]{2,1,0:T(8,128)S(1)} %get-tuple-element.28), channel_id=1, source_target_pairs={{0,1},{1,2},{2,3},{3,4},{4,5},{5,6},{6,7},{7,8},{8,9},{9,10},{10,1... | collective-permute-start | bytes 1449224 | tf_op jit(solution)/shard_map/ppermute | solution.py:26
  34.4 14.2 %collective-permute-start.3 = (f32[6,68,296]{2,1,0:T(8,128)S(1)}, f32[6,68,296]{2,1,0:T(8,128)}, u32[]{:S(2)}, u32[]{:S(2)}) collective-permute-start(f32[6,68,296]{2,1,0:T(8,128)S(1)} %get-tuple-element.27), channel_id=1, source_target_pairs={{1,0},{2,1},{3,2},{4,3},{5,4},{6,5},{7,6},{8,7},{9,8},{10,9},{11,1... | collective-permute-start | bytes 1449224 | tf_op jit(solution)/shard_map/ppermute | solution.py:26
  38.4 11.3 %copy-start.1 = (f32[6,112,84]{2,1,0:T(8,128)S(1)}, f32[6,112,84]{2,1,0:T(8,128)}, u32[]{:S(2)}) copy-start(f32[6,112,84]{2,1,0:T(8,128)} %copy-done) | copy-start | bytes 677380
  63.9 1.4 %copy-start.3 = (f32[184,256]{1,0:T(8,128)S(1)}, f32[184,256]{1,0:T(8,128)}, u32[]{:S(2)}) copy-start(f32[184,256]{1,0:T(8,128)} %get-tuple-element.13) | copy-start | bytes 565252
  63.9 1.4 %copy-start.4 = (f32[184,256]{1,0:T(8,128)S(1)}, f32[184,256]{1,0:T(8,128)}, u32[]{:S(2)}) copy-start(f32[184,256]{1,0:T(8,128)} %get-tuple-element.14) | copy-start | bytes 565252
  63.9 1.4 %copy-start.5 = (f32[184,256]{1,0:T(8,128)S(1)}, f32[184,256]{1,0:T(8,128)}, u32[]{:S(2)}) copy-start(f32[184,256]{1,0:T(8,128)} %get-tuple-element.15) | copy-start | bytes 565252
  73.4 25.7 %copy-start.6 = (f32[112,128]{1,0:T(8,128)S(1)}, f32[112,128]{1,0:T(8,128)}, u32[]{:S(2)}) copy-start(f32[112,128]{1,0:T(8,128)} %get-tuple-element.18) | copy-start | bytes 172036
  73.4 25.7 %copy-start.7 = (f32[112,128]{1,0:T(8,128)S(1)}, f32[112,128]{1,0:T(8,128)}, u32[]{:S(2)}) copy-start(f32[112,128]{1,0:T(8,128)} %get-tuple-element.19) | copy-start | bytes 172036
  73.4 25.7 %copy-start.8 = (f32[112,128]{1,0:T(8,128)S(1)}, f32[112,128]{1,0:T(8,128)}, u32[]{:S(2)}) copy-start(f32[112,128]{1,0:T(8,128)} %get-tuple-element.20) | copy-start | bytes 172036
  74.4 11.1 %collective-permute-start.4 = (f32[3,112,42]{2,1,0:T(8,128)S(1)}, f32[3,112,42]{2,1,0:T(8,128)S(1)}, u32[]{:S(2)}, u32[]{:S(2)}) collective-permute-start(f32[3,112,42]{2,1,0:T(8,128)S(1)} %get-tuple-element.39), channel_id=1, source_target_pairs={{0,16},{16,32},{32,48},{48,64},{64,80},{80,96},{96,112},{112,128},... | collective-permute-start | bytes 169352 | tf_op jit(solution)/shard_map/ppermute | solution.py:398
  76.4 10.7 %collective-permute-start.5 = (f32[3,112,42]{2,1,0:T(8,128)S(1)}, f32[3,112,42]{2,1,0:T(8,128)S(1)}, u32[]{:S(2)}, u32[]{:S(2)}) collective-permute-start(f32[3,112,42]{2,1,0:T(8,128)S(1)} %get-tuple-element.40), channel_id=1, source_target_pairs={{16,0},{32,16},{48,32},{64,48},{80,64},{96,80},{112,96},{128,112},... | collective-permute-start | bytes 169352 | tf_op jit(solution)/shard_map/ppermute | solution.py:401
  88.0 4.8 %collective-permute-start.6 = (f32[3,34,212]{2,1,0:T(8,128)S(1)}, f32[3,34,212]{2,1,0:T(8,128)S(1)}, u32[]{:S(2)}, u32[]{:S(2)}) collective-permute-start(f32[3,34,212]{2,1,0:T(8,128)S(1)} %get-tuple-element.36), channel_id=1, source_target_pairs={{0,1},{1,2},{2,3},{3,4},{4,5},{5,6},{6,7},{7,8},{8,9},{9,10},{10,1... | collective-permute-start | bytes 259496 | tf_op jit(solution)/shard_map/ppermute | solution.py:26
  90.7 8.3 %collective-permute-start.7 = (f32[3,34,212]{2,1,0:T(8,128)S(1)}, f32[3,34,212]{2,1,0:T(8,128)S(1)}, u32[]{:S(2)}, u32[]{:S(2)}) collective-permute-start(f32[3,34,212]{2,1,0:T(8,128)S(1)} %get-tuple-element.35), channel_id=1, source_target_pairs={{1,0},{2,1},{3,2},{4,3},{5,4},{6,5},{7,6},{8,7},{9,8},{10,9},{11,1... | collective-permute-start | bytes 259496 | tf_op jit(solution)/shard_map/ppermute | solution.py:26

commit v9 on v8

--- a/solution.py
+++ b/solution.py
@@ -396,18 +396,22 @@
 def halo_box(fields, wide_x, wide_y, place, count, padded_shape):
     lon_count = lax.axis_size("lon")
     west = lax.ppermute(
-        fields[:, :, -wide_x:], "lon", [(i, (i + 1) % lon_count) for i in range(lon_count)]
+        jnp.stack([field[:, -wide_x:] for field in fields]), "lon",
+        [(i, (i + 1) % lon_count) for i in range(lon_count)],
     )
     east = lax.ppermute(
-        fields[:, :, :wide_x], "lon", [((i + 1) % lon_count, i) for i in range(lon_count)]
-    )
-    wide = jnp.concatenate([west, fields, east], axis=2)
-    above = passed_along(wide[:, -wide_y:], "lat", 1)
-    below = passed_along(wide[:, :wide_y], "lat", -1)
-    above = jnp.where(place == 0, wide[:, wide_y - 1 :: -1], above)
-    below = jnp.where(place == count - 1, wide[:, : -wide_y - 1 : -1], below)
-    box = jnp.concatenate([above, wide, below], axis=1)
-    return pad_to(box, padded_shape)
+        jnp.stack([field[:, :wide_x] for field in fields]), "lon",
+        [((i + 1) % lon_count, i) for i in range(lon_count)],
+    )
+    wide = [jnp.concatenate([west[k], field, east[k]], axis=1) for k, field in enumerate(fields)]
+    above = passed_along(jnp.stack([field[-wide_y:] for field in wide]), "lat", 1)
+    below = passed_along(jnp.stack([field[:wide_y] for field in wide]), "lat", -1)
+    boxes = []
+    for k, field in enumerate(wide):
+        top = jnp.where(place == 0, field[wide_y - 1 :: -1], above[k])
+        bottom = jnp.where(place == count - 1, field[: -wide_y - 1 : -1], below[k])
+        boxes.append(pad_to(jnp.concatenate([top, field, bottom], axis=0), padded_shape))
+    return boxes
 
 
 def pad_to(values, shape):
@@ -481,7 +485,7 @@
     initial = (surface, momentum_x, momentum_y)
 
     big = halo_box(
-        jnp.stack([surface, momentum_x, momentum_y, water_depth, wet_float, lift]),
+        [surface, momentum_x, momentum_y, water_depth, wet_float, lift],
         2 * wide_x, 2 * wide_y, place, count, ring.padded,
     )
     ring_state = ring_step(
@@ -492,7 +496,7 @@
     depth_box, wet_box = ring_state[3], ring_state[4]
     for first, second in ((0.75, 0.25), (1.0 / 3.0, 2.0 / 3.0)):
         if box is None:
-            box = halo_box(jnp.stack(list(current)), wide_x, wide_y, place, count, plain.padded)
+            box = halo_box(list(current), wide_x, wide_y, place, count, plain.padded)
         next_surface, next_east, next_north, velocity_u, velocity_v = section_step(
             (box[0], box[1], box[2], depth_box, wet_box), plain_keep, plain_mirror, lift, initial,
             plain.first_row, plain.box_cols, plain.offset, (first, second),

time: 107 us -> 117 us (1.093)
  local copies, waits for them, and re-layouts: 11.1 us -> 27.3 us
  waiting for transfers between devices: 24.1 us -> 17.9 us
    rev x4 -> x18, local copies, waits for them, and re-layouts: 1.44 us -> 13.5 us  [the longest x9 6.75 us: halo_box(): top = jnp.where(place == 0, field[wide_y - 1::-1], above[k])]
    concatenate x3 -> x12, other arithmetic: 1.16 us -> 6.4 us  [the longest x6 5.66 us: halo_box(): jnp.concatenate([top, field, bottom], axis=0)]
    unnamed x22 -> x54, local copies, waits for them, and re-layouts: 4.07 us -> 8.8 us
    ppermute x4, waiting for transfers between devices: 15.2 us -> 10.6 us  [passed_along(): return lax.ppermute(x, axis, pairs)]
    select_n x4, other arithmetic: 2.37 us -> 0.24 us  [the longest x2 0.13 us: halo_box(): top = jnp.where(place == 0, field[wide_y - 1::-1], above[k])]
    another operation x1 -> x5, local copies, waits for them, and re-layouts: 0.01 us -> 1.91 us  [the longest x4 1.2 us: halo_box(): jnp.stack([field[:, -wide_x:] for field in fields])]
    ppermute x4, waiting for transfers between devices: 8.96 us -> 7.26 us  [the longest x2 4.92 us: halo_box(): lax.ppermute(jnp.stack([field[:, -wide_x:] for field in fields]), 'lon',...]
    squeeze x1 -> x4, local copies, waits for them, and re-layouts: 1.43 us -> 0.07 us  [the longest x2 0.04 us: halo_box(): west[k]]
  transfers between devices with their start and end apart: 8 -> 8, of which waited for: 7 -> 6; matrix products, arithmetic and copies ran while one was open for 4% -> 13% of each run, Pallas kernels for 0% -> 0%
where the time goes in v9:
time: 117 us; the launch traced here: 116 us
  starting transfers between devices  35.6 us (30%)
  local copies, waits for them, and re-layouts  27.3 us (23%)
  Pallas kernels  23.1 us (20%)
  waiting for transfers between devices  17.9 us (15%)
  other arithmetic  11.1 us (9%)
  between operations  1.26 us (1%)
    ppermute x2, starting transfers between devices, halo_box(): lax.ppermute(jnp.stack([field[:, :wide_x] for field in fields]), 'lon', [...  20.3 us
    pallas_call x2, Pallas kernels, section_step(): pl.pallas_call(lambda *refs: section_kernel(*refs, first_row=first_row, u...  11.9 us
    pallas_call x1, Pallas kernels, ring_step(): pl.pallas_call(lambda *refs: ring_kernel(*refs, first_row=first_row, used...  11.3 us
    ppermute x4, waiting for transfers between devices, passed_along(): return lax.ppermute(x, axis, pairs)  10.6 us
    ppermute x4, starting transfers between devices, passed_along(): return lax.ppermute(x, axis, pairs)  9.85 us
    unnamed x54, local copies, waits for them, and re-layouts  8.8 us
    rev x9, local copies, waits for them, and re-layouts, halo_box(): top = jnp.where(place == 0, field[wide_y - 1::-1], above[k])  6.75 us
    rev x9, local copies, waits for them, and re-layouts, halo_box(): bottom = jnp.where(place == count - 1, field[:-wide_y - 1:-1], below[k])  6.72 us
  transfers between devices with their start and end apart: 8, of which 6 were waited for; matrix products, arithmetic and copies ran while one was open for 13% of the time, Pallas kernels for 0%

profile of v9, /device:TPU:25, one launch (start us, length us, event | category | flops | bytes accessed | tf_op | source)
XLA Modules:
  0.0 116.3 jit_solution(3466231135958490699)
XLA Ops:
  5.4 3.5 %collective-permute-start = (f32[6,112,84]{2,1,0:T(8,128)S(1)}, f32[6,112,84]{2,1,0:T(8,128)S(1)}, u32[]{:S(2)}, u32[]{:S(2)}) collective-permute-start(f32[6,112,84]{2,1,0:T(8,128)S(1)} %get-tuple-element.96), channel_id=1, source_target_pairs={{0,16},{16,32},{32,48},{48,64},{64,80},{80,96},{96,112},{112,128},... | collective-permute-start | bytes 677384 | tf_op jit(solution)/shard_map/ppermute | solution.py:398
  9.0 12.0 %collective-permute-start.1 = (f32[6,112,84]{2,1,0:T(8,128)S(1)}, f32[6,112,84]{2,1,0:T(8,128)S(1)}, u32[]{:S(2)}, u32[]{:S(2)}) collective-permute-start(f32[6,112,84]{2,1,0:T(8,128)S(1)} %get-tuple-element.97), channel_id=1, source_target_pairs={{16,0},{32,16},{48,32},{64,48},{80,64},{96,80},{112,96},{128,112},... | collective-permute-start | bytes 677384 | tf_op jit(solution)/shard_map/ppermute | solution.py:402
  22.7 4.1 %collective-permute-done = f32[6,112,84]{2,1,0:T(8,128)S(1)} collective-permute-done((f32[6,112,84]{2,1,0:T(8,128)S(1)}, f32[6,112,84]{2,1,0:T(8,128)S(1)}, u32[]{:S(2)}, u32[]{:S(2)}) %collective-permute-start) | collective-permute-done | bytes 225824 | tf_op jit(solution)/shard_map/ppermute | solution.py:398
  32.7 3.3 %collective-permute-start.2 = (f32[6,68,296]{2,1,0:T(8,128)}, f32[6,68,296]{2,1,0:T(8,128)S(1)}, u32[]{:S(2)}, u32[]{:S(2)}) collective-permute-start(f32[6,68,296]{2,1,0:T(8,128)} %get-tuple-element.70), channel_id=1, source_target_pairs={{0,1},{1,2},{2,3},{3,4},{4,5},{5,6},{6,7},{7,8},{8,9},{9,10},{10,1... | collective-permute-start | bytes 1449224 | tf_op jit(solution)/shard_map/ppermute | solution.py:26
  36.2 1.3 %rev.68 = f32[68,296]{1,0:T(8,128)} reverse(f32[68,296]{1,0:T(8,128)S(1)} %get-tuple-element.62), dimensions={0} | reverse | bytes 161024 | tf_op jit(solution)/shard_map/rev | solution.py:411
  38.7 1.3 %rev.64 = f32[68,296]{1,0:T(8,128)} reverse(f32[68,296]{1,0:T(8,128)S(1)} %get-tuple-element.66), dimensions={0} | reverse | bytes 161024 | tf_op jit(solution)/shard_map/rev | solution.py:411
  40.0 1.3 %rev.62 = f32[68,296]{1,0:T(8,128)} reverse(f32[68,296]{1,0:T(8,128)S(1)} %get-tuple-element.68), dimensions={0} | reverse | bytes 161024 | tf_op jit(solution)/shard_map/rev | solution.py:411
  41.3 2.1 %collective-permute-start.3 = (f32[6,68,296]{2,1,0:T(8,128)}, f32[6,68,296]{2,1,0:T(8,128)S(1)}, u32[]{:S(2)}, u32[]{:S(2)}) collective-permute-start(f32[6,68,296]{2,1,0:T(8,128)} %get-tuple-element.71), channel_id=1, source_target_pairs={{1,0},{2,1},{3,2},{4,3},{5,4},{6,5},{7,6},{8,7},{9,8},{10,9},{11,1... | collective-permute-start | bytes 1449224 | tf_op jit(solution)/shard_map/ppermute | solution.py:26
  43.4 1.3 %rev.60 = f32[68,296]{1,0:T(8,128)} reverse(f32[68,296]{1,0:T(8,128)S(1)} %get-tuple-element.82), dimensions={0} | reverse | bytes 161024 | tf_op jit(solution)/shard_map/rev | solution.py:411
  44.8 1.3 %rev.69 = f32[68,296]{1,0:T(8,128)} reverse(f32[68,296]{1,0:T(8,128)S(1)} %get-tuple-element.63), dimensions={0} | reverse | bytes 161024 | tf_op jit(solution)/shard_map/rev | solution.py:412
  46.0 1.3 %rev.67 = f32[68,296]{1,0:T(8,128)} reverse(f32[68,296]{1,0:T(8,128)S(1)} %get-tuple-element.65), dimensions={0} | reverse | bytes 161024 | tf_op jit(solution)/shard_map/rev | solution.py:412
  47.3 1.3 %rev.65 = f32[68,296]{1,0:T(8,128)} reverse(f32[68,296]{1,0:T(8,128)S(1)} %get-tuple-element.67), dimensions={0} | reverse | bytes 161024 | tf_op jit(solution)/shard_map/rev | solution.py:412
  48.6 1.3 %rev.63 = f32[68,296]{1,0:T(8,128)} reverse(f32[68,296]{1,0:T(8,128)S(1)} %get-tuple-element.69), dimensions={0} | reverse | bytes 161024 | tf_op jit(solution)/shard_map/rev | solution.py:412
  49.8 1.3 %rev.61 = f32[68,296]{1,0:T(8,128)} reverse(f32[68,296]{1,0:T(8,128)S(1)} %get-tuple-element.83), dimensions={0} | reverse | bytes 161024 | tf_op jit(solution)/shard_map/rev | solution.py:412
  51.3 4.3 %collective-permute-done.3 = f32[6,68,296]{2,1,0:T(8,128)S(1)} collective-permute-done((f32[6,68,296]{2,1,0:T(8,128)}, f32[6,68,296]{2,1,0:T(8,128)S(1)}, u32[]{:S(2)}, u32[]{:S(2)}) %collective-permute-start.3) | collective-permute-done | bytes 483104 | tf_op jit(solution)/shard_map/ppermute | solution.py:26
  59.9 11.3 %ring_step.1 = (f32[184,256]{1,0:T(8,128)}, f32[184,256]{1,0:T(8,128)}, f32[184,256]{1,0:T(8,128)}, f32[184,256]{1,0:T(8,128)}, f32[184,256]{1,0:T(8,128)}) custom-call(f32[248,384]{1,0:T(8,128)} %get-tuple-element.113.refs_0_, f32[248,384]{1,0:T(8,128)} %get-tuple-element.112.refs_1_, f32[248,384]{1,0:T(8,128)} %get-tuple-element.111.refs_2_, ...), custom_call_target="tpu_custom_call" | custom-call | tf_op jit(solution)/shard_map/ring_step/pallas_call | solution.py:369
  75.6 5.9 %section_step.2 = (f32[112,128]{1,0:T(8,128)}, f32[112,128]{1,0:T(8,128)}, f32[112,128]{1,0:T(8,128)}, f32[112,128]{1,0:T(8,128)}, f32[112,128]{1,0:T(8,128)}) custom-call(f32[184,256]{1,0:T(8,128)} %get-tuple-element.35.refs_0_, f32[184,256]{1,0:T(8,128)} %get-tuple-element.34.refs_1_, f32[184,256]{1,0:T(8,128)} %get-tuple-element.33.refs_2_, ...), custom_call_target="tpu_custom_call" | custom-call | tf_op jit(solution)/shard_map/section_step/pallas_call | solution.py:384
  83.4 1.9 %collective-permute-start.4 = (f32[3,112,42]{2,1,0:T(8,128)S(1)}, f32[3,112,42]{2,1,0:T(8,128)S(1)}, u32[]{:S(2)}, u32[]{:S(2)}) collective-permute-start(f32[3,112,42]{2,1,0:T(8,128)S(1)} %pad_maximum_fusion.7), channel_id=1, source_target_pairs={{0,16},{16,32},{32,48},{48,64},{64,80},{80,96},{96,112},{112,128},... | collective-permute-start | bytes 169352 | tf_op jit(solution)/shard_map/ppermute | solution.py:398
  85.4 8.3 %collective-permute-start.5 = (f32[3,112,42]{2,1,0:T(8,128)S(1)}, f32[3,112,42]{2,1,0:T(8,128)S(1)}, u32[]{:S(2)}, u32[]{:S(2)}) collective-permute-start(f32[3,112,42]{2,1,0:T(8,128)S(1)} %pad_maximum_fusion.8), channel_id=1, source_target_pairs={{16,0},{32,16},{48,32},{64,48},{80,64},{96,80},{112,96},{128,112},... | collective-permute-start | bytes 169352 | tf_op jit(solution)/shard_map/ppermute | solution.py:402
  94.6 1.5 %collective-permute-done.5 = f32[3,112,42]{2,1,0:T(8,128)S(1)} collective-permute-done((f32[3,112,42]{2,1,0:T(8,128)S(1)}, f32[3,112,42]{2,1,0:T(8,128)S(1)}, u32[]{:S(2)}, u32[]{:S(2)}) %collective-permute-start.5) | collective-permute-done | bytes 56480 | tf_op jit(solution)/shard_map/ppermute | solution.py:402
  96.8 2.6 %collective-permute-start.6 = (f32[3,34,212]{2,1,0:T(8,128)S(1)}, f32[3,34,212]{2,1,0:T(8,128)S(1)}, u32[]{:S(2)}, u32[]{:S(2)}) collective-permute-start(f32[3,34,212]{2,1,0:T(8,128)S(1)} %pad_maximum_fusion.9), channel_id=1, source_target_pairs={{0,1},{1,2},{2,3},{3,4},{4,5},{5,6},{6,7},{7,8},{8,9},{9,10},{10,1... | collective-permute-start | bytes 259496 | tf_op jit(solution)/shard_map/ppermute | solution.py:26
  99.7 1.9 %collective-permute-start.7 = (f32[3,34,212]{2,1,0:T(8,128)S(1)}, f32[3,34,212]{2,1,0:T(8,128)S(1)}, u32[]{:S(2)}, u32[]{:S(2)}) collective-permute-start(f32[3,34,212]{2,1,0:T(8,128)S(1)} %pad_maximum_fusion.10), channel_id=1, source_target_pairs={{1,0},{2,1},{3,2},{4,3},{5,4},{6,5},{7,6},{8,7},{9,8},{10,9},{11,1... | collective-permute-start | bytes 259496 | tf_op jit(solution)/shard_map/ppermute | solution.py:26
  101.6 6.3 %collective-permute-done.7 = f32[3,34,212]{2,1,0:T(8,128)S(1)} collective-permute-done((f32[3,34,212]{2,1,0:T(8,128)S(1)}, f32[3,34,212]{2,1,0:T(8,128)S(1)}, u32[]{:S(2)}, u32[]{:S(2)}) %collective-permute-start.7) | collective-permute-done | bytes 86528 | tf_op jit(solution)/shard_map/ppermute | solution.py:26
  110.4 5.9 %section_step.3 = (f32[112,128]{1,0:T(8,128)}, f32[112,128]{1,0:T(8,128)}, f32[112,128]{1,0:T(8,128)}, f32[112,128]{1,0:T(8,128)}, f32[112,128]{1,0:T(8,128)}) custom-call(f32[184,256]{1,0:T(8,128)} %select_maximum_fusion.30.refs_0_, f32[184,256]{1,0:T(8,128)} %select_maximum_fusion.26.refs_1_, f32[184,256]{1,0:T(8,128)} %select_maximum_fusion.22.refs_2_, ...), custom_call_target="tpu_custom_call" | custom-call | tf_op jit(solution)/shard_map/section_step/pallas_call | solution.py:384
  (129 shorter events, 28.6 us)
Async XLA Ops:
  0.6 1.0 copy-start.20
  5.3 50.4 %copy-start = (f32[14336]{0:T(1024)}, f32[14336]{0:T(1024)S(1)}, u32[]{:S(2)}) copy-start(f32[14336]{0:T(1024)S(1)} %scatter_custom_fusion) | copy-start | bytes 172036
  5.4 21.4 %collective-permute-start = (f32[6,112,84]{2,1,0:T(8,128)S(1)}, f32[6,112,84]{2,1,0:T(8,128)S(1)}, u32[]{:S(2)}, u32[]{:S(2)}) collective-permute-start(f32[6,112,84]{2,1,0:T(8,128)S(1)} %get-tuple-element.96), channel_id=1, source_target_pairs={{0,16},{16,32},{32,48},{48,64},{64,80},{80,96},{96,112},{112,128},... | collective-permute-start | bytes 677384 | tf_op jit(solution)/shard_map/ppermute | solution.py:398
  9.0 18.7 %collective-permute-start.1 = (f32[6,112,84]{2,1,0:T(8,128)S(1)}, f32[6,112,84]{2,1,0:T(8,128)S(1)}, u32[]{:S(2)}, u32[]{:S(2)}) collective-permute-start(f32[6,112,84]{2,1,0:T(8,128)S(1)} %get-tuple-element.97), channel_id=1, source_target_pairs={{16,0},{32,16},{48,32},{64,48},{80,64},{96,80},{112,96},{128,112},... | collective-permute-start | bytes 677384 | tf_op jit(solution)/shard_map/ppermute | solution.py:402
  32.7 18.4 %collective-permute-start.2 = (f32[6,68,296]{2,1,0:T(8,128)}, f32[6,68,296]{2,1,0:T(8,128)S(1)}, u32[]{:S(2)}, u32[]{:S(2)}) collective-permute-start(f32[6,68,296]{2,1,0:T(8,128)} %get-tuple-element.70), channel_id=1, source_target_pairs={{0,1},{1,2},{2,3},{3,4},{4,5},{5,6},{6,7},{7,8},{8,9},{9,10},{10,1... | collective-permute-start | bytes 1449224 | tf_op jit(solution)/shard_map/ppermute | solution.py:26
  41.3 14.3 %collective-permute-start.3 = (f32[6,68,296]{2,1,0:T(8,128)}, f32[6,68,296]{2,1,0:T(8,128)S(1)}, u32[]{:S(2)}, u32[]{:S(2)}) collective-permute-start(f32[6,68,296]{2,1,0:T(8,128)} %get-tuple-element.71), channel_id=1, source_target_pairs={{1,0},{2,1},{3,2},{4,3},{5,4},{6,5},{7,6},{8,7},{9,8},{10,9},{11,1... | collective-permute-start | bytes 1449224 | tf_op jit(solution)/shard_map/ppermute | solution.py:26
  48.6 2.6 %copy-start.13 = (f32[68,296]{1,0:T(8,128)S(1)}, f32[68,296]{1,0:T(8,128)}, u32[]{:S(2)}) copy-start(f32[68,296]{1,0:T(8,128)} %rev.64) | copy-start | bytes 241540
  48.6 2.6 %copy-start.14 = (f32[68,296]{1,0:T(8,128)S(1)}, f32[68,296]{1,0:T(8,128)}, u32[]{:S(2)}) copy-start(f32[68,296]{1,0:T(8,128)} %rev.62) | copy-start | bytes 241540
  49.8 1.3 %copy-start.11 = (f32[68,296]{1,0:T(8,128)S(1)}, f32[68,296]{1,0:T(8,128)}, u32[]{:S(2)}) copy-start(f32[68,296]{1,0:T(8,128)} %rev.68) | copy-start | bytes 241540
  49.8 1.3 %copy-start.12 = (f32[68,296]{1,0:T(8,128)S(1)}, f32[68,296]{1,0:T(8,128)}, u32[]{:S(2)}) copy-start(f32[68,296]{1,0:T(8,128)} %rev.66) | copy-start | bytes 241540
  51.1 4.5 %copy-start.15 = (f32[68,296]{1,0:T(8,128)S(1)}, f32[68,296]{1,0:T(8,128)}, u32[]{:S(2)}) copy-start(f32[68,296]{1,0:T(8,128)} %rev.69) | copy-start | bytes 241540
  51.1 4.5 %copy-start.16 = (f32[68,296]{1,0:T(8,128)S(1)}, f32[68,296]{1,0:T(8,128)}, u32[]{:S(2)}) copy-start(f32[68,296]{1,0:T(8,128)} %rev.67) | copy-start | bytes 241540
  51.1 4.5 %copy-start.17 = (f32[68,296]{1,0:T(8,128)S(1)}, f32[68,296]{1,0:T(8,128)}, u32[]{:S(2)}) copy-start(f32[68,296]{1,0:T(8,128)} %rev.65) | copy-start | bytes 241540
  51.1 4.5 %copy-start.18 = (f32[68,296]{1,0:T(8,128)S(1)}, f32[68,296]{1,0:T(8,128)}, u32[]{:S(2)}) copy-start(f32[68,296]{1,0:T(8,128)} %rev.63) | copy-start | bytes 241540
  51.1 4.5 %copy-start.19 = (f32[68,296]{1,0:T(8,128)S(1)}, f32[68,296]{1,0:T(8,128)}, u32[]{:S(2)}) copy-start(f32[68,296]{1,0:T(8,128)} %rev.61) | copy-start | bytes 241540
  72.3 0.9 copy-start.10
  72.3 1.0 copy-start.8
  72.4 1.1 copy-start.9
  81.5 1.0 copy-start.5
  83.4 11.1 %collective-permute-start.4 = (f32[3,112,42]{2,1,0:T(8,128)S(1)}, f32[3,112,42]{2,1,0:T(8,128)S(1)}, u32[]{:S(2)}, u32[]{:S(2)}) collective-permute-start(f32[3,112,42]{2,1,0:T(8,128)S(1)} %pad_maximum_fusion.7), channel_id=1, source_target_pairs={{0,16},{16,32},{32,48},{48,64},{64,80},{80,96},{96,112},{112,128},... | collective-permute-start | bytes 169352 | tf_op jit(solution)/shard_map/ppermute | solution.py:398
  85.4 10.7 %collective-permute-start.5 = (f32[3,112,42]{2,1,0:T(8,128)S(1)}, f32[3,112,42]{2,1,0:T(8,128)S(1)}, u32[]{:S(2)}, u32[]{:S(2)}) collective-permute-start(f32[3,112,42]{2,1,0:T(8,128)S(1)} %pad_maximum_fusion.8), channel_id=1, source_target_pairs={{16,0},{32,16},{48,32},{64,48},{80,64},{96,80},{112,96},{128,112},... | collective-permute-start | bytes 169352 | tf_op jit(solution)/shard_map/ppermute | solution.py:402
  94.6 1.5 %copy-start.4 = (f32[112,128]{1,0:T(8,128)S(1)}, f32[112,128]{1,0:T(8,128)}, u32[]{:S(2)}) copy-start(f32[112,128]{1,0:T(8,128)} %get-tuple-element.18) | copy-start | bytes 172036
  96.8 4.8 %collective-permute-start.6 = (f32[3,34,212]{2,1,0:T(8,128)S(1)}, f32[3,34,212]{2,1,0:T(8,128)S(1)}, u32[]{:S(2)}, u32[]{:S(2)}) collective-permute-start(f32[3,34,212]{2,1,0:T(8,128)S(1)} %pad_maximum_fusion.9), channel_id=1, source_target_pairs={{0,1},{1,2},{2,3},{3,4},{4,5},{5,6},{6,7},{7,8},{8,9},{9,10},{10,1... | collective-permute-start | bytes 259496 | tf_op jit(solution)/shard_map/ppermute | solution.py:26
  99.7 8.3 %collective-permute-start.7 = (f32[3,34,212]{2,1,0:T(8,128)S(1)}, f32[3,34,212]{2,1,0:T(8,128)S(1)}, u32[]{:S(2)}, u32[]{:S(2)}) collective-permute-start(f32[3,34,212]{2,1,0:T(8,128)S(1)} %pad_maximum_fusion.10), channel_id=1, source_target_pairs={{1,0},{2,1},{3,2},{4,3},{5,4},{6,5},{7,6},{8,7},{9,8},{10,9},{11,1... | collective-permute-start | bytes 259496 | tf_op jit(solution)/shard_map/ppermute | solution.py:26
  (6 other events, 4.8 us)

commit v10 on v8

--- a/solution.py
+++ b/solution.py
@@ -404,8 +404,14 @@
     wide = jnp.concatenate([west, fields, east], axis=2)
     above = passed_along(wide[:, -wide_y:], "lat", 1)
     below = passed_along(wide[:, :wide_y], "lat", -1)
-    above = jnp.where(place == 0, wide[:, wide_y - 1 :: -1], above)
-    below = jnp.where(place == count - 1, wide[:, : -wide_y - 1 : -1], below)
+    above = jnp.where(
+        place == 0, jnp.concatenate([above[:, :-2], wide[:, 1:2], wide[:, 0:1]], axis=1), above
+    )
+    below = jnp.where(
+        place == count - 1,
+        jnp.concatenate([wide[:, -1:], wide[:, -2:-1], below[:, 2:]], axis=1),
+        below,
+    )
     box = jnp.concatenate([above, wide, below], axis=1)
     return pad_to(box, padded_shape)
 
@@ -418,13 +424,22 @@
 
 
 def wall_mirrored(values, halo, place, count, rows):
-    top = jnp.concatenate([values[..., 2 * halo - 1 : halo - 1 : -1, :], values[..., halo:, :]], axis=-2)
+    top = jnp.concatenate(
+        [
+            values[..., : halo - 2, :],
+            values[..., halo + 1 : halo + 2, :],
+            values[..., halo : halo + 1, :],
+            values[..., halo:, :],
+        ],
+        axis=-2,
+    )
     values = jnp.where(place == 0, top, values)
     bottom = jnp.concatenate(
         [
             values[..., : rows - halo, :],
-            values[..., rows - halo - 1 : rows - 2 * halo - 1 : -1, :],
-            values[..., rows:, :],
+            values[..., rows - halo - 1 : rows - halo, :],
+            values[..., rows - halo - 2 : rows - halo - 1, :],
+            values[..., rows - halo + 2 :, :],
         ],
         axis=-2,
     )

time: 107 us -> 109 us (1.019)
  starting transfers between devices: 35.7 us -> 40.4 us
  other arithmetic: 11.1 us -> 9.25 us
  local copies, waits for them, and re-layouts: 11.1 us -> 9.52 us
    ppermute x4, starting transfers between devices: 9.9 us -> 15.2 us  [passed_along(): return lax.ppermute(x, axis, pairs)]
    select_n x4 -> x3, other arithmetic: 2.37 us -> 0.47 us  [the longest x2 0.36 us: halo_box(): jnp.where(place == 0, jnp.concatenate([above[:, :-2], wide[:, 1:2], wide[...]
    ppermute x2, waiting for transfers between devices: 6.62 us -> 8.48 us  [halo_box(): lax.ppermute(fields[:, :, -wide_x:], 'lon', [(i, (i + 1) % lon_count) for...]
    rev x6 -> x0, local copies, waits for them, and re-layouts: 1.84 us -> none  [the longest x2 0.74 us: halo_box(): below = jnp.where(place == count - 1, wide[:, :-wide_y - 1:-1], below)]
    unnamed x22 -> x18, local copies, waits for them, and re-layouts: 4.07 us -> 3.38 us
  transfers between devices with their start and end apart: 8 -> 8, of which waited for: 7 -> 8; matrix products, arithmetic and copies ran while one was open for 4% -> 2% of each run, Pallas kernels for 0% -> 0%
where the time goes in v10:
time: 109 us; the launch traced here: 108 us
  starting transfers between devices  40.4 us (37%)
  waiting for transfers between devices  25 us (23%)
  Pallas kernels  23.3 us (21%)
  local copies, waits for them, and re-layouts  9.52 us (9%)
  other arithmetic  9.25 us (8%)
    ppermute x2, starting transfers between devices, halo_box(): lax.ppermute(fields[:, :, :wide_x], 'lon', [((i + 1) % lon_count, i) for...  19.7 us
    ppermute x4, starting transfers between devices, passed_along(): return lax.ppermute(x, axis, pairs)  15.2 us
    ppermute x4, waiting for transfers between devices, passed_along(): return lax.ppermute(x, axis, pairs)  14.8 us
    pallas_call x2, Pallas kernels, section_step(): pl.pallas_call(lambda *refs: section_kernel(*refs, first_row=first_row, u...  12 us
    pallas_call x1, Pallas kernels, ring_step(): pl.pallas_call(lambda *refs: ring_kernel(*refs, first_row=first_row, used...  11.3 us
    ppermute x2, waiting for transfers between devices, halo_box(): lax.ppermute(fields[:, :, -wide_x:], 'lon', [(i, (i + 1) % lon_count) for...  8.48 us
    ppermute x2, starting transfers between devices, halo_box(): lax.ppermute(fields[:, :, -wide_x:], 'lon', [(i, (i + 1) % lon_count) for...  5.46 us
    unnamed x18, local copies, waits for them, and re-layouts  3.38 us
  transfers between devices with their start and end apart: 8, of which 8 were waited for; matrix products, arithmetic and copies ran while one was open for 2% of the time, Pallas kernels for 0%

profile of v10, /device:TPU:25, one launch (start us, length us, event | category | flops | bytes accessed | tf_op | source)
XLA Modules:
  0.0 108.4 jit_solution(7757678051682608122)
XLA Ops:
  5.4 1.1 scatter_custom_fusion
  6.7 3.5 %collective-permute-start = (f32[6,112,84]{2,1,0:T(8,128)S(1)}, f32[6,112,84]{2,1,0:T(8,128)S(1)}, u32[]{:S(2)}, u32[]{:S(2)}) collective-permute-start(f32[6,112,84]{2,1,0:T(8,128)S(1)} %get-tuple-element.43), channel_id=1, source_target_pairs={{0,16},{16,32},{32,48},{48,64},{64,80},{80,96},{96,112},{112,128},... | collective-permute-start | bytes 677384 | tf_op jit(solution)/shard_map/ppermute | solution.py:398
  10.2 12.0 %collective-permute-start.1 = (f32[6,112,84]{2,1,0:T(8,128)S(1)}, f32[6,112,84]{2,1,0:T(8,128)S(1)}, u32[]{:S(2)}, u32[]{:S(2)}) collective-permute-start(f32[6,112,84]{2,1,0:T(8,128)S(1)} %get-tuple-element.44), channel_id=1, source_target_pairs={{16,0},{32,16},{48,32},{64,48},{80,64},{96,80},{112,96},{128,112},... | collective-permute-start | bytes 677384 | tf_op jit(solution)/shard_map/ppermute | solution.py:401
  22.2 5.8 %collective-permute-done = f32[6,112,84]{2,1,0:T(8,128)S(1)} collective-permute-done((f32[6,112,84]{2,1,0:T(8,128)S(1)}, f32[6,112,84]{2,1,0:T(8,128)S(1)}, u32[]{:S(2)}, u32[]{:S(2)}) %collective-permute-start) | collective-permute-done | bytes 225824 | tf_op jit(solution)/shard_map/ppermute | solution.py:398
  29.3 0.9 fusion.55
  30.3 3.4 %collective-permute-start.3 = (f32[6,68,296]{2,1,0:T(8,128)}, f32[6,68,296]{2,1,0:T(8,128)S(1)}, u32[]{:S(2)}, u32[]{:S(2)}) collective-permute-start(f32[6,68,296]{2,1,0:T(8,128)} %get-tuple-element.30), channel_id=1, source_target_pairs={{1,0},{2,1},{3,2},{4,3},{5,4},{6,5},{7,6},{8,7},{9,8},{10,9},{11,1... | collective-permute-start | bytes 1449224 | tf_op jit(solution)/shard_map/ppermute | solution.py:26
  33.7 4.2 %collective-permute-start.2 = (f32[6,68,296]{2,1,0:T(8,128)S(1)}, f32[6,68,296]{2,1,0:T(8,128)S(1)}, u32[]{:S(2)}, u32[]{:S(2)}) collective-permute-start(f32[6,68,296]{2,1,0:T(8,128)S(1)} %get-tuple-element.29), channel_id=1, source_target_pairs={{0,1},{1,2},{2,3},{3,4},{4,5},{5,6},{6,7},{7,8},{8,9},{9,10},{10,1... | collective-permute-start | bytes 1449224 | tf_op jit(solution)/shard_map/ppermute | solution.py:26
  38.7 0.9 select_select_fusion.refs_6_
  39.6 4.9 %collective-permute-done.3 = f32[6,68,296]{2,1,0:T(8,128)S(1)} collective-permute-done((f32[6,68,296]{2,1,0:T(8,128)}, f32[6,68,296]{2,1,0:T(8,128)S(1)}, u32[]{:S(2)}, u32[]{:S(2)}) %collective-permute-start.3) | collective-permute-done | bytes 483104 | tf_op jit(solution)/shard_map/ppermute | solution.py:26
  44.6 0.9 collective-permute-done.2
  46.3 1.4 %slice_bitcast_fusion = (f32[248,384]{1,0:T(8,128)}, f32[248,384]{1,0:T(8,128)}, f32[248,384]{1,0:T(8,128)}, f32[248,384]{1,0:T(8,128)}, f32[248,384]{1,0:T(8,128)}, /*index=5*/f32[248,384]{1,0:T(8,128)}) fusion(f32[6,248,384]{2,1,0:T(8,128)S(1)} %select_maximum_fusion), kind=kLoop, calls=%fused_computation.52 | loop fusion | bytes 4571136 | tf_op jit(solution)/shard_map/squeeze | solution.py:503
  48.6 11.3 %ring_step.1 = (f32[184,256]{1,0:T(8,128)}, f32[184,256]{1,0:T(8,128)}, f32[184,256]{1,0:T(8,128)}, f32[184,256]{1,0:T(8,128)}, f32[184,256]{1,0:T(8,128)}) custom-call(f32[248,384]{1,0:T(8,128)} %get-tuple-element.26.refs_0_, f32[248,384]{1,0:T(8,128)} %get-tuple-element.25.refs_1_, f32[248,384]{1,0:T(8,128)} %get-tuple-element.24.refs_2_, ...), custom_call_target="tpu_custom_call" | custom-call | tf_op jit(solution)/shard_map/ring_step/pallas_call | solution.py:369
  59.9 1.2 %pad_maximum_fusion.5 = f32[3,184,256]{2,1,0:T(8,128)S(1)} fusion(f32[1,184,256]{2,1,0:T(8,128)} %bitcast.71, f32[1,184,256]{2,1,0:T(8,128)} %bitcast.69, f32[1,184,256]{2,1,0:T(8,128)} %bitcast.67), kind=kLoop, calls=%fused_computation.49 | loop fusion | flops 282624 | bytes 1130496 | tf_op jit(solution)/shard_map/stack | solution.py:506
  63.1 6.1 %section_step.2 = (f32[112,128]{1,0:T(8,128)}, f32[112,128]{1,0:T(8,128)}, f32[112,128]{1,0:T(8,128)}, f32[112,128]{1,0:T(8,128)}, f32[112,128]{1,0:T(8,128)}) custom-call(f32[184,256]{1,0:T(8,128)} %get-tuple-element.36.refs_0_, f32[184,256]{1,0:T(8,128)} %get-tuple-element.35.refs_1_, f32[184,256]{1,0:T(8,128)} %get-tuple-element.34.refs_2_, ...), custom_call_target="tpu_custom_call" | custom-call | tf_op jit(solution)/shard_map/section_step/pallas_call | solution.py:384
  69.2 0.9 pad_maximum_fusion.7
  70.3 1.9 %collective-permute-start.4 = (f32[3,112,42]{2,1,0:T(8,128)S(1)}, f32[3,112,42]{2,1,0:T(8,128)S(1)}, u32[]{:S(2)}, u32[]{:S(2)}) collective-permute-start(f32[3,112,42]{2,1,0:T(8,128)S(1)} %get-tuple-element.45), channel_id=1, source_target_pairs={{0,16},{16,32},{32,48},{48,64},{64,80},{80,96},{96,112},{112,128},... | collective-permute-start | bytes 169352 | tf_op jit(solution)/shard_map/ppermute | solution.py:398
  72.2 7.7 %collective-permute-start.5 = (f32[3,112,42]{2,1,0:T(8,128)S(1)}, f32[3,112,42]{2,1,0:T(8,128)S(1)}, u32[]{:S(2)}, u32[]{:S(2)}) collective-permute-start(f32[3,112,42]{2,1,0:T(8,128)S(1)} %get-tuple-element.46), channel_id=1, source_target_pairs={{16,0},{32,16},{48,32},{64,48},{80,64},{96,80},{112,96},{128,112},... | collective-permute-start | bytes 169352 | tf_op jit(solution)/shard_map/ppermute | solution.py:401
  79.9 2.7 %collective-permute-done.4 = f32[3,112,42]{2,1,0:T(8,128)S(1)} collective-permute-done((f32[3,112,42]{2,1,0:T(8,128)S(1)}, f32[3,112,42]{2,1,0:T(8,128)S(1)}, u32[]{:S(2)}, u32[]{:S(2)}) %collective-permute-start.4) | collective-permute-done | bytes 56480 | tf_op jit(solution)/shard_map/ppermute | solution.py:398
  83.5 1.1 pad_maximum_fusion.6
  84.6 5.6 %collective-permute-start.6 = (f32[3,34,212]{2,1,0:T(8,128)S(1)}, f32[3,34,212]{2,1,0:T(8,128)S(1)}, u32[]{:S(2)}, u32[]{:S(2)}) collective-permute-start(f32[3,34,212]{2,1,0:T(8,128)S(1)} %slice.185), channel_id=1, source_target_pairs={{0,1},{1,2},{2,3},{3,4},{4,5},{5,6},{6,7},{7,8},{8,9},{9,10},{10,1... | collective-permute-start | bytes 259496 | tf_op jit(solution)/shard_map/ppermute | solution.py:26
  90.3 1.8 %collective-permute-done.6 = f32[3,34,212]{2,1,0:T(8,128)S(1)} collective-permute-done((f32[3,34,212]{2,1,0:T(8,128)S(1)}, f32[3,34,212]{2,1,0:T(8,128)S(1)}, u32[]{:S(2)}, u32[]{:S(2)}) %collective-permute-start.6) | collective-permute-done | bytes 86528 | tf_op jit(solution)/shard_map/ppermute | solution.py:26
  92.3 1.9 %collective-permute-start.7 = (f32[3,34,212]{2,1,0:T(8,128)S(1)}, f32[3,34,212]{2,1,0:T(8,128)S(1)}, u32[]{:S(2)}, u32[]{:S(2)}) collective-permute-start(f32[3,34,212]{2,1,0:T(8,128)S(1)} %get-tuple-element.42), channel_id=1, source_target_pairs={{1,0},{2,1},{3,2},{4,3},{5,4},{6,5},{7,6},{8,7},{9,8},{10,9},{11,1... | collective-permute-start | bytes 259496 | tf_op jit(solution)/shard_map/ppermute | solution.py:26
  94.2 7.1 %collective-permute-done.7 = f32[3,34,212]{2,1,0:T(8,128)S(1)} collective-permute-done((f32[3,34,212]{2,1,0:T(8,128)S(1)}, f32[3,34,212]{2,1,0:T(8,128)S(1)}, u32[]{:S(2)}, u32[]{:S(2)}) %collective-permute-start.7) | collective-permute-done | bytes 86528 | tf_op jit(solution)/shard_map/ppermute | solution.py:26
  102.5 5.9 %section_step.3 = (f32[112,128]{1,0:T(8,128)}, f32[112,128]{1,0:T(8,128)}, f32[112,128]{1,0:T(8,128)}, f32[112,128]{1,0:T(8,128)}, f32[112,128]{1,0:T(8,128)}) custom-call(f32[184,256]{1,0:T(8,128)} %get-tuple-element.33.refs_0_, f32[184,256]{1,0:T(8,128)} %get-tuple-element.32.refs_1_, f32[184,256]{1,0:T(8,128)} %get-tuple-element.31.refs_2_, ...), custom_call_target="tpu_custom_call" | custom-call | tf_op jit(solution)/shard_map/section_step/pallas_call | solution.py:384
  (54 shorter events, 13.0 us)
Async XLA Ops:
  6.5 23.8 %copy-start.3 = (f32[14336]{0:T(1024)}, f32[14336]{0:T(1024)S(1)}, u32[]{:S(2)}) copy-start(f32[14336]{0:T(1024)S(1)} %scatter_custom_fusion) | copy-start | bytes 172036
  6.7 21.4 %collective-permute-start = (f32[6,112,84]{2,1,0:T(8,128)S(1)}, f32[6,112,84]{2,1,0:T(8,128)S(1)}, u32[]{:S(2)}, u32[]{:S(2)}) collective-permute-start(f32[6,112,84]{2,1,0:T(8,128)S(1)} %get-tuple-element.43), channel_id=1, source_target_pairs={{0,16},{16,32},{32,48},{48,64},{64,80},{80,96},{96,112},{112,128},... | collective-permute-start | bytes 677384 | tf_op jit(solution)/shard_map/ppermute | solution.py:398
  10.2 18.7 %collective-permute-start.1 = (f32[6,112,84]{2,1,0:T(8,128)S(1)}, f32[6,112,84]{2,1,0:T(8,128)S(1)}, u32[]{:S(2)}, u32[]{:S(2)}) collective-permute-start(f32[6,112,84]{2,1,0:T(8,128)S(1)} %get-tuple-element.44), channel_id=1, source_target_pairs={{16,0},{32,16},{48,32},{64,48},{80,64},{96,80},{112,96},{128,112},... | collective-permute-start | bytes 677384 | tf_op jit(solution)/shard_map/ppermute | solution.py:401
  30.3 14.3 %collective-permute-start.3 = (f32[6,68,296]{2,1,0:T(8,128)}, f32[6,68,296]{2,1,0:T(8,128)S(1)}, u32[]{:S(2)}, u32[]{:S(2)}) collective-permute-start(f32[6,68,296]{2,1,0:T(8,128)} %get-tuple-element.30), channel_id=1, source_target_pairs={{1,0},{2,1},{3,2},{4,3},{5,4},{6,5},{7,6},{8,7},{9,8},{10,9},{11,1... | collective-permute-start | bytes 1449224 | tf_op jit(solution)/shard_map/ppermute | solution.py:26
  33.7 11.8 %collective-permute-start.2 = (f32[6,68,296]{2,1,0:T(8,128)S(1)}, f32[6,68,296]{2,1,0:T(8,128)S(1)}, u32[]{:S(2)}, u32[]{:S(2)}) collective-permute-start(f32[6,68,296]{2,1,0:T(8,128)S(1)} %get-tuple-element.29), channel_id=1, source_target_pairs={{0,1},{1,2},{2,3},{3,4},{4,5},{5,6},{6,7},{7,8},{8,9},{9,10},{10,1... | collective-permute-start | bytes 1449224 | tf_op jit(solution)/shard_map/ppermute | solution.py:26
  59.9 1.3 %copy-start.4 = (f32[184,256]{1,0:T(8,128)S(1)}, f32[184,256]{1,0:T(8,128)}, u32[]{:S(2)}) copy-start(f32[184,256]{1,0:T(8,128)} %get-tuple-element.13) | copy-start | bytes 565252
  59.9 1.3 %copy-start.5 = (f32[184,256]{1,0:T(8,128)S(1)}, f32[184,256]{1,0:T(8,128)}, u32[]{:S(2)}) copy-start(f32[184,256]{1,0:T(8,128)} %get-tuple-element.14) | copy-start | bytes 565252
  59.9 1.4 %copy-start.6 = (f32[184,256]{1,0:T(8,128)S(1)}, f32[184,256]{1,0:T(8,128)}, u32[]{:S(2)}) copy-start(f32[184,256]{1,0:T(8,128)} %get-tuple-element.15) | copy-start | bytes 565252
  69.2 22.9 %copy-start = (f32[112,128]{1,0:T(8,128)S(1)}, f32[112,128]{1,0:T(8,128)}, u32[]{:S(2)}) copy-start(f32[112,128]{1,0:T(8,128)} %get-tuple-element.18) | copy-start | bytes 172036
  69.2 22.9 %copy-start.1 = (f32[112,128]{1,0:T(8,128)S(1)}, f32[112,128]{1,0:T(8,128)}, u32[]{:S(2)}) copy-start(f32[112,128]{1,0:T(8,128)} %get-tuple-element.19) | copy-start | bytes 172036
  69.2 22.9 %copy-start.2 = (f32[112,128]{1,0:T(8,128)S(1)}, f32[112,128]{1,0:T(8,128)}, u32[]{:S(2)}) copy-start(f32[112,128]{1,0:T(8,128)} %get-tuple-element.20) | copy-start | bytes 172036
  70.3 12.4 %collective-permute-start.4 = (f32[3,112,42]{2,1,0:T(8,128)S(1)}, f32[3,112,42]{2,1,0:T(8,128)S(1)}, u32[]{:S(2)}, u32[]{:S(2)}) collective-permute-start(f32[3,112,42]{2,1,0:T(8,128)S(1)} %get-tuple-element.45), channel_id=1, source_target_pairs={{0,16},{16,32},{32,48},{48,64},{64,80},{80,96},{96,112},{112,128},... | collective-permute-start | bytes 169352 | tf_op jit(solution)/shard_map/ppermute | solution.py:398
  72.2 11.3 %collective-permute-start.5 = (f32[3,112,42]{2,1,0:T(8,128)S(1)}, f32[3,112,42]{2,1,0:T(8,128)S(1)}, u32[]{:S(2)}, u32[]{:S(2)}) collective-permute-start(f32[3,112,42]{2,1,0:T(8,128)S(1)} %get-tuple-element.46), channel_id=1, source_target_pairs={{16,0},{32,16},{48,32},{64,48},{80,64},{96,80},{112,96},{128,112},... | collective-permute-start | bytes 169352 | tf_op jit(solution)/shard_map/ppermute | solution.py:401
  84.6 7.5 %collective-permute-start.6 = (f32[3,34,212]{2,1,0:T(8,128)S(1)}, f32[3,34,212]{2,1,0:T(8,128)S(1)}, u32[]{:S(2)}, u32[]{:S(2)}) collective-permute-start(f32[3,34,212]{2,1,0:T(8,128)S(1)} %slice.185), channel_id=1, source_target_pairs={{0,1},{1,2},{2,3},{3,4},{4,5},{5,6},{6,7},{7,8},{8,9},{9,10},{10,1... | collective-permute-start | bytes 259496 | tf_op jit(solution)/shard_map/ppermute | solution.py:26
  92.3 9.0 %collective-permute-start.7 = (f32[3,34,212]{2,1,0:T(8,128)S(1)}, f32[3,34,212]{2,1,0:T(8,128)S(1)}, u32[]{:S(2)}, u32[]{:S(2)}) collective-permute-start(f32[3,34,212]{2,1,0:T(8,128)S(1)} %get-tuple-element.42), channel_id=1, source_target_pairs={{1,0},{2,1},{3,2},{4,3},{5,4},{6,5},{7,6},{8,7},{9,8},{10,9},{11,1... | collective-permute-start | bytes 259496 | tf_op jit(solution)/shard_map/ppermute | solution.py:26

commit v11 on v8

--- a/solution.py
+++ b/solution.py
@@ -216,9 +216,10 @@
     return rights / main_band
 
 
-def tendency_body(surface_ref, east_ref, north_ref, depth_ref, wet_ref, keep_ref, mirror_ref,
+def tendency_body(surface_ref, east_ref, north_ref, depth_ref, wet_ref, place_ref, layout,
                   first_row, used_cols, tile_offset):
-    rows, cols = mirror_ref.shape
+    rows, cols, box_rows, region_above, tile_rows, count = layout
+    place = place_ref[0]
     depth = depth_ref[pl.ds(first_row, rows), :]
     surface = surface_ref[pl.ds(first_row, rows), :]
     coef = depth * depth / (3.0 * LON_SPACING * LON_SPACING)
@@ -233,7 +234,9 @@
     )
     full_depth = depth_ref[...]
     coef = full_depth * full_depth / (3.0 * LAT_SPACING * LAT_SPACING)
-    keep = keep_ref[...] > 0.0
+    box_row = lax.broadcasted_iota(jnp.int32, depth_ref.shape, 0)
+    global_row = place * tile_rows - region_above - tile_offset[0] + box_row
+    keep = (global_row >= 0) & (global_row < count * tile_rows) & (box_row < box_rows)
     rights = north_ref[...] / (full_depth + surface_ref[...])
     north_raw = reduce_lines(
         jnp.where(keep, -coef, 0.0),
@@ -252,9 +255,16 @@
     depth = wrapped(depth)
     velocity_u = wet * wrapped(east_raw)
     velocity_v = wet * wrapped(north_raw)
-    mirror = mirror_ref[...]
-    for code, shift in ((1, rows - 1), (2, rows - 3), (3, 1), (4, 3)):
-        velocity_v = jnp.where(mirror == code, -pltpu.roll(velocity_v, shift, 0), velocity_v)
+    wrapped_row = lax.broadcasted_iota(jnp.int32, (rows, cols), 0)
+    tile_row = jnp.where(wrapped_row >= rows - 2, wrapped_row - rows, wrapped_row) - region_above
+    top = place == 0
+    bottom = place == count - 1
+    for wall, row, shift in (
+        (top, -1, rows - 1), (top, -2, rows - 3), (bottom, tile_rows, 1), (bottom, tile_rows + 1, 3)
+    ):
+        velocity_v = jnp.where(
+            wall & (tile_row == row), -pltpu.roll(velocity_v, shift, 0), velocity_v
+        )
 
     def east_of(values):
         return pltpu.roll(values, cols - 1, 1)
@@ -309,16 +319,16 @@
     return (rate_surface, rate_east, rate_north), (surface, velocity_u, velocity_v), wrapped
 
 
-def section_kernel(surface_ref, east_ref, north_ref, depth_ref, wet_ref, keep_ref, mirror_ref,
+def section_kernel(surface_ref, east_ref, north_ref, depth_ref, wet_ref, place_ref,
                    lift_ref, start_surface, start_east, start_north,
                    next_surface, next_east, next_north, east_out, north_out, *,
-                   first_row, used_cols, tile_offset, weights):
+                   first_row, used_cols, tile_offset, weights, layout):
     tile_rows, tile_cols = lift_ref.shape
     rates, (surface, velocity_u, velocity_v), wrapped = tendency_body(
-        surface_ref, east_ref, north_ref, depth_ref, wet_ref, keep_ref, mirror_ref,
+        surface_ref, east_ref, north_ref, depth_ref, wet_ref, place_ref, layout,
         first_row, used_cols, tile_offset,
     )
-    rows = mirror_ref.shape[0]
+    rows = layout[0]
     nows = (
         surface,
         wrapped(east_ref[pl.ds(first_row, rows), :]),
@@ -341,13 +351,13 @@
     north_out[...] = velocity_v[:tile_rows, :tile_cols]
 
 
-def ring_kernel(surface_ref, east_ref, north_ref, depth_ref, wet_ref, keep_ref, mirror_ref,
+def ring_kernel(surface_ref, east_ref, north_ref, depth_ref, wet_ref, place_ref,
                 lift_ref, next_surface, next_east, next_north, depth_out, wet_out, *,
-                first_row, used_cols, tile_offset):
-    rows = mirror_ref.shape[0]
+                first_row, used_cols, tile_offset, layout):
+    rows = layout[0]
     out_rows, out_cols = next_surface.shape
     rates, (surface, _, _), wrapped = tendency_body(
-        surface_ref, east_ref, north_ref, depth_ref, wet_ref, keep_ref, mirror_ref,
+        surface_ref, east_ref, north_ref, depth_ref, wet_ref, place_ref, layout,
         first_row, used_cols, tile_offset,
     )
     lift = wrapped(lift_ref[pl.ds(first_row, rows), :])
@@ -363,34 +373,37 @@
     wet_out[...] = wrapped(wet_ref[pl.ds(first_row, rows), :])[:out_rows, :out_cols]
 
 
-def ring_step(fields, keep, mirror, out_shape, first_row, used_cols, tile_offset):
+def ring_step(fields, place, layout, out_shape, first_row, used_cols, tile_offset):
     spec = pl.BlockSpec(memory_space=pltpu.VMEM)
+    scalar = pl.BlockSpec(memory_space=pltpu.SMEM)
     shape = jax.ShapeDtypeStruct(out_shape, jnp.float32)
     return pl.pallas_call(
         lambda *refs: ring_kernel(
-            *refs, first_row=first_row, used_cols=used_cols, tile_offset=tile_offset
+            *refs, first_row=first_row, used_cols=used_cols, tile_offset=tile_offset,
+            layout=layout,
         ),
         out_shape=(shape,) * 5,
-        in_specs=[spec] * 8,
+        in_specs=[spec] * 5 + [scalar, spec],
         out_specs=(spec,) * 5,
         name="ring_step",
-    )(*fields[:5], keep, mirror, fields[5])
-
-
-def section_step(fields, keep, mirror, lift, initial, first_row, used_cols, tile_offset,
+    )(*fields[:5], place, fields[5])
+
+
+def section_step(fields, place, layout, lift, initial, first_row, used_cols, tile_offset,
                  weights):
     spec = pl.BlockSpec(memory_space=pltpu.VMEM)
+    scalar = pl.BlockSpec(memory_space=pltpu.SMEM)
     shape = jax.ShapeDtypeStruct(lift.shape, jnp.float32)
     return pl.pallas_call(
         lambda *refs: section_kernel(
             *refs, first_row=first_row, used_cols=used_cols, tile_offset=tile_offset,
-            weights=weights,
+            weights=weights, layout=layout,
         ),
         out_shape=(shape,) * 5,
-        in_specs=[spec] * 11,
+        in_specs=[spec] * 5 + [scalar] + [spec] * 4,
         out_specs=(spec,) * 5,
         name="section_step",
-    )(*fields, keep, mirror, lift, *initial)
+    )(*fields, place, lift, *initial)
 
 
 def halo_box(fields, wide_x, wide_y, place, count, padded_shape):
@@ -476,8 +489,9 @@
     )
     ring = Geometry(tile_rows + 2 * wide_y, tile_cols + 2 * wide_x, wide_y, wide_x)
     plain = Geometry(tile_rows, tile_cols, wide_y, wide_x)
-    ring_keep, ring_mirror = ring.masks(wide_y, place, count, tile_rows)
-    plain_keep, plain_mirror = plain.masks(0, place, count, tile_rows)
+    place_array = jnp.reshape(place, (1,)).astype(jnp.int32)
+    ring_layout = (ring.rows, ring.padded[1], ring.box_rows, wide_y, tile_rows, count)
+    plain_layout = (plain.rows, plain.padded[1], plain.box_rows, 0, tile_rows, count)
     initial = (surface, momentum_x, momentum_y)
 
     big = halo_box(
@@ -485,7 +499,7 @@
         2 * wide_x, 2 * wide_y, place, count, ring.padded,
     )
     ring_state = ring_step(
-        tuple(big[k] for k in range(6)), ring_keep, ring_mirror, plain.padded,
+        tuple(big[k] for k in range(6)), place_array, ring_layout, plain.padded,
         ring.first_row, ring.box_cols, ring.offset,
     )
     box = wall_mirrored(jnp.stack(ring_state[:3]), wide_y, place, count, plain.box_rows)
@@ -494,7 +508,7 @@
         if box is None:
             box = halo_box(jnp.stack(list(current)), wide_x, wide_y, place, count, plain.padded)
         next_surface, next_east, next_north, velocity_u, velocity_v = section_step(
-            (box[0], box[1], box[2], depth_box, wet_box), plain_keep, plain_mirror, lift, initial,
+            (box[0], box[1], box[2], depth_box, wet_box), place_array, plain_layout, lift, initial,
             plain.first_row, plain.box_cols, plain.offset, (first, second),
         )
         current = (next_surface, next_east, next_north)

time: 107 us -> 105 us (0.981)
  the two profiles are of different devices: /device:TPU:25 before, /device:TPU:2 now
where the time goes in v11:
time: 105 us; the launch traced here: 104 us
  starting transfers between devices  34.9 us (33%)
  waiting for transfers between devices  26 us (25%)
  Pallas kernels  22.9 us (22%)
  local copies, waits for them, and re-layouts  9.52 us (9%)
  other arithmetic  9.37 us (9%)
    ppermute x2, starting transfers between devices, halo_box(): lax.ppermute(fields[:, :, :wide_x], 'lon', [((i + 1) % lon_count, i) for...  18.6 us
    ppermute x4, waiting for transfers between devices, passed_along(): return lax.ppermute(x, axis, pairs)  15.8 us
    pallas_call x2, Pallas kernels, section_step(): pl.pallas_call(lambda *refs: section_kernel(*refs, first_row=first_row, u...  11.8 us
    pallas_call x1, Pallas kernels, ring_step(): pl.pallas_call(lambda *refs: ring_kernel(*refs, first_row=first_row, used...  11.1 us
    ppermute x4, starting transfers between devices, passed_along(): return lax.ppermute(x, axis, pairs)  10.6 us
    ppermute x2, waiting for transfers between devices, halo_box(): lax.ppermute(fields[:, :, -wide_x:], 'lon', [(i, (i + 1) % lon_count) for...  7.56 us
    ppermute x2, starting transfers between devices, halo_box(): lax.ppermute(fields[:, :, -wide_x:], 'lon', [(i, (i + 1) % lon_count) for...  5.74 us
    unnamed x22, local copies, waits for them, and re-layouts  4.07 us
  transfers between devices with their start and end apart: 8, of which 7 were waited for; matrix products, arithmetic and copies ran while one was open for 3% of the time, Pallas kernels for 0%

profile of v11, /device:TPU:2, one launch (start us, length us, event | category | flops | bytes accessed | tf_op | source)
XLA Modules:
  0.0 103.7 jit_solution(15193171210462559186)
XLA Ops:
  5.4 1.1 %scatter_custom_fusion = f32[14336]{0:T(1024)S(1)} fusion(s32[64]{0:T(128)S(1)} %fusion.22, f32[64]{0:T(128)} %bitcast.66, f32[]{:T(128)} %constant.3.clone.1), kind=kCustom, calls=%fused_computation.60 | custom fusion | flops 64 | bytes 57856 | tf_op jit(solution)/shard_map/scatter-add | solution.py:487
  6.7 3.8 %collective-permute-start = (f32[6,112,84]{2,1,0:T(8,128)S(1)}, f32[6,112,84]{2,1,0:T(8,128)S(1)}, u32[]{:S(2)}, u32[]{:S(2)}) collective-permute-start(f32[6,112,84]{2,1,0:T(8,128)S(1)} %get-tuple-element.37), channel_id=1, source_target_pairs={{0,16},{16,32},{32,48},{48,64},{64,80},{80,96},{96,112},{112,128},... | collective-permute-start | bytes 677384 | tf_op jit(solution)/shard_map/ppermute | solution.py:411
  10.5 11.1 %collective-permute-start.1 = (f32[6,112,84]{2,1,0:T(8,128)S(1)}, f32[6,112,84]{2,1,0:T(8,128)S(1)}, u32[]{:S(2)}, u32[]{:S(2)}) collective-permute-start(f32[6,112,84]{2,1,0:T(8,128)S(1)} %get-tuple-element.38), channel_id=1, source_target_pairs={{16,0},{32,16},{48,32},{64,48},{80,64},{96,80},{112,96},{128,112},... | collective-permute-start | bytes 677384 | tf_op jit(solution)/shard_map/ppermute | solution.py:414
  21.6 6.1 %collective-permute-done = f32[6,112,84]{2,1,0:T(8,128)S(1)} collective-permute-done((f32[6,112,84]{2,1,0:T(8,128)S(1)}, f32[6,112,84]{2,1,0:T(8,128)S(1)}, u32[]{:S(2)}, u32[]{:S(2)}) %collective-permute-start) | collective-permute-done | bytes 225824 | tf_op jit(solution)/shard_map/ppermute | solution.py:411
  27.7 1.2 %collective-permute-done.1 = f32[6,112,84]{2,1,0:T(8,128)S(1)} collective-permute-done((f32[6,112,84]{2,1,0:T(8,128)S(1)}, f32[6,112,84]{2,1,0:T(8,128)S(1)}, u32[]{:S(2)}, u32[]{:S(2)}) %collective-permute-start.1) | collective-permute-done | bytes 225824 | tf_op jit(solution)/shard_map/ppermute | solution.py:414
  30.1 4.4 %collective-permute-start.3 = (f32[6,68,296]{2,1,0:T(8,128)S(1)}, f32[6,68,296]{2,1,0:T(8,128)}, u32[]{:S(2)}, u32[]{:S(2)}) collective-permute-start(f32[6,68,296]{2,1,0:T(8,128)S(1)} %get-tuple-element.27), channel_id=1, source_target_pairs={{1,0},{2,1},{3,2},{4,3},{5,4},{6,5},{7,6},{8,7},{9,8},{10,9},{11,1... | collective-permute-start | bytes 1449224 | tf_op jit(solution)/shard_map/ppermute | solution.py:26
  34.5 1.9 %collective-permute-start.2 = (f32[6,68,296]{2,1,0:T(8,128)S(1)}, f32[6,68,296]{2,1,0:T(8,128)}, u32[]{:S(2)}, u32[]{:S(2)}) collective-permute-start(f32[6,68,296]{2,1,0:T(8,128)S(1)} %get-tuple-element.28), channel_id=1, source_target_pairs={{0,1},{1,2},{2,3},{3,4},{4,5},{5,6},{6,7},{7,8},{8,9},{9,10},{10,1... | collective-permute-start | bytes 1449224 | tf_op jit(solution)/shard_map/ppermute | solution.py:26
  37.7 5.0 %collective-permute-done.3 = f32[6,68,296]{2,1,0:T(8,128)} collective-permute-done((f32[6,68,296]{2,1,0:T(8,128)S(1)}, f32[6,68,296]{2,1,0:T(8,128)}, u32[]{:S(2)}, u32[]{:S(2)}) %collective-permute-start.3) | collective-permute-done | bytes 483104 | tf_op jit(solution)/shard_map/ppermute | solution.py:26
  42.7 1.2 %broadcast_select_fusion = f32[6,68,296]{2,1,0:T(8,128)S(1)} fusion(f32[6,68,296]{2,1,0:T(8,128)S(1)} %rev.19, f32[6,68,296]{2,1,0:T(8,128)} %collective-permute-done.3, pred[]{:T(512)S(6)} %eq.5), kind=kLoop, calls=%fused_computation.38 | loop fusion | flops 120768 | bytes 1449217 | tf_op jit(solution)/shard_map/jit(_where)/select_n | solution.py:421
  43.9 4.9 %collective-permute-done.2 = f32[6,68,296]{2,1,0:T(8,128)} collective-permute-done((f32[6,68,296]{2,1,0:T(8,128)S(1)}, f32[6,68,296]{2,1,0:T(8,128)}, u32[]{:S(2)}, u32[]{:S(2)}) %collective-permute-start.2) | collective-permute-done | bytes 483104 | tf_op jit(solution)/shard_map/ppermute | solution.py:26
  48.7 1.2 %broadcast_select_fusion.1 = f32[6,68,296]{2,1,0:T(8,128)S(1)} fusion(f32[6,68,296]{2,1,0:T(8,128)S(1)} %rev.18, f32[6,68,296]{2,1,0:T(8,128)} %collective-permute-done.2, pred[]{:T(512)S(6)} %eq.4), kind=kLoop, calls=%fused_computation.39 | loop fusion | flops 120768 | bytes 1449217 | tf_op jit(solution)/shard_map/jit(_where)/select_n | solution.py:420
  50.4 1.4 %slice_bitcast_fusion = (f32[248,384]{1,0:T(8,128)}, f32[248,384]{1,0:T(8,128)}, f32[248,384]{1,0:T(8,128)}, f32[248,384]{1,0:T(8,128)}, f32[248,384]{1,0:T(8,128)}, /*index=5*/f32[248,384]{1,0:T(8,128)}) fusion(f32[6,248,384]{2,1,0:T(8,128)S(1)} %select_maximum_fusion), kind=kLoop, calls=%fused_computation.32 | loop fusion | bytes 4571136 | tf_op jit(solution)/shard_map/squeeze | solution.py:502
  51.8 11.1 %ring_step.1 = (f32[184,256]{1,0:T(8,128)}, f32[184,256]{1,0:T(8,128)}, f32[184,256]{1,0:T(8,128)}, f32[184,256]{1,0:T(8,128)}, f32[184,256]{1,0:T(8,128)}) custom-call(f32[248,384]{1,0:T(8,128)} %get-tuple-element.26.refs_0_, f32[248,384]{1,0:T(8,128)} %get-tuple-element.25.refs_1_, f32[248,384]{1,0:T(8,128)} %get-tuple-element.24.refs_2_, ...), custom_call_target="tpu_custom_call" | custom-call | tf_op jit(solution)/shard_map/ring_step/pallas_call | solution.py:380
  63.0 1.2 %pad_maximum_fusion.1 = f32[3,184,256]{2,1,0:T(8,128)S(1)} fusion(f32[1,184,256]{2,1,0:T(8,128)} %bitcast.55, f32[1,184,256]{2,1,0:T(8,128)} %bitcast.53, f32[1,184,256]{2,1,0:T(8,128)} %bitcast.51), kind=kLoop, calls=%fused_computation.29 | loop fusion | flops 282624 | bytes 1130496 | tf_op jit(solution)/shard_map/stack | solution.py:505
  65.8 5.9 %section_step.2 = (f32[112,128]{1,0:T(8,128)}, f32[112,128]{1,0:T(8,128)}, f32[112,128]{1,0:T(8,128)}, f32[112,128]{1,0:T(8,128)}, f32[112,128]{1,0:T(8,128)}) custom-call(f32[184,256]{1,0:T(8,128)} %get-tuple-element.34.refs_0_, f32[184,256]{1,0:T(8,128)} %get-tuple-element.33.refs_1_, f32[184,256]{1,0:T(8,128)} %get-tuple-element.32.refs_2_, ...), custom_call_target="tpu_custom_call" | custom-call | tf_op jit(solution)/shard_map/section_step/pallas_call | solution.py:397
  72.7 1.9 %collective-permute-start.4 = (f32[3,112,42]{2,1,0:T(8,128)S(1)}, f32[3,112,42]{2,1,0:T(8,128)S(1)}, u32[]{:S(2)}, u32[]{:S(2)}) collective-permute-start(f32[3,112,42]{2,1,0:T(8,128)S(1)} %get-tuple-element.39), channel_id=1, source_target_pairs={{0,16},{16,32},{32,48},{48,64},{64,80},{80,96},{96,112},{112,128},... | collective-permute-start | bytes 169352 | tf_op jit(solution)/shard_map/ppermute | solution.py:411
  74.7 7.5 %collective-permute-start.5 = (f32[3,112,42]{2,1,0:T(8,128)S(1)}, f32[3,112,42]{2,1,0:T(8,128)S(1)}, u32[]{:S(2)}, u32[]{:S(2)}) collective-permute-start(f32[3,112,42]{2,1,0:T(8,128)S(1)} %get-tuple-element.40), channel_id=1, source_target_pairs={{16,0},{32,16},{48,32},{64,48},{80,64},{96,80},{112,96},{128,112},... | collective-permute-start | bytes 169352 | tf_op jit(solution)/shard_map/ppermute | solution.py:414
  82.2 1.4 %collective-permute-done.4 = f32[3,112,42]{2,1,0:T(8,128)S(1)} collective-permute-done((f32[3,112,42]{2,1,0:T(8,128)S(1)}, f32[3,112,42]{2,1,0:T(8,128)S(1)}, u32[]{:S(2)}, u32[]{:S(2)}) %collective-permute-start.4) | collective-permute-done | bytes 56480 | tf_op jit(solution)/shard_map/ppermute | solution.py:411
  83.7 1.5 %collective-permute-done.5 = f32[3,112,42]{2,1,0:T(8,128)S(1)} collective-permute-done((f32[3,112,42]{2,1,0:T(8,128)S(1)}, f32[3,112,42]{2,1,0:T(8,128)S(1)}, u32[]{:S(2)}, u32[]{:S(2)}) %collective-permute-start.5) | collective-permute-done | bytes 56480 | tf_op jit(solution)/shard_map/ppermute | solution.py:414
  85.1 1.0 pad_maximum_fusion.7
  86.1 2.1 %collective-permute-start.7 = (f32[3,34,212]{2,1,0:T(8,128)S(1)}, f32[3,34,212]{2,1,0:T(8,128)S(1)}, u32[]{:S(2)}, u32[]{:S(2)}) collective-permute-start(f32[3,34,212]{2,1,0:T(8,128)S(1)} %get-tuple-element.35), channel_id=1, source_target_pairs={{1,0},{2,1},{3,2},{4,3},{5,4},{6,5},{7,6},{8,7},{9,8},{10,9},{11,1... | collective-permute-start | bytes 259496 | tf_op jit(solution)/shard_map/ppermute | solution.py:26
  88.4 2.3 %collective-permute-start.6 = (f32[3,34,212]{2,1,0:T(8,128)S(1)}, f32[3,34,212]{2,1,0:T(8,128)S(1)}, u32[]{:S(2)}, u32[]{:S(2)}) collective-permute-start(f32[3,34,212]{2,1,0:T(8,128)S(1)} %get-tuple-element.36), channel_id=1, source_target_pairs={{0,1},{1,2},{2,3},{3,4},{4,5},{5,6},{6,7},{7,8},{8,9},{9,10},{10,1... | collective-permute-start | bytes 259496 | tf_op jit(solution)/shard_map/ppermute | solution.py:26
  90.7 6.0 %collective-permute-done.6 = f32[3,34,212]{2,1,0:T(8,128)S(1)} collective-permute-done((f32[3,34,212]{2,1,0:T(8,128)S(1)}, f32[3,34,212]{2,1,0:T(8,128)S(1)}, u32[]{:S(2)}, u32[]{:S(2)}) %collective-permute-start.6) | collective-permute-done | bytes 86528 | tf_op jit(solution)/shard_map/ppermute | solution.py:26
  97.8 5.9 %section_step.3 = (f32[112,128]{1,0:T(8,128)}, f32[112,128]{1,0:T(8,128)}, f32[112,128]{1,0:T(8,128)}, f32[112,128]{1,0:T(8,128)}, f32[112,128]{1,0:T(8,128)}) custom-call(f32[184,256]{1,0:T(8,128)} %get-tuple-element.31.refs_0_, f32[184,256]{1,0:T(8,128)} %get-tuple-element.30.refs_1_, f32[184,256]{1,0:T(8,128)} %get-tuple-element.29.refs_2_, ...), custom_call_target="tpu_custom_call" | custom-call | tf_op jit(solution)/shard_map/section_step/pallas_call | solution.py:397
  (50 shorter events, 11.9 us)
Async XLA Ops:
  6.5 23.7 %copy-start.2 = (f32[14336]{0:T(1024)}, f32[14336]{0:T(1024)S(1)}, u32[]{:S(2)}) copy-start(f32[14336]{0:T(1024)S(1)} %scatter_custom_fusion) | copy-start | bytes 172036
  6.7 21.0 %collective-permute-start = (f32[6,112,84]{2,1,0:T(8,128)S(1)}, f32[6,112,84]{2,1,0:T(8,128)S(1)}, u32[]{:S(2)}, u32[]{:S(2)}) collective-permute-start(f32[6,112,84]{2,1,0:T(8,128)S(1)} %get-tuple-element.37), channel_id=1, source_target_pairs={{0,16},{16,32},{32,48},{48,64},{64,80},{80,96},{96,112},{112,128},... | collective-permute-start | bytes 677384 | tf_op jit(solution)/shard_map/ppermute | solution.py:411
  10.5 18.4 %collective-permute-start.1 = (f32[6,112,84]{2,1,0:T(8,128)S(1)}, f32[6,112,84]{2,1,0:T(8,128)S(1)}, u32[]{:S(2)}, u32[]{:S(2)}) collective-permute-start(f32[6,112,84]{2,1,0:T(8,128)S(1)} %get-tuple-element.38), channel_id=1, source_target_pairs={{16,0},{32,16},{48,32},{64,48},{80,64},{96,80},{112,96},{128,112},... | collective-permute-start | bytes 677384 | tf_op jit(solution)/shard_map/ppermute | solution.py:414
  28.9 0.7 copy-start
  30.1 12.5 %collective-permute-start.3 = (f32[6,68,296]{2,1,0:T(8,128)S(1)}, f32[6,68,296]{2,1,0:T(8,128)}, u32[]{:S(2)}, u32[]{:S(2)}) collective-permute-start(f32[6,68,296]{2,1,0:T(8,128)S(1)} %get-tuple-element.27), channel_id=1, source_target_pairs={{1,0},{2,1},{3,2},{4,3},{5,4},{6,5},{7,6},{8,7},{9,8},{10,9},{11,1... | collective-permute-start | bytes 1449224 | tf_op jit(solution)/shard_map/ppermute | solution.py:26
  34.5 14.2 %collective-permute-start.2 = (f32[6,68,296]{2,1,0:T(8,128)S(1)}, f32[6,68,296]{2,1,0:T(8,128)}, u32[]{:S(2)}, u32[]{:S(2)}) collective-permute-start(f32[6,68,296]{2,1,0:T(8,128)S(1)} %get-tuple-element.28), channel_id=1, source_target_pairs={{0,1},{1,2},{2,3},{3,4},{4,5},{5,6},{6,7},{7,8},{8,9},{9,10},{10,1... | collective-permute-start | bytes 1449224 | tf_op jit(solution)/shard_map/ppermute | solution.py:26
  37.7 12.2 %copy-start.1 = (f32[6,112,84]{2,1,0:T(8,128)S(1)}, f32[6,112,84]{2,1,0:T(8,128)}, u32[]{:S(2)}) copy-start(f32[6,112,84]{2,1,0:T(8,128)} %copy-done) | copy-start | bytes 677380
  63.0 1.4 %copy-start.3 = (f32[184,256]{1,0:T(8,128)S(1)}, f32[184,256]{1,0:T(8,128)}, u32[]{:S(2)}) copy-start(f32[184,256]{1,0:T(8,128)} %get-tuple-element.13) | copy-start | bytes 565252
  63.0 1.4 %copy-start.4 = (f32[184,256]{1,0:T(8,128)S(1)}, f32[184,256]{1,0:T(8,128)}, u32[]{:S(2)}) copy-start(f32[184,256]{1,0:T(8,128)} %get-tuple-element.14) | copy-start | bytes 565252
  63.0 1.4 %copy-start.5 = (f32[184,256]{1,0:T(8,128)S(1)}, f32[184,256]{1,0:T(8,128)}, u32[]{:S(2)}) copy-start(f32[184,256]{1,0:T(8,128)} %get-tuple-element.15) | copy-start | bytes 565252
  71.7 25.1 %copy-start.6 = (f32[112,128]{1,0:T(8,128)S(1)}, f32[112,128]{1,0:T(8,128)}, u32[]{:S(2)}) copy-start(f32[112,128]{1,0:T(8,128)} %get-tuple-element.18) | copy-start | bytes 172036
  71.7 25.1 %copy-start.7 = (f32[112,128]{1,0:T(8,128)S(1)}, f32[112,128]{1,0:T(8,128)}, u32[]{:S(2)}) copy-start(f32[112,128]{1,0:T(8,128)} %get-tuple-element.19) | copy-start | bytes 172036
  71.7 25.1 %copy-start.8 = (f32[112,128]{1,0:T(8,128)S(1)}, f32[112,128]{1,0:T(8,128)}, u32[]{:S(2)}) copy-start(f32[112,128]{1,0:T(8,128)} %get-tuple-element.20) | copy-start | bytes 172036
  72.7 10.9 %collective-permute-start.4 = (f32[3,112,42]{2,1,0:T(8,128)S(1)}, f32[3,112,42]{2,1,0:T(8,128)S(1)}, u32[]{:S(2)}, u32[]{:S(2)}) collective-permute-start(f32[3,112,42]{2,1,0:T(8,128)S(1)} %get-tuple-element.39), channel_id=1, source_target_pairs={{0,16},{16,32},{32,48},{48,64},{64,80},{80,96},{96,112},{112,128},... | collective-permute-start | bytes 169352 | tf_op jit(solution)/shard_map/ppermute | solution.py:411
  74.7 10.4 %collective-permute-start.5 = (f32[3,112,42]{2,1,0:T(8,128)S(1)}, f32[3,112,42]{2,1,0:T(8,128)S(1)}, u32[]{:S(2)}, u32[]{:S(2)}) collective-permute-start(f32[3,112,42]{2,1,0:T(8,128)S(1)} %get-tuple-element.40), channel_id=1, source_target_pairs={{16,0},{32,16},{48,32},{64,48},{80,64},{96,80},{112,96},{128,112},... | collective-permute-start | bytes 169352 | tf_op jit(solution)/shard_map/ppermute | solution.py:414
  86.1 4.6 %collective-permute-start.7 = (f32[3,34,212]{2,1,0:T(8,128)S(1)}, f32[3,34,212]{2,1,0:T(8,128)S(1)}, u32[]{:S(2)}, u32[]{:S(2)}) collective-permute-start(f32[3,34,212]{2,1,0:T(8,128)S(1)} %get-tuple-element.35), channel_id=1, source_target_pairs={{1,0},{2,1},{3,2},{4,3},{5,4},{6,5},{7,6},{8,7},{9,8},{10,9},{11,1... | collective-permute-start | bytes 259496 | tf_op jit(solution)/shard_map/ppermute | solution.py:26
  88.4 8.3 %collective-permute-start.6 = (f32[3,34,212]{2,1,0:T(8,128)S(1)}, f32[3,34,212]{2,1,0:T(8,128)S(1)}, u32[]{:S(2)}, u32[]{:S(2)}) collective-permute-start(f32[3,34,212]{2,1,0:T(8,128)S(1)} %get-tuple-element.36), channel_id=1, source_target_pairs={{0,1},{1,2},{2,3},{3,4},{4,5},{5,6},{6,7},{7,8},{8,9},{9,10},{10,1... | collective-permute-start | bytes 259496 | tf_op jit(solution)/shard_map/ppermute | solution.py:26

commit v12 on v11

--- a/solution.py
+++ b/solution.py
@@ -417,8 +417,14 @@
     wide = jnp.concatenate([west, fields, east], axis=2)
     above = passed_along(wide[:, -wide_y:], "lat", 1)
     below = passed_along(wide[:, :wide_y], "lat", -1)
-    above = jnp.where(place == 0, wide[:, wide_y - 1 :: -1], above)
-    below = jnp.where(place == count - 1, wide[:, : -wide_y - 1 : -1], below)
+    above = jnp.where(
+        place == 0, jnp.concatenate([above[:, :-2], wide[:, 1:2], wide[:, 0:1]], axis=1), above
+    )
+    below = jnp.where(
+        place == count - 1,
+        jnp.concatenate([wide[:, -1:], wide[:, -2:-1], below[:, 2:]], axis=1),
+        below,
+    )
     box = jnp.concatenate([above, wide, below], axis=1)
     return pad_to(box, padded_shape)
 
@@ -431,13 +437,22 @@
 
 
 def wall_mirrored(values, halo, place, count, rows):
-    top = jnp.concatenate([values[..., 2 * halo - 1 : halo - 1 : -1, :], values[..., halo:, :]], axis=-2)
+    top = jnp.concatenate(
+        [
+            values[..., : halo - 2, :],
+            values[..., halo + 1 : halo + 2, :],
+            values[..., halo : halo + 1, :],
+            values[..., halo:, :],
+        ],
+        axis=-2,
+    )
     values = jnp.where(place == 0, top, values)
     bottom = jnp.concatenate(
         [
             values[..., : rows - halo, :],
-            values[..., rows - halo - 1 : rows - 2 * halo - 1 : -1, :],
-            values[..., rows:, :],
+            values[..., rows - halo - 1 : rows - halo, :],
+            values[..., rows - halo - 2 : rows - halo - 1, :],
+            values[..., rows - halo + 2 :, :],
         ],
         axis=-2,
     )

time: 105 us -> 107 us (1.019)
  the two profiles are of different devices: /device:TPU:2 before, /device:TPU:25 now
where the time goes in v12:
time: 107 us
  starting transfers between devices  40.4 us (38%)
  waiting for transfers between devices  26.7 us (25%)
  Pallas kernels  23.1 us (22%)
  local copies, waits for them, and re-layouts  7.93 us (7%)
  other arithmetic  7.55 us (7%)
    ppermute x2, starting transfers between devices, halo_box(): lax.ppermute(fields[:, :, :wide_x], 'lon', [((i + 1) % lon_count, i) for...  19.7 us
    ppermute x4, waiting for transfers between devices, passed_along(): return lax.ppermute(x, axis, pairs)  16.5 us
    ppermute x4, starting transfers between devices, passed_along(): return lax.ppermute(x, axis, pairs)  15.2 us
    pallas_call x2, Pallas kernels, section_step(): pl.pallas_call(lambda *refs: section_kernel(*refs, first_row=first_row, u...  11.9 us
    pallas_call x1, Pallas kernels, ring_step(): pl.pallas_call(lambda *refs: ring_kernel(*refs, first_row=first_row, used...  11.1 us
    ppermute x2, waiting for transfers between devices, halo_box(): lax.ppermute(fields[:, :, -wide_x:], 'lon', [(i, (i + 1) % lon_count) for...  8.54 us
    ppermute x2, starting transfers between devices, halo_box(): lax.ppermute(fields[:, :, -wide_x:], 'lon', [(i, (i + 1) % lon_count) for...  5.46 us
    unnamed x18, local copies, waits for them, and re-layouts  3.38 us
  transfers between devices with their start and end apart: 8, of which 8 were waited for; matrix products, arithmetic and copies ran while one was open for 0% of the time, Pallas kernels for 0%

profile of v12, /device:TPU:25, one launch (start us, length us, event | category | flops | bytes accessed | tf_op | source)
XLA Modules:
  0.0 106.5 jit_solution(16718693791584780578)
XLA Ops:
  5.4 1.1 scatter_custom_fusion
  6.7 3.5 %collective-permute-start = (f32[6,112,84]{2,1,0:T(8,128)S(1)}, f32[6,112,84]{2,1,0:T(8,128)S(1)}, u32[]{:S(2)}, u32[]{:S(2)}) collective-permute-start(f32[6,112,84]{2,1,0:T(8,128)S(1)} %get-tuple-element.43), channel_id=1, source_target_pairs={{0,16},{16,32},{32,48},{48,64},{64,80},{80,96},{96,112},{112,128},... | collective-permute-start | bytes 677384 | tf_op jit(solution)/shard_map/ppermute | solution.py:411
  10.2 12.0 %collective-permute-start.1 = (f32[6,112,84]{2,1,0:T(8,128)S(1)}, f32[6,112,84]{2,1,0:T(8,128)S(1)}, u32[]{:S(2)}, u32[]{:S(2)}) collective-permute-start(f32[6,112,84]{2,1,0:T(8,128)S(1)} %get-tuple-element.44), channel_id=1, source_target_pairs={{16,0},{32,16},{48,32},{64,48},{80,64},{96,80},{112,96},{128,112},... | collective-permute-start | bytes 677384 | tf_op jit(solution)/shard_map/ppermute | solution.py:414
  22.2 5.8 %collective-permute-done = f32[6,112,84]{2,1,0:T(8,128)S(1)} collective-permute-done((f32[6,112,84]{2,1,0:T(8,128)S(1)}, f32[6,112,84]{2,1,0:T(8,128)S(1)}, u32[]{:S(2)}, u32[]{:S(2)}) %collective-permute-start) | collective-permute-done | bytes 225824 | tf_op jit(solution)/shard_map/ppermute | solution.py:411
  28.0 0.9 collective-permute-done.1
  29.3 0.9 fusion.39
  30.3 3.4 %collective-permute-start.3 = (f32[6,68,296]{2,1,0:T(8,128)}, f32[6,68,296]{2,1,0:T(8,128)S(1)}, u32[]{:S(2)}, u32[]{:S(2)}) collective-permute-start(f32[6,68,296]{2,1,0:T(8,128)} %get-tuple-element.30), channel_id=1, source_target_pairs={{1,0},{2,1},{3,2},{4,3},{5,4},{6,5},{7,6},{8,7},{9,8},{10,9},{11,1... | collective-permute-start | bytes 1449224 | tf_op jit(solution)/shard_map/ppermute | solution.py:26
  33.7 4.2 %collective-permute-start.2 = (f32[6,68,296]{2,1,0:T(8,128)S(1)}, f32[6,68,296]{2,1,0:T(8,128)S(1)}, u32[]{:S(2)}, u32[]{:S(2)}) collective-permute-start(f32[6,68,296]{2,1,0:T(8,128)S(1)} %get-tuple-element.29), channel_id=1, source_target_pairs={{0,1},{1,2},{2,3},{3,4},{4,5},{5,6},{6,7},{7,8},{8,9},{9,10},{10,1... | collective-permute-start | bytes 1449224 | tf_op jit(solution)/shard_map/ppermute | solution.py:26
  37.9 6.6 %collective-permute-done.3 = f32[6,68,296]{2,1,0:T(8,128)S(1)} collective-permute-done((f32[6,68,296]{2,1,0:T(8,128)}, f32[6,68,296]{2,1,0:T(8,128)S(1)}, u32[]{:S(2)}, u32[]{:S(2)}) %collective-permute-start.3) | collective-permute-done | bytes 483104 | tf_op jit(solution)/shard_map/ppermute | solution.py:26
  44.6 0.9 collective-permute-done.2
  46.3 1.4 %slice_bitcast_fusion = (f32[248,384]{1,0:T(8,128)}, f32[248,384]{1,0:T(8,128)}, f32[248,384]{1,0:T(8,128)}, f32[248,384]{1,0:T(8,128)}, f32[248,384]{1,0:T(8,128)}, /*index=5*/f32[248,384]{1,0:T(8,128)}) fusion(f32[6,248,384]{2,1,0:T(8,128)S(1)} %select_maximum_fusion), kind=kLoop, calls=%fused_computation.52 | loop fusion | bytes 4571136 | tf_op jit(solution)/shard_map/squeeze | solution.py:517
  47.7 11.1 %ring_step.1 = (f32[184,256]{1,0:T(8,128)}, f32[184,256]{1,0:T(8,128)}, f32[184,256]{1,0:T(8,128)}, f32[184,256]{1,0:T(8,128)}, f32[184,256]{1,0:T(8,128)}) custom-call(f32[248,384]{1,0:T(8,128)} %get-tuple-element.26.refs_0_, f32[248,384]{1,0:T(8,128)} %get-tuple-element.25.refs_1_, f32[248,384]{1,0:T(8,128)} %get-tuple-element.24.refs_2_, ...), custom_call_target="tpu_custom_call" | custom-call | tf_op jit(solution)/shard_map/ring_step/pallas_call | solution.py:380
  58.8 1.2 %pad_maximum_fusion.5 = f32[3,184,256]{2,1,0:T(8,128)S(1)} fusion(f32[1,184,256]{2,1,0:T(8,128)} %bitcast.72, f32[1,184,256]{2,1,0:T(8,128)} %bitcast.70, f32[1,184,256]{2,1,0:T(8,128)} %bitcast.68), kind=kLoop, calls=%fused_computation.49 | loop fusion | flops 282624 | bytes 1130496 | tf_op jit(solution)/shard_map/stack | solution.py:520
  61.3 6.1 %section_step.2 = (f32[112,128]{1,0:T(8,128)}, f32[112,128]{1,0:T(8,128)}, f32[112,128]{1,0:T(8,128)}, f32[112,128]{1,0:T(8,128)}, f32[112,128]{1,0:T(8,128)}) custom-call(f32[184,256]{1,0:T(8,128)} %get-tuple-element.36.refs_0_, f32[184,256]{1,0:T(8,128)} %get-tuple-element.35.refs_1_, f32[184,256]{1,0:T(8,128)} %get-tuple-element.34.refs_2_, ...), custom_call_target="tpu_custom_call" | custom-call | tf_op jit(solution)/shard_map/section_step/pallas_call | solution.py:397
  67.4 0.9 pad_maximum_fusion.7
  68.4 1.9 %collective-permute-start.4 = (f32[3,112,42]{2,1,0:T(8,128)S(1)}, f32[3,112,42]{2,1,0:T(8,128)S(1)}, u32[]{:S(2)}, u32[]{:S(2)}) collective-permute-start(f32[3,112,42]{2,1,0:T(8,128)S(1)} %get-tuple-element.45), channel_id=1, source_target_pairs={{0,16},{16,32},{32,48},{48,64},{64,80},{80,96},{96,112},{112,128},... | collective-permute-start | bytes 169352 | tf_op jit(solution)/shard_map/ppermute | solution.py:411
  70.4 7.7 %collective-permute-start.5 = (f32[3,112,42]{2,1,0:T(8,128)S(1)}, f32[3,112,42]{2,1,0:T(8,128)S(1)}, u32[]{:S(2)}, u32[]{:S(2)}) collective-permute-start(f32[3,112,42]{2,1,0:T(8,128)S(1)} %get-tuple-element.46), channel_id=1, source_target_pairs={{16,0},{32,16},{48,32},{64,48},{80,64},{96,80},{112,96},{128,112},... | collective-permute-start | bytes 169352 | tf_op jit(solution)/shard_map/ppermute | solution.py:414
  78.1 2.7 %collective-permute-done.4 = f32[3,112,42]{2,1,0:T(8,128)S(1)} collective-permute-done((f32[3,112,42]{2,1,0:T(8,128)S(1)}, f32[3,112,42]{2,1,0:T(8,128)S(1)}, u32[]{:S(2)}, u32[]{:S(2)}) %collective-permute-start.4) | collective-permute-done | bytes 56480 | tf_op jit(solution)/shard_map/ppermute | solution.py:411
  81.7 1.1 %pad_maximum_fusion.6 = f32[3,112,212]{2,1,0:T(8,128)S(1)} fusion(f32[3,112,42]{2,1,0:T(8,128)S(1)} %collective-permute-done.5, f32[1,112,128]{2,1,0:T(8,128)} %bitcast.62, f32[1,112,128]{2,1,0:T(8,128)} %bitcast.57, f32[1,112,128]{2,1,0:T(8,128)} %bitcast.52, f32[3,112,42]{2,1,0:T(8,128)S(1)} %collective-permute-done.4), kind=kLoop, calls=%fused_computation.58 | loop fusion | flops 284928 | bytes 569856 | tf_op jit(solution)/shard_map/concatenate | solution.py:417
  82.8 5.6 %collective-permute-start.6 = (f32[3,34,212]{2,1,0:T(8,128)S(1)}, f32[3,34,212]{2,1,0:T(8,128)S(1)}, u32[]{:S(2)}, u32[]{:S(2)}) collective-permute-start(f32[3,34,212]{2,1,0:T(8,128)S(1)} %slice.185), channel_id=1, source_target_pairs={{0,1},{1,2},{2,3},{3,4},{4,5},{5,6},{6,7},{7,8},{8,9},{9,10},{10,1... | collective-permute-start | bytes 259496 | tf_op jit(solution)/shard_map/ppermute | solution.py:26
  88.4 1.8 %collective-permute-done.6 = f32[3,34,212]{2,1,0:T(8,128)S(1)} collective-permute-done((f32[3,34,212]{2,1,0:T(8,128)S(1)}, f32[3,34,212]{2,1,0:T(8,128)S(1)}, u32[]{:S(2)}, u32[]{:S(2)}) %collective-permute-start.6) | collective-permute-done | bytes 86528 | tf_op jit(solution)/shard_map/ppermute | solution.py:26
  90.4 1.9 %collective-permute-start.7 = (f32[3,34,212]{2,1,0:T(8,128)S(1)}, f32[3,34,212]{2,1,0:T(8,128)S(1)}, u32[]{:S(2)}, u32[]{:S(2)}) collective-permute-start(f32[3,34,212]{2,1,0:T(8,128)S(1)} %get-tuple-element.42), channel_id=1, source_target_pairs={{1,0},{2,1},{3,2},{4,3},{5,4},{6,5},{7,6},{8,7},{9,8},{10,9},{11,1... | collective-permute-start | bytes 259496 | tf_op jit(solution)/shard_map/ppermute | solution.py:26
  92.4 7.1 %collective-permute-done.7 = f32[3,34,212]{2,1,0:T(8,128)S(1)} collective-permute-done((f32[3,34,212]{2,1,0:T(8,128)S(1)}, f32[3,34,212]{2,1,0:T(8,128)S(1)}, u32[]{:S(2)}, u32[]{:S(2)}) %collective-permute-start.7) | collective-permute-done | bytes 86528 | tf_op jit(solution)/shard_map/ppermute | solution.py:26
  100.7 5.9 %section_step.3 = (f32[112,128]{1,0:T(8,128)}, f32[112,128]{1,0:T(8,128)}, f32[112,128]{1,0:T(8,128)}, f32[112,128]{1,0:T(8,128)}, f32[112,128]{1,0:T(8,128)}) custom-call(f32[184,256]{1,0:T(8,128)} %get-tuple-element.33.refs_0_, f32[184,256]{1,0:T(8,128)} %get-tuple-element.32.refs_1_, f32[184,256]{1,0:T(8,128)} %get-tuple-element.31.refs_2_, ...), custom_call_target="tpu_custom_call" | custom-call | tf_op jit(solution)/shard_map/section_step/pallas_call | solution.py:397
  (44 shorter events, 9.7 us)
Async XLA Ops:
  6.5 23.8 %copy-start.3 = (f32[14336]{0:T(1024)}, f32[14336]{0:T(1024)S(1)}, u32[]{:S(2)}) copy-start(f32[14336]{0:T(1024)S(1)} %scatter_custom_fusion) | copy-start | bytes 172036
  6.7 21.4 %collective-permute-start = (f32[6,112,84]{2,1,0:T(8,128)S(1)}, f32[6,112,84]{2,1,0:T(8,128)S(1)}, u32[]{:S(2)}, u32[]{:S(2)}) collective-permute-start(f32[6,112,84]{2,1,0:T(8,128)S(1)} %get-tuple-element.43), channel_id=1, source_target_pairs={{0,16},{16,32},{32,48},{48,64},{64,80},{80,96},{96,112},{112,128},... | collective-permute-start | bytes 677384 | tf_op jit(solution)/shard_map/ppermute | solution.py:411
  10.2 18.7 %collective-permute-start.1 = (f32[6,112,84]{2,1,0:T(8,128)S(1)}, f32[6,112,84]{2,1,0:T(8,128)S(1)}, u32[]{:S(2)}, u32[]{:S(2)}) collective-permute-start(f32[6,112,84]{2,1,0:T(8,128)S(1)} %get-tuple-element.44), channel_id=1, source_target_pairs={{16,0},{32,16},{48,32},{64,48},{80,64},{96,80},{112,96},{128,112},... | collective-permute-start | bytes 677384 | tf_op jit(solution)/shard_map/ppermute | solution.py:414
  30.3 14.3 %collective-permute-start.3 = (f32[6,68,296]{2,1,0:T(8,128)}, f32[6,68,296]{2,1,0:T(8,128)S(1)}, u32[]{:S(2)}, u32[]{:S(2)}) collective-permute-start(f32[6,68,296]{2,1,0:T(8,128)} %get-tuple-element.30), channel_id=1, source_target_pairs={{1,0},{2,1},{3,2},{4,3},{5,4},{6,5},{7,6},{8,7},{9,8},{10,9},{11,1... | collective-permute-start | bytes 1449224 | tf_op jit(solution)/shard_map/ppermute | solution.py:26
  33.7 11.8 %collective-permute-start.2 = (f32[6,68,296]{2,1,0:T(8,128)S(1)}, f32[6,68,296]{2,1,0:T(8,128)S(1)}, u32[]{:S(2)}, u32[]{:S(2)}) collective-permute-start(f32[6,68,296]{2,1,0:T(8,128)S(1)} %get-tuple-element.29), channel_id=1, source_target_pairs={{0,1},{1,2},{2,3},{3,4},{4,5},{5,6},{6,7},{7,8},{8,9},{9,10},{10,1... | collective-permute-start | bytes 1449224 | tf_op jit(solution)/shard_map/ppermute | solution.py:26
  58.8 1.3 %copy-start.4 = (f32[184,256]{1,0:T(8,128)S(1)}, f32[184,256]{1,0:T(8,128)}, u32[]{:S(2)}) copy-start(f32[184,256]{1,0:T(8,128)} %get-tuple-element.13) | copy-start | bytes 565252
  58.8 1.3 %copy-start.5 = (f32[184,256]{1,0:T(8,128)S(1)}, f32[184,256]{1,0:T(8,128)}, u32[]{:S(2)}) copy-start(f32[184,256]{1,0:T(8,128)} %get-tuple-element.14) | copy-start | bytes 565252
  58.8 1.4 %copy-start.6 = (f32[184,256]{1,0:T(8,128)S(1)}, f32[184,256]{1,0:T(8,128)}, u32[]{:S(2)}) copy-start(f32[184,256]{1,0:T(8,128)} %get-tuple-element.15) | copy-start | bytes 565252
  67.4 22.9 %copy-start = (f32[112,128]{1,0:T(8,128)S(1)}, f32[112,128]{1,0:T(8,128)}, u32[]{:S(2)}) copy-start(f32[112,128]{1,0:T(8,128)} %get-tuple-element.18) | copy-start | bytes 172036
  67.4 22.9 %copy-start.1 = (f32[112,128]{1,0:T(8,128)S(1)}, f32[112,128]{1,0:T(8,128)}, u32[]{:S(2)}) copy-start(f32[112,128]{1,0:T(8,128)} %get-tuple-element.19) | copy-start | bytes 172036
  67.4 22.9 %copy-start.2 = (f32[112,128]{1,0:T(8,128)S(1)}, f32[112,128]{1,0:T(8,128)}, u32[]{:S(2)}) copy-start(f32[112,128]{1,0:T(8,128)} %get-tuple-element.20) | copy-start | bytes 172036
  68.4 12.4 %collective-permute-start.4 = (f32[3,112,42]{2,1,0:T(8,128)S(1)}, f32[3,112,42]{2,1,0:T(8,128)S(1)}, u32[]{:S(2)}, u32[]{:S(2)}) collective-permute-start(f32[3,112,42]{2,1,0:T(8,128)S(1)} %get-tuple-element.45), channel_id=1, source_target_pairs={{0,16},{16,32},{32,48},{48,64},{64,80},{80,96},{96,112},{112,128},... | collective-permute-start | bytes 169352 | tf_op jit(solution)/shard_map/ppermute | solution.py:411
  70.4 11.3 %collective-permute-start.5 = (f32[3,112,42]{2,1,0:T(8,128)S(1)}, f32[3,112,42]{2,1,0:T(8,128)S(1)}, u32[]{:S(2)}, u32[]{:S(2)}) collective-permute-start(f32[3,112,42]{2,1,0:T(8,128)S(1)} %get-tuple-element.46), channel_id=1, source_target_pairs={{16,0},{32,16},{48,32},{64,48},{80,64},{96,80},{112,96},{128,112},... | collective-permute-start | bytes 169352 | tf_op jit(solution)/shard_map/ppermute | solution.py:414
  82.8 7.5 %collective-permute-start.6 = (f32[3,34,212]{2,1,0:T(8,128)S(1)}, f32[3,34,212]{2,1,0:T(8,128)S(1)}, u32[]{:S(2)}, u32[]{:S(2)}) collective-permute-start(f32[3,34,212]{2,1,0:T(8,128)S(1)} %slice.185), channel_id=1, source_target_pairs={{0,1},{1,2},{2,3},{3,4},{4,5},{5,6},{6,7},{7,8},{8,9},{9,10},{10,1... | collective-permute-start | bytes 259496 | tf_op jit(solution)/shard_map/ppermute | solution.py:26
  90.4 9.0 %collective-permute-start.7 = (f32[3,34,212]{2,1,0:T(8,128)S(1)}, f32[3,34,212]{2,1,0:T(8,128)S(1)}, u32[]{:S(2)}, u32[]{:S(2)}) collective-permute-start(f32[3,34,212]{2,1,0:T(8,128)S(1)} %get-tuple-element.42), channel_id=1, source_target_pairs={{1,0},{2,1},{3,2},{4,3},{5,4},{6,5},{7,6},{8,7},{9,8},{10,9},{11,1... | collective-permute-start | bytes 259496 | tf_op jit(solution)/shard_map/ppermute | solution.py:26

commit v13 on v11

--- a/solution.py
+++ b/solution.py
@@ -321,8 +321,7 @@
 
 def section_kernel(surface_ref, east_ref, north_ref, depth_ref, wet_ref, place_ref,
                    lift_ref, start_surface, start_east, start_north,
-                   next_surface, next_east, next_north, east_out, north_out, *,
-                   first_row, used_cols, tile_offset, weights, layout):
+                   *outs, first_row, used_cols, tile_offset, weights, layout):
     tile_rows, tile_cols = lift_ref.shape
     rates, (surface, velocity_u, velocity_v), wrapped = tendency_body(
         surface_ref, east_ref, north_ref, depth_ref, wet_ref, place_ref, layout,
@@ -340,11 +339,14 @@
         rates[1][:tile_rows, :tile_cols],
         rates[2][:tile_rows, :tile_cols],
     )
+    if len(outs) == 3:
+        next_state, east_out, north_out = outs
+        nexts = (next_state.at[0], next_state.at[1], next_state.at[2])
+    else:
+        next_surface, next_east, next_north, east_out, north_out = outs
+        nexts = (next_surface, next_east, next_north)
     for out, start, now, rate in zip(
-        (next_surface, next_east, next_north),
-        (start_surface, start_east, start_north),
-        nows,
-        rates,
+        nexts, (start_surface, start_east, start_north), nows, rates
     ):
         out[...] = first * start[...] + second * (now[:tile_rows, :tile_cols] + TIME_STEP * rate)
     east_out[...] = velocity_u[:tile_rows, :tile_cols]
@@ -352,10 +354,10 @@
 
 
 def ring_kernel(surface_ref, east_ref, north_ref, depth_ref, wet_ref, place_ref,
-                lift_ref, next_surface, next_east, next_north, depth_out, wet_out, *,
+                lift_ref, next_state, depth_out, wet_out, *,
                 first_row, used_cols, tile_offset, layout):
     rows = layout[0]
-    out_rows, out_cols = next_surface.shape
+    out_rows, out_cols = depth_out.shape
     rates, (surface, _, _), wrapped = tendency_body(
         surface_ref, east_ref, north_ref, depth_ref, wet_ref, place_ref, layout,
         first_row, used_cols, tile_offset,
@@ -367,8 +369,8 @@
         wrapped(north_ref[pl.ds(first_row, rows), :]),
     )
     rates = (rates[0] + lift, rates[1], rates[2])
-    for out, now, rate in zip((next_surface, next_east, next_north), nows, rates):
-        out[...] = (0.0 * now + 1.0 * (now + TIME_STEP * rate))[:out_rows, :out_cols]
+    for k, (now, rate) in enumerate(zip(nows, rates)):
+        next_state[k] = (0.0 * now + 1.0 * (now + TIME_STEP * rate))[:out_rows, :out_cols]
     depth_out[...] = wrapped(depth_ref[pl.ds(first_row, rows), :])[:out_rows, :out_cols]
     wet_out[...] = wrapped(wet_ref[pl.ds(first_row, rows), :])[:out_rows, :out_cols]
 
@@ -382,15 +384,15 @@
             *refs, first_row=first_row, used_cols=used_cols, tile_offset=tile_offset,
             layout=layout,
         ),
-        out_shape=(shape,) * 5,
+        out_shape=(jax.ShapeDtypeStruct((3,) + out_shape, jnp.float32), shape, shape),
         in_specs=[spec] * 5 + [scalar, spec],
-        out_specs=(spec,) * 5,
+        out_specs=(spec,) * 3,
         name="ring_step",
     )(*fields[:5], place, fields[5])
 
 
 def section_step(fields, place, layout, lift, initial, first_row, used_cols, tile_offset,
-                 weights):
+                 weights, stacked_out):
     spec = pl.BlockSpec(memory_space=pltpu.VMEM)
     scalar = pl.BlockSpec(memory_space=pltpu.SMEM)
     shape = jax.ShapeDtypeStruct(lift.shape, jnp.float32)
@@ -399,11 +401,30 @@
             *refs, first_row=first_row, used_cols=used_cols, tile_offset=tile_offset,
             weights=weights, layout=layout,
         ),
-        out_shape=(shape,) * 5,
+        out_shape=(
+            (jax.ShapeDtypeStruct((3,) + lift.shape, jnp.float32), shape, shape)
+            if stacked_out else (shape,) * 5
+        ),
         in_specs=[spec] * 5 + [scalar] + [spec] * 4,
-        out_specs=(spec,) * 5,
+        out_specs=(spec,) * (3 if stacked_out else 5),
         name="section_step",
     )(*fields, place, lift, *initial)
+
+
+def stack_kernel(*refs):
+    for k, field in enumerate(refs[:-1]):
+        refs[-1][k] = field[...]
+
+
+def stacked(fields):
+    spec = pl.BlockSpec(memory_space=pltpu.VMEM)
+    return pl.pallas_call(
+        stack_kernel,
+        out_shape=jax.ShapeDtypeStruct((len(fields),) + fields[0].shape, jnp.float32),
+        in_specs=[spec] * len(fields),
+        out_specs=spec,
+        name="stacked",
+    )(*fields)
 
 
 def halo_box(fields, wide_x, wide_y, place, count, padded_shape):
@@ -495,25 +516,24 @@
     initial = (surface, momentum_x, momentum_y)
 
     big = halo_box(
-        jnp.stack([surface, momentum_x, momentum_y, water_depth, wet_float, lift]),
+        stacked([surface, momentum_x, momentum_y, water_depth, wet_float, lift]),
         2 * wide_x, 2 * wide_y, place, count, ring.padded,
     )
     ring_state = ring_step(
         tuple(big[k] for k in range(6)), place_array, ring_layout, plain.padded,
         ring.first_row, ring.box_cols, ring.offset,
     )
-    box = wall_mirrored(jnp.stack(ring_state[:3]), wide_y, place, count, plain.box_rows)
-    depth_box, wet_box = ring_state[3], ring_state[4]
-    for first, second in ((0.75, 0.25), (1.0 / 3.0, 2.0 / 3.0)):
-        if box is None:
-            box = halo_box(jnp.stack(list(current)), wide_x, wide_y, place, count, plain.padded)
-        next_surface, next_east, next_north, velocity_u, velocity_v = section_step(
-            (box[0], box[1], box[2], depth_box, wet_box), place_array, plain_layout, lift, initial,
-            plain.first_row, plain.box_cols, plain.offset, (first, second),
-        )
-        current = (next_surface, next_east, next_north)
-        box = None
-    return (current[0], current[1], current[2], velocity_u, velocity_v)
+    box = wall_mirrored(ring_state[0], wide_y, place, count, plain.box_rows)
+    depth_box, wet_box = ring_state[1], ring_state[2]
+    second_state = section_step(
+        (box[0], box[1], box[2], depth_box, wet_box), place_array, plain_layout, lift, initial,
+        plain.first_row, plain.box_cols, plain.offset, (0.75, 0.25), True,
+    )[0]
+    box = halo_box(second_state, wide_x, wide_y, place, count, plain.padded)
+    return section_step(
+        (box[0], box[1], box[2], depth_box, wet_box), place_array, plain_layout, lift, initial,
+        plain.first_row, plain.box_cols, plain.offset, (1.0 / 3.0, 2.0 / 3.0), False,
+    )
 
 
 def solution(mesh):

time: 105 us -> 107 us (1.019)
  Pallas kernels: 22.9 us -> 24.7 us
  other arithmetic: 9.37 us -> 10.5 us
    unnamed x22 -> x4, local copies, waits for them, and re-layouts: 4.07 us -> 0.01 us
    slice x2, local copies, waits for them, and re-layouts: 0.27 us -> 2.4 us  [halo_box(): fields[:, :, -wide_x:]]
    another operation x2 -> x0, other arithmetic: 2.12 us -> none  [the longest x1 1.2 us: local(): jnp.stack(ring_state[:3])]
    pallas_call x0 -> x1, Pallas kernels: none -> 1.71 us  [stacked(): pl.pallas_call(stack_kernel, out_shape=jax.ShapeDtypeStruct((len(fields),...]
    convert_element_type x0 -> x1, other arithmetic: none -> 1.45 us  [local(): wet_float = wet_mask.astype(jnp.float32)]
where the time goes in v13:
time: 107 us
  starting transfers between devices  34.9 us (33%)
  waiting for transfers between devices  26 us (24%)
  Pallas kernels  24.7 us (23%)
  other arithmetic  10.5 us (10%)
  local copies, waits for them, and re-layouts  9.46 us (9%)
    ppermute x2, starting transfers between devices, halo_box(): lax.ppermute(fields[:, :, :wide_x], 'lon', [((i + 1) % lon_count, i) for...  18.6 us
    ppermute x4, waiting for transfers between devices, passed_along(): return lax.ppermute(x, axis, pairs)  15.8 us
    pallas_call x2, Pallas kernels, section_step(): pl.pallas_call(lambda *refs: section_kernel(*refs, first_row=first_row, u...  11.8 us
    pallas_call x1, Pallas kernels, ring_step(): pl.pallas_call(lambda *refs: ring_kernel(*refs, first_row=first_row, used...  11.2 us
    ppermute x4, starting transfers between devices, passed_along(): return lax.ppermute(x, axis, pairs)  10.6 us
    ppermute x2, waiting for transfers between devices, halo_box(): lax.ppermute(fields[:, :, -wide_x:], 'lon', [(i, (i + 1) % lon_count) for...  7.56 us
    ppermute x2, starting transfers between devices, halo_box(): lax.ppermute(fields[:, :, -wide_x:], 'lon', [(i, (i + 1) % lon_count) for...  5.75 us
    ppermute x2, waiting for transfers between devices, halo_box(): lax.ppermute(fields[:, :, :wide_x], 'lon', [((i + 1) % lon_count, i) for...  2.64 us
  transfers between devices with their start and end apart: 8, of which 7 were waited for; matrix products, arithmetic and copies ran while one was open for 3% of the time, Pallas kernels for 0%

profile of v13, /device:TPU:2, one launch (start us, length us, event | category | flops | bytes accessed | tf_op | source)
XLA Modules:
  0.0 106.5 jit_solution(5580235821752290630)
XLA Ops:
  1.3 1.4 %convert_element_type.7.refs_4_ = f32[112,128]{1,0:T(8,128)} convert(s32[112,128]{1,0:T(8,128)} %param.11) | non-fusion elementwise | flops 14336 | bytes 114688 | tf_op jit(solution)/shard_map/convert_element_type | solution.py:499
  2.7 1.6 %scatter_custom_fusion = f32[14336]{0:T(1024)} fusion(s32[64]{0:T(128)S(1)} %fusion.16, f32[64]{0:T(128)} %bitcast.34, f32[]{:T(128)} %constant.3.clone.1), kind=kCustom, calls=%fused_computation.44 | custom fusion | flops 64 | bytes 57856 | tf_op jit(solution)/shard_map/scatter-add | solution.py:508
  4.4 1.7 %stacked.1 = f32[6,112,128]{2,1,0:T(8,128)} custom-call(f32[112,128]{1,0:T(8,128)} %refs_7_.3, f32[112,128]{1,0:T(8,128)} %refs_8_.3, f32[112,128]{1,0:T(8,128)} %refs_9_.3, f32[112,128]{1,0:T(8,128)} %refs_3_.1, f32[112,128]{1,0:T(8,128)} %convert_element_type.7.refs_4_, f32[112,128]{1,0:T(8,128)} %bitcast.31), custom_call_target="tpu_custom_call" | custom-call | tf_op jit(solution)/shard_map/stacked/pallas_call | solution.py:421
  6.1 1.2 %fusion.18 = (f32[6,112,84]{2,1,0:T(8,128)S(1)}, f32[6,112,84]{2,1,0:T(8,128)S(1)}) fusion(f32[6,112,128]{2,1,0:T(8,128)} %stacked.1), kind=kLoop, calls=%fused_computation.49 | loop fusion | bytes 903168 | tf_op jit(solution)/shard_map/slice | solution.py:433
  7.3 3.8 %collective-permute-start = (f32[6,112,84]{2,1,0:T(8,128)S(1)}, f32[6,112,84]{2,1,0:T(8,128)S(1)}, u32[]{:S(2)}, u32[]{:S(2)}) collective-permute-start(f32[6,112,84]{2,1,0:T(8,128)S(1)} %get-tuple-element.29), channel_id=1, source_target_pairs={{0,16},{16,32},{32,48},{48,64},{64,80},{80,96},{96,112},{112,128},... | collective-permute-start | bytes 677384 | tf_op jit(solution)/shard_map/ppermute | solution.py:432
  11.1 11.1 %collective-permute-start.1 = (f32[6,112,84]{2,1,0:T(8,128)S(1)}, f32[6,112,84]{2,1,0:T(8,128)S(1)}, u32[]{:S(2)}, u32[]{:S(2)}) collective-permute-start(f32[6,112,84]{2,1,0:T(8,128)S(1)} %get-tuple-element.30), channel_id=1, source_target_pairs={{16,0},{32,16},{48,32},{64,48},{80,64},{96,80},{112,96},{128,112},... | collective-permute-start | bytes 677384 | tf_op jit(solution)/shard_map/ppermute | solution.py:435
  22.2 6.1 %collective-permute-done = f32[6,112,84]{2,1,0:T(8,128)S(1)} collective-permute-done((f32[6,112,84]{2,1,0:T(8,128)S(1)}, f32[6,112,84]{2,1,0:T(8,128)S(1)}, u32[]{:S(2)}, u32[]{:S(2)}) %collective-permute-start) | collective-permute-done | bytes 225824 | tf_op jit(solution)/shard_map/ppermute | solution.py:432
  28.3 1.2 %collective-permute-done.1 = f32[6,112,84]{2,1,0:T(8,128)S(1)} collective-permute-done((f32[6,112,84]{2,1,0:T(8,128)S(1)}, f32[6,112,84]{2,1,0:T(8,128)S(1)}, u32[]{:S(2)}, u32[]{:S(2)}) %collective-permute-start.1) | collective-permute-done | bytes 225824 | tf_op jit(solution)/shard_map/ppermute | solution.py:435
  29.5 1.4 %pad_maximum_fusion = f32[6,112,296]{2,1,0:T(8,128)S(1)} fusion(f32[6,112,84]{2,1,0:T(8,128)S(1)} %collective-permute-done.1, f32[6,112,128]{2,1,0:T(8,128)} %stacked.1, f32[6,112,84]{2,1,0:T(8,128)S(1)} %collective-permute-done), kind=kLoop, calls=%fused_computation.9 | loop fusion | flops 397824 | bytes 1591296 | tf_op jit(solution)/shard_map/concatenate | solution.py:438
  31.0 4.4 %collective-permute-start.3 = (f32[6,68,296]{2,1,0:T(8,128)S(1)}, f32[6,68,296]{2,1,0:T(8,128)}, u32[]{:S(2)}, u32[]{:S(2)}) collective-permute-start(f32[6,68,296]{2,1,0:T(8,128)S(1)} %get-tuple-element.19), channel_id=1, source_target_pairs={{1,0},{2,1},{3,2},{4,3},{5,4},{6,5},{7,6},{8,7},{9,8},{10,9},{11,1... | collective-permute-start | bytes 1449224 | tf_op jit(solution)/shard_map/ppermute | solution.py:26
  35.4 1.9 %collective-permute-start.2 = (f32[6,68,296]{2,1,0:T(8,128)S(1)}, f32[6,68,296]{2,1,0:T(8,128)}, u32[]{:S(2)}, u32[]{:S(2)}) collective-permute-start(f32[6,68,296]{2,1,0:T(8,128)S(1)} %get-tuple-element.20), channel_id=1, source_target_pairs={{0,1},{1,2},{2,3},{3,4},{4,5},{5,6},{6,7},{7,8},{8,9},{9,10},{10,1... | collective-permute-start | bytes 1449224 | tf_op jit(solution)/shard_map/ppermute | solution.py:26
  38.6 5.0 %collective-permute-done.3 = f32[6,68,296]{2,1,0:T(8,128)} collective-permute-done((f32[6,68,296]{2,1,0:T(8,128)S(1)}, f32[6,68,296]{2,1,0:T(8,128)}, u32[]{:S(2)}, u32[]{:S(2)}) %collective-permute-start.3) | collective-permute-done | bytes 483104 | tf_op jit(solution)/shard_map/ppermute | solution.py:26
  44.7 4.9 %collective-permute-done.2 = f32[6,68,296]{2,1,0:T(8,128)} collective-permute-done((f32[6,68,296]{2,1,0:T(8,128)S(1)}, f32[6,68,296]{2,1,0:T(8,128)}, u32[]{:S(2)}, u32[]{:S(2)}) %collective-permute-start.2) | collective-permute-done | bytes 483104 | tf_op jit(solution)/shard_map/ppermute | solution.py:26
  51.3 1.4 %slice_bitcast_fusion = (f32[248,384]{1,0:T(8,128)}, f32[248,384]{1,0:T(8,128)}, f32[248,384]{1,0:T(8,128)}, f32[248,384]{1,0:T(8,128)}, f32[248,384]{1,0:T(8,128)}, /*index=5*/f32[248,384]{1,0:T(8,128)}) fusion(f32[6,248,384]{2,1,0:T(8,128)S(1)} %select_maximum_fusion), kind=kLoop, calls=%fused_computation.25 | loop fusion | bytes 4571136 | tf_op jit(solution)/shard_map/squeeze | solution.py:523
  52.7 11.2 %ring_step.1 = (f32[3,184,256]{2,1,0:T(8,128)}, f32[184,256]{1,0:T(8,128)}, f32[184,256]{1,0:T(8,128)}) custom-call(f32[248,384]{1,0:T(8,128)} %get-tuple-element.18.refs_0_, f32[248,384]{1,0:T(8,128)} %get-tuple-element.17.refs_1_, f32[248,384]{1,0:T(8,128)} %get-tuple-element.16.refs_2_, f32[248,384]{1,0:T(8,128)} %get-tuple-element.15.refs_3_, ...), custom_call_target="tpu_custom_call" | custom-call | tf_op jit(solution)/shard_map/ring_step/pallas_call | solution.py:382
  68.4 5.9 %section_step.2 = (f32[3,112,128]{2,1,0:T(8,128)}, f32[112,128]{1,0:T(8,128)}, f32[112,128]{1,0:T(8,128)}) custom-call(f32[184,256]{1,0:T(8,128)} %get-tuple-element.26.refs_0_, f32[184,256]{1,0:T(8,128)} %get-tuple-element.25.refs_1_, f32[184,256]{1,0:T(8,128)} %get-tuple-element.24.refs_2_, f32[184,256]{1,0:T(8,128)} %get-tuple-element.10.refs_3_, ...), custom_call_target="tpu_custom_call" | custom-call | tf_op jit(solution)/shard_map/section_step/pallas_call | solution.py:399
  75.5 1.9 %collective-permute-start.4 = (f32[3,112,42]{2,1,0:T(8,128)S(1)}, f32[3,112,42]{2,1,0:T(8,128)S(1)}, u32[]{:S(2)}, u32[]{:S(2)}) collective-permute-start(f32[3,112,42]{2,1,0:T(8,128)S(1)} %get-tuple-element.31), channel_id=1, source_target_pairs={{0,16},{16,32},{32,48},{48,64},{64,80},{80,96},{96,112},{112,128},... | collective-permute-start | bytes 169352 | tf_op jit(solution)/shard_map/ppermute | solution.py:432
  77.5 7.5 %collective-permute-start.5 = (f32[3,112,42]{2,1,0:T(8,128)S(1)}, f32[3,112,42]{2,1,0:T(8,128)S(1)}, u32[]{:S(2)}, u32[]{:S(2)}) collective-permute-start(f32[3,112,42]{2,1,0:T(8,128)S(1)} %get-tuple-element.32), channel_id=1, source_target_pairs={{16,0},{32,16},{48,32},{64,48},{80,64},{96,80},{112,96},{128,112},... | collective-permute-start | bytes 169352 | tf_op jit(solution)/shard_map/ppermute | solution.py:435
  85.0 1.4 %collective-permute-done.4 = f32[3,112,42]{2,1,0:T(8,128)S(1)} collective-permute-done((f32[3,112,42]{2,1,0:T(8,128)S(1)}, f32[3,112,42]{2,1,0:T(8,128)S(1)}, u32[]{:S(2)}, u32[]{:S(2)}) %collective-permute-start.4) | collective-permute-done | bytes 56480 | tf_op jit(solution)/shard_map/ppermute | solution.py:432
  86.4 1.5 %collective-permute-done.5 = f32[3,112,42]{2,1,0:T(8,128)S(1)} collective-permute-done((f32[3,112,42]{2,1,0:T(8,128)S(1)}, f32[3,112,42]{2,1,0:T(8,128)S(1)}, u32[]{:S(2)}, u32[]{:S(2)}) %collective-permute-start.5) | collective-permute-done | bytes 56480 | tf_op jit(solution)/shard_map/ppermute | solution.py:435
  88.9 2.1 %collective-permute-start.7 = (f32[3,34,212]{2,1,0:T(8,128)S(1)}, f32[3,34,212]{2,1,0:T(8,128)S(1)}, u32[]{:S(2)}, u32[]{:S(2)}) collective-permute-start(f32[3,34,212]{2,1,0:T(8,128)S(1)} %get-tuple-element.27), channel_id=1, source_target_pairs={{1,0},{2,1},{3,2},{4,3},{5,4},{6,5},{7,6},{8,7},{9,8},{10,9},{11,1... | collective-permute-start | bytes 259496 | tf_op jit(solution)/shard_map/ppermute | solution.py:26
  91.2 2.3 %collective-permute-start.6 = (f32[3,34,212]{2,1,0:T(8,128)S(1)}, f32[3,34,212]{2,1,0:T(8,128)S(1)}, u32[]{:S(2)}, u32[]{:S(2)}) collective-permute-start(f32[3,34,212]{2,1,0:T(8,128)S(1)} %get-tuple-element.28), channel_id=1, source_target_pairs={{0,1},{1,2},{2,3},{3,4},{4,5},{5,6},{6,7},{7,8},{8,9},{9,10},{10,1... | collective-permute-start | bytes 259496 | tf_op jit(solution)/shard_map/ppermute | solution.py:26
  93.5 6.0 %collective-permute-done.6 = f32[3,34,212]{2,1,0:T(8,128)S(1)} collective-permute-done((f32[3,34,212]{2,1,0:T(8,128)S(1)}, f32[3,34,212]{2,1,0:T(8,128)S(1)}, u32[]{:S(2)}, u32[]{:S(2)}) %collective-permute-start.6) | collective-permute-done | bytes 86528 | tf_op jit(solution)/shard_map/ppermute | solution.py:26
  100.6 5.9 %section_step.3 = (f32[112,128]{1,0:T(8,128)}, f32[112,128]{1,0:T(8,128)}, f32[112,128]{1,0:T(8,128)}, f32[112,128]{1,0:T(8,128)}, f32[112,128]{1,0:T(8,128)}) custom-call(f32[184,256]{1,0:T(8,128)} %get-tuple-element.23.refs_0_, f32[184,256]{1,0:T(8,128)} %get-tuple-element.22.refs_1_, f32[184,256]{1,0:T(8,128)} %get-tuple-element.21.refs_2_, ...), custom_call_target="tpu_custom_call" | custom-call | tf_op jit(solution)/shard_map/section_step/pallas_call | solution.py:399
  (30 shorter events, 12.9 us)
Async XLA Ops:
  7.3 21.0 %collective-permute-start = (f32[6,112,84]{2,1,0:T(8,128)S(1)}, f32[6,112,84]{2,1,0:T(8,128)S(1)}, u32[]{:S(2)}, u32[]{:S(2)}) collective-permute-start(f32[6,112,84]{2,1,0:T(8,128)S(1)} %get-tuple-element.29), channel_id=1, source_target_pairs={{0,16},{16,32},{32,48},{48,64},{64,80},{80,96},{96,112},{112,128},... | collective-permute-start | bytes 677384 | tf_op jit(solution)/shard_map/ppermute | solution.py:432
  11.1 18.4 %collective-permute-start.1 = (f32[6,112,84]{2,1,0:T(8,128)S(1)}, f32[6,112,84]{2,1,0:T(8,128)S(1)}, u32[]{:S(2)}, u32[]{:S(2)}) collective-permute-start(f32[6,112,84]{2,1,0:T(8,128)S(1)} %get-tuple-element.30), channel_id=1, source_target_pairs={{16,0},{32,16},{48,32},{64,48},{80,64},{96,80},{112,96},{128,112},... | collective-permute-start | bytes 677384 | tf_op jit(solution)/shard_map/ppermute | solution.py:435
  31.0 12.5 %collective-permute-start.3 = (f32[6,68,296]{2,1,0:T(8,128)S(1)}, f32[6,68,296]{2,1,0:T(8,128)}, u32[]{:S(2)}, u32[]{:S(2)}) collective-permute-start(f32[6,68,296]{2,1,0:T(8,128)S(1)} %get-tuple-element.19), channel_id=1, source_target_pairs={{1,0},{2,1},{3,2},{4,3},{5,4},{6,5},{7,6},{8,7},{9,8},{10,9},{11,1... | collective-permute-start | bytes 1449224 | tf_op jit(solution)/shard_map/ppermute | solution.py:26
  35.4 14.2 %collective-permute-start.2 = (f32[6,68,296]{2,1,0:T(8,128)S(1)}, f32[6,68,296]{2,1,0:T(8,128)}, u32[]{:S(2)}, u32[]{:S(2)}) collective-permute-start(f32[6,68,296]{2,1,0:T(8,128)S(1)} %get-tuple-element.20), channel_id=1, source_target_pairs={{0,1},{1,2},{2,3},{3,4},{4,5},{5,6},{6,7},{7,8},{8,9},{9,10},{10,1... | collective-permute-start | bytes 1449224 | tf_op jit(solution)/shard_map/ppermute | solution.py:26
  38.6 12.2 %copy-start = (f32[6,112,128]{2,1,0:T(8,128)S(1)}, f32[6,112,128]{2,1,0:T(8,128)}, u32[]{:S(2)}) copy-start(f32[6,112,128]{2,1,0:T(8,128)} %stacked.1) | copy-start | bytes 1032196
  74.3 25.2 %copy-start.1 = (f32[3,112,128]{2,1,0:T(8,128)S(1)}, f32[3,112,128]{2,1,0:T(8,128)}, u32[]{:S(2)}) copy-start(f32[3,112,128]{2,1,0:T(8,128)} %get-tuple-element.12) | copy-start | bytes 516100
  75.5 10.9 %collective-permute-start.4 = (f32[3,112,42]{2,1,0:T(8,128)S(1)}, f32[3,112,42]{2,1,0:T(8,128)S(1)}, u32[]{:S(2)}, u32[]{:S(2)}) collective-permute-start(f32[3,112,42]{2,1,0:T(8,128)S(1)} %get-tuple-element.31), channel_id=1, source_target_pairs={{0,16},{16,32},{32,48},{48,64},{64,80},{80,96},{96,112},{112,128},... | collective-permute-start | bytes 169352 | tf_op jit(solution)/shard_map/ppermute | solution.py:432
  77.5 10.4 %collective-permute-start.5 = (f32[3,112,42]{2,1,0:T(8,128)S(1)}, f32[3,112,42]{2,1,0:T(8,128)S(1)}, u32[]{:S(2)}, u32[]{:S(2)}) collective-permute-start(f32[3,112,42]{2,1,0:T(8,128)S(1)} %get-tuple-element.32), channel_id=1, source_target_pairs={{16,0},{32,16},{48,32},{64,48},{80,64},{96,80},{112,96},{128,112},... | collective-permute-start | bytes 169352 | tf_op jit(solution)/shard_map/ppermute | solution.py:435
  88.9 4.6 %collective-permute-start.7 = (f32[3,34,212]{2,1,0:T(8,128)S(1)}, f32[3,34,212]{2,1,0:T(8,128)S(1)}, u32[]{:S(2)}, u32[]{:S(2)}) collective-permute-start(f32[3,34,212]{2,1,0:T(8,128)S(1)} %get-tuple-element.27), channel_id=1, source_target_pairs={{1,0},{2,1},{3,2},{4,3},{5,4},{6,5},{7,6},{8,7},{9,8},{10,9},{11,1... | collective-permute-start | bytes 259496 | tf_op jit(solution)/shard_map/ppermute | solution.py:26
  91.2 8.3 %collective-permute-start.6 = (f32[3,34,212]{2,1,0:T(8,128)S(1)}, f32[3,34,212]{2,1,0:T(8,128)S(1)}, u32[]{:S(2)}, u32[]{:S(2)}) collective-permute-start(f32[3,34,212]{2,1,0:T(8,128)S(1)} %get-tuple-element.28), channel_id=1, source_target_pairs={{0,1},{1,2},{2,3},{3,4},{4,5},{5,6},{6,7},{7,8},{8,9},{9,10},{10,1... | collective-permute-start | bytes 259496 | tf_op jit(solution)/shard_map/ppermute | solution.py:26

commit v14 on v11

--- a/solution.py
+++ b/solution.py
@@ -408,18 +408,18 @@
 
 def halo_box(fields, wide_x, wide_y, place, count, padded_shape):
     lon_count = lax.axis_size("lon")
+    above = passed_along(fields[:, -wide_y:], "lat", 1)
+    below = passed_along(fields[:, :wide_y], "lat", -1)
+    above = jnp.where(place == 0, fields[:, wide_y - 1 :: -1], above)
+    below = jnp.where(place == count - 1, fields[:, : -wide_y - 1 : -1], below)
+    tall = jnp.concatenate([above, fields, below], axis=1)
     west = lax.ppermute(
-        fields[:, :, -wide_x:], "lon", [(i, (i + 1) % lon_count) for i in range(lon_count)]
+        tall[:, :, -wide_x:], "lon", [(i, (i + 1) % lon_count) for i in range(lon_count)]
     )
     east = lax.ppermute(
-        fields[:, :, :wide_x], "lon", [((i + 1) % lon_count, i) for i in range(lon_count)]
-    )
-    wide = jnp.concatenate([west, fields, east], axis=2)
-    above = passed_along(wide[:, -wide_y:], "lat", 1)
-    below = passed_along(wide[:, :wide_y], "lat", -1)
-    above = jnp.where(place == 0, wide[:, wide_y - 1 :: -1], above)
-    below = jnp.where(place == count - 1, wide[:, : -wide_y - 1 : -1], below)
-    box = jnp.concatenate([above, wide, below], axis=1)
+        tall[:, :, :wide_x], "lon", [((i + 1) % lon_count, i) for i in range(lon_count)]
+    )
+    box = jnp.concatenate([west, tall, east], axis=2)
     return pad_to(box, padded_shape)
 
 

time: 105 us -> 110 us (1.048)
  starting transfers between devices: 34.9 us -> 39 us
  waiting for transfers between devices: 26 us -> 29.5 us
  other arithmetic: 9.37 us -> 7.02 us
    ppermute x4, waiting for transfers between devices: 10.2 us -> 16.9 us  [the longest x2 10.8 us: halo_box(): lax.ppermute(tall[:, :, -wide_x:], 'lon', [(i, (i + 1) % lon_count) for i...]
    ppermute x4, starting transfers between devices: 10.6 us -> 14.4 us  [passed_along(): return lax.ppermute(x, axis, pairs)]
    ppermute x4, waiting for transfers between devices: 15.8 us -> 12.6 us  [passed_along(): return lax.ppermute(x, axis, pairs)]
    select_n x4, other arithmetic: 2.37 us -> 0.07 us  [the longest x2 0.03 us: halo_box(): below = jnp.where(place == count - 1, fields[:, :-wide_y - 1:-1], below)]
    ppermute x0 -> x2, local copies, waits for them, and re-layouts: none -> 1.58 us  [the longest x1 1.31 us: halo_box(): lax.ppermute(tall[:, :, -wide_x:], 'lon', [(i, (i + 1) % lon_count) for i...]
    unnamed x22 -> x18, local copies, waits for them, and re-layouts: 4.07 us -> 3.32 us
  transfers between devices with their start and end apart: 8 -> 8, of which waited for: 7 -> 7; matrix products, arithmetic and copies ran while one was open for 3% -> 1% of each run, Pallas kernels for 0% -> 0%
where the time goes in v14:
time: 110 us; the launch traced here: 109 us
  starting transfers between devices  39 us (35%)
  waiting for transfers between devices  29.5 us (27%)
  Pallas kernels  22.9 us (21%)
  local copies, waits for them, and re-layouts  10 us (9%)
  other arithmetic  7.02 us (6%)
    ppermute x2, starting transfers between devices, halo_box(): lax.ppermute(tall[:, :, :wide_x], 'lon', [((i + 1) % lon_count, i) for i...  20.8 us
    ppermute x4, starting transfers between devices, passed_along(): return lax.ppermute(x, axis, pairs)  14.4 us
    ppermute x4, waiting for transfers between devices, passed_along(): return lax.ppermute(x, axis, pairs)  12.6 us
    pallas_call x2, Pallas kernels, section_step(): pl.pallas_call(lambda *refs: section_kernel(*refs, first_row=first_row, u...  11.8 us
    pallas_call x1, Pallas kernels, ring_step(): pl.pallas_call(lambda *refs: ring_kernel(*refs, first_row=first_row, used...  11.1 us
    ppermute x2, waiting for transfers between devices, halo_box(): lax.ppermute(tall[:, :, -wide_x:], 'lon', [(i, (i + 1) % lon_count) for i...  10.8 us
    ppermute x2, waiting for transfers between devices, halo_box(): lax.ppermute(tall[:, :, :wide_x], 'lon', [((i + 1) % lon_count, i) for i...  6.09 us
    ppermute x2, starting transfers between devices, halo_box(): lax.ppermute(tall[:, :, -wide_x:], 'lon', [(i, (i + 1) % lon_count) for i...  3.84 us
  transfers between devices with their start and end apart: 8, of which 7 were waited for; matrix products, arithmetic and copies ran while one was open for 1% of the time, Pallas kernels for 0%

profile of v14, /device:TPU:2, one launch (start us, length us, event | category | flops | bytes accessed | tf_op | source)
XLA Modules:
  0.0 109.3 jit_solution(11592535044679715996)
XLA Ops:
  5.4 1.1 scatter_custom_fusion
  6.5 4.3 %collective-permute-start.1 = (f32[6,68,128]{2,1,0:T(8,128)S(1)}, f32[6,68,128]{2,1,0:T(8,128)S(1)}, u32[]{:S(2)}, u32[]{:S(2)}) collective-permute-start(f32[6,68,128]{2,1,0:T(8,128)S(1)} %get-tuple-element.35), channel_id=1, source_target_pairs={{1,0},{2,1},{3,2},{4,3},{5,4},{6,5},{7,6},{8,7},{9,8},{10,9},{11,1... | collective-permute-start | bytes 626696 | tf_op jit(solution)/shard_map/ppermute | solution.py:26
  10.9 1.9 %collective-permute-start = (f32[6,68,128]{2,1,0:T(8,128)S(1)}, f32[6,68,128]{2,1,0:T(8,128)S(1)}, u32[]{:S(2)}, u32[]{:S(2)}) collective-permute-start(f32[6,68,128]{2,1,0:T(8,128)S(1)} %get-tuple-element.36), channel_id=1, source_target_pairs={{0,1},{1,2},{2,3},{3,4},{4,5},{5,6},{6,7},{7,8},{8,9},{9,10},{10,1... | collective-permute-start | bytes 626696 | tf_op jit(solution)/shard_map/ppermute | solution.py:26
  13.3 1.0 collective-permute-done.1
  14.3 5.9 %collective-permute-done = f32[6,68,128]{2,1,0:T(8,128)S(1)} collective-permute-done((f32[6,68,128]{2,1,0:T(8,128)S(1)}, f32[6,68,128]{2,1,0:T(8,128)S(1)}, u32[]{:S(2)}, u32[]{:S(2)}) %collective-permute-start) | collective-permute-done | bytes 208928 | tf_op jit(solution)/shard_map/ppermute | solution.py:26
  20.9 13.3 %collective-permute-start.3 = (f32[6,248,84]{1,2,0:T(8,128)S(1)}, f32[6,248,84]{1,2,0:T(8,128)S(1)}, u32[]{:S(2)}, u32[]{:S(2)}) collective-permute-start(f32[6,248,84]{1,2,0:T(8,128)S(1)} %copy.13), channel_id=1, source_target_pairs={{16,0},{32,16},{48,32},{64,48},{80,64},{96,80},{112,96},{128,112},... | collective-permute-start | bytes 1499912 | tf_op jit(solution)/shard_map/ppermute | solution.py:419
  34.5 1.9 %collective-permute-start.2 = (f32[6,248,84]{1,2,0:T(8,128)S(1)}, f32[6,248,84]{1,2,0:T(8,128)}, u32[]{:S(2)}, u32[]{:S(2)}) collective-permute-start(f32[6,248,84]{1,2,0:T(8,128)S(1)} %copy.12), channel_id=1, source_target_pairs={{0,16},{16,32},{32,48},{48,64},{64,80},{80,96},{96,112},{112,128},... | collective-permute-start | bytes 1499912 | tf_op jit(solution)/shard_map/ppermute | solution.py:416
  36.4 4.6 %collective-permute-done.3 = f32[6,248,84]{1,2,0:T(8,128)S(1)} collective-permute-done((f32[6,248,84]{1,2,0:T(8,128)S(1)}, f32[6,248,84]{1,2,0:T(8,128)S(1)}, u32[]{:S(2)}, u32[]{:S(2)}) %collective-permute-start.3) | collective-permute-done | bytes 500000 | tf_op jit(solution)/shard_map/ppermute | solution.py:419
  41.3 8.1 %collective-permute-done.2 = f32[6,248,84]{1,2,0:T(8,128)} collective-permute-done((f32[6,248,84]{1,2,0:T(8,128)S(1)}, f32[6,248,84]{1,2,0:T(8,128)}, u32[]{:S(2)}, u32[]{:S(2)}) %collective-permute-start.2) | collective-permute-done | bytes 500000 | tf_op jit(solution)/shard_map/ppermute | solution.py:416
  49.4 1.3 %copy.14 = f32[6,248,84]{2,1,0:T(8,128)S(1)} copy(f32[6,248,84]{1,2,0:T(8,128)} %collective-permute-done.2) | data formatting | bytes 999936 | tf_op jit(solution)/shard_map/ppermute | solution.py:416
  50.8 0.9 select_maximum_fusion
  51.6 1.5 %slice_bitcast_fusion = (f32[248,384]{1,0:T(8,128)}, f32[248,384]{1,0:T(8,128)}, f32[248,384]{1,0:T(8,128)}, f32[248,384]{1,0:T(8,128)}, f32[248,384]{1,0:T(8,128)}, /*index=5*/f32[248,384]{1,0:T(8,128)}) fusion(f32[6,248,384]{2,1,0:T(8,128)S(1)} %select_maximum_fusion), kind=kLoop, calls=%fused_computation.32 | loop fusion | bytes 4571136 | tf_op jit(solution)/shard_map/squeeze | solution.py:502
  53.1 11.1 %ring_step.1 = (f32[184,256]{1,0:T(8,128)}, f32[184,256]{1,0:T(8,128)}, f32[184,256]{1,0:T(8,128)}, f32[184,256]{1,0:T(8,128)}, f32[184,256]{1,0:T(8,128)}) custom-call(f32[248,384]{1,0:T(8,128)} %get-tuple-element.26.refs_0_, f32[248,384]{1,0:T(8,128)} %get-tuple-element.25.refs_1_, f32[248,384]{1,0:T(8,128)} %get-tuple-element.24.refs_2_, ...), custom_call_target="tpu_custom_call" | custom-call | tf_op jit(solution)/shard_map/ring_step/pallas_call | solution.py:380
  64.2 1.2 %pad_maximum_fusion.1 = f32[3,184,256]{2,1,0:T(8,128)S(1)} fusion(f32[1,184,256]{2,1,0:T(8,128)} %bitcast.55, f32[1,184,256]{2,1,0:T(8,128)} %bitcast.53, f32[1,184,256]{2,1,0:T(8,128)} %bitcast.51), kind=kLoop, calls=%fused_computation.29 | loop fusion | flops 282624 | bytes 1130496 | tf_op jit(solution)/shard_map/stack | solution.py:505
  67.0 5.9 %section_step.2 = (f32[112,128]{1,0:T(8,128)}, f32[112,128]{1,0:T(8,128)}, f32[112,128]{1,0:T(8,128)}, f32[112,128]{1,0:T(8,128)}, f32[112,128]{1,0:T(8,128)}) custom-call(f32[184,256]{1,0:T(8,128)} %get-tuple-element.34.refs_0_, f32[184,256]{1,0:T(8,128)} %get-tuple-element.33.refs_1_, f32[184,256]{1,0:T(8,128)} %get-tuple-element.32.refs_2_, ...), custom_call_target="tpu_custom_call" | custom-call | tf_op jit(solution)/shard_map/section_step/pallas_call | solution.py:397
  73.8 6.2 %collective-permute-start.5 = (f32[3,34,128]{2,1,0:T(8,128)S(1)}, f32[3,34,128]{2,1,0:T(8,128)S(1)}, u32[]{:S(2)}, u32[]{:S(2)}) collective-permute-start(f32[3,34,128]{2,1,0:T(8,128)S(1)} %get-tuple-element.39), channel_id=1, source_target_pairs={{1,0},{2,1},{3,2},{4,3},{5,4},{6,5},{7,6},{8,7},{9,8},{10,9},{11,1... | collective-permute-start | bytes 156680 | tf_op jit(solution)/shard_map/ppermute | solution.py:26
  80.1 1.9 %collective-permute-start.4 = (f32[3,34,128]{2,1,0:T(8,128)S(1)}, f32[3,34,128]{2,1,0:T(8,128)S(1)}, u32[]{:S(2)}, u32[]{:S(2)}) collective-permute-start(f32[3,34,128]{2,1,0:T(8,128)S(1)} %get-tuple-element.40), channel_id=1, source_target_pairs={{0,1},{1,2},{2,3},{3,4},{4,5},{5,6},{6,7},{7,8},{8,9},{9,10},{10,1... | collective-permute-start | bytes 156680 | tf_op jit(solution)/shard_map/ppermute | solution.py:26
  82.0 5.7 %collective-permute-done.4 = f32[3,34,128]{2,1,0:T(8,128)S(1)} collective-permute-done((f32[3,34,128]{2,1,0:T(8,128)S(1)}, f32[3,34,128]{2,1,0:T(8,128)S(1)}, u32[]{:S(2)}, u32[]{:S(2)}) %collective-permute-start.4) | collective-permute-done | bytes 52256 | tf_op jit(solution)/shard_map/ppermute | solution.py:26
  87.7 0.9 pad_maximum_fusion.2
  88.8 1.9 %collective-permute-start.6 = (f32[3,180,42]{2,1,0:T(8,128)S(1)}, f32[3,180,42]{2,1,0:T(8,128)S(1)}, u32[]{:S(2)}, u32[]{:S(2)}) collective-permute-start(f32[3,180,42]{2,1,0:T(8,128)S(1)} %get-tuple-element.37), channel_id=1, source_target_pairs={{0,16},{16,32},{32,48},{48,64},{64,80},{80,96},{96,112},{112,128},... | collective-permute-start | bytes 272168 | tf_op jit(solution)/shard_map/ppermute | solution.py:416
  90.7 7.5 %collective-permute-start.7 = (f32[3,180,42]{2,1,0:T(8,128)S(1)}, f32[3,180,42]{2,1,0:T(8,128)S(1)}, u32[]{:S(2)}, u32[]{:S(2)}) collective-permute-start(f32[3,180,42]{2,1,0:T(8,128)S(1)} %get-tuple-element.38), channel_id=1, source_target_pairs={{16,0},{32,16},{48,32},{64,48},{80,64},{96,80},{112,96},{128,112},... | collective-permute-start | bytes 272168 | tf_op jit(solution)/shard_map/ppermute | solution.py:419
  98.2 2.6 %collective-permute-done.6 = f32[3,180,42]{2,1,0:T(8,128)S(1)} collective-permute-done((f32[3,180,42]{2,1,0:T(8,128)S(1)}, f32[3,180,42]{2,1,0:T(8,128)S(1)}, u32[]{:S(2)}, u32[]{:S(2)}) %collective-permute-start.6) | collective-permute-done | bytes 90752 | tf_op jit(solution)/shard_map/ppermute | solution.py:416
  100.9 1.5 %collective-permute-done.7 = f32[3,180,42]{2,1,0:T(8,128)S(1)} collective-permute-done((f32[3,180,42]{2,1,0:T(8,128)S(1)}, f32[3,180,42]{2,1,0:T(8,128)S(1)}, u32[]{:S(2)}, u32[]{:S(2)}) %collective-permute-start.7) | collective-permute-done | bytes 90752 | tf_op jit(solution)/shard_map/ppermute | solution.py:419
  103.5 5.9 %section_step.3 = (f32[112,128]{1,0:T(8,128)}, f32[112,128]{1,0:T(8,128)}, f32[112,128]{1,0:T(8,128)}, f32[112,128]{1,0:T(8,128)}, f32[112,128]{1,0:T(8,128)}) custom-call(f32[184,256]{1,0:T(8,128)} %get-tuple-element.31.refs_0_, f32[184,256]{1,0:T(8,128)} %get-tuple-element.30.refs_1_, f32[184,256]{1,0:T(8,128)} %get-tuple-element.29.refs_2_, ...), custom_call_target="tpu_custom_call" | custom-call | tf_op jit(solution)/shard_map/section_step/pallas_call | solution.py:397
  (50 shorter events, 10.2 us)
Async XLA Ops:
  6.5 13.9 %copy-start = (f32[14336]{0:T(1024)}, f32[14336]{0:T(1024)S(1)}, u32[]{:S(2)}) copy-start(f32[14336]{0:T(1024)S(1)} %scatter_custom_fusion) | copy-start | bytes 172036
  6.5 7.8 %collective-permute-start.1 = (f32[6,68,128]{2,1,0:T(8,128)S(1)}, f32[6,68,128]{2,1,0:T(8,128)S(1)}, u32[]{:S(2)}, u32[]{:S(2)}) collective-permute-start(f32[6,68,128]{2,1,0:T(8,128)S(1)} %get-tuple-element.35), channel_id=1, source_target_pairs={{1,0},{2,1},{3,2},{4,3},{5,4},{6,5},{7,6},{8,7},{9,8},{10,9},{11,1... | collective-permute-start | bytes 626696 | tf_op jit(solution)/shard_map/ppermute | solution.py:26
  10.9 9.4 %collective-permute-start = (f32[6,68,128]{2,1,0:T(8,128)S(1)}, f32[6,68,128]{2,1,0:T(8,128)S(1)}, u32[]{:S(2)}, u32[]{:S(2)}) collective-permute-start(f32[6,68,128]{2,1,0:T(8,128)S(1)} %get-tuple-element.36), channel_id=1, source_target_pairs={{0,1},{1,2},{2,3},{3,4},{4,5},{5,6},{6,7},{7,8},{8,9},{9,10},{10,1... | collective-permute-start | bytes 626696 | tf_op jit(solution)/shard_map/ppermute | solution.py:26
  20.9 20.1 %collective-permute-start.3 = (f32[6,248,84]{1,2,0:T(8,128)S(1)}, f32[6,248,84]{1,2,0:T(8,128)S(1)}, u32[]{:S(2)}, u32[]{:S(2)}) collective-permute-start(f32[6,248,84]{1,2,0:T(8,128)S(1)} %copy.13), channel_id=1, source_target_pairs={{16,0},{32,16},{48,32},{64,48},{80,64},{96,80},{112,96},{128,112},... | collective-permute-start | bytes 1499912 | tf_op jit(solution)/shard_map/ppermute | solution.py:419
  34.5 15.0 %collective-permute-start.2 = (f32[6,248,84]{1,2,0:T(8,128)S(1)}, f32[6,248,84]{1,2,0:T(8,128)}, u32[]{:S(2)}, u32[]{:S(2)}) collective-permute-start(f32[6,248,84]{1,2,0:T(8,128)S(1)} %copy.12), channel_id=1, source_target_pairs={{0,16},{16,32},{32,48},{48,64},{64,80},{80,96},{96,112},{112,128},... | collective-permute-start | bytes 1499912 | tf_op jit(solution)/shard_map/ppermute | solution.py:416
  64.2 1.6 %copy-start.1 = (f32[184,256]{1,0:T(8,128)S(1)}, f32[184,256]{1,0:T(8,128)}, u32[]{:S(2)}) copy-start(f32[184,256]{1,0:T(8,128)} %get-tuple-element.13) | copy-start | bytes 565252
  64.2 1.6 %copy-start.2 = (f32[184,256]{1,0:T(8,128)S(1)}, f32[184,256]{1,0:T(8,128)}, u32[]{:S(2)}) copy-start(f32[184,256]{1,0:T(8,128)} %get-tuple-element.14) | copy-start | bytes 565252
  64.2 1.6 %copy-start.3 = (f32[184,256]{1,0:T(8,128)S(1)}, f32[184,256]{1,0:T(8,128)}, u32[]{:S(2)}) copy-start(f32[184,256]{1,0:T(8,128)} %get-tuple-element.15) | copy-start | bytes 565252
  72.9 29.4 %copy-start.4 = (f32[112,128]{1,0:T(8,128)S(1)}, f32[112,128]{1,0:T(8,128)}, u32[]{:S(2)}) copy-start(f32[112,128]{1,0:T(8,128)} %get-tuple-element.18) | copy-start | bytes 172036
  72.9 29.4 %copy-start.5 = (f32[112,128]{1,0:T(8,128)S(1)}, f32[112,128]{1,0:T(8,128)}, u32[]{:S(2)}) copy-start(f32[112,128]{1,0:T(8,128)} %get-tuple-element.19) | copy-start | bytes 172036
  72.9 29.4 %copy-start.6 = (f32[112,128]{1,0:T(8,128)S(1)}, f32[112,128]{1,0:T(8,128)}, u32[]{:S(2)}) copy-start(f32[112,128]{1,0:T(8,128)} %get-tuple-element.20) | copy-start | bytes 172036
  73.8 8.2 %collective-permute-start.5 = (f32[3,34,128]{2,1,0:T(8,128)S(1)}, f32[3,34,128]{2,1,0:T(8,128)S(1)}, u32[]{:S(2)}, u32[]{:S(2)}) collective-permute-start(f32[3,34,128]{2,1,0:T(8,128)S(1)} %get-tuple-element.39), channel_id=1, source_target_pairs={{1,0},{2,1},{3,2},{4,3},{5,4},{6,5},{7,6},{8,7},{9,8},{10,9},{11,1... | collective-permute-start | bytes 156680 | tf_op jit(solution)/shard_map/ppermute | solution.py:26
  80.1 7.7 %collective-permute-start.4 = (f32[3,34,128]{2,1,0:T(8,128)S(1)}, f32[3,34,128]{2,1,0:T(8,128)S(1)}, u32[]{:S(2)}, u32[]{:S(2)}) collective-permute-start(f32[3,34,128]{2,1,0:T(8,128)S(1)} %get-tuple-element.40), channel_id=1, source_target_pairs={{0,1},{1,2},{2,3},{3,4},{4,5},{5,6},{6,7},{7,8},{8,9},{9,10},{10,1... | collective-permute-start | bytes 156680 | tf_op jit(solution)/shard_map/ppermute | solution.py:26
  88.8 12.1 %collective-permute-start.6 = (f32[3,180,42]{2,1,0:T(8,128)S(1)}, f32[3,180,42]{2,1,0:T(8,128)S(1)}, u32[]{:S(2)}, u32[]{:S(2)}) collective-permute-start(f32[3,180,42]{2,1,0:T(8,128)S(1)} %get-tuple-element.37), channel_id=1, source_target_pairs={{0,16},{16,32},{32,48},{48,64},{64,80},{80,96},{96,112},{112,128},... | collective-permute-start | bytes 272168 | tf_op jit(solution)/shard_map/ppermute | solution.py:416
  90.7 11.6 %collective-permute-start.7 = (f32[3,180,42]{2,1,0:T(8,128)S(1)}, f32[3,180,42]{2,1,0:T(8,128)S(1)}, u32[]{:S(2)}, u32[]{:S(2)}) collective-permute-start(f32[3,180,42]{2,1,0:T(8,128)S(1)} %get-tuple-element.38), channel_id=1, source_target_pairs={{16,0},{32,16},{48,32},{64,48},{80,64},{96,80},{112,96},{128,112},... | collective-permute-start | bytes 272168 | tf_op jit(solution)/shard_map/ppermute | solution.py:419

commit v15 on v11

--- a/solution.py
+++ b/solution.py
@@ -11,7 +11,7 @@
 TIME_STEP = 0.1
 WINDOW_LON = 40
 WINDOW_LAT = 32
-PCR_STEPS = 6
+PCR_STEPS = (5, 6)
 
 
 def shifted(block, axis, distance):
@@ -192,7 +192,7 @@
     length = rights.shape[along_axis]
     position = lax.broadcasted_iota(jnp.int32, rights.shape, along_axis)
     stride = 1
-    for _ in range(PCR_STEPS):
+    for _ in range(PCR_STEPS[along_axis]):
         def from_lower(values, fill):
             return jnp.where(position >= stride, pltpu.roll(values, stride, along_axis), fill)
 

time: 105 us -> 104 us (level)
  no operation moved by 1% of the time
where the time goes in v15:
time: 104 us; the launch traced here: 103 us
  starting transfers between devices  34.9 us (34%)
  waiting for transfers between devices  26 us (25%)
  Pallas kernels  22.1 us (21%)
  local copies, waits for them, and re-layouts  9.52 us (9%)
  other arithmetic  9.37 us (9%)
    ppermute x2, starting transfers between devices, halo_box(): lax.ppermute(fields[:, :, :wide_x], 'lon', [((i + 1) % lon_count, i) for...  18.6 us
    ppermute x4, waiting for transfers between devices, passed_along(): return lax.ppermute(x, axis, pairs)  15.8 us
    pallas_call x2, Pallas kernels, section_step(): pl.pallas_call(lambda *refs: section_kernel(*refs, first_row=first_row, u...  11.3 us
    pallas_call x1, Pallas kernels, ring_step(): pl.pallas_call(lambda *refs: ring_kernel(*refs, first_row=first_row, used...  10.8 us
    ppermute x4, starting transfers between devices, passed_along(): return lax.ppermute(x, axis, pairs)  10.6 us
    ppermute x2, waiting for transfers between devices, halo_box(): lax.ppermute(fields[:, :, -wide_x:], 'lon', [(i, (i + 1) % lon_count) for...  7.56 us
    ppermute x2, starting transfers between devices, halo_box(): lax.ppermute(fields[:, :, -wide_x:], 'lon', [(i, (i + 1) % lon_count) for...  5.74 us
    unnamed x22, local copies, waits for them, and re-layouts  4.07 us
  transfers between devices with their start and end apart: 8, of which 7 were waited for; matrix products, arithmetic and copies ran while one was open for 3% of the time, Pallas kernels for 0%

profile of v15, /device:TPU:2, one launch (start us, length us, event | category | flops | bytes accessed | tf_op | source)
XLA Modules:
  0.0 103.0 jit_solution(14049383134133431832)
XLA Ops:
  5.4 1.1 %scatter_custom_fusion = f32[14336]{0:T(1024)S(1)} fusion(s32[64]{0:T(128)S(1)} %fusion.22, f32[64]{0:T(128)} %bitcast.66, f32[]{:T(128)} %constant.3.clone.1), kind=kCustom, calls=%fused_computation.60 | custom fusion | flops 64 | bytes 57856 | tf_op jit(solution)/shard_map/scatter-add | solution.py:487
  6.7 3.8 %collective-permute-start = (f32[6,112,84]{2,1,0:T(8,128)S(1)}, f32[6,112,84]{2,1,0:T(8,128)S(1)}, u32[]{:S(2)}, u32[]{:S(2)}) collective-permute-start(f32[6,112,84]{2,1,0:T(8,128)S(1)} %get-tuple-element.37), channel_id=1, source_target_pairs={{0,16},{16,32},{32,48},{48,64},{64,80},{80,96},{96,112},{112,128},... | collective-permute-start | bytes 677384 | tf_op jit(solution)/shard_map/ppermute | solution.py:411
  10.5 11.1 %collective-permute-start.1 = (f32[6,112,84]{2,1,0:T(8,128)S(1)}, f32[6,112,84]{2,1,0:T(8,128)S(1)}, u32[]{:S(2)}, u32[]{:S(2)}) collective-permute-start(f32[6,112,84]{2,1,0:T(8,128)S(1)} %get-tuple-element.38), channel_id=1, source_target_pairs={{16,0},{32,16},{48,32},{64,48},{80,64},{96,80},{112,96},{128,112},... | collective-permute-start | bytes 677384 | tf_op jit(solution)/shard_map/ppermute | solution.py:414
  21.6 6.1 %collective-permute-done = f32[6,112,84]{2,1,0:T(8,128)S(1)} collective-permute-done((f32[6,112,84]{2,1,0:T(8,128)S(1)}, f32[6,112,84]{2,1,0:T(8,128)S(1)}, u32[]{:S(2)}, u32[]{:S(2)}) %collective-permute-start) | collective-permute-done | bytes 225824 | tf_op jit(solution)/shard_map/ppermute | solution.py:411
  27.7 1.2 %collective-permute-done.1 = f32[6,112,84]{2,1,0:T(8,128)S(1)} collective-permute-done((f32[6,112,84]{2,1,0:T(8,128)S(1)}, f32[6,112,84]{2,1,0:T(8,128)S(1)}, u32[]{:S(2)}, u32[]{:S(2)}) %collective-permute-start.1) | collective-permute-done | bytes 225824 | tf_op jit(solution)/shard_map/ppermute | solution.py:414
  30.1 4.4 %collective-permute-start.3 = (f32[6,68,296]{2,1,0:T(8,128)S(1)}, f32[6,68,296]{2,1,0:T(8,128)}, u32[]{:S(2)}, u32[]{:S(2)}) collective-permute-start(f32[6,68,296]{2,1,0:T(8,128)S(1)} %get-tuple-element.27), channel_id=1, source_target_pairs={{1,0},{2,1},{3,2},{4,3},{5,4},{6,5},{7,6},{8,7},{9,8},{10,9},{11,1... | collective-permute-start | bytes 1449224 | tf_op jit(solution)/shard_map/ppermute | solution.py:26
  34.5 1.9 %collective-permute-start.2 = (f32[6,68,296]{2,1,0:T(8,128)S(1)}, f32[6,68,296]{2,1,0:T(8,128)}, u32[]{:S(2)}, u32[]{:S(2)}) collective-permute-start(f32[6,68,296]{2,1,0:T(8,128)S(1)} %get-tuple-element.28), channel_id=1, source_target_pairs={{0,1},{1,2},{2,3},{3,4},{4,5},{5,6},{6,7},{7,8},{8,9},{9,10},{10,1... | collective-permute-start | bytes 1449224 | tf_op jit(solution)/shard_map/ppermute | solution.py:26
  37.7 5.0 %collective-permute-done.3 = f32[6,68,296]{2,1,0:T(8,128)} collective-permute-done((f32[6,68,296]{2,1,0:T(8,128)S(1)}, f32[6,68,296]{2,1,0:T(8,128)}, u32[]{:S(2)}, u32[]{:S(2)}) %collective-permute-start.3) | collective-permute-done | bytes 483104 | tf_op jit(solution)/shard_map/ppermute | solution.py:26
  42.7 1.2 %broadcast_select_fusion = f32[6,68,296]{2,1,0:T(8,128)S(1)} fusion(f32[6,68,296]{2,1,0:T(8,128)S(1)} %rev.19, f32[6,68,296]{2,1,0:T(8,128)} %collective-permute-done.3, pred[]{:T(512)S(6)} %eq.5), kind=kLoop, calls=%fused_computation.38 | loop fusion | flops 120768 | bytes 1449217 | tf_op jit(solution)/shard_map/jit(_where)/select_n | solution.py:421
  43.9 4.9 %collective-permute-done.2 = f32[6,68,296]{2,1,0:T(8,128)} collective-permute-done((f32[6,68,296]{2,1,0:T(8,128)S(1)}, f32[6,68,296]{2,1,0:T(8,128)}, u32[]{:S(2)}, u32[]{:S(2)}) %collective-permute-start.2) | collective-permute-done | bytes 483104 | tf_op jit(solution)/shard_map/ppermute | solution.py:26
  48.7 1.2 %broadcast_select_fusion.1 = f32[6,68,296]{2,1,0:T(8,128)S(1)} fusion(f32[6,68,296]{2,1,0:T(8,128)S(1)} %rev.18, f32[6,68,296]{2,1,0:T(8,128)} %collective-permute-done.2, pred[]{:T(512)S(6)} %eq.4), kind=kLoop, calls=%fused_computation.39 | loop fusion | flops 120768 | bytes 1449217 | tf_op jit(solution)/shard_map/jit(_where)/select_n | solution.py:420
  50.4 1.4 %slice_bitcast_fusion = (f32[248,384]{1,0:T(8,128)}, f32[248,384]{1,0:T(8,128)}, f32[248,384]{1,0:T(8,128)}, f32[248,384]{1,0:T(8,128)}, f32[248,384]{1,0:T(8,128)}, /*index=5*/f32[248,384]{1,0:T(8,128)}) fusion(f32[6,248,384]{2,1,0:T(8,128)S(1)} %select_maximum_fusion), kind=kLoop, calls=%fused_computation.32 | loop fusion | bytes 4571136 | tf_op jit(solution)/shard_map/squeeze | solution.py:502
  51.8 10.8 %ring_step.1 = (f32[184,256]{1,0:T(8,128)}, f32[184,256]{1,0:T(8,128)}, f32[184,256]{1,0:T(8,128)}, f32[184,256]{1,0:T(8,128)}, f32[184,256]{1,0:T(8,128)}) custom-call(f32[248,384]{1,0:T(8,128)} %get-tuple-element.26.refs_0_, f32[248,384]{1,0:T(8,128)} %get-tuple-element.25.refs_1_, f32[248,384]{1,0:T(8,128)} %get-tuple-element.24.refs_2_, ...), custom_call_target="tpu_custom_call" | custom-call | tf_op jit(solution)/shard_map/ring_step/pallas_call | solution.py:380
  62.7 1.2 %pad_maximum_fusion.1 = f32[3,184,256]{2,1,0:T(8,128)S(1)} fusion(f32[1,184,256]{2,1,0:T(8,128)} %bitcast.55, f32[1,184,256]{2,1,0:T(8,128)} %bitcast.53, f32[1,184,256]{2,1,0:T(8,128)} %bitcast.51), kind=kLoop, calls=%fused_computation.29 | loop fusion | flops 282624 | bytes 1130496 | tf_op jit(solution)/shard_map/stack | solution.py:505
  65.5 5.7 %section_step.2 = (f32[112,128]{1,0:T(8,128)}, f32[112,128]{1,0:T(8,128)}, f32[112,128]{1,0:T(8,128)}, f32[112,128]{1,0:T(8,128)}, f32[112,128]{1,0:T(8,128)}) custom-call(f32[184,256]{1,0:T(8,128)} %get-tuple-element.34.refs_0_, f32[184,256]{1,0:T(8,128)} %get-tuple-element.33.refs_1_, f32[184,256]{1,0:T(8,128)} %get-tuple-element.32.refs_2_, ...), custom_call_target="tpu_custom_call" | custom-call | tf_op jit(solution)/shard_map/section_step/pallas_call | solution.py:397
  72.2 1.9 %collective-permute-start.4 = (f32[3,112,42]{2,1,0:T(8,128)S(1)}, f32[3,112,42]{2,1,0:T(8,128)S(1)}, u32[]{:S(2)}, u32[]{:S(2)}) collective-permute-start(f32[3,112,42]{2,1,0:T(8,128)S(1)} %get-tuple-element.39), channel_id=1, source_target_pairs={{0,16},{16,32},{32,48},{48,64},{64,80},{80,96},{96,112},{112,128},... | collective-permute-start | bytes 169352 | tf_op jit(solution)/shard_map/ppermute | solution.py:411
  74.1 7.5 %collective-permute-start.5 = (f32[3,112,42]{2,1,0:T(8,128)S(1)}, f32[3,112,42]{2,1,0:T(8,128)S(1)}, u32[]{:S(2)}, u32[]{:S(2)}) collective-permute-start(f32[3,112,42]{2,1,0:T(8,128)S(1)} %get-tuple-element.40), channel_id=1, source_target_pairs={{16,0},{32,16},{48,32},{64,48},{80,64},{96,80},{112,96},{128,112},... | collective-permute-start | bytes 169352 | tf_op jit(solution)/shard_map/ppermute | solution.py:414
  81.7 1.4 %collective-permute-done.4 = f32[3,112,42]{2,1,0:T(8,128)S(1)} collective-permute-done((f32[3,112,42]{2,1,0:T(8,128)S(1)}, f32[3,112,42]{2,1,0:T(8,128)S(1)}, u32[]{:S(2)}, u32[]{:S(2)}) %collective-permute-start.4) | collective-permute-done | bytes 56480 | tf_op jit(solution)/shard_map/ppermute | solution.py:411
  83.1 1.5 %collective-permute-done.5 = f32[3,112,42]{2,1,0:T(8,128)S(1)} collective-permute-done((f32[3,112,42]{2,1,0:T(8,128)S(1)}, f32[3,112,42]{2,1,0:T(8,128)S(1)}, u32[]{:S(2)}, u32[]{:S(2)}) %collective-permute-start.5) | collective-permute-done | bytes 56480 | tf_op jit(solution)/shard_map/ppermute | solution.py:414
  84.6 1.0 pad_maximum_fusion.7
  85.6 2.1 %collective-permute-start.7 = (f32[3,34,212]{2,1,0:T(8,128)S(1)}, f32[3,34,212]{2,1,0:T(8,128)S(1)}, u32[]{:S(2)}, u32[]{:S(2)}) collective-permute-start(f32[3,34,212]{2,1,0:T(8,128)S(1)} %get-tuple-element.35), channel_id=1, source_target_pairs={{1,0},{2,1},{3,2},{4,3},{5,4},{6,5},{7,6},{8,7},{9,8},{10,9},{11,1... | collective-permute-start | bytes 259496 | tf_op jit(solution)/shard_map/ppermute | solution.py:26
  87.9 2.3 %collective-permute-start.6 = (f32[3,34,212]{2,1,0:T(8,128)S(1)}, f32[3,34,212]{2,1,0:T(8,128)S(1)}, u32[]{:S(2)}, u32[]{:S(2)}) collective-permute-start(f32[3,34,212]{2,1,0:T(8,128)S(1)} %get-tuple-element.36), channel_id=1, source_target_pairs={{0,1},{1,2},{2,3},{3,4},{4,5},{5,6},{6,7},{7,8},{8,9},{9,10},{10,1... | collective-permute-start | bytes 259496 | tf_op jit(solution)/shard_map/ppermute | solution.py:26
  90.2 6.0 %collective-permute-done.6 = f32[3,34,212]{2,1,0:T(8,128)S(1)} collective-permute-done((f32[3,34,212]{2,1,0:T(8,128)S(1)}, f32[3,34,212]{2,1,0:T(8,128)S(1)}, u32[]{:S(2)}, u32[]{:S(2)}) %collective-permute-start.6) | collective-permute-done | bytes 86528 | tf_op jit(solution)/shard_map/ppermute | solution.py:26
  97.3 5.7 %section_step.3 = (f32[112,128]{1,0:T(8,128)}, f32[112,128]{1,0:T(8,128)}, f32[112,128]{1,0:T(8,128)}, f32[112,128]{1,0:T(8,128)}, f32[112,128]{1,0:T(8,128)}) custom-call(f32[184,256]{1,0:T(8,128)} %get-tuple-element.31.refs_0_, f32[184,256]{1,0:T(8,128)} %get-tuple-element.30.refs_1_, f32[184,256]{1,0:T(8,128)} %get-tuple-element.29.refs_2_, ...), custom_call_target="tpu_custom_call" | custom-call | tf_op jit(solution)/shard_map/section_step/pallas_call | solution.py:397
  (50 shorter events, 11.9 us)
Async XLA Ops:
  6.5 23.7 %copy-start.2 = (f32[14336]{0:T(1024)}, f32[14336]{0:T(1024)S(1)}, u32[]{:S(2)}) copy-start(f32[14336]{0:T(1024)S(1)} %scatter_custom_fusion) | copy-start | bytes 172036
  6.7 21.0 %collective-permute-start = (f32[6,112,84]{2,1,0:T(8,128)S(1)}, f32[6,112,84]{2,1,0:T(8,128)S(1)}, u32[]{:S(2)}, u32[]{:S(2)}) collective-permute-start(f32[6,112,84]{2,1,0:T(8,128)S(1)} %get-tuple-element.37), channel_id=1, source_target_pairs={{0,16},{16,32},{32,48},{48,64},{64,80},{80,96},{96,112},{112,128},... | collective-permute-start | bytes 677384 | tf_op jit(solution)/shard_map/ppermute | solution.py:411
  10.5 18.4 %collective-permute-start.1 = (f32[6,112,84]{2,1,0:T(8,128)S(1)}, f32[6,112,84]{2,1,0:T(8,128)S(1)}, u32[]{:S(2)}, u32[]{:S(2)}) collective-permute-start(f32[6,112,84]{2,1,0:T(8,128)S(1)} %get-tuple-element.38), channel_id=1, source_target_pairs={{16,0},{32,16},{48,32},{64,48},{80,64},{96,80},{112,96},{128,112},... | collective-permute-start | bytes 677384 | tf_op jit(solution)/shard_map/ppermute | solution.py:414
  28.9 0.7 copy-start
  30.1 12.5 %collective-permute-start.3 = (f32[6,68,296]{2,1,0:T(8,128)S(1)}, f32[6,68,296]{2,1,0:T(8,128)}, u32[]{:S(2)}, u32[]{:S(2)}) collective-permute-start(f32[6,68,296]{2,1,0:T(8,128)S(1)} %get-tuple-element.27), channel_id=1, source_target_pairs={{1,0},{2,1},{3,2},{4,3},{5,4},{6,5},{7,6},{8,7},{9,8},{10,9},{11,1... | collective-permute-start | bytes 1449224 | tf_op jit(solution)/shard_map/ppermute | solution.py:26
  34.5 14.2 %collective-permute-start.2 = (f32[6,68,296]{2,1,0:T(8,128)S(1)}, f32[6,68,296]{2,1,0:T(8,128)}, u32[]{:S(2)}, u32[]{:S(2)}) collective-permute-start(f32[6,68,296]{2,1,0:T(8,128)S(1)} %get-tuple-element.28), channel_id=1, source_target_pairs={{0,1},{1,2},{2,3},{3,4},{4,5},{5,6},{6,7},{7,8},{8,9},{9,10},{10,1... | collective-permute-start | bytes 1449224 | tf_op jit(solution)/shard_map/ppermute | solution.py:26
  37.7 12.2 %copy-start.1 = (f32[6,112,84]{2,1,0:T(8,128)S(1)}, f32[6,112,84]{2,1,0:T(8,128)}, u32[]{:S(2)}) copy-start(f32[6,112,84]{2,1,0:T(8,128)} %copy-done) | copy-start | bytes 677380
  62.6 1.4 %copy-start.3 = (f32[184,256]{1,0:T(8,128)S(1)}, f32[184,256]{1,0:T(8,128)}, u32[]{:S(2)}) copy-start(f32[184,256]{1,0:T(8,128)} %get-tuple-element.13) | copy-start | bytes 565252
  62.6 1.4 %copy-start.4 = (f32[184,256]{1,0:T(8,128)S(1)}, f32[184,256]{1,0:T(8,128)}, u32[]{:S(2)}) copy-start(f32[184,256]{1,0:T(8,128)} %get-tuple-element.14) | copy-start | bytes 565252
  62.6 1.4 %copy-start.5 = (f32[184,256]{1,0:T(8,128)S(1)}, f32[184,256]{1,0:T(8,128)}, u32[]{:S(2)}) copy-start(f32[184,256]{1,0:T(8,128)} %get-tuple-element.15) | copy-start | bytes 565252
  71.2 25.1 %copy-start.6 = (f32[112,128]{1,0:T(8,128)S(1)}, f32[112,128]{1,0:T(8,128)}, u32[]{:S(2)}) copy-start(f32[112,128]{1,0:T(8,128)} %get-tuple-element.18) | copy-start | bytes 172036
  71.2 25.1 %copy-start.7 = (f32[112,128]{1,0:T(8,128)S(1)}, f32[112,128]{1,0:T(8,128)}, u32[]{:S(2)}) copy-start(f32[112,128]{1,0:T(8,128)} %get-tuple-element.19) | copy-start | bytes 172036
  71.2 25.1 %copy-start.8 = (f32[112,128]{1,0:T(8,128)S(1)}, f32[112,128]{1,0:T(8,128)}, u32[]{:S(2)}) copy-start(f32[112,128]{1,0:T(8,128)} %get-tuple-element.20) | copy-start | bytes 172036
  72.2 10.9 %collective-permute-start.4 = (f32[3,112,42]{2,1,0:T(8,128)S(1)}, f32[3,112,42]{2,1,0:T(8,128)S(1)}, u32[]{:S(2)}, u32[]{:S(2)}) collective-permute-start(f32[3,112,42]{2,1,0:T(8,128)S(1)} %get-tuple-element.39), channel_id=1, source_target_pairs={{0,16},{16,32},{32,48},{48,64},{64,80},{80,96},{96,112},{112,128},... | collective-permute-start | bytes 169352 | tf_op jit(solution)/shard_map/ppermute | solution.py:411
  74.1 10.4 %collective-permute-start.5 = (f32[3,112,42]{2,1,0:T(8,128)S(1)}, f32[3,112,42]{2,1,0:T(8,128)S(1)}, u32[]{:S(2)}, u32[]{:S(2)}) collective-permute-start(f32[3,112,42]{2,1,0:T(8,128)S(1)} %get-tuple-element.40), channel_id=1, source_target_pairs={{16,0},{32,16},{48,32},{64,48},{80,64},{96,80},{112,96},{128,112},... | collective-permute-start | bytes 169352 | tf_op jit(solution)/shard_map/ppermute | solution.py:414
  85.6 4.6 %collective-permute-start.7 = (f32[3,34,212]{2,1,0:T(8,128)S(1)}, f32[3,34,212]{2,1,0:T(8,128)S(1)}, u32[]{:S(2)}, u32[]{:S(2)}) collective-permute-start(f32[3,34,212]{2,1,0:T(8,128)S(1)} %get-tuple-element.35), channel_id=1, source_target_pairs={{1,0},{2,1},{3,2},{4,3},{5,4},{6,5},{7,6},{8,7},{9,8},{10,9},{11,1... | collective-permute-start | bytes 259496 | tf_op jit(solution)/shard_map/ppermute | solution.py:26
  87.9 8.3 %collective-permute-start.6 = (f32[3,34,212]{2,1,0:T(8,128)S(1)}, f32[3,34,212]{2,1,0:T(8,128)S(1)}, u32[]{:S(2)}, u32[]{:S(2)}) collective-permute-start(f32[3,34,212]{2,1,0:T(8,128)S(1)} %get-tuple-element.36), channel_id=1, source_target_pairs={{0,1},{1,2},{2,3},{3,4},{4,5},{5,6},{6,7},{7,8},{8,9},{9,10},{10,1... | collective-permute-start | bytes 259496 | tf_op jit(solution)/shard_map/ppermute | solution.py:26

commit v16 on v15

--- a/solution.py
+++ b/solution.py
@@ -406,6 +406,22 @@
     )(*fields, place, lift, *initial)
 
 
+def stack_kernel(*refs):
+    for k, field in enumerate(refs[:-1]):
+        refs[-1][k] = field[...]
+
+
+def stacked(fields):
+    spec = pl.BlockSpec(memory_space=pltpu.VMEM)
+    return pl.pallas_call(
+        stack_kernel,
+        out_shape=jax.ShapeDtypeStruct((len(fields),) + fields[0].shape, jnp.float32),
+        in_specs=[spec] * len(fields),
+        out_specs=spec,
+        name="stacked",
+    )(*fields)
+
+
 def halo_box(fields, wide_x, wide_y, place, count, padded_shape):
     lon_count = lax.axis_size("lon")
     west = lax.ppermute(
@@ -495,7 +511,7 @@
     initial = (surface, momentum_x, momentum_y)
 
     big = halo_box(
-        jnp.stack([surface, momentum_x, momentum_y, water_depth, wet_float, lift]),
+        stacked([surface, momentum_x, momentum_y, water_depth, wet_float, lift]),
         2 * wide_x, 2 * wide_y, place, count, ring.padded,
     )
     ring_state = ring_step(

time: 104 us -> 105 us (level)
  local copies, waits for them, and re-layouts: 9.52 us -> 6.5 us
  other arithmetic: 9.37 us -> 11.5 us
  Pallas kernels: 22.1 us -> 23.9 us
    unnamed x22 -> x14, local copies, waits for them, and re-layouts: 4.07 us -> 0.03 us
    pallas_call x0 -> x1, Pallas kernels: none -> 1.71 us  [stacked(): pl.pallas_call(stack_kernel, out_shape=jax.ShapeDtypeStruct((len(fields),...]
    convert_element_type x0 -> x1, other arithmetic: none -> 1.45 us  [local(): wet_float = wet_mask.astype(jnp.float32)]
    slice x2, local copies, waits for them, and re-layouts: 0.27 us -> 1.34 us  [halo_box(): fields[:, :, -wide_x:]]
where the time goes in v16:
time: 105 us; the launch traced here: 104 us
  starting transfers between devices  35 us (33%)
  waiting for transfers between devices  26 us (25%)
  Pallas kernels  23.9 us (23%)
  other arithmetic  11.5 us (11%)
  local copies, waits for them, and re-layouts  6.5 us (6%)
    ppermute x2, starting transfers between devices, halo_box(): lax.ppermute(fields[:, :, :wide_x], 'lon', [((i + 1) % lon_count, i) for...  18.6 us
    ppermute x4, waiting for transfers between devices, passed_along(): return lax.ppermute(x, axis, pairs)  15.8 us
    pallas_call x2, Pallas kernels, section_step(): pl.pallas_call(lambda *refs: section_kernel(*refs, first_row=first_row, u...  11.3 us
    pallas_call x1, Pallas kernels, ring_step(): pl.pallas_call(lambda *refs: ring_kernel(*refs, first_row=first_row, used...  10.8 us
    ppermute x4, starting transfers between devices, passed_along(): return lax.ppermute(x, axis, pairs)  10.6 us
    ppermute x2, waiting for transfers between devices, halo_box(): lax.ppermute(fields[:, :, -wide_x:], 'lon', [(i, (i + 1) % lon_count) for...  7.56 us
    ppermute x2, starting transfers between devices, halo_box(): lax.ppermute(fields[:, :, -wide_x:], 'lon', [(i, (i + 1) % lon_count) for...  5.75 us
    ppermute x2, waiting for transfers between devices, halo_box(): lax.ppermute(fields[:, :, :wide_x], 'lon', [((i + 1) % lon_count, i) for...  2.64 us
  transfers between devices with their start and end apart: 8, of which 7 were waited for; matrix products, arithmetic and copies ran while one was open for 3% of the time, Pallas kernels for 0%

profile of v16, /device:TPU:2, one launch (start us, length us, event | category | flops | bytes accessed | tf_op | source)
XLA Modules:
  0.0 103.8 jit_solution(9529666240587076503)
XLA Ops:
  1.3 1.4 %convert_element_type.7.refs_4_ = f32[112,128]{1,0:T(8,128)} convert(s32[112,128]{1,0:T(8,128)} %param.11) | non-fusion elementwise | flops 14336 | bytes 114688 | tf_op jit(solution)/shard_map/convert_element_type | solution.py:494
  2.7 1.6 %scatter_custom_fusion = f32[14336]{0:T(1024)} fusion(s32[64]{0:T(128)S(1)} %fusion.22, f32[64]{0:T(128)} %bitcast.55, f32[]{:T(128)} %constant.3.clone.1), kind=kCustom, calls=%fused_computation.54 | custom fusion | flops 64 | bytes 57856 | tf_op jit(solution)/shard_map/scatter-add | solution.py:503
  4.4 1.7 %stacked.1 = f32[6,112,128]{2,1,0:T(8,128)} custom-call(f32[112,128]{1,0:T(8,128)} %refs_7_.3, f32[112,128]{1,0:T(8,128)} %refs_8_.3, f32[112,128]{1,0:T(8,128)} %refs_9_.3, f32[112,128]{1,0:T(8,128)} %refs_3_.1, f32[112,128]{1,0:T(8,128)} %convert_element_type.7.refs_4_, f32[112,128]{1,0:T(8,128)} %bitcast.37), custom_call_target="tpu_custom_call" | custom-call | tf_op jit(solution)/shard_map/stacked/pallas_call | solution.py:416
  6.1 1.2 %fusion.24 = (f32[6,112,84]{2,1,0:T(8,128)S(1)}, f32[6,112,84]{2,1,0:T(8,128)S(1)}) fusion(f32[6,112,128]{2,1,0:T(8,128)} %stacked.1), kind=kLoop, calls=%fused_computation.59 | loop fusion | bytes 903168 | tf_op jit(solution)/shard_map/slice | solution.py:428
  7.3 3.8 %collective-permute-start = (f32[6,112,84]{2,1,0:T(8,128)S(1)}, f32[6,112,84]{2,1,0:T(8,128)S(1)}, u32[]{:S(2)}, u32[]{:S(2)}) collective-permute-start(f32[6,112,84]{2,1,0:T(8,128)S(1)} %get-tuple-element.37), channel_id=1, source_target_pairs={{0,16},{16,32},{32,48},{48,64},{64,80},{80,96},{96,112},{112,128},... | collective-permute-start | bytes 677384 | tf_op jit(solution)/shard_map/ppermute | solution.py:427
  11.1 11.1 %collective-permute-start.1 = (f32[6,112,84]{2,1,0:T(8,128)S(1)}, f32[6,112,84]{2,1,0:T(8,128)S(1)}, u32[]{:S(2)}, u32[]{:S(2)}) collective-permute-start(f32[6,112,84]{2,1,0:T(8,128)S(1)} %get-tuple-element.38), channel_id=1, source_target_pairs={{16,0},{32,16},{48,32},{64,48},{80,64},{96,80},{112,96},{128,112},... | collective-permute-start | bytes 677384 | tf_op jit(solution)/shard_map/ppermute | solution.py:430
  22.2 6.1 %collective-permute-done = f32[6,112,84]{2,1,0:T(8,128)S(1)} collective-permute-done((f32[6,112,84]{2,1,0:T(8,128)S(1)}, f32[6,112,84]{2,1,0:T(8,128)S(1)}, u32[]{:S(2)}, u32[]{:S(2)}) %collective-permute-start) | collective-permute-done | bytes 225824 | tf_op jit(solution)/shard_map/ppermute | solution.py:427
  29.5 1.4 %pad_maximum_fusion = f32[6,112,296]{2,1,0:T(8,128)S(1)} fusion(f32[6,112,84]{2,1,0:T(8,128)S(1)} %collective-permute-done.1, f32[6,112,128]{2,1,0:T(8,128)} %stacked.1, f32[6,112,84]{2,1,0:T(8,128)S(1)} %collective-permute-done), kind=kLoop, calls=%fused_computation.9 | loop fusion | flops 397824 | bytes 1591296 | tf_op jit(solution)/shard_map/concatenate | solution.py:433
  31.0 4.4 %collective-permute-start.3 = (f32[6,68,296]{2,1,0:T(8,128)S(1)}, f32[6,68,296]{2,1,0:T(8,128)}, u32[]{:S(2)}, u32[]{:S(2)}) collective-permute-start(f32[6,68,296]{2,1,0:T(8,128)S(1)} %get-tuple-element.27), channel_id=1, source_target_pairs={{1,0},{2,1},{3,2},{4,3},{5,4},{6,5},{7,6},{8,7},{9,8},{10,9},{11,1... | collective-permute-start | bytes 1449224 | tf_op jit(solution)/shard_map/ppermute | solution.py:26
  35.4 1.9 %collective-permute-start.2 = (f32[6,68,296]{2,1,0:T(8,128)S(1)}, f32[6,68,296]{2,1,0:T(8,128)}, u32[]{:S(2)}, u32[]{:S(2)}) collective-permute-start(f32[6,68,296]{2,1,0:T(8,128)S(1)} %get-tuple-element.28), channel_id=1, source_target_pairs={{0,1},{1,2},{2,3},{3,4},{4,5},{5,6},{6,7},{7,8},{8,9},{9,10},{10,1... | collective-permute-start | bytes 1449224 | tf_op jit(solution)/shard_map/ppermute | solution.py:26
  38.6 5.0 %collective-permute-done.3 = f32[6,68,296]{2,1,0:T(8,128)} collective-permute-done((f32[6,68,296]{2,1,0:T(8,128)S(1)}, f32[6,68,296]{2,1,0:T(8,128)}, u32[]{:S(2)}, u32[]{:S(2)}) %collective-permute-start.3) | collective-permute-done | bytes 483104 | tf_op jit(solution)/shard_map/ppermute | solution.py:26
  44.7 4.9 %collective-permute-done.2 = f32[6,68,296]{2,1,0:T(8,128)} collective-permute-done((f32[6,68,296]{2,1,0:T(8,128)S(1)}, f32[6,68,296]{2,1,0:T(8,128)}, u32[]{:S(2)}, u32[]{:S(2)}) %collective-permute-start.2) | collective-permute-done | bytes 483104 | tf_op jit(solution)/shard_map/ppermute | solution.py:26
  51.3 1.5 %slice_bitcast_fusion = (f32[248,384]{1,0:T(8,128)}, f32[248,384]{1,0:T(8,128)}, f32[248,384]{1,0:T(8,128)}, f32[248,384]{1,0:T(8,128)}, f32[248,384]{1,0:T(8,128)}, /*index=5*/f32[248,384]{1,0:T(8,128)}) fusion(f32[6,248,384]{2,1,0:T(8,128)S(1)} %select_maximum_fusion), kind=kLoop, calls=%fused_computation.32 | loop fusion | bytes 4571136 | tf_op jit(solution)/shard_map/squeeze | solution.py:518
  52.7 10.8 %ring_step.1 = (f32[184,256]{1,0:T(8,128)}, f32[184,256]{1,0:T(8,128)}, f32[184,256]{1,0:T(8,128)}, f32[184,256]{1,0:T(8,128)}, f32[184,256]{1,0:T(8,128)}) custom-call(f32[248,384]{1,0:T(8,128)} %get-tuple-element.26.refs_0_, f32[248,384]{1,0:T(8,128)} %get-tuple-element.25.refs_1_, f32[248,384]{1,0:T(8,128)} %get-tuple-element.24.refs_2_, ...), custom_call_target="tpu_custom_call" | custom-call | tf_op jit(solution)/shard_map/ring_step/pallas_call | solution.py:380
  63.5 1.2 %pad_maximum_fusion.1 = f32[3,184,256]{2,1,0:T(8,128)S(1)} fusion(f32[1,184,256]{2,1,0:T(8,128)} %bitcast.44, f32[1,184,256]{2,1,0:T(8,128)} %bitcast.42, f32[1,184,256]{2,1,0:T(8,128)} %bitcast.40), kind=kLoop, calls=%fused_computation.29 | loop fusion | flops 282624 | bytes 1130496 | tf_op jit(solution)/shard_map/stack | solution.py:521
  66.3 5.7 %section_step.2 = (f32[112,128]{1,0:T(8,128)}, f32[112,128]{1,0:T(8,128)}, f32[112,128]{1,0:T(8,128)}, f32[112,128]{1,0:T(8,128)}, f32[112,128]{1,0:T(8,128)}) custom-call(f32[184,256]{1,0:T(8,128)} %get-tuple-element.34.refs_0_, f32[184,256]{1,0:T(8,128)} %get-tuple-element.33.refs_1_, f32[184,256]{1,0:T(8,128)} %get-tuple-element.32.refs_2_, ...), custom_call_target="tpu_custom_call" | custom-call | tf_op jit(solution)/shard_map/section_step/pallas_call | solution.py:397
  73.1 1.9 %collective-permute-start.4 = (f32[3,112,42]{2,1,0:T(8,128)S(1)}, f32[3,112,42]{2,1,0:T(8,128)S(1)}, u32[]{:S(2)}, u32[]{:S(2)}) collective-permute-start(f32[3,112,42]{2,1,0:T(8,128)S(1)} %get-tuple-element.39), channel_id=1, source_target_pairs={{0,16},{16,32},{32,48},{48,64},{64,80},{80,96},{96,112},{112,128},... | collective-permute-start | bytes 169352 | tf_op jit(solution)/shard_map/ppermute | solution.py:427
  75.0 7.5 %collective-permute-start.5 = (f32[3,112,42]{2,1,0:T(8,128)S(1)}, f32[3,112,42]{2,1,0:T(8,128)S(1)}, u32[]{:S(2)}, u32[]{:S(2)}) collective-permute-start(f32[3,112,42]{2,1,0:T(8,128)S(1)} %get-tuple-element.40), channel_id=1, source_target_pairs={{16,0},{32,16},{48,32},{64,48},{80,64},{96,80},{112,96},{128,112},... | collective-permute-start | bytes 169352 | tf_op jit(solution)/shard_map/ppermute | solution.py:430
  82.5 1.4 %collective-permute-done.4 = f32[3,112,42]{2,1,0:T(8,128)S(1)} collective-permute-done((f32[3,112,42]{2,1,0:T(8,128)S(1)}, f32[3,112,42]{2,1,0:T(8,128)S(1)}, u32[]{:S(2)}, u32[]{:S(2)}) %collective-permute-start.4) | collective-permute-done | bytes 56480 | tf_op jit(solution)/shard_map/ppermute | solution.py:427
  84.0 1.5 %collective-permute-done.5 = f32[3,112,42]{2,1,0:T(8,128)S(1)} collective-permute-done((f32[3,112,42]{2,1,0:T(8,128)S(1)}, f32[3,112,42]{2,1,0:T(8,128)S(1)}, u32[]{:S(2)}, u32[]{:S(2)}) %collective-permute-start.5) | collective-permute-done | bytes 56480 | tf_op jit(solution)/shard_map/ppermute | solution.py:430
  86.4 2.1 %collective-permute-start.7 = (f32[3,34,212]{2,1,0:T(8,128)S(1)}, f32[3,34,212]{2,1,0:T(8,128)S(1)}, u32[]{:S(2)}, u32[]{:S(2)}) collective-permute-start(f32[3,34,212]{2,1,0:T(8,128)S(1)} %get-tuple-element.35), channel_id=1, source_target_pairs={{1,0},{2,1},{3,2},{4,3},{5,4},{6,5},{7,6},{8,7},{9,8},{10,9},{11,1... | collective-permute-start | bytes 259496 | tf_op jit(solution)/shard_map/ppermute | solution.py:26
  88.7 2.3 %collective-permute-start.6 = (f32[3,34,212]{2,1,0:T(8,128)S(1)}, f32[3,34,212]{2,1,0:T(8,128)S(1)}, u32[]{:S(2)}, u32[]{:S(2)}) collective-permute-start(f32[3,34,212]{2,1,0:T(8,128)S(1)} %get-tuple-element.36), channel_id=1, source_target_pairs={{0,1},{1,2},{2,3},{3,4},{4,5},{5,6},{6,7},{7,8},{8,9},{9,10},{10,1... | collective-permute-start | bytes 259496 | tf_op jit(solution)/shard_map/ppermute | solution.py:26
  91.0 6.0 %collective-permute-done.6 = f32[3,34,212]{2,1,0:T(8,128)S(1)} collective-permute-done((f32[3,34,212]{2,1,0:T(8,128)S(1)}, f32[3,34,212]{2,1,0:T(8,128)S(1)}, u32[]{:S(2)}, u32[]{:S(2)}) %collective-permute-start.6) | collective-permute-done | bytes 86528 | tf_op jit(solution)/shard_map/ppermute | solution.py:26
  98.1 5.7 %section_step.3 = (f32[112,128]{1,0:T(8,128)}, f32[112,128]{1,0:T(8,128)}, f32[112,128]{1,0:T(8,128)}, f32[112,128]{1,0:T(8,128)}, f32[112,128]{1,0:T(8,128)}) custom-call(f32[184,256]{1,0:T(8,128)} %get-tuple-element.31.refs_0_, f32[184,256]{1,0:T(8,128)} %get-tuple-element.30.refs_1_, f32[184,256]{1,0:T(8,128)} %get-tuple-element.29.refs_2_, ...), custom_call_target="tpu_custom_call" | custom-call | tf_op jit(solution)/shard_map/section_step/pallas_call | solution.py:397
  (42 shorter events, 10.9 us)
Async XLA Ops:
  7.3 21.0 %collective-permute-start = (f32[6,112,84]{2,1,0:T(8,128)S(1)}, f32[6,112,84]{2,1,0:T(8,128)S(1)}, u32[]{:S(2)}, u32[]{:S(2)}) collective-permute-start(f32[6,112,84]{2,1,0:T(8,128)S(1)} %get-tuple-element.37), channel_id=1, source_target_pairs={{0,16},{16,32},{32,48},{48,64},{64,80},{80,96},{96,112},{112,128},... | collective-permute-start | bytes 677384 | tf_op jit(solution)/shard_map/ppermute | solution.py:427
  11.1 18.4 %collective-permute-start.1 = (f32[6,112,84]{2,1,0:T(8,128)S(1)}, f32[6,112,84]{2,1,0:T(8,128)S(1)}, u32[]{:S(2)}, u32[]{:S(2)}) collective-permute-start(f32[6,112,84]{2,1,0:T(8,128)S(1)} %get-tuple-element.38), channel_id=1, source_target_pairs={{16,0},{32,16},{48,32},{64,48},{80,64},{96,80},{112,96},{128,112},... | collective-permute-start | bytes 677384 | tf_op jit(solution)/shard_map/ppermute | solution.py:430
  31.0 12.5 %collective-permute-start.3 = (f32[6,68,296]{2,1,0:T(8,128)S(1)}, f32[6,68,296]{2,1,0:T(8,128)}, u32[]{:S(2)}, u32[]{:S(2)}) collective-permute-start(f32[6,68,296]{2,1,0:T(8,128)S(1)} %get-tuple-element.27), channel_id=1, source_target_pairs={{1,0},{2,1},{3,2},{4,3},{5,4},{6,5},{7,6},{8,7},{9,8},{10,9},{11,1... | collective-permute-start | bytes 1449224 | tf_op jit(solution)/shard_map/ppermute | solution.py:26
  35.4 14.2 %collective-permute-start.2 = (f32[6,68,296]{2,1,0:T(8,128)S(1)}, f32[6,68,296]{2,1,0:T(8,128)}, u32[]{:S(2)}, u32[]{:S(2)}) collective-permute-start(f32[6,68,296]{2,1,0:T(8,128)S(1)} %get-tuple-element.28), channel_id=1, source_target_pairs={{0,1},{1,2},{2,3},{3,4},{4,5},{5,6},{6,7},{7,8},{8,9},{9,10},{10,1... | collective-permute-start | bytes 1449224 | tf_op jit(solution)/shard_map/ppermute | solution.py:26
  38.6 12.2 %copy-start = (f32[6,112,128]{2,1,0:T(8,128)S(1)}, f32[6,112,128]{2,1,0:T(8,128)}, u32[]{:S(2)}) copy-start(f32[6,112,128]{2,1,0:T(8,128)} %stacked.1) | copy-start | bytes 1032196
  63.5 1.4 %copy-start.1 = (f32[184,256]{1,0:T(8,128)S(1)}, f32[184,256]{1,0:T(8,128)}, u32[]{:S(2)}) copy-start(f32[184,256]{1,0:T(8,128)} %get-tuple-element.13) | copy-start | bytes 565252
  63.5 1.4 %copy-start.2 = (f32[184,256]{1,0:T(8,128)S(1)}, f32[184,256]{1,0:T(8,128)}, u32[]{:S(2)}) copy-start(f32[184,256]{1,0:T(8,128)} %get-tuple-element.14) | copy-start | bytes 565252
  63.5 1.4 %copy-start.3 = (f32[184,256]{1,0:T(8,128)S(1)}, f32[184,256]{1,0:T(8,128)}, u32[]{:S(2)}) copy-start(f32[184,256]{1,0:T(8,128)} %get-tuple-element.15) | copy-start | bytes 565252
  72.0 25.1 %copy-start.4 = (f32[112,128]{1,0:T(8,128)S(1)}, f32[112,128]{1,0:T(8,128)}, u32[]{:S(2)}) copy-start(f32[112,128]{1,0:T(8,128)} %get-tuple-element.18) | copy-start | bytes 172036
  72.0 25.1 %copy-start.5 = (f32[112,128]{1,0:T(8,128)S(1)}, f32[112,128]{1,0:T(8,128)}, u32[]{:S(2)}) copy-start(f32[112,128]{1,0:T(8,128)} %get-tuple-element.19) | copy-start | bytes 172036
  72.0 25.1 %copy-start.6 = (f32[112,128]{1,0:T(8,128)S(1)}, f32[112,128]{1,0:T(8,128)}, u32[]{:S(2)}) copy-start(f32[112,128]{1,0:T(8,128)} %get-tuple-element.20) | copy-start | bytes 172036
  73.1 10.9 %collective-permute-start.4 = (f32[3,112,42]{2,1,0:T(8,128)S(1)}, f32[3,112,42]{2,1,0:T(8,128)S(1)}, u32[]{:S(2)}, u32[]{:S(2)}) collective-permute-start(f32[3,112,42]{2,1,0:T(8,128)S(1)} %get-tuple-element.39), channel_id=1, source_target_pairs={{0,16},{16,32},{32,48},{48,64},{64,80},{80,96},{96,112},{112,128},... | collective-permute-start | bytes 169352 | tf_op jit(solution)/shard_map/ppermute | solution.py:427
  75.0 10.4 %collective-permute-start.5 = (f32[3,112,42]{2,1,0:T(8,128)S(1)}, f32[3,112,42]{2,1,0:T(8,128)S(1)}, u32[]{:S(2)}, u32[]{:S(2)}) collective-permute-start(f32[3,112,42]{2,1,0:T(8,128)S(1)} %get-tuple-element.40), channel_id=1, source_target_pairs={{16,0},{32,16},{48,32},{64,48},{80,64},{96,80},{112,96},{128,112},... | collective-permute-start | bytes 169352 | tf_op jit(solution)/shard_map/ppermute | solution.py:430
  86.4 4.6 %collective-permute-start.7 = (f32[3,34,212]{2,1,0:T(8,128)S(1)}, f32[3,34,212]{2,1,0:T(8,128)S(1)}, u32[]{:S(2)}, u32[]{:S(2)}) collective-permute-start(f32[3,34,212]{2,1,0:T(8,128)S(1)} %get-tuple-element.35), channel_id=1, source_target_pairs={{1,0},{2,1},{3,2},{4,3},{5,4},{6,5},{7,6},{8,7},{9,8},{10,9},{11,1... | collective-permute-start | bytes 259496 | tf_op jit(solution)/shard_map/ppermute | solution.py:26
  88.7 8.3 %collective-permute-start.6 = (f32[3,34,212]{2,1,0:T(8,128)S(1)}, f32[3,34,212]{2,1,0:T(8,128)S(1)}, u32[]{:S(2)}, u32[]{:S(2)}) collective-permute-start(f32[3,34,212]{2,1,0:T(8,128)S(1)} %get-tuple-element.36), channel_id=1, source_target_pairs={{0,1},{1,2},{2,3},{3,4},{4,5},{5,6},{6,7},{7,8},{8,9},{9,10},{10,1... | collective-permute-start | bytes 259496 | tf_op jit(solution)/shard_map/ppermute | solution.py:26
